TPU v7x, 128 devices: a whole 4x4x4 slice. The times are simulated.
128 devices in a mesh: grp: 4 (over y_lo, core), band: 32 (over y_hi, x, z).
Axes of the slice: x: 4, y: 4 (y_hi: 2, y_lo: 2; y = y_hi * 2 + y_lo), z: 4, core: 2. Of those that a mesh axis runs over, the one named last changes fastest.
Arguments:
- prior_samples: bfloat16 [32, 69, 64, 1024], P('grp', None, 'band'), may hold values from -6 to 6
- conv1_weight: bfloat16 [3, 3, 256, 69], replicated, may hold values from -0.25 to 0.25
- conv1_bias: float32 [256], replicated, may hold values from -3 to 3
- conv2_weight: bfloat16 [3, 3, 69, 256], replicated, may hold values from -0.125 to 0.125
- conv2_bias: float32 [69], replicated, may hold values from -3 to 3
- obs_index: int32 [256, 256], P(('grp', 'band')), may hold values from 0 to 17663
- obs_values: float32 [256, 256], P(('grp', 'band')), may hold values from -6 to 6
- obs_prec: float32 [256, 256], P(('grp', 'band')), may hold values from 0.25 to 4
- neighbours: int32 [256, 8], P(('grp', 'band')), may hold values from 0 to 255
- loc_weight: float32 [256, 8], P(('grp', 'band')), may hold values from 0.2 to 1
Outputs:
- analysis: float32 [32, 69, 64, 1024], P(None, None, 'band', 'grp')
Inputs may be any that keep to these rules, and one draw needn't show every extreme that they name: `neighbours`: neighbour patch numbers; a number may repeat or name the patch itself. `obs_index`: observed entry as channel * 256 + column within the patch.
All inputs are finite; a program needn't handle non-finite values.
Results may differ from a plain program's by a relative error of at most 0.0021.
Values may be sent and summed in bfloat16 or wider, within the bound.
No kernel may reach another device: no remote copies, remote signals or barrier semaphores. Data moves between devices by JAX's collectives and lax.ppermute only.
A program may use at most 128 MiB of HBM per device.

v0:
```python
import jax
import jax.numpy as jnp
from jax import lax
from jax.sharding import PartitionSpec as P

NS_ITERS = 6


def padded_2(cells, sides, width):
    for axis, dim in sides:
        count = lax.axis_size(axis)
        ends = count - 1
        head = lax.slice_in_dim(cells, 0, width, axis=dim)
        tail = lax.slice_in_dim(cells, cells.shape[dim] - width, cells.shape[dim], axis=dim)
        cells = jnp.concatenate(
            [
                lax.ppermute(tail, axis, [(i, (i + 1) % count) for i in range(ends)]),
                cells,
                lax.ppermute(head, axis, [((i + 1) % count, i) for i in range(ends)]),
            ],
            axis=dim,
        )
    return cells


def from_behind(block, axis, distance):
    devices = range(lax.axis_size(axis))
    route = [(i - distance, i) for i in devices if i - distance in devices]
    return lax.ppermute(block, axis, route)


def convolve(padded, kernel, height):
    summed = jnp.zeros((kernel.shape[2], height, padded.shape[2]), jnp.float32)
    for row_shift in range(3):
        window = padded[:, row_shift : row_shift + height, :]
        for col_shift in range(3):
            shifted = jnp.roll(window, 1 - col_shift, axis=2)
            summed = summed + jnp.einsum(
                "oc,crl->orl",
                kernel[row_shift, col_shift],
                shifted,
                preferred_element_type=jnp.float32,
            )
    return summed


def grams_of(perturb, obs_prec, innovation):
    highest = lax.Precision.HIGHEST
    gram_local = jnp.einsum("pmo,po,pno->pmn", perturb, obs_prec, perturb, precision=highest)
    pull_vec = jnp.einsum("pmo,po->pm", perturb, obs_prec * innovation, precision=highest)
    return (gram_local, pull_vec)


def on_device(
    prior_samples,
    conv1_weight,
    conv1_bias,
    conv2_weight,
    conv2_bias,
    obs_index,
    obs_values,
    obs_prec,
    neighbours,
    loc_weight,
):
    highest = lax.Precision.HIGHEST
    height = prior_samples.shape[2]
    padded = padded_2(prior_samples, (("band", 2),), 1)

    def first_layer(member):
        return jax.nn.silu(
            convolve(member, conv1_weight, height) + conv1_bias[:, None, None]
        ).astype(jnp.bfloat16)

    hidden_fields = lax.map(first_layer, padded)
    northern_halo = from_behind(hidden_fields[:, :, height - 1 :, :], "band", 1)
    southern_halo = from_behind(hidden_fields[:, :, :1, :], "band", -1)

    def output_layer(inputs):
        member, own_rows, above_row, below_row = inputs
        extended = jnp.concatenate([above_row, own_rows, below_row], axis=1)
        summed = (
            member.astype(jnp.float32)
            + convolve(extended, conv2_weight, height)
            + conv2_bias[:, None, None]
        )
        return summed.astype(jnp.bfloat16)

    predicted_samples = lax.map(
        output_layer, (prior_samples, hidden_fields, northern_halo, southern_halo)
    )
    patch_block_slice = lax.all_to_all(
        predicted_samples, "grp", split_axis=3, concat_axis=0, tiled=True
    )
    ensemble = patch_block_slice.shape[0]
    channels = patch_block_slice.shape[1]
    patch_width = patch_block_slice.shape[3]
    realization_grid = jnp.transpose(patch_block_slice, (2, 0, 1, 3)).reshape(
        height, ensemble, channels * patch_width
    )
    count_obs = obs_index.shape[1]
    chosen = jnp.broadcast_to(obs_index[:, None, :], (height, ensemble, count_obs))
    predicted = jnp.take_along_axis(realization_grid, chosen, axis=2).astype(jnp.float32)
    predicted_mean = jnp.mean(predicted, axis=1)
    perturb = predicted - predicted_mean[:, None, :]
    innovation = obs_values - predicted_mean
    gram_local, pull_vec = grams_of(perturb, obs_prec, innovation)
    total_patches = height * lax.axis_size("grp") * lax.axis_size("band")
    patch_ids = jnp.arange(total_patches, dtype=jnp.int32)
    matches = (neighbours[:, :, None] == patch_ids[None, None, :]).astype(jnp.float32)
    spread_weights = jnp.sum(loc_weight[:, :, None] * matches, axis=1)
    piece_gram, piece_pull = grams_of(
        lax.all_gather(perturb, ("grp", "band"), axis=0, tiled=True),
        lax.all_gather(obs_prec, ("grp", "band"), axis=0, tiled=True),
        lax.all_gather(innovation, ("grp", "band"), axis=0, tiled=True),
    )
    gram_sum = jnp.einsum("pj,jab->pab", spread_weights, piece_gram, precision=highest)
    pull_sum = jnp.einsum("pj,ja->pa", spread_weights, piece_pull, precision=highest)
    identity = jnp.broadcast_to(jnp.eye(ensemble, dtype=jnp.float32), (height, ensemble, ensemble))
    matrix = (ensemble - 1.0) * identity + gram_local + gram_sum
    pulled = pull_vec + pull_sum
    norm_scale = jnp.sqrt(jnp.sum(matrix * matrix, axis=(1, 2)))
    sqrt_iter = matrix / norm_scale[:, None, None]
    inverse_root = identity
    for sweep in range(NS_ITERS):
        half_step = 1.5 * identity - 0.5 * jnp.einsum(
            "pab,pbc->pac", inverse_root, sqrt_iter, precision=highest
        )
        sqrt_iter = jnp.einsum("pab,pbc->pac", sqrt_iter, half_step, precision=highest)
        inverse_root = jnp.einsum("pab,pbc->pac", half_step, inverse_root, precision=highest)
    once_applied = jnp.einsum("pab,pb->pa", inverse_root, pulled, precision=highest)
    mean_weight = (
        jnp.einsum("pab,pb->pa", inverse_root, once_applied, precision=highest)
        / norm_scale[:, None]
    )
    transform = (jnp.sqrt(ensemble - 1.0) / jnp.sqrt(norm_scale))[
        :, None, None
    ] * inverse_root + mean_weight[:, :, None]
    field = realization_grid.astype(jnp.float32)
    centre = jnp.mean(field, axis=1)
    spread = field - centre[:, None, :]
    analysed = centre[:, None, :] + jnp.einsum("pkm,pkc->pmc", transform, spread, precision=highest)
    return analysed.reshape(height, ensemble, channels, patch_width).transpose(1, 2, 0, 3)


def solution(mesh):
    placed = (
        P("grp", None, "band", None),
        P(),
        P(),
        P(),
        P(),
        P(("grp", "band"), None),
        P(("grp", "band"), None),
        P(("grp", "band"), None),
        P(("grp", "band"), None),
        P(("grp", "band"), None),
    )
    return jax.shard_map(
        on_device,
        mesh=mesh,
        in_specs=placed,
        out_specs=P(None, None, "band", "grp"),
        check_vma=False,
    )
```

profile of v0, /device:TPU:48, one launch (start us, length us, event | category | flops | bytes accessed | tf_op | source)
XLA Modules:
  0.0 1311.0 jit_solution(5187582412730233797)
XLA Ops:
  6.5 5.9 fusion.156
  12.9 4.0 collective-permute-start
  16.9 1.4 copy.95
  18.3 2.0 collective-permute-start.1
  21.0 20.6 %collective-permute-done = bf16[8,69,1,1024]{3,0,2,1:T(8,128)(2,1)} collective-permute-done((bf16[8,69,1,1024]{3,0,2,1:T(8,128)(2,1)S(1)}, bf16[8,69,1,1024]{3,0,2,1:T(8,128)(2,1)}, u32[]{:S(2)}, u32[]{:S(2)}) %collective-permute-start) | collective-permute-done | bytes 1130528 | tf_op jit(solution)/shard_map/ppermute | solution.py:17
  41.7 1.9 copy.66
  43.6 3.3 collective-permute-done.1
  46.8 1.9 copy.68
  48.7 2.5 pad_maximum_fusion.6
  51.3 73.3 %while.20 = (s32[]{:T(128)}, bf16[8,256,2,1024]{3,1,2,0:T(8,128)(2,1)}, bf16[8,69,4,1024]{3,1,2,0:T(8,128)(2,1)}, bf16[3,3,256,69]{2,3,1,0:T(8,128)(2,1)S(1)}, f32[256]{0:T(256)S(1)}, /*index=5*/s32[]{:T(128)}) while((s32[]{:T(128)}, bf16[8,256,2,1024]{3,1,2,0:T(8,128)(2,1)}, bf16[8,69,4,1024]{3,1,2,0:T(8,128)(2,1)}, ...), condition=%wide.region_1.2_spmd, body=%wide.region_0.1_spmd.sunk | while | flops 661897216 | bytes 47412808 | solution.py:75
  124.5 6.1 fusion.155
  130.6 3.5 collective-permute-start.2
  134.1 4.2 collective-permute-start.3
  138.4 87.3 %collective-permute-done.2 = bf16[8,256,1,1024]{3,1,2,0:T(8,128)(2,1)} collective-permute-done((bf16[8,256,1,1024]{3,1,2,0:T(8,128)(2,1)}, bf16[8,256,1,1024]{3,1,2,0:T(8,128)(2,1)}, u32[]{:S(2)}, u32[]{:S(2)}) %collective-permute-start.2) | collective-permute-done | bytes 4194336 | tf_op jit(solution)/shard_map/ppermute | solution.py:29
  225.7 2.4 collective-permute-done.3
  228.0 70.6 %while.21 = (s32[]{:T(128)}, bf16[8,69,2,1024]{3,1,2,0:T(8,128)(2,1)S(1)}, bf16[8,69,2,1024]{3,1,2,0:T(8,128)(2,1)}, bf16[8,256,1,1024]{3,1,2,0:T(8,128)(2,1)}, ...) while((s32[]{:T(128)}, ...), condition=%wide.region_3.4_spmd, body=%wide.region_2.3_spmd.sunk | while | flops 675929088 | bytes 41343592 | solution.py:89
  228.0 1.3 dynamic-slice_bitcast_fusion.9
  230.6 1.4 fusion.307
  236.9 1.3 dynamic-slice_bitcast_fusion.9
  239.4 1.4 fusion.307
  245.7 1.3 dynamic-slice_bitcast_fusion.9
  248.3 1.4 fusion.307
  254.5 1.3 dynamic-slice_bitcast_fusion.9
  257.1 1.4 fusion.307
  263.3 1.3 dynamic-slice_bitcast_fusion.9
  265.9 1.4 fusion.307
  272.1 1.3 dynamic-slice_bitcast_fusion.9
  274.7 1.4 fusion.307
  281.0 1.3 dynamic-slice_bitcast_fusion.9
  283.5 1.4 fusion.307
  289.8 1.3 dynamic-slice_bitcast_fusion.9
  292.4 1.4 fusion.307
  298.6 7.7 copy.73
  306.3 5.0 all-to-all-start
  311.4 48.1 %all-to-all-done = bf16[8,69,2,1024]{1,2,0,3:T(2,128)(2,1)} async-done(((bf16[8,69,2,1024]{1,2,0,3:T(2,128)(2,1)}), bf16[8,69,2,1024]{1,2,0,3:T(2,128)(2,1)}, u32[]{:S(2)}, u32[]{:S(2)}) %all-to-all-start) | async-done | bytes 2261024 | tf_op jit(solution)/shard_map/all_to_all | solution.py:92
  359.5 10.5 copy.90
  370.0 2.7 copy.91
  372.7 3.1 reshape.45
  375.9 159.3 %gather_fusion = bf16[16384]{0:T(1024)(128)(2,1)S(1)} fusion(bf16[2,32,17664]{2,1,0:T(8,128)(2,1)S(1)} %reshape.45, s32[16384]{0:T(1024)S(1)} %bitcast.273), kind=kCustom, calls=%fused_computation | custom fusion | bytes 262144 | tf_op jit(solution)/shard_map/jit(take_along_axis)/gather | solution.py:103
  535.9 356.6 %all-gather = f32[128,2,256]{2,1,0:T(2,128)S(1)} all-gather(f32[1,2,256]{2,1,0:T(2,128)S(1)} %bitcast.281), channel_id=1, replica_groups=mesh['grp'=4,'band'=32] {'grp','band'}, dimensions={0}, use_global_device_ids=true | all-gather | bytes 264192 | tf_op jit(solution)/shard_map/all_gather | solution.py:114
  892.8 356.1 %all-gather.1 = f32[128,2,256]{2,1,0:T(2,128)S(1)} all-gather(f32[1,2,256]{2,1,0:T(2,128)S(1)} %get-tuple-element.172), channel_id=1, replica_groups=mesh['grp'=4,'band'=32] {'grp','band'}, dimensions={0}, use_global_device_ids=true | all-gather | bytes 264192 | tf_op jit(solution)/shard_map/all_gather | solution.py:115
  1249.3 2.9 convert_reduce_fusion
  1252.3 14.7 %fusion.116 = f32[256,32,32]{2,1,0:T(8,128)S(1)} fusion(f32[256,32,256]{2,1,0:T(8,128)} %all-gather.4.cloned.1.call-done, f32[256,256]{1,0:T(8,128)S(1)} %reshape.55), kind=kOutput, calls=%fused_computation.146 | convolution fusion | flops 807403520 | bytes 9699328 | tf_op jit(solution)/shard_map/pmo,po,pno->pmn/dot_general | solution.py:49
  1267.0 4.3 fusion.120
  1274.7 9.9 fusion.131
  1285.2 5.6 convolution_add_fusion.7
  1290.8 5.1 reshape.46
  1296.0 7.9 copy.80
  (271 shorter events, 128.0 us)
Async XLA Ops:
  12.9 7.4 copy-start
  12.9 28.8 %collective-permute-start = (bf16[8,69,1,1024]{3,0,2,1:T(8,128)(2,1)S(1)}, bf16[8,69,1,1024]{3,0,2,1:T(8,128)(2,1)}, u32[]{:S(2)}, u32[]{:S(2)}) collective-permute-start(bf16[8,69,1,1024]{3,0,2,1:T(8,128)(2,1)S(1)} %copy.94), channel_id=1, source_target_pairs={{0,1},{1,2},{2,3},{3,4},{4,5},{5,6},{6,7},{7,8},{8,9},{9,10},{10,1... | collective-permute-start | bytes 3391496 | tf_op jit(solution)/shard_map/ppermute | solution.py:17
  18.3 28.6 %collective-permute-start.1 = (bf16[8,69,1,1024]{3,0,2,1:T(8,128)(2,1)}, bf16[8,69,1,1024]{3,0,2,1:T(8,128)(2,1)}, u32[]{:S(2)}, u32[]{:S(2)}) collective-permute-start(bf16[8,69,1,1024]{3,0,2,1:T(8,128)(2,1)} %copy.95), channel_id=1, source_target_pairs={{1,0},{2,1},{3,2},{4,3},{5,4},{6,5},{7,6},{8,7},{9,8},{10,9},{11,1... | collective-permute-start | bytes 3391496 | tf_op jit(solution)/shard_map/ppermute | solution.py:19
  21.0 27.7 %copy-start.2 = (bf16[8,69,2,1024]{3,1,2,0:T(8,128)(2,1)}, bf16[8,69,2,1024]{3,1,2,0:T(8,128)(2,1)S(1)}, u32[]{:S(2)}) copy-start(bf16[8,69,2,1024]{3,1,2,0:T(8,128)(2,1)S(1)} %copy.71) | copy-start | bytes 6782980
  48.7 2.6 copy-start.3
  48.7 2.5 copy-start.6
  124.5 103.5 %copy-start.4 = (bf16[3,3,69,256]{3,2,1,0:T(8,128)(2,1)S(1)}, bf16[3,3,69,256]{3,2,1,0:T(8,128)(2,1)}, u32[]{:S(2)}) copy-start(bf16[3,3,69,256]{3,2,1,0:T(8,128)(2,1)} %param.17) | copy-start | bytes 953860
  124.5 103.5 %copy-start.11 = (f32[69]{0:T(128)S(1)}, f32[69]{0:T(128)}, u32[]{:S(2)}) copy-start(f32[69]{0:T(128)} %param.18) | copy-start | bytes 832
  130.6 95.0 %collective-permute-start.2 = (bf16[8,256,1,1024]{3,1,2,0:T(8,128)(2,1)}, bf16[8,256,1,1024]{3,1,2,0:T(8,128)(2,1)}, u32[]{:S(2)}, u32[]{:S(2)}) collective-permute-start(bf16[8,256,1,1024]{3,1,2,0:T(8,128)(2,1)} %get-tuple-element.169), channel_id=1, source_target_pairs={{0,1},{1,2},{2,3},{3,4},{4,5},{5,6},{6,7},{7,8},{8,9},{9,10},{10,1... | collective-permute-start | bytes 12582920 | tf_op jit(solution)/shard_map/ppermute | solution.py:29
  134.1 93.9 %collective-permute-start.3 = (bf16[8,256,1,1024]{3,1,2,0:T(8,128)(2,1)}, bf16[8,256,1,1024]{3,1,2,0:T(8,128)(2,1)}, u32[]{:S(2)}, u32[]{:S(2)}) collective-permute-start(bf16[8,256,1,1024]{3,1,2,0:T(8,128)(2,1)} %get-tuple-element.168), channel_id=1, source_target_pairs={{1,0},{2,1},{3,2},{4,3},{5,4},{6,5},{7,6},{8,7},{9,8},{10,9},{11,1... | collective-permute-start | bytes 12582920 | tf_op jit(solution)/shard_map/ppermute | solution.py:29
  306.3 5.0 copy-start.5
  306.3 53.2 %all-to-all-start = ((bf16[8,69,2,1024]{1,2,0,3:T(2,128)(2,1)}), bf16[8,69,2,1024]{1,2,0,3:T(2,128)(2,1)}, u32[]{:S(2)}, u32[]{:S(2)}) async-start(bf16[8,69,2,1024]{1,2,0,3:T(2,128)(2,1)} %copy.73), calls=%async_computation | async-start | bytes 8388608 | tf_op jit(solution)/shard_map/all_to_all | solution.py:92
  311.3 941.0 %all-gather.4.cloned.1.call-start = ((), (), s32[]{:S(2)}) async-start(), calls=%async_computation.1 | async-start | bytes 8454144 | tf_op jit(solution)/shard_map/all_gather | solution.py:113
  370.0 2.7 copy-start.1
  375.8 159.4 %copy-start.7 = (f32[2,256]{1,0:T(2,128)S(1)}, f32[2,256]{1,0:T(2,128)}, u32[]{:S(2)}) copy-start(f32[2,256]{1,0:T(2,128)} %param.21) | copy-start | bytes 6148
  375.8 159.4 %copy-start.8 = (f32[2,256]{1,0:T(2,128)S(1)}, f32[2,256]{1,0:T(2,128)}, u32[]{:S(2)}) copy-start(f32[2,256]{1,0:T(2,128)} %param.20) | copy-start | bytes 6148
  375.8 516.9 %copy-start.9 = (f32[2,8]{1,0:T(2,128)S(1)}, f32[2,8]{1,0:T(2,128)}, u32[]{:S(2)}) copy-start(f32[2,8]{1,0:T(2,128)} %param.23) | copy-start | bytes 196
  375.8 516.9 %copy-start.10 = (s32[2,8]{1,0:T(2,128)S(1)}, s32[2,8]{1,0:T(2,128)}, u32[]{:S(2)}) copy-start(s32[2,8]{1,0:T(2,128)} %param.22) | copy-start | bytes 196
Sparse Core Ops, SparseCore 0:
  536.0 320.7 all-gather.3
where the time goes:
time: 1320 us; the launch traced here: 1310 us
  blocking collectives  713 us (54%)
  local copies, waits for them, and re-layouts  261 us (20%)
  waiting for transfers between devices  162 us (12%)
  matrix products  123 us (9%)
  starting transfers between devices  18.7 us (1%)
  other arithmetic  18.6 us (1%)
  between operations  14.1 us (1%)
    all_gather x1, blocking collectives, on_device(): lax.all_gather(obs_prec, ('grp', 'band'), axis=0, tiled=True)  357 us
    all_gather x1, blocking collectives, on_device(): lax.all_gather(innovation, ('grp', 'band'), axis=0, tiled=True)  356 us
    gather x2, local copies, waits for them, and re-layouts, on_device(): jnp.take_along_axis(realization_grid, chosen, axis=2).astype(jnp.float32)  159 us
    ppermute x2, waiting for transfers between devices, from_behind(): return lax.ppermute(block, axis, route)  89.7 us
    dot_general x144, matrix products, convolve(): jnp.einsum('oc,crl->orl', kernel[row_shift, col_shift], shifted, preferre...  84.6 us
    all_to_all x1, waiting for transfers between devices, on_device(): lax.all_to_all(predicted_samples, 'grp', split_axis=3, concat_axis=0, til...  48.1 us
  transfers between devices with their start and end apart: 6, of which 5 were waited for; matrix products, arithmetic and copies ran while one was open for 1% of the time, Pallas kernels for 0%

commit v1 on v0

v1 whole, which is shorter than its diff:
```python
import jax
import jax.numpy as jnp
import numpy as np
from jax import lax
from jax.sharding import Mesh
from jax.sharding import PartitionSpec as P

NS_ITERS = 6

GRP = ("y_lo", "core")
BAND = ("y_hi", "x", "z")
GATHER_ORDER = ("z", "x", "y_hi", "core", "y_lo")


def shift_pairs(count, step):
    return [(i, i + step) for i in range(count) if 0 <= i + step < count]


def padded_2(cells, band_size, width):
    head = lax.slice_in_dim(cells, 0, width, axis=2)
    tail = lax.slice_in_dim(cells, cells.shape[2] - width, cells.shape[2], axis=2)
    return jnp.concatenate(
        [
            lax.ppermute(tail, BAND, shift_pairs(band_size, 1)),
            cells,
            lax.ppermute(head, BAND, shift_pairs(band_size, -1)),
        ],
        axis=2,
    )


def convolve(padded, kernel, height):
    summed = jnp.zeros((kernel.shape[2], height, padded.shape[2]), jnp.float32)
    for row_shift in range(3):
        window = padded[:, row_shift : row_shift + height, :]
        for col_shift in range(3):
            shifted = jnp.roll(window, 1 - col_shift, axis=2)
            summed = summed + jnp.einsum(
                "oc,crl->orl",
                kernel[row_shift, col_shift],
                shifted,
                preferred_element_type=jnp.float32,
            )
    return summed


def make_on_device(band_size):
    def on_device(
        prior_samples,
        conv1_weight,
        conv1_bias,
        conv2_weight,
        conv2_bias,
        obs_index,
        obs_values,
        obs_prec,
        neighbours,
        loc_weight,
    ):
        highest = lax.Precision.HIGHEST
        height = prior_samples.shape[2]
        padded = padded_2(prior_samples, band_size, 1)

        def first_layer(member):
            return jax.nn.silu(
                convolve(member, conv1_weight, height) + conv1_bias[:, None, None]
            ).astype(jnp.bfloat16)

        hidden_fields = lax.map(first_layer, padded)
        northern_halo = lax.ppermute(
            hidden_fields[:, :, height - 1 :, :], BAND, shift_pairs(band_size, 1)
        )
        southern_halo = lax.ppermute(
            hidden_fields[:, :, :1, :], BAND, shift_pairs(band_size, -1)
        )

        def output_layer(inputs):
            member, own_rows, above_row, below_row = inputs
            extended = jnp.concatenate([above_row, own_rows, below_row], axis=1)
            summed = (
                member.astype(jnp.float32)
                + convolve(extended, conv2_weight, height)
                + conv2_bias[:, None, None]
            )
            return summed.astype(jnp.bfloat16)

        predicted_samples = lax.map(
            output_layer, (prior_samples, hidden_fields, northern_halo, southern_halo)
        )
        patch_block_slice = lax.all_to_all(
            predicted_samples, GRP, split_axis=3, concat_axis=0, tiled=True
        )
        ensemble = patch_block_slice.shape[0]
        channels = patch_block_slice.shape[1]
        patch_width = patch_block_slice.shape[3]

        column = obs_index % patch_width
        channel = obs_index // patch_width
        column_hot = (
            column[:, :, None] == jnp.arange(patch_width, dtype=jnp.int32)[None, None, :]
        ).astype(jnp.bfloat16)
        by_column = jnp.einsum(
            "mcil,iol->icmo", patch_block_slice, column_hot,
            preferred_element_type=jnp.float32,
        )
        channel_hot = (
            channel[:, None, :] == jnp.arange(channels, dtype=jnp.int32)[None, :, None]
        ).astype(jnp.float32)
        predicted = jnp.sum(by_column * channel_hot[:, :, None, :], axis=1)

        predicted_mean = jnp.mean(predicted, axis=1)
        perturb = predicted - predicted_mean[:, None, :]
        innovation = obs_values - predicted_mean
        gram_local = jnp.einsum(
            "pmo,po,pno->pmn", perturb, obs_prec, perturb, precision=highest
        )
        pull_vec = jnp.einsum(
            "pmo,po->pm", perturb, obs_prec * innovation, precision=highest
        )
        count = gram_local.shape[0]
        packed = jnp.concatenate(
            [gram_local.reshape(count, ensemble * ensemble), pull_vec], axis=1
        )
        for axis in GATHER_ORDER:
            packed = lax.all_gather(packed, axis, axis=0, tiled=False)
        packed = packed.reshape(-1, ensemble * ensemble + ensemble)
        total_patches = packed.shape[0]
        patch_ids = jnp.arange(total_patches, dtype=jnp.int32)
        matches = (neighbours[:, :, None] == patch_ids[None, None, :]).astype(jnp.float32)
        spread_weights = jnp.sum(loc_weight[:, :, None] * matches, axis=1)
        summed = jnp.einsum("pj,jf->pf", spread_weights, packed, precision=highest)
        gram_sum = summed[:, : ensemble * ensemble].reshape(count, ensemble, ensemble)
        pull_sum = summed[:, ensemble * ensemble :]
        identity = jnp.broadcast_to(
            jnp.eye(ensemble, dtype=jnp.float32), (height, ensemble, ensemble)
        )
        matrix = (ensemble - 1.0) * identity + gram_local + gram_sum
        pulled = pull_vec + pull_sum
        norm_scale = jnp.sqrt(jnp.sum(matrix * matrix, axis=(1, 2)))
        sqrt_iter = matrix / norm_scale[:, None, None]
        inverse_root = identity
        for sweep in range(NS_ITERS):
            half_step = 1.5 * identity - 0.5 * jnp.einsum(
                "pab,pbc->pac", inverse_root, sqrt_iter, precision=highest
            )
            sqrt_iter = jnp.einsum("pab,pbc->pac", sqrt_iter, half_step, precision=highest)
            inverse_root = jnp.einsum("pab,pbc->pac", half_step, inverse_root, precision=highest)
        once_applied = jnp.einsum("pab,pb->pa", inverse_root, pulled, precision=highest)
        mean_weight = (
            jnp.einsum("pab,pb->pa", inverse_root, once_applied, precision=highest)
            / norm_scale[:, None]
        )
        transform = (jnp.sqrt(ensemble - 1.0) / jnp.sqrt(norm_scale))[
            :, None, None
        ] * inverse_root + mean_weight[:, :, None]
        realization_grid = jnp.transpose(patch_block_slice, (2, 0, 1, 3)).reshape(
            height, ensemble, channels * patch_width
        )
        field = realization_grid.astype(jnp.float32)
        centre = jnp.mean(field, axis=1)
        spread = field - centre[:, None, :]
        analysed = centre[:, None, :] + jnp.einsum(
            "pkm,pkc->pmc", transform, spread, precision=highest
        )
        return analysed.reshape(height, ensemble, channels, patch_width).transpose(1, 2, 0, 3)

    return on_device


def solution(mesh):
    grp_size, band_size = mesh.devices.shape
    fine = Mesh(
        mesh.devices.reshape(grp_size // 2, 2, 2, band_size // 32 * 4, 4),
        GRP + BAND,
    )
    placed = (
        P(GRP, None, BAND, None),
        P(),
        P(),
        P(),
        P(),
        P(GRP + BAND, None),
        P(GRP + BAND, None),
        P(GRP + BAND, None),
        P(GRP + BAND, None),
        P(GRP + BAND, None),
    )
    return jax.shard_map(
        make_on_device(band_size),
        mesh=fine,
        in_specs=placed,
        out_specs=P(None, None, BAND, GRP),
        check_vma=False,
    )
```

time: 1320 us -> 480 us (0.36)
  the two profiles are of different devices: /device:TPU:48 before, /device:TPU:1 now
where the time goes in v1:
time: 480 us; the launch traced here: 478 us
  waiting for transfers between devices  178 us (37%)
  local copies, waits for them, and re-layouts  108 us (22%)
  matrix products  97.1 us (20%)
  blocking collectives  42.5 us (9%)
  starting transfers between devices  20.8 us (4%)
  other arithmetic  17.9 us (4%)
  between operations  13.8 us (3%)
    ppermute x1, waiting for transfers between devices, on_device(): lax.ppermute(hidden_fields[:, :, height - 1:, :], BAND, shift_pairs(band_...  84.9 us
    dot_general x144, matrix products, convolve(): jnp.einsum('oc,crl->orl', kernel[row_shift, col_shift], shifted, preferre...  84.5 us
    all_to_all x1, waiting for transfers between devices, on_device(): lax.all_to_all(predicted_samples, GRP, split_axis=3, concat_axis=0, tiled...  47.3 us
    all_gather x4, blocking collectives, on_device(): packed = lax.all_gather(packed, axis, axis=0, tiled=False)  42.5 us
    squeeze x16, local copies, waits for them, and re-layouts, on_device(): lax.map(output_layer, (prior_samples, hidden_fields, northern_halo, south...  20.6 us
    ppermute x1, waiting for transfers between devices, padded_2(): lax.ppermute(tail, BAND, shift_pairs(band_size, 1))  19.1 us
    all_gather x1, waiting for transfers between devices, on_device(): packed = lax.all_gather(packed, axis, axis=0, tiled=False)  15.9 us
    all_to_all x2, local copies, waits for them, and re-layouts, on_device(): lax.all_to_all(predicted_samples, GRP, split_axis=3, concat_axis=0, tiled...  14.3 us
  transfers between devices with their start and end apart: 6, of which 6 were waited for; matrix products, arithmetic and copies ran while one was open for 3% of the time, Pallas kernels for 0%

profile of v1, /device:TPU:1, one launch (start us, length us, event | category | flops | bytes accessed | tf_op | source)
XLA Modules:
  0.0 478.3 jit_solution(13882782711208538704)
XLA Ops:
  6.5 5.9 %fusion.154 = (bf16[8,69,1,1024]{3,2,1,0:T(2,128)(2,1)S(1)}, bf16[8,69,1,1024]{3,2,1,0:T(2,128)(2,1)S(1)}) fusion(bf16[8,69,2,1024]{3,2,1,0:T(2,128)(2,1)} %param.14), kind=kLoop, calls=%fused_computation.215 | loop fusion | bytes 4521984 | tf_op jit(solution)/shard_map/slice | solution.py:21
  12.9 5.5 %collective-permute-start = (bf16[8,69,1,1024]{3,0,2,1:T(8,128)(2,1)S(1)}, bf16[8,69,1,1024]{3,0,2,1:T(8,128)(2,1)}, u32[]{:S(2)}, u32[]{:S(2)}) collective-permute-start(bf16[8,69,1,1024]{3,0,2,1:T(8,128)(2,1)S(1)} %copy.75), channel_id=1, source_target_pairs={{0,1},{1,2},{2,3},{3,4},{4,5},{5,6},{6,7},{7,8},{8,9},{9,10},{10,1... | collective-permute-start | bytes 3391496 | tf_op jit(solution)/shard_map/ppermute | solution.py:24
  18.4 1.4 copy.76
  21.9 19.1 %collective-permute-done = bf16[8,69,1,1024]{3,0,2,1:T(8,128)(2,1)} collective-permute-done((bf16[8,69,1,1024]{3,0,2,1:T(8,128)(2,1)S(1)}, bf16[8,69,1,1024]{3,0,2,1:T(8,128)(2,1)}, u32[]{:S(2)}, u32[]{:S(2)}) %collective-permute-start) | collective-permute-done | bytes 1130528 | tf_op jit(solution)/shard_map/ppermute | solution.py:24
  41.0 1.9 copy.50
  42.8 4.7 collective-permute-done.1
  47.5 1.9 copy.52
  49.4 2.5 pad_maximum_fusion.6
  51.9 73.3 %while.20 = (s32[]{:T(128)}, bf16[8,256,2,1024]{3,1,2,0:T(8,128)(2,1)}, bf16[8,69,4,1024]{3,1,2,0:T(8,128)(2,1)}, bf16[3,3,256,69]{2,3,1,0:T(8,128)(2,1)S(1)}, f32[256]{0:T(256)S(1)}, /*index=5*/s32[]{:T(128)}) while((s32[]{:T(128)}, bf16[8,256,2,1024]{3,1,2,0:T(8,128)(2,1)}, bf16[8,69,4,1024]{3,1,2,0:T(8,128)(2,1)}, ...), condition=%wide.region_1.2_spmd, body=%wide.region_0.1_spmd.sunk | while | flops 661897216 | bytes 47412808 | solution.py:69
  125.2 6.1 %fusion.153 = (bf16[8,256,1,1024]{3,1,2,0:T(8,128)(2,1)}, bf16[8,256,1,1024]{3,1,2,0:T(8,128)(2,1)}) fusion(bf16[8,256,2,1024]{3,1,2,0:T(8,128)(2,1)} %get-tuple-element.324), kind=kLoop, calls=%fused_computation.214 | loop fusion | bytes 16777216 | tf_op jit(solution)/shard_map/slice | solution.py:74
  131.3 4.5 collective-permute-start.2
  135.8 1.5 collective-permute-start.3
  137.2 84.9 %collective-permute-done.2 = bf16[8,256,1,1024]{3,1,2,0:T(8,128)(2,1)} collective-permute-done((bf16[8,256,1,1024]{3,1,2,0:T(8,128)(2,1)}, bf16[8,256,1,1024]{3,1,2,0:T(8,128)(2,1)}, u32[]{:S(2)}, u32[]{:S(2)}) %collective-permute-start.2) | collective-permute-done | bytes 4194336 | tf_op jit(solution)/shard_map/ppermute | solution.py:70
  222.1 5.8 %collective-permute-done.3 = bf16[8,256,1,1024]{3,1,2,0:T(8,128)(2,1)} collective-permute-done((bf16[8,256,1,1024]{3,1,2,0:T(8,128)(2,1)}, bf16[8,256,1,1024]{3,1,2,0:T(8,128)(2,1)}, u32[]{:S(2)}, u32[]{:S(2)}) %collective-permute-start.3) | collective-permute-done | bytes 4194336 | tf_op jit(solution)/shard_map/ppermute | solution.py:73
  227.9 70.6 %while.21 = (s32[]{:T(128)}, bf16[8,69,2,1024]{3,1,2,0:T(8,128)(2,1)S(1)}, bf16[8,69,2,1024]{3,1,2,0:T(8,128)(2,1)}, bf16[8,256,1,1024]{3,1,2,0:T(8,128)(2,1)}, ...) while((s32[]{:T(128)}, ...), condition=%wide.region_3.4_spmd, body=%wide.region_2.3_spmd.sunk | while | flops 675929088 | bytes 41343592 | solution.py:87
  227.9 1.3 dynamic-slice_bitcast_fusion.9
  230.5 1.4 fusion.305
  236.7 1.3 dynamic-slice_bitcast_fusion.9
  239.3 1.4 fusion.305
  245.5 1.3 dynamic-slice_bitcast_fusion.9
  248.1 1.4 fusion.305
  254.4 1.3 dynamic-slice_bitcast_fusion.9
  256.9 1.4 fusion.305
  263.2 1.3 dynamic-slice_bitcast_fusion.9
  265.8 1.4 fusion.305
  272.0 1.3 dynamic-slice_bitcast_fusion.9
  274.6 1.4 fusion.305
  279.5 1.3 fusion.308
  280.8 1.3 dynamic-slice_bitcast_fusion.9
  283.4 1.4 fusion.305
  289.7 1.3 dynamic-slice_bitcast_fusion.9
  292.2 1.4 fusion.305
  298.5 7.7 %copy.57 = bf16[8,69,2,1024]{1,2,0,3:T(2,128)(2,1)} copy(bf16[8,69,2,1024]{3,1,2,0:T(8,128)(2,1)S(1)} %get-tuple-element.75) | data formatting | bytes 4521984 | tf_op jit(solution)/shard_map/while | solution.py:87
  306.1 8.0 %all-to-all-start = ((bf16[8,69,2,1024]{1,2,0,3:T(2,128)(2,1)}), bf16[8,69,2,1024]{1,2,0,3:T(2,128)(2,1)}, u32[]{:S(2)}, u32[]{:S(2)}) async-start(bf16[8,69,2,1024]{1,2,0,3:T(2,128)(2,1)} %copy.57), calls=%async_computation | async-start | bytes 8388608 | tf_op jit(solution)/shard_map/all_to_all | solution.py:90
  314.2 47.3 %all-to-all-done = bf16[8,69,2,1024]{1,2,0,3:T(2,128)(2,1)} async-done(((bf16[8,69,2,1024]{1,2,0,3:T(2,128)(2,1)}), bf16[8,69,2,1024]{1,2,0,3:T(2,128)(2,1)}, u32[]{:S(2)}, u32[]{:S(2)}) %all-to-all-start) | async-done | bytes 2261024 | tf_op jit(solution)/shard_map/all_to_all | solution.py:90
  361.5 11.4 %copy.72 = bf16[8,69,2,4,256]{4,3,0,2,1:T(4,128)(2,1)} copy(bf16[8,69,2,4,256]{1,2,0,4,3:T(2,128)(2,1)} %bitcast.45) | data formatting | bytes 4521984 | tf_op jit(solution)/shard_map/all_to_all | solution.py:90
  372.9 2.9 copy.59
  377.3 9.3 %all-gather.5 = f32[4,2,1056]{2,1,0:T(2,128)S(1)} all-gather(f32[1,2,1056]{2,1,0:T(2,128)S(1)} %maximum_bitcast_fusion), channel_id=2, replica_groups=mesh['y_lo'=2,'core'=2,'y_hi'=2,'x'=4,'z'=4] {'z'}, dimensions={0}, use_global_device_ids=true | all-gather | bytes 42240 | tf_op jit(solution)/shard_map/all_gather | solution.py:125
  386.6 17.7 %all-gather.1 = f32[16,2,1056]{2,1,0:T(2,128)S(1)} all-gather(f32[4,2,1056]{2,1,0:T(2,128)S(1)} %all-gather.5), channel_id=3, replica_groups=mesh['y_lo'=2,'core'=2,'y_hi'=2,'x'=4,'z'=4] {'x'}, dimensions={0}, use_global_device_ids=true | all-gather | bytes 168960 | tf_op jit(solution)/shard_map/all_gather | solution.py:125
  404.3 6.2 %all-gather.2 = f32[8,4,2,1056]{3,1,2,0:T(4,128)S(1)} all-gather(f32[4,4,2,1056]{3,1,2,0:T(4,128)S(1)} %copy.60), channel_id=4, replica_groups=mesh['y_lo'=2,'core'=2,'y_hi'=2,'x'=4,'z'=4] {'y_hi'}, dimensions={0}, use_global_device_ids=true | all-gather | bytes 405504 | tf_op jit(solution)/shard_map/all_gather | solution.py:125
  410.5 9.4 %all-gather.3 = f32[4,4,4,2,1056]{4,2,3,1,0:T(4,128)} all-gather(f32[2,4,4,2,1056]{4,2,3,1,0:T(4,128)S(1)} %bitcast.284), channel_id=5, replica_groups=mesh['y_lo'=2,'core'=2,'y_hi'=2,'x'=4,'z'=4] {'core'}, dimensions={0}, use_global_device_ids=true | all-gather | bytes 811008 | tf_op jit(solution)/shard_map/all_gather | solution.py:125
  420.0 2.5 convert_bitcast_fusion
  422.5 5.1 %reshape.55 = f32[2,32,17664]{2,1,0:T(8,128)} reshape(f32[2,32,69,256]{3,2,1,0:T(8,128)} %convert_bitcast_fusion) | data formatting | bytes 9043968 | tf_op jit(solution)/shard_map/convert_element_type | solution.py:159
  428.1 15.9 %all-gather.8.cloned.1.call-done = f32[4,2,4,4,2,1056]{5,3,4,2,1,0:T(4,128)} async-done(((f32[2,2,4,4,2,1056]{5,3,4,2,1,0:T(4,128)}), f32[4,2,4,4,2,1056]{5,3,4,2,1,0:T(4,128)}) %all-gather.8.cloned.1.call-update) | async-done | bytes 1081360 | tf_op jit(solution)/shard_map/all_gather | solution.py:125
  444.0 1.9 copy.61
  451.0 7.4 %convolution_add_fusion.7 = f32[2,32,17664]{2,1,0:T(8,128)} fusion(f32[2,32,17664]{2,1,0:T(8,128)} %reshape.55, f32[2,17664]{1,0:T(2,128)S(1)} %bitcast.286, f32[2,32,32]{2,1,0:T(8,128)S(1)} %fusion.164, f32[2,32]{1,0:T(2,128)S(1)} %broadcast_divide_fusion.3, f32[2]{0:T(128)S(1)} %get-tuple-element.172), kind=kOutput, calls=%fused_computation.144 | convolution fusion | flops 436375552 | bytes 9193736 | tf_op jit(solution)/shard_map/pkm,pkc->pmc/dot_general | solution.py:162
  458.4 5.1 %reshape.53 = f32[2,32,69,256]{3,2,1,0:T(8,128)} reshape(f32[2,32,17664]{2,1,0:T(8,128)} %convolution_add_fusion.7) | data formatting | bytes 9043968 | tf_op jit(solution)/shard_map/reshape | solution.py:165
  463.5 7.9 %copy.63 = f32[32,69,2,256]{3,2,1,0:T(2,128)} copy(f32[32,69,2,256]{3,1,0,2:T(8,128)} %bitcast.281) | data formatting | bytes 9043968 | tf_op jit(solution)/shard_map/transpose | solution.py:165
  (271 shorter events, 129.6 us)
Async XLA Ops:
  12.9 8.3 %copy-start = (bf16[8,69,2,1024]{3,2,1,0:T(2,128)(2,1)S(1)}, bf16[8,69,2,1024]{3,2,1,0:T(2,128)(2,1)}, u32[]{:S(2)}) copy-start(bf16[8,69,2,1024]{3,2,1,0:T(2,128)(2,1)} %param.14) | copy-start | bytes 6782980
  12.9 28.1 %collective-permute-start = (bf16[8,69,1,1024]{3,0,2,1:T(8,128)(2,1)S(1)}, bf16[8,69,1,1024]{3,0,2,1:T(8,128)(2,1)}, u32[]{:S(2)}, u32[]{:S(2)}) collective-permute-start(bf16[8,69,1,1024]{3,0,2,1:T(8,128)(2,1)S(1)} %copy.75), channel_id=1, source_target_pairs={{0,1},{1,2},{2,3},{3,4},{4,5},{5,6},{6,7},{7,8},{8,9},{9,10},{10,1... | collective-permute-start | bytes 3391496 | tf_op jit(solution)/shard_map/ppermute | solution.py:24
  19.8 27.7 %collective-permute-start.1 = (bf16[8,69,1,1024]{3,0,2,1:T(8,128)(2,1)}, bf16[8,69,1,1024]{3,0,2,1:T(8,128)(2,1)}, u32[]{:S(2)}, u32[]{:S(2)}) collective-permute-start(bf16[8,69,1,1024]{3,0,2,1:T(8,128)(2,1)} %copy.76), channel_id=1, source_target_pairs={{1,0},{2,1},{3,2},{4,3},{5,4},{6,5},{7,6},{8,7},{9,8},{10,9},{11,1... | collective-permute-start | bytes 3391496 | tf_op jit(solution)/shard_map/ppermute | solution.py:26
  21.9 27.5 %copy-start.1 = (bf16[8,69,2,1024]{3,1,2,0:T(8,128)(2,1)}, bf16[8,69,2,1024]{3,1,2,0:T(8,128)(2,1)S(1)}, u32[]{:S(2)}) copy-start(bf16[8,69,2,1024]{3,1,2,0:T(8,128)(2,1)S(1)} %copy.55) | copy-start | bytes 6782980
  49.4 2.5 copy-start.2
  49.4 2.5 copy-start.4
  125.2 102.7 %copy-start.3 = (bf16[3,3,69,256]{3,2,1,0:T(8,128)(2,1)S(1)}, bf16[3,3,69,256]{3,2,1,0:T(8,128)(2,1)}, u32[]{:S(2)}) copy-start(bf16[3,3,69,256]{3,2,1,0:T(8,128)(2,1)} %param.17) | copy-start | bytes 953860
  125.2 102.7 %copy-start.10 = (f32[69]{0:T(128)S(1)}, f32[69]{0:T(128)}, u32[]{:S(2)}) copy-start(f32[69]{0:T(128)} %param.18) | copy-start | bytes 832
  131.3 90.8 %collective-permute-start.2 = (bf16[8,256,1,1024]{3,1,2,0:T(8,128)(2,1)}, bf16[8,256,1,1024]{3,1,2,0:T(8,128)(2,1)}, u32[]{:S(2)}, u32[]{:S(2)}) collective-permute-start(bf16[8,256,1,1024]{3,1,2,0:T(8,128)(2,1)} %get-tuple-element.165), channel_id=1, source_target_pairs={{0,1},{1,2},{2,3},{3,4},{4,5},{5,6},{6,7},{7,8},{8,9},{9,10},{10,1... | collective-permute-start | bytes 12582920 | tf_op jit(solution)/shard_map/ppermute | solution.py:70
  135.8 92.1 %collective-permute-start.3 = (bf16[8,256,1,1024]{3,1,2,0:T(8,128)(2,1)}, bf16[8,256,1,1024]{3,1,2,0:T(8,128)(2,1)}, u32[]{:S(2)}, u32[]{:S(2)}) collective-permute-start(bf16[8,256,1,1024]{3,1,2,0:T(8,128)(2,1)} %get-tuple-element.164), channel_id=1, source_target_pairs={{1,0},{2,1},{3,2},{4,3},{5,4},{6,5},{7,6},{8,7},{9,8},{10,9},{11,1... | collective-permute-start | bytes 12582920 | tf_op jit(solution)/shard_map/ppermute | solution.py:73
  306.1 8.0 %copy-start.6 = (s32[2,256]{1,0:T(2,128)S(1)}, s32[2,256]{1,0:T(2,128)}, u32[]{:S(2)}) copy-start(s32[2,256]{1,0:T(2,128)} %param.19) | copy-start | bytes 6148
  306.1 55.4 %all-to-all-start = ((bf16[8,69,2,1024]{1,2,0,3:T(2,128)(2,1)}), bf16[8,69,2,1024]{1,2,0,3:T(2,128)(2,1)}, u32[]{:S(2)}, u32[]{:S(2)}) async-start(bf16[8,69,2,1024]{1,2,0,3:T(2,128)(2,1)} %copy.57), calls=%async_computation | async-start | bytes 8388608 | tf_op jit(solution)/shard_map/all_to_all | solution.py:90
  314.1 129.9 %all-gather.8.cloned.1.call-start = ((), (), s32[]{:S(2)}) async-start(), calls=%async_computation.1 | async-start | bytes 1769472 | tf_op jit(solution)/shard_map/all_gather | solution.py:125
  375.8 1.0 copy-start.5
  375.8 1.0 copy-start.7
  376.8 43.2 %copy-start.8 = (f32[2,8]{1,0:T(2,128)S(1)}, f32[2,8]{1,0:T(2,128)}, u32[]{:S(2)}) copy-start(f32[2,8]{1,0:T(2,128)} %param.23) | copy-start | bytes 196
  376.8 43.2 %copy-start.9 = (s32[2,8]{1,0:T(2,128)S(1)}, s32[2,8]{1,0:T(2,128)}, u32[]{:S(2)}) copy-start(s32[2,8]{1,0:T(2,128)} %param.22) | copy-start | bytes 196
Sparse Core Ops, SparseCore 0:
  420.0 23.9 all-gather.7

commit v2 on v1

--- a/solution.py
+++ b/solution.py
@@ -29,19 +29,16 @@
     )
 
 
-def convolve(padded, kernel, height):
-    summed = jnp.zeros((kernel.shape[2], height, padded.shape[2]), jnp.float32)
-    for row_shift in range(3):
-        window = padded[:, row_shift : row_shift + height, :]
-        for col_shift in range(3):
-            shifted = jnp.roll(window, 1 - col_shift, axis=2)
-            summed = summed + jnp.einsum(
-                "oc,crl->orl",
-                kernel[row_shift, col_shift],
-                shifted,
-                preferred_element_type=jnp.float32,
-            )
-    return summed
+def convolve(padded, kernel):
+    wrapped = jnp.concatenate([padded[..., -1:], padded, padded[..., :1]], axis=-1)
+    return lax.conv_general_dilated(
+        wrapped,
+        jnp.transpose(kernel, (2, 3, 0, 1)),
+        window_strides=(1, 1),
+        padding="VALID",
+        dimension_numbers=("NCHW", "OIHW", "NCHW"),
+        preferred_element_type=jnp.float32,
+    )
 
 
 def make_on_device(band_size):
@@ -61,32 +58,21 @@
         height = prior_samples.shape[2]
         padded = padded_2(prior_samples, band_size, 1)
 
-        def first_layer(member):
-            return jax.nn.silu(
-                convolve(member, conv1_weight, height) + conv1_bias[:, None, None]
-            ).astype(jnp.bfloat16)
-
-        hidden_fields = lax.map(first_layer, padded)
+        hidden_fields = jax.nn.silu(
+            convolve(padded, conv1_weight) + conv1_bias[None, :, None, None]
+        ).astype(jnp.bfloat16)
         northern_halo = lax.ppermute(
             hidden_fields[:, :, height - 1 :, :], BAND, shift_pairs(band_size, 1)
         )
         southern_halo = lax.ppermute(
             hidden_fields[:, :, :1, :], BAND, shift_pairs(band_size, -1)
         )
-
-        def output_layer(inputs):
-            member, own_rows, above_row, below_row = inputs
-            extended = jnp.concatenate([above_row, own_rows, below_row], axis=1)
-            summed = (
-                member.astype(jnp.float32)
-                + convolve(extended, conv2_weight, height)
-                + conv2_bias[:, None, None]
-            )
-            return summed.astype(jnp.bfloat16)
-
-        predicted_samples = lax.map(
-            output_layer, (prior_samples, hidden_fields, northern_halo, southern_halo)
-        )
+        extended = jnp.concatenate([northern_halo, hidden_fields, southern_halo], axis=2)
+        predicted_samples = (
+            prior_samples.astype(jnp.float32)
+            + convolve(extended, conv2_weight)
+            + conv2_bias[None, :, None, None]
+        ).astype(jnp.bfloat16)
         patch_block_slice = lax.all_to_all(
             predicted_samples, GRP, split_axis=3, concat_axis=0, tiled=True
         )

time: 480 us -> 385 us (0.80)
  local copies, waits for them, and re-layouts: 108 us -> 65 us
  matrix products: 97.1 us -> 63.2 us
  other arithmetic: 17.9 us -> 7.45 us
  waiting for transfers between devices: 178 us -> 171 us
    dot_general x144 -> x0, matrix products: 84.5 us -> none  [convolve(): jnp.einsum('oc,crl->orl', kernel[row_shift, col_shift], shifted, preferre...]
    conv_general_dilated x0 -> x2, matrix products: none -> 50.7 us  [convolve(): lax.conv_general_dilated(wrapped, jnp.transpose(kernel, (2, 3, 0, 1)), wi...]
    squeeze x24 -> x0, local copies, waits for them, and re-layouts: 29.4 us -> none  [the longest x16 20.6 us: on_device(): lax.map(output_layer, (prior_samples, hidden_fields, northern_halo, south...]
    concatenate x17 -> x0, other arithmetic: 14.7 us -> none  [the longest x16 12.1 us: output_layer(): extended = jnp.concatenate([above_row, own_rows, below_row], axis=1)]
    dynamic_update_slice x16 -> x0, local copies, waits for them, and re-layouts: 12.8 us -> none  [on_device(): hidden_fields = lax.map(first_layer, padded)]
    slice x17 -> x1, local copies, waits for them, and re-layouts: 10.1 us -> 0.59 us  [on_device(): hidden_fields[:, :, height - 1:, :]]
    while x2 -> x0, local copies, waits for them, and re-layouts: 8.39 us -> none  [on_device(): lax.map(output_layer, (prior_samples, hidden_fields, northern_halo, south...]
    conv_general_dilated x0 -> x1, local copies, waits for them, and re-layouts: none -> 7.96 us  [convolve(): lax.conv_general_dilated(wrapped, jnp.transpose(kernel, (2, 3, 0, 1)), wi...]
  transfers between devices with their start and end apart: 6 -> 6, of which waited for: 6 -> 6; matrix products, arithmetic and copies ran while one was open for 3% -> 5% of each run, Pallas kernels for 0% -> 0%
where the time goes in v2:
time: 385 us; the launch traced here: 384 us
  waiting for transfers between devices  171 us (44%)
  local copies, waits for them, and re-layouts  65 us (17%)
  matrix products  63.2 us (16%)
  blocking collectives  44.7 us (12%)
  starting transfers between devices  18.9 us (5%)
  between operations  13.8 us (4%)
  other arithmetic  7.45 us (2%)
    ppermute x1, waiting for transfers between devices, on_device(): lax.ppermute(hidden_fields[:, :, height - 1:, :], BAND, shift_pairs(band_...  86.2 us
    conv_general_dilated x2, matrix products, convolve(): lax.conv_general_dilated(wrapped, jnp.transpose(kernel, (2, 3, 0, 1)), wi...  50.7 us
    all_to_all x1, waiting for transfers between devices, on_device(): lax.all_to_all(predicted_samples, GRP, split_axis=3, concat_axis=0, tiled...  47.3 us
    all_gather x4, blocking collectives, on_device(): packed = lax.all_gather(packed, axis, axis=0, tiled=False)  44.7 us
    all_gather x1, waiting for transfers between devices, on_device(): packed = lax.all_gather(packed, axis, axis=0, tiled=False)  15.9 us
    ppermute x1, waiting for transfers between devices, padded_2(): lax.ppermute(tail, BAND, shift_pairs(band_size, 1))  14.4 us
    unnamed x28, local copies, waits for them, and re-layouts  8.71 us
    all_to_all x1, starting transfers between devices, on_device(): lax.all_to_all(predicted_samples, GRP, split_axis=3, concat_axis=0, tiled...  7.99 us
  transfers between devices with their start and end apart: 6, of which 6 were waited for; matrix products, arithmetic and copies ran while one was open for 5% of the time, Pallas kernels for 0%

profile of v2, /device:TPU:1, one launch (start us, length us, event | category | flops | bytes accessed | tf_op | source)
XLA Modules:
  0.0 383.8 jit_solution(8780914249732328955)
XLA Ops:
  6.5 5.9 %fusion.62 = (bf16[8,69,1,1024]{3,2,1,0:T(2,128)(2,1)S(1)}, bf16[8,69,1,1024]{3,2,1,0:T(2,128)(2,1)S(1)}) fusion(bf16[8,69,2,1024]{3,2,1,0:T(2,128)(2,1)} %param.10), kind=kLoop, calls=%fused_computation.100 | loop fusion | bytes 4521984 | tf_op jit(solution)/shard_map/slice | solution.py:21
  12.4 1.4 copy.75
  13.8 5.4 %collective-permute-start = (bf16[8,69,1,1024]{3,0,2,1:T(8,128)(2,1)}, bf16[8,69,1,1024]{3,0,2,1:T(8,128)(2,1)}, u32[]{:S(2)}, u32[]{:S(2)}) collective-permute-start(bf16[8,69,1,1024]{3,0,2,1:T(8,128)(2,1)} %copy.75), channel_id=1, source_target_pairs={{0,1},{1,2},{2,3},{3,4},{4,5},{5,6},{6,7},{7,8},{8,9},{9,10},{10,1... | collective-permute-start | bytes 3391496 | tf_op jit(solution)/shard_map/ppermute | solution.py:24
  19.2 1.4 copy.74
  20.6 1.3 collective-permute-start.1
  21.9 5.7 %copy.53 = bf16[8,69,2,1024]{1,0,3,2:T(8,128)(2,1)} copy(bf16[8,69,2,1024]{3,2,1,0:T(2,128)(2,1)S(1)} %copy-done.2) | data formatting | bytes 4521984 | tf_op args[0]
  27.7 14.4 %collective-permute-done = bf16[8,69,1,1024]{3,0,2,1:T(8,128)(2,1)} collective-permute-done((bf16[8,69,1,1024]{3,0,2,1:T(8,128)(2,1)}, bf16[8,69,1,1024]{3,0,2,1:T(8,128)(2,1)}, u32[]{:S(2)}, u32[]{:S(2)}) %collective-permute-start) | collective-permute-done | bytes 1130528 | tf_op jit(solution)/shard_map/ppermute | solution.py:24
  42.1 3.4 copy.52
  45.5 2.8 collective-permute-done.1
  48.3 4.1 %copy.54 = bf16[8,69,1,1024]{1,0,3,2:T(8,128)(2,1)} copy(bf16[8,69,1,1024]{3,0,2,1:T(8,128)(2,1)} %collective-permute-done.1) | data formatting | bytes 2260992 | tf_op jit(solution)/shard_map/ppermute | solution.py:26
  52.4 21.3 %multiply_convert_fusion = bf16[8,256,2,1024]{1,0,3,2:T(8,128)(2,1)S(1)} fusion(f32[256]{0:T(256)S(1)} %copy-done.11, bf16[3,3,256,69]{2,3,1,0:T(8,128)(2,1)S(1)} %copy-done, bf16[8,69,1,1024]{1,0,3,2:T(8,128)(2,1)} %copy.54, bf16[8,69,2,1024]{1,0,3,2:T(8,128)(2,1)} %copy.53, bf16[8,69,1,1024]{1,0,3,2:T(8,128)(2,1)S(1)} %copy.52), kind=kOutput, calls=%fused_computation.15 | convolution fusion | flops 5252614656 | bytes 13229568 | tf_op jit(solution)/shard_map/conv_general_dilated | solution.py:34
  73.8 0.6 fusion.61
  74.4 2.8 collective-permute-start.2
  77.1 1.5 collective-permute-start.3
  78.6 86.2 %collective-permute-done.2 = bf16[8,256,1,1024]{1,0,3,2:T(8,128)(2,1)S(1)} collective-permute-done((bf16[8,256,1,1024]{1,0,3,2:T(8,128)(2,1)S(1)}, bf16[8,256,1,1024]{1,0,3,2:T(8,128)(2,1)S(1)}, u32[]{:S(2)}, u32[]{:S(2)}) %collective-permute-start.2) | collective-permute-done | bytes 4194336 | tf_op jit(solution)/shard_map/ppermute | solution.py:64
  164.9 4.1 %collective-permute-done.3 = bf16[8,256,1,1024]{1,0,3,2:T(8,128)(2,1)S(1)} collective-permute-done((bf16[8,256,1,1024]{1,0,3,2:T(8,128)(2,1)S(1)}, bf16[8,256,1,1024]{1,0,3,2:T(8,128)(2,1)S(1)}, u32[]{:S(2)}, u32[]{:S(2)}) %collective-permute-start.3) | collective-permute-done | bytes 4194336 | tf_op jit(solution)/shard_map/ppermute | solution.py:67
  169.0 29.4 %fusion.1 = f32[8,69,2,1024]{1,0,3,2:T(8,128)} fusion(bf16[3,3,69,256]{3,2,1,0:T(8,128)(2,1)S(1)} %copy-done.10, bf16[8,256,1,1024]{1,0,3,2:T(8,128)(2,1)S(1)} %collective-permute-done.3, bf16[8,256,2,1024]{1,0,3,2:T(8,128)(2,1)S(1)} %multiply_convert_fusion, bf16[8,256,1,1024]{1,0,3,2:T(8,128)(2,1)S(1)} %collective-permute-done.2), kind=kOutput, calls=%fused_computation.3 | convolution fusion | flops 5276565504 | bytes 21617152 | tf_op jit(solution)/shard_map/conv_general_dilated | solution.py:34
  198.3 8.0 %copy.55 = f32[8,69,2,1024]{3,0,2,1:T(8,128)} copy(f32[8,69,2,1024]{1,0,3,2:T(8,128)} %fusion.1) | data formatting | bytes 9043968 | tf_op jit(solution)/shard_map/conv_general_dilated | solution.py:34
  206.3 4.2 %add_convert_fusion = bf16[8,69,2,1024]{3,0,2,1:T(8,128)(2,1)} fusion(f32[8,69,2,1024]{3,0,2,1:T(8,128)} %copy.55, f32[69]{0:T(128)S(1)} %copy-done.9, bf16[8,69,2,1024]{3,2,1,0:T(2,128)(2,1)S(1)} %copy-done.3), kind=kLoop, calls=%fused_computation.34 | loop fusion | flops 4521984 | bytes 9044244 | tf_op jit(solution)/shard_map/convert_element_type | solution.py:75
  210.5 6.7 %copy.56 = bf16[8,69,2,1024]{1,0,2,3:T(8,128)(2,1)} copy(bf16[8,69,2,1024]{3,0,2,1:T(8,128)(2,1)} %add_convert_fusion) | data formatting | bytes 4521984 | tf_op jit(solution)/shard_map/convert_element_type | solution.py:75
  217.2 8.0 %all-to-all-start = ((bf16[8,69,2,1024]{1,0,2,3:T(8,128)(2,1)}), bf16[8,69,2,1024]{1,0,2,3:T(8,128)(2,1)}, u32[]{:S(2)}, u32[]{:S(2)}) async-start(bf16[8,69,2,1024]{1,0,2,3:T(8,128)(2,1)} %copy.56), calls=%async_computation | async-start | bytes 8388608 | tf_op jit(solution)/shard_map/all_to_all | solution.py:76
  225.3 47.3 %all-to-all-done = bf16[8,69,2,1024]{1,0,2,3:T(8,128)(2,1)} async-done(((bf16[8,69,2,1024]{1,0,2,3:T(8,128)(2,1)}), bf16[8,69,2,1024]{1,0,2,3:T(8,128)(2,1)}, u32[]{:S(2)}, u32[]{:S(2)}) %all-to-all-start) | async-done | bytes 2261024 | tf_op jit(solution)/shard_map/all_to_all | solution.py:76
  272.6 6.5 %copy.57 = bf16[8,69,2,4,256]{4,1,0,3,2:T(8,128)(2,1)S(1)} copy(bf16[8,69,2,4,256]{1,0,2,4,3:T(8,128)(2,1)} %bitcast) | data formatting | bytes 4521984 | tf_op jit(solution)/shard_map/all_to_all | solution.py:76
  279.2 1.0 fusion.25
  280.2 0.2 fusion.39
  280.4 0.2 fusion.42
  280.6 11.4 %all-gather.5 = f32[4,2,1056]{2,1,0:T(2,128)S(1)} all-gather(f32[1,2,1056]{2,1,0:T(2,128)S(1)} %maximum_bitcast_fusion), channel_id=2, replica_groups=mesh['y_lo'=2,'core'=2,'y_hi'=2,'x'=4,'z'=4] {'z'}, dimensions={0}, use_global_device_ids=true | all-gather | bytes 42240 | tf_op jit(solution)/shard_map/all_gather | solution.py:111
  292.1 17.7 %all-gather.1 = f32[16,2,1056]{2,1,0:T(2,128)S(1)} all-gather(f32[4,2,1056]{2,1,0:T(2,128)S(1)} %all-gather.5), channel_id=3, replica_groups=mesh['y_lo'=2,'core'=2,'y_hi'=2,'x'=4,'z'=4] {'x'}, dimensions={0}, use_global_device_ids=true | all-gather | bytes 168960 | tf_op jit(solution)/shard_map/all_gather | solution.py:111
  309.8 6.2 %all-gather.2 = f32[8,4,2,1056]{3,1,2,0:T(4,128)S(1)} all-gather(f32[4,4,2,1056]{3,1,2,0:T(4,128)S(1)} %copy.58), channel_id=4, replica_groups=mesh['y_lo'=2,'core'=2,'y_hi'=2,'x'=4,'z'=4] {'y_hi'}, dimensions={0}, use_global_device_ids=true | all-gather | bytes 405504 | tf_op jit(solution)/shard_map/all_gather | solution.py:111
  316.0 9.4 %all-gather.3 = f32[4,4,4,2,1056]{4,2,3,1,0:T(4,128)} all-gather(f32[2,4,4,2,1056]{4,2,3,1,0:T(4,128)S(1)} %bitcast.88), channel_id=5, replica_groups=mesh['y_lo'=2,'core'=2,'y_hi'=2,'x'=4,'z'=4] {'core'}, dimensions={0}, use_global_device_ids=true | all-gather | bytes 811008 | tf_op jit(solution)/shard_map/all_gather | solution.py:111
  325.5 2.5 convert_bitcast_fusion
  328.0 5.1 %reshape.52 = f32[2,32,17664]{2,1,0:T(8,128)} reshape(f32[2,32,69,256]{3,2,1,0:T(8,128)} %convert_bitcast_fusion) | data formatting | bytes 9043968 | tf_op jit(solution)/shard_map/convert_element_type | solution.py:145
  333.2 0.3 convert_reduce_fusion
  333.6 15.9 %all-gather.8.cloned.1.call-done = f32[4,2,4,4,2,1056]{5,3,4,2,1,0:T(4,128)} async-done(((f32[2,2,4,4,2,1056]{5,3,4,2,1,0:T(4,128)}), f32[4,2,4,4,2,1056]{5,3,4,2,1,0:T(4,128)}) %all-gather.8.cloned.1.call-update) | async-done | bytes 1081360 | tf_op jit(solution)/shard_map/all_gather | solution.py:111
  349.5 1.9 copy.59
  351.4 0.8 reshape.49
  352.2 0.7 fusion.63
  353.1 0.3 fusion.33
  353.3 0.2 fusion.57
  353.7 0.2 fusion.32
  354.2 0.2 fusion.31
  354.8 0.2 fusion.30
  355.3 0.2 fusion.29
  355.8 0.2 fusion.28
  356.3 0.2 fusion.73
  356.5 7.4 %convolution_add_fusion = f32[2,32,17664]{2,1,0:T(8,128)} fusion(f32[2,32,17664]{2,1,0:T(8,128)} %reshape.52, f32[2,17664]{1,0:T(2,128)S(1)} %bitcast.90, f32[2,32,32]{2,1,0:T(8,128)S(1)} %fusion.72, f32[2,32]{1,0:T(2,128)S(1)} %broadcast_divide_fusion.3, f32[2]{0:T(128)S(1)} %get-tuple-element.17), kind=kOutput, calls=%fused_computation | convolution fusion | flops 436375552 | bytes 9193736 | tf_op jit(solution)/shard_map/pkm,pkc->pmc/dot_general | solution.py:148
  363.9 5.1 %reshape.51 = f32[2,32,69,256]{3,2,1,0:T(8,128)} reshape(f32[2,32,17664]{2,1,0:T(8,128)} %convolution_add_fusion) | data formatting | bytes 9043968 | tf_op jit(solution)/shard_map/reshape | solution.py:151
  369.0 8.0 %copy.61 = f32[32,69,2,256]{3,2,1,0:T(2,128)} copy(f32[32,69,2,256]{3,1,0,2:T(8,128)} %bitcast.86) | data formatting | bytes 9043968 | tf_op jit(solution)/shard_map/transpose | solution.py:151
  (55 shorter events, 2.5 us)
Async XLA Ops:
  6.5 45.9 %copy-start = (bf16[3,3,256,69]{2,3,1,0:T(8,128)(2,1)S(1)}, bf16[3,3,256,69]{2,3,1,0:T(8,128)(2,1)}, u32[]{:S(2)}) copy-start(bf16[3,3,256,69]{2,3,1,0:T(8,128)(2,1)} %param.11) | copy-start | bytes 953860
  12.4 9.5 %copy-start.2 = (bf16[8,69,2,1024]{3,2,1,0:T(2,128)(2,1)S(1)}, bf16[8,69,2,1024]{3,2,1,0:T(2,128)(2,1)}, u32[]{:S(2)}) copy-start(bf16[8,69,2,1024]{3,2,1,0:T(2,128)(2,1)} %param.10) | copy-start | bytes 6782980
  13.8 28.2 %collective-permute-start = (bf16[8,69,1,1024]{3,0,2,1:T(8,128)(2,1)}, bf16[8,69,1,1024]{3,0,2,1:T(8,128)(2,1)}, u32[]{:S(2)}, u32[]{:S(2)}) collective-permute-start(bf16[8,69,1,1024]{3,0,2,1:T(8,128)(2,1)} %copy.75), channel_id=1, source_target_pairs={{0,1},{1,2},{2,3},{3,4},{4,5},{5,6},{6,7},{7,8},{8,9},{9,10},{10,1... | collective-permute-start | bytes 3391496 | tf_op jit(solution)/shard_map/ppermute | solution.py:24
  20.6 27.7 %collective-permute-start.1 = (bf16[8,69,1,1024]{3,0,2,1:T(8,128)(2,1)}, bf16[8,69,1,1024]{3,0,2,1:T(8,128)(2,1)}, u32[]{:S(2)}, u32[]{:S(2)}) collective-permute-start(bf16[8,69,1,1024]{3,0,2,1:T(8,128)(2,1)} %copy.74), channel_id=1, source_target_pairs={{1,0},{2,1},{3,2},{4,3},{5,4},{6,5},{7,6},{8,7},{9,8},{10,9},{11,1... | collective-permute-start | bytes 3391496 | tf_op jit(solution)/shard_map/ppermute | solution.py:26
  27.7 24.8 %copy-start.11 = (f32[256]{0:T(256)S(1)}, f32[256]{0:T(256)}, u32[]{:S(2)}) copy-start(f32[256]{0:T(256)} %param.12) | copy-start | bytes 3076
  73.8 95.2 %copy-start.10 = (bf16[3,3,69,256]{3,2,1,0:T(8,128)(2,1)S(1)}, bf16[3,3,69,256]{3,2,1,0:T(8,128)(2,1)}, u32[]{:S(2)}) copy-start(bf16[3,3,69,256]{3,2,1,0:T(8,128)(2,1)} %param.13) | copy-start | bytes 953860
  74.4 90.5 %collective-permute-start.2 = (bf16[8,256,1,1024]{1,0,3,2:T(8,128)(2,1)S(1)}, bf16[8,256,1,1024]{1,0,3,2:T(8,128)(2,1)S(1)}, u32[]{:S(2)}, u32[]{:S(2)}) collective-permute-start(bf16[8,256,1,1024]{1,0,3,2:T(8,128)(2,1)S(1)} %get-tuple-element.9), channel_id=1, source_target_pairs={{0,1},{1,2},{2,3},{3,4},{4,5},{5,6},{6,7},{7,8},{8,9},{9,10},{10,1... | collective-permute-start | bytes 12582920 | tf_op jit(solution)/shard_map/ppermute | solution.py:64
  77.1 91.8 %collective-permute-start.3 = (bf16[8,256,1,1024]{1,0,3,2:T(8,128)(2,1)S(1)}, bf16[8,256,1,1024]{1,0,3,2:T(8,128)(2,1)S(1)}, u32[]{:S(2)}, u32[]{:S(2)}) collective-permute-start(bf16[8,256,1,1024]{1,0,3,2:T(8,128)(2,1)S(1)} %get-tuple-element.10), channel_id=1, source_target_pairs={{1,0},{2,1},{3,2},{4,3},{5,4},{6,5},{7,6},{8,7},{9,8},{10,9},{11,1... | collective-permute-start | bytes 12582920 | tf_op jit(solution)/shard_map/ppermute | solution.py:67
  198.3 8.0 %copy-start.3 = (bf16[8,69,2,1024]{3,2,1,0:T(2,128)(2,1)S(1)}, bf16[8,69,2,1024]{3,2,1,0:T(2,128)(2,1)}, u32[]{:S(2)}) copy-start(bf16[8,69,2,1024]{3,2,1,0:T(2,128)(2,1)} %param.10) | copy-start | bytes 6782980
  198.3 8.0 %copy-start.9 = (f32[69]{0:T(128)S(1)}, f32[69]{0:T(128)}, u32[]{:S(2)}) copy-start(f32[69]{0:T(128)} %param.14) | copy-start | bytes 832
  217.2 8.0 %copy-start.5 = (s32[2,256]{1,0:T(2,128)S(1)}, s32[2,256]{1,0:T(2,128)}, u32[]{:S(2)}) copy-start(s32[2,256]{1,0:T(2,128)} %param.15) | copy-start | bytes 6148
  217.2 55.4 %all-to-all-start = ((bf16[8,69,2,1024]{1,0,2,3:T(8,128)(2,1)}), bf16[8,69,2,1024]{1,0,2,3:T(8,128)(2,1)}, u32[]{:S(2)}, u32[]{:S(2)}) async-start(bf16[8,69,2,1024]{1,0,2,3:T(8,128)(2,1)} %copy.56), calls=%async_computation | async-start | bytes 8388608 | tf_op jit(solution)/shard_map/all_to_all | solution.py:76
  225.2 124.3 %all-gather.8.cloned.1.call-start = ((), (), s32[]{:S(2)}) async-start(), calls=%async_computation.1 | async-start | bytes 1769472 | tf_op jit(solution)/shard_map/all_gather | solution.py:111
  279.1 1.0 copy-start.4
  279.1 1.0 copy-start.6
  279.1 46.3 %copy-start.7 = (f32[2,8]{1,0:T(2,128)S(1)}, f32[2,8]{1,0:T(2,128)}, u32[]{:S(2)}) copy-start(f32[2,8]{1,0:T(2,128)} %param.19) | copy-start | bytes 196
  279.1 46.3 %copy-start.8 = (s32[2,8]{1,0:T(2,128)S(1)}, s32[2,8]{1,0:T(2,128)}, u32[]{:S(2)}) copy-start(s32[2,8]{1,0:T(2,128)} %param.18) | copy-start | bytes 196
  369.0 8.0 %copy-start.1 = (bf16[3,3,256,69]{2,3,1,0:T(8,128)(2,1)S(1)}, bf16[3,3,256,69]{2,3,1,0:T(8,128)(2,1)}, u32[]{:S(2)}) copy-start(bf16[3,3,256,69]{2,3,1,0:T(8,128)(2,1)} %param.11) | copy-start | bytes 953860
Sparse Core Ops, SparseCore 0:
  325.5 23.9 all-gather.7

commit v3 on v2

--- a/solution.py
+++ b/solution.py
@@ -56,18 +56,16 @@
     ):
         highest = lax.Precision.HIGHEST
         height = prior_samples.shape[2]
-        padded = padded_2(prior_samples, band_size, 1)
-
+        padded = padded_2(prior_samples, band_size, height)
         hidden_fields = jax.nn.silu(
             convolve(padded, conv1_weight) + conv1_bias[None, :, None, None]
         ).astype(jnp.bfloat16)
-        northern_halo = lax.ppermute(
-            hidden_fields[:, :, height - 1 :, :], BAND, shift_pairs(band_size, 1)
+        place = lax.axis_index(BAND)
+        row_ids = jnp.arange(height + 2, dtype=jnp.int32)[None, None, :, None]
+        outside = ((place == 0) & (row_ids == 0)) | (
+            (place == band_size - 1) & (row_ids == height + 1)
         )
-        southern_halo = lax.ppermute(
-            hidden_fields[:, :, :1, :], BAND, shift_pairs(band_size, -1)
-        )
-        extended = jnp.concatenate([northern_halo, hidden_fields, southern_halo], axis=2)
+        extended = jnp.where(outside, jnp.zeros_like(hidden_fields), hidden_fields)
         predicted_samples = (
             prior_samples.astype(jnp.float32)
             + convolve(extended, conv2_weight)

time: 385 us -> 317 us (0.82)
  waiting for transfers between devices: 171 us -> 102 us
  matrix products: 63.2 us -> 72.5 us
  starting transfers between devices: 18.9 us -> 13.5 us
  blocking collectives: 44.7 us -> 40 us
    ppermute x2 -> x0, waiting for transfers between devices: 90.3 us -> none  [the longest x1 86.2 us: on_device(): lax.ppermute(hidden_fields[:, :, height - 1:, :], BAND, shift_pairs(band_...]
    ppermute x1, waiting for transfers between devices: 14.4 us -> 39.6 us  [padded_2(): lax.ppermute(tail, BAND, shift_pairs(band_size, 1))]
    conv_general_dilated x2, matrix products: 50.7 us -> 60 us  [convolve(): lax.conv_general_dilated(wrapped, jnp.transpose(kernel, (2, 3, 0, 1)), wi...]
    slice x2 -> x1, local copies, waits for them, and re-layouts: 6.44 us -> 0.01 us  [convolve(): padded[..., -1:]]
    all_gather x4, blocking collectives: 44.7 us -> 40 us  [on_device(): packed = lax.all_gather(packed, axis, axis=0, tiled=False)]
    ppermute x2 -> x0, starting transfers between devices: 4.25 us -> none  [the longest x1 2.78 us: on_device(): lax.ppermute(hidden_fields[:, :, height - 1:, :], BAND, shift_pairs(band_...]
    unnamed x28 -> x27, local copies, waits for them, and re-layouts: 8.71 us -> 9.77 us
  transfers between devices with their start and end apart: 6 -> 4, of which waited for: 6 -> 3; matrix products, arithmetic and copies ran while one was open for 5% -> 7% of each run, Pallas kernels for 0% -> 0%
where the time goes in v3:
time: 317 us; the launch traced here: 315 us
  waiting for transfers between devices  102 us (32%)
  matrix products  72.5 us (23%)
  local copies, waits for them, and re-layouts  65.5 us (21%)
  blocking collectives  40 us (13%)
  between operations  13.8 us (4%)
  starting transfers between devices  13.5 us (4%)
  other arithmetic  7.48 us (2%)
    conv_general_dilated x2, matrix products, convolve(): lax.conv_general_dilated(wrapped, jnp.transpose(kernel, (2, 3, 0, 1)), wi...  60 us
    all_to_all x1, waiting for transfers between devices, on_device(): lax.all_to_all(predicted_samples, GRP, split_axis=3, concat_axis=0, tiled...  47.3 us
    all_gather x4, blocking collectives, on_device(): packed = lax.all_gather(packed, axis, axis=0, tiled=False)  40 us
    ppermute x1, waiting for transfers between devices, padded_2(): lax.ppermute(tail, BAND, shift_pairs(band_size, 1))  39.6 us
    all_gather x1, waiting for transfers between devices, on_device(): packed = lax.all_gather(packed, axis, axis=0, tiled=False)  15.5 us
    unnamed x27, local copies, waits for them, and re-layouts  9.77 us
    conv_general_dilated x1, local copies, waits for them, and re-layouts, convolve(): lax.conv_general_dilated(wrapped, jnp.transpose(kernel, (2, 3, 0, 1)), wi...  7.96 us
    transpose x1, local copies, waits for them, and re-layouts, on_device(): analysed.reshape(height, ensemble, channels, patch_width)  7.94 us
  transfers between devices with their start and end apart: 4, of which 3 were waited for; matrix products, arithmetic and copies ran while one was open for 7% of the time, Pallas kernels for 0%

profile of v3, /device:TPU:1, one launch (start us, length us, event | category | flops | bytes accessed | tf_op | source)
XLA Modules:
  0.0 315.4 jit_solution(11202129687380166503)
XLA Ops:
  6.5 3.9 %copy.49 = bf16[8,69,2,1024]{3,0,2,1:T(8,128)(2,1)} copy(bf16[8,69,2,1024]{3,2,1,0:T(2,128)(2,1)} %param.10) | data formatting | bytes 4521984 | tf_op args[0]
  10.4 5.8 %collective-permute-start = (bf16[8,69,2,1024]{3,0,2,1:T(8,128)(2,1)}, bf16[8,69,2,1024]{3,0,2,1:T(8,128)(2,1)}, u32[]{:S(2)}, u32[]{:S(2)}) collective-permute-start(bf16[8,69,2,1024]{3,0,2,1:T(8,128)(2,1)} %copy.49), channel_id=1, source_target_pairs={{0,1},{1,2},{2,3},{3,4},{4,5},{5,6},{6,7},{7,8},{8,9},{9,10},{10,1... | collective-permute-start | bytes 6782984 | tf_op jit(solution)/shard_map/ppermute | solution.py:24
  16.2 1.3 collective-permute-start.1
  17.5 5.8 %copy.53 = bf16[8,69,2,1024]{1,0,3,2:T(8,128)(2,1)} copy(bf16[8,69,2,1024]{3,2,1,0:T(2,128)(2,1)S(1)} %copy-done.2) | data formatting | bytes 4521984 | tf_op args[0]
  23.3 39.6 %collective-permute-done = bf16[8,69,2,1024]{3,0,2,1:T(8,128)(2,1)} collective-permute-done((bf16[8,69,2,1024]{3,0,2,1:T(8,128)(2,1)}, bf16[8,69,2,1024]{3,0,2,1:T(8,128)(2,1)}, u32[]{:S(2)}, u32[]{:S(2)}) %collective-permute-start) | collective-permute-done | bytes 2261024 | tf_op jit(solution)/shard_map/ppermute | solution.py:24
  62.9 6.8 %copy.52 = bf16[8,69,2,1024]{1,0,3,2:T(8,128)(2,1)} copy(bf16[8,69,2,1024]{3,0,2,1:T(8,128)(2,1)} %collective-permute-done) | data formatting | bytes 4521984 | tf_op jit(solution)/shard_map/ppermute | solution.py:24
  69.6 6.7 %copy.54 = bf16[8,69,2,1024]{1,0,3,2:T(8,128)(2,1)} copy(bf16[8,69,2,1024]{3,0,2,1:T(8,128)(2,1)} %collective-permute-done.1) | data formatting | bytes 4521984 | tf_op jit(solution)/shard_map/ppermute | solution.py:26
  76.4 37.8 %fusion.6 = bf16[8,256,4,1024]{1,0,3,2:T(8,128)(2,1)S(1)} fusion(f32[256]{0:T(256)S(1)} %copy-done.11, pred[4]{0:T(512)(128)(4,1)S(1)} %and_or_fusion, bf16[3,3,256,69]{2,3,1,0:T(8,128)(2,1)S(1)} %copy-done, bf16[8,69,2,1024]{1,0,3,2:T(8,128)(2,1)} %copy.54, bf16[8,69,2,1024]{1,0,3,2:T(8,128)(2,1)} %copy.53, bf16[8,69,2,1024]{1,0,3,2:T(8,128)(2,1)} %copy.52), kind=kOutput, calls=%fused_computation.8 | convolution fusion | flops 10504556544 | bytes 23879172 | tf_op jit(solution)/shard_map/conv_general_dilated | solution.py:34
  114.2 22.2 %fusion = f32[8,69,2,1024]{1,0,3,2:T(8,128)} fusion(bf16[3,3,69,256]{3,2,1,0:T(8,128)(2,1)S(1)} %copy-done.10, bf16[8,256,4,1]{1,0,3,2:T(8,128)(2,1)S(1)} %get-tuple-element.10, bf16[8,256,4,1024]{1,0,3,2:T(8,128)(2,1)S(1)} %fusion.6, bf16[8,256,4,1]{1,0,3,2:T(8,128)(2,1)S(1)} %get-tuple-element.9), kind=kOutput, calls=%fused_computation.2 | convolution fusion | flops 5226135552 | bytes 21649920 | tf_op jit(solution)/shard_map/conv_general_dilated | solution.py:34
  136.4 8.0 %copy.55 = f32[8,69,2,1024]{3,0,2,1:T(8,128)} copy(f32[8,69,2,1024]{1,0,3,2:T(8,128)} %fusion) | data formatting | bytes 9043968 | tf_op jit(solution)/shard_map/conv_general_dilated | solution.py:34
  144.3 4.2 %add_convert_fusion = bf16[8,69,2,1024]{3,0,2,1:T(8,128)(2,1)} fusion(f32[8,69,2,1024]{3,0,2,1:T(8,128)} %copy.55, f32[69]{0:T(128)S(1)} %copy-done.9, bf16[8,69,2,1024]{3,2,1,0:T(2,128)(2,1)S(1)} %copy-done.3), kind=kLoop, calls=%fused_computation.27 | loop fusion | flops 4521984 | bytes 9044244 | tf_op jit(solution)/shard_map/convert_element_type | solution.py:73
  148.6 6.7 %copy.56 = bf16[8,69,2,1024]{1,0,2,3:T(8,128)(2,1)} copy(bf16[8,69,2,1024]{3,0,2,1:T(8,128)(2,1)} %add_convert_fusion) | data formatting | bytes 4521984 | tf_op jit(solution)/shard_map/convert_element_type | solution.py:73
  155.3 6.5 %all-to-all-start = ((bf16[8,69,2,1024]{1,0,2,3:T(8,128)(2,1)}), bf16[8,69,2,1024]{1,0,2,3:T(8,128)(2,1)}, u32[]{:S(2)}, u32[]{:S(2)}) async-start(bf16[8,69,2,1024]{1,0,2,3:T(8,128)(2,1)} %copy.56), calls=%async_computation | async-start | bytes 8388608 | tf_op jit(solution)/shard_map/all_to_all | solution.py:74
  161.8 47.3 %all-to-all-done = bf16[8,69,2,1024]{1,0,2,3:T(8,128)(2,1)} async-done(((bf16[8,69,2,1024]{1,0,2,3:T(8,128)(2,1)}), bf16[8,69,2,1024]{1,0,2,3:T(8,128)(2,1)}, u32[]{:S(2)}, u32[]{:S(2)}) %all-to-all-start) | async-done | bytes 2261024 | tf_op jit(solution)/shard_map/all_to_all | solution.py:74
  209.1 6.5 %copy.57 = bf16[8,69,2,4,256]{4,1,0,3,2:T(8,128)(2,1)S(1)} copy(bf16[8,69,2,4,256]{1,0,2,4,3:T(8,128)(2,1)} %bitcast) | data formatting | bytes 4521984 | tf_op jit(solution)/shard_map/all_to_all | solution.py:74
  215.7 1.0 fusion.20
  216.7 0.2 fusion.34
  216.9 0.2 fusion.37
  217.2 10.8 %all-gather.5 = f32[4,2,1056]{2,1,0:T(2,128)S(1)} all-gather(f32[1,2,1056]{2,1,0:T(2,128)S(1)} %maximum_bitcast_fusion), channel_id=2, replica_groups=mesh['y_lo'=2,'core'=2,'y_hi'=2,'x'=4,'z'=4] {'z'}, dimensions={0}, use_global_device_ids=true | all-gather | bytes 42240 | tf_op jit(solution)/shard_map/all_gather | solution.py:109
  228.0 11.4 %all-gather.1 = f32[16,2,1056]{2,1,0:T(2,128)S(1)} all-gather(f32[4,2,1056]{2,1,0:T(2,128)S(1)} %all-gather.5), channel_id=3, replica_groups=mesh['y_lo'=2,'core'=2,'y_hi'=2,'x'=4,'z'=4] {'x'}, dimensions={0}, use_global_device_ids=true | all-gather | bytes 168960 | tf_op jit(solution)/shard_map/all_gather | solution.py:109
  239.4 8.4 %all-gather.2 = f32[8,4,2,1056]{3,1,2,0:T(4,128)S(1)} all-gather(f32[4,4,2,1056]{3,1,2,0:T(4,128)S(1)} %copy.58), channel_id=4, replica_groups=mesh['y_lo'=2,'core'=2,'y_hi'=2,'x'=4,'z'=4] {'y_hi'}, dimensions={0}, use_global_device_ids=true | all-gather | bytes 405504 | tf_op jit(solution)/shard_map/all_gather | solution.py:109
  247.8 9.5 %all-gather.3 = f32[4,4,4,2,1056]{4,2,3,1,0:T(4,128)} all-gather(f32[2,4,4,2,1056]{4,2,3,1,0:T(4,128)S(1)} %bitcast.88), channel_id=5, replica_groups=mesh['y_lo'=2,'core'=2,'y_hi'=2,'x'=4,'z'=4] {'core'}, dimensions={0}, use_global_device_ids=true | all-gather | bytes 811008 | tf_op jit(solution)/shard_map/all_gather | solution.py:109
  257.4 2.5 convert_bitcast_fusion
  259.9 5.1 %reshape.67 = f32[2,32,17664]{2,1,0:T(8,128)} reshape(f32[2,32,69,256]{3,2,1,0:T(8,128)} %convert_bitcast_fusion) | data formatting | bytes 9043968 | tf_op jit(solution)/shard_map/convert_element_type | solution.py:143
  265.1 0.3 convert_reduce_fusion
  265.5 15.5 %all-gather.8.cloned.1.call-done = f32[4,2,4,4,2,1056]{5,3,4,2,1,0:T(4,128)} async-done(((f32[2,2,4,4,2,1056]{5,3,4,2,1,0:T(4,128)}), f32[4,2,4,4,2,1056]{5,3,4,2,1,0:T(4,128)}) %all-gather.8.cloned.1.call-update) | async-done | bytes 1081360 | tf_op jit(solution)/shard_map/all_gather | solution.py:109
  281.0 1.9 copy.59
  282.9 0.8 reshape.64
  283.7 0.7 fusion.57
  284.6 0.3 fusion.28
  284.9 0.2 fusion.52
  285.3 0.2 fusion.27
  285.5 0.2 fusion.59
  285.6 0.2 fusion.58
  285.8 0.2 fusion.26
  286.0 0.2 fusion.61
  286.1 0.2 fusion.60
  286.3 0.2 fusion.25
  286.5 0.2 fusion.63
  286.6 0.2 fusion.62
  286.8 0.2 fusion.24
  287.0 0.2 fusion.65
  287.2 0.2 fusion.64
  287.3 0.2 fusion.23
  287.8 0.2 fusion.67
  288.1 7.4 %convolution_add_fusion = f32[2,32,17664]{2,1,0:T(8,128)} fusion(f32[2,32,17664]{2,1,0:T(8,128)} %reshape.67, f32[2,17664]{1,0:T(2,128)S(1)} %bitcast.90, f32[2,32,32]{2,1,0:T(8,128)S(1)} %fusion.66, f32[2,32]{1,0:T(2,128)S(1)} %broadcast_divide_fusion.3, f32[2]{0:T(128)S(1)} %get-tuple-element.15), kind=kOutput, calls=%fused_computation.1 | convolution fusion | flops 436375552 | bytes 9193736 | tf_op jit(solution)/shard_map/pkm,pkc->pmc/dot_general | solution.py:146
  295.4 5.2 %reshape.66 = f32[2,32,69,256]{3,2,1,0:T(8,128)} reshape(f32[2,32,17664]{2,1,0:T(8,128)} %convolution_add_fusion) | data formatting | bytes 9043968 | tf_op jit(solution)/shard_map/reshape | solution.py:149
  300.6 7.9 %copy.61 = f32[32,69,2,256]{3,2,1,0:T(2,128)} copy(f32[32,69,2,256]{3,1,0,2:T(8,128)} %bitcast.86) | data formatting | bytes 9043968 | tf_op jit(solution)/shard_map/transpose | solution.py:149
  (50 shorter events, 1.2 us)
Async XLA Ops:
  6.5 69.8 %copy-start = (bf16[3,3,256,69]{2,3,1,0:T(8,128)(2,1)S(1)}, bf16[3,3,256,69]{2,3,1,0:T(8,128)(2,1)}, u32[]{:S(2)}) copy-start(bf16[3,3,256,69]{2,3,1,0:T(8,128)(2,1)} %param.11) | copy-start | bytes 953860
  6.5 10.9 %copy-start.2 = (bf16[8,69,2,1024]{3,2,1,0:T(2,128)(2,1)S(1)}, bf16[8,69,2,1024]{3,2,1,0:T(2,128)(2,1)}, u32[]{:S(2)}) copy-start(bf16[8,69,2,1024]{3,2,1,0:T(2,128)(2,1)} %param.10) | copy-start | bytes 6782980
  10.4 52.5 %collective-permute-start = (bf16[8,69,2,1024]{3,0,2,1:T(8,128)(2,1)}, bf16[8,69,2,1024]{3,0,2,1:T(8,128)(2,1)}, u32[]{:S(2)}, u32[]{:S(2)}) collective-permute-start(bf16[8,69,2,1024]{3,0,2,1:T(8,128)(2,1)} %copy.49), channel_id=1, source_target_pairs={{0,1},{1,2},{2,3},{3,4},{4,5},{5,6},{6,7},{7,8},{8,9},{9,10},{10,1... | collective-permute-start | bytes 6782984 | tf_op jit(solution)/shard_map/ppermute | solution.py:24
  16.2 53.5 %collective-permute-start.1 = (bf16[8,69,2,1024]{3,0,2,1:T(8,128)(2,1)}, bf16[8,69,2,1024]{3,0,2,1:T(8,128)(2,1)}, u32[]{:S(2)}, u32[]{:S(2)}) collective-permute-start(bf16[8,69,2,1024]{3,0,2,1:T(8,128)(2,1)} %copy.49), channel_id=1, source_target_pairs={{1,0},{2,1},{3,2},{4,3},{5,4},{6,5},{7,6},{8,7},{9,8},{10,9},{11,1... | collective-permute-start | bytes 6782984 | tf_op jit(solution)/shard_map/ppermute | solution.py:26
  69.6 6.7 %copy-start.11 = (f32[256]{0:T(256)S(1)}, f32[256]{0:T(256)}, u32[]{:S(2)}) copy-start(f32[256]{0:T(256)} %param.12) | copy-start | bytes 3076
  76.4 37.8 %copy-start.10 = (bf16[3,3,69,256]{3,2,1,0:T(8,128)(2,1)S(1)}, bf16[3,3,69,256]{3,2,1,0:T(8,128)(2,1)}, u32[]{:S(2)}) copy-start(bf16[3,3,69,256]{3,2,1,0:T(8,128)(2,1)} %param.13) | copy-start | bytes 953860
  136.4 8.0 %copy-start.3 = (bf16[8,69,2,1024]{3,2,1,0:T(2,128)(2,1)S(1)}, bf16[8,69,2,1024]{3,2,1,0:T(2,128)(2,1)}, u32[]{:S(2)}) copy-start(bf16[8,69,2,1024]{3,2,1,0:T(2,128)(2,1)} %param.10) | copy-start | bytes 6782980
  136.4 8.0 %copy-start.9 = (f32[69]{0:T(128)S(1)}, f32[69]{0:T(128)}, u32[]{:S(2)}) copy-start(f32[69]{0:T(128)} %param.14) | copy-start | bytes 832
  155.3 6.5 %copy-start.5 = (s32[2,256]{1,0:T(2,128)S(1)}, s32[2,256]{1,0:T(2,128)}, u32[]{:S(2)}) copy-start(s32[2,256]{1,0:T(2,128)} %param.15) | copy-start | bytes 6148
  155.3 53.9 %all-to-all-start = ((bf16[8,69,2,1024]{1,0,2,3:T(8,128)(2,1)}), bf16[8,69,2,1024]{1,0,2,3:T(8,128)(2,1)}, u32[]{:S(2)}, u32[]{:S(2)}) async-start(bf16[8,69,2,1024]{1,0,2,3:T(8,128)(2,1)} %copy.56), calls=%async_computation | async-start | bytes 8388608 | tf_op jit(solution)/shard_map/all_to_all | solution.py:74
  161.7 119.3 %all-gather.8.cloned.1.call-start = ((), (), s32[]{:S(2)}) async-start(), calls=%async_computation.1 | async-start | bytes 1769472 | tf_op jit(solution)/shard_map/all_gather | solution.py:109
  215.6 1.0 copy-start.4
  215.6 1.0 copy-start.6
  215.7 41.6 %copy-start.7 = (f32[2,8]{1,0:T(2,128)S(1)}, f32[2,8]{1,0:T(2,128)}, u32[]{:S(2)}) copy-start(f32[2,8]{1,0:T(2,128)} %param.19) | copy-start | bytes 196
  215.7 41.6 %copy-start.8 = (s32[2,8]{1,0:T(2,128)S(1)}, s32[2,8]{1,0:T(2,128)}, u32[]{:S(2)}) copy-start(s32[2,8]{1,0:T(2,128)} %param.18) | copy-start | bytes 196
  295.4 13.1 %copy-start.1 = (bf16[3,3,256,69]{2,3,1,0:T(8,128)(2,1)S(1)}, bf16[3,3,256,69]{2,3,1,0:T(8,128)(2,1)}, u32[]{:S(2)}) copy-start(bf16[3,3,256,69]{2,3,1,0:T(8,128)(2,1)} %param.11) | copy-start | bytes 953860
Sparse Core Ops, SparseCore 0:
  257.4 23.5 all-gather.7

commit v4 on v3

--- a/solution.py
+++ b/solution.py
@@ -71,27 +71,31 @@
             + convolve(extended, conv2_weight)
             + conv2_bias[None, :, None, None]
         ).astype(jnp.bfloat16)
+        ensemble_part = predicted_samples.shape[0]
+        channels = predicted_samples.shape[1]
+        quarters = lax.psum(1, GRP)
+        patch_width = predicted_samples.shape[3] // quarters
+        row_index = lax.all_gather(obs_index, GRP, axis=0, tiled=False)
+        column = row_index % patch_width
+        channel = row_index // patch_width
+        column_hot = (
+            column[..., None] == jnp.arange(patch_width, dtype=jnp.int32)
+        ).astype(jnp.bfloat16)
+        by_column = jnp.einsum(
+            "mciql,qiol->qicmo",
+            predicted_samples.reshape(ensemble_part, channels, height, quarters, patch_width),
+            column_hot,
+            preferred_element_type=jnp.float32,
+        )
+        channel_hot = (
+            channel[:, :, None, :] == jnp.arange(channels, dtype=jnp.int32)[None, None, :, None]
+        ).astype(jnp.float32)
+        own_members = jnp.sum(by_column * channel_hot[:, :, :, None, :], axis=2)
+        predicted = lax.all_to_all(own_members, GRP, split_axis=0, concat_axis=2, tiled=True)[0]
         patch_block_slice = lax.all_to_all(
             predicted_samples, GRP, split_axis=3, concat_axis=0, tiled=True
         )
         ensemble = patch_block_slice.shape[0]
-        channels = patch_block_slice.shape[1]
-        patch_width = patch_block_slice.shape[3]
-
-        column = obs_index % patch_width
-        channel = obs_index // patch_width
-        column_hot = (
-            column[:, :, None] == jnp.arange(patch_width, dtype=jnp.int32)[None, None, :]
-        ).astype(jnp.bfloat16)
-        by_column = jnp.einsum(
-            "mcil,iol->icmo", patch_block_slice, column_hot,
-            preferred_element_type=jnp.float32,
-        )
-        channel_hot = (
-            channel[:, None, :] == jnp.arange(channels, dtype=jnp.int32)[None, :, None]
-        ).astype(jnp.float32)
-        predicted = jnp.sum(by_column * channel_hot[:, :, None, :], axis=1)
-
         predicted_mean = jnp.mean(predicted, axis=1)
         perturb = predicted - predicted_mean[:, None, :]
         innovation = obs_values - predicted_mean

time: 317 us -> 314 us (level)
  waiting for transfers between devices: 102 us -> 83.6 us
  blocking collectives: 40 us -> 53.2 us
  matrix products: 72.5 us -> 76.5 us
  local copies, waits for them, and re-layouts: 65.5 us -> 69.4 us
  other arithmetic: 7.48 us -> 3.82 us
    all_to_all x1, waiting for transfers between devices: 47.3 us -> 27.5 us  [on_device(): lax.all_to_all(predicted_samples, GRP, split_axis=3, concat_axis=0, tiled...]
    convert_element_type x1 -> x3, local copies, waits for them, and re-layouts: 5.13 us -> 15.8 us  [on_device(): field = realization_grid.astype(jnp.float32)]
    all_gather x1, waiting for transfers between devices: 15.5 us -> 23.8 us  [on_device(): packed = lax.all_gather(packed, axis, axis=0, tiled=False)]
    conv_general_dilated x1 -> x0, local copies, waits for them, and re-layouts: 7.96 us -> none  [convolve(): lax.conv_general_dilated(wrapped, jnp.transpose(kernel, (2, 3, 0, 1)), wi...]
    all_to_all x0 -> x1, blocking collectives: none -> 7.45 us  [on_device(): lax.all_to_all(own_members, GRP, split_axis=0, concat_axis=2, tiled=True)[0]]
    ppermute x1, waiting for transfers between devices: 39.6 us -> 32.2 us  [padded_2(): lax.ppermute(tail, BAND, shift_pairs(band_size, 1))]
    all_gather x0 -> x1, blocking collectives: none -> 5.9 us  [on_device(): row_index = lax.all_gather(obs_index, GRP, axis=0, tiled=False)]
    convert_element_type x3 -> x1, other arithmetic: 6.79 us -> 0.9 us  [on_device(): channel_hot = (channel[:, :, None, :] == jnp.arange(channels, dtype=jnp.i...]
  transfers between devices with their start and end apart: 4 -> 4, of which waited for: 3 -> 3; matrix products, arithmetic and copies ran while one was open for 7% -> 8% of each run, Pallas kernels for 0% -> 0%
where the time goes in v4:
time: 314 us; the launch traced here: 313 us
  waiting for transfers between devices  83.6 us (27%)
  matrix products  76.5 us (24%)
  local copies, waits for them, and re-layouts  69.4 us (22%)
  blocking collectives  53.2 us (17%)
  between operations  13.8 us (4%)
  starting transfers between devices  12.3 us (4%)
  other arithmetic  3.82 us (1%)
    conv_general_dilated x2, matrix products, convolve(): lax.conv_general_dilated(wrapped, jnp.transpose(kernel, (2, 3, 0, 1)), wi...  62.7 us
    all_gather x4, blocking collectives, on_device(): packed = lax.all_gather(packed, axis, axis=0, tiled=False)  39.8 us
    ppermute x1, waiting for transfers between devices, padded_2(): lax.ppermute(tail, BAND, shift_pairs(band_size, 1))  32.2 us
    all_to_all x1, waiting for transfers between devices, on_device(): lax.all_to_all(predicted_samples, GRP, split_axis=3, concat_axis=0, tiled...  27.5 us
    all_gather x1, waiting for transfers between devices, on_device(): packed = lax.all_gather(packed, axis, axis=0, tiled=False)  23.8 us
    convert_element_type x3, local copies, waits for them, and re-layouts, on_device(): field = realization_grid.astype(jnp.float32)  15.8 us
    unnamed x34, local copies, waits for them, and re-layouts  12.2 us
    transpose x1, local copies, waits for them, and re-layouts, on_device(): analysed.reshape(height, ensemble, channels, patch_width)  7.94 us
  transfers between devices with their start and end apart: 4, of which 3 were waited for; matrix products, arithmetic and copies ran while one was open for 8% of the time, Pallas kernels for 0%

profile of v4, /device:TPU:1, one launch (start us, length us, event | category | flops | bytes accessed | tf_op | source)
XLA Modules:
  0.0 312.5 jit_solution(16915041965266291866)
XLA Ops:
  6.5 3.9 %copy.95 = bf16[8,69,2,1024]{3,0,2,1:T(8,128)(2,1)} copy(bf16[8,69,2,1024]{3,2,1,0:T(2,128)(2,1)} %param.10) | data formatting | bytes 4521984 | tf_op args[0]
  10.4 5.8 %collective-permute-start = (bf16[8,69,2,1024]{3,0,2,1:T(8,128)(2,1)}, bf16[8,69,2,1024]{3,0,2,1:T(8,128)(2,1)}, u32[]{:S(2)}, u32[]{:S(2)}) collective-permute-start(bf16[8,69,2,1024]{3,0,2,1:T(8,128)(2,1)} %copy.95), channel_id=1, source_target_pairs={{0,1},{1,2},{2,3},{3,4},{4,5},{5,6},{6,7},{7,8},{8,9},{9,10},{10,1... | collective-permute-start | bytes 6782984 | tf_op jit(solution)/shard_map/ppermute | solution.py:24
  16.2 1.3 collective-permute-start.1
  17.5 5.7 %copy.94 = bf16[8,69,2,1024]{1,0,3,2:T(8,128)(2,1)} copy(bf16[8,69,2,1024]{3,2,1,0:T(2,128)(2,1)S(1)} %copy-done.2) | data formatting | bytes 4521984 | tf_op args[0]
  23.3 5.9 %all-gather.6 = s32[4,2,256]{2,1,0:T(2,128)S(1)} all-gather(s32[1,2,256]{2,1,0:T(2,128)S(1)} %bitcast.110), channel_id=2, replica_groups=mesh['y_lo'=2,'core'=2,'y_hi'=2,'x'=4,'z'=4] {'y_lo','core'}, dimensions={0}, use_global_device_ids=true | all-gather | bytes 10240 | tf_op jit(solution)/shard_map/all_gather | solution.py:78
  29.2 0.6 and_select_fusion.1
  29.8 0.9 fusion.39
  30.7 32.2 %collective-permute-done = bf16[8,69,2,1024]{3,0,2,1:T(8,128)(2,1)} collective-permute-done((bf16[8,69,2,1024]{3,0,2,1:T(8,128)(2,1)}, bf16[8,69,2,1024]{3,0,2,1:T(8,128)(2,1)}, u32[]{:S(2)}, u32[]{:S(2)}) %collective-permute-start) | collective-permute-done | bytes 2261024 | tf_op jit(solution)/shard_map/ppermute | solution.py:24
  62.9 6.7 %copy.97 = bf16[8,69,2,1024]{1,0,3,2:T(8,128)(2,1)} copy(bf16[8,69,2,1024]{3,0,2,1:T(8,128)(2,1)} %collective-permute-done) | data formatting | bytes 4521984 | tf_op jit(solution)/shard_map/ppermute | solution.py:24
  69.6 6.7 %copy.99 = bf16[8,69,2,1024]{1,0,3,2:T(8,128)(2,1)} copy(bf16[8,69,2,1024]{3,0,2,1:T(8,128)(2,1)} %collective-permute-done.1) | data formatting | bytes 4521984 | tf_op jit(solution)/shard_map/ppermute | solution.py:26
  76.4 39.8 %fusion.6 = bf16[8,256,4,1024]{1,0,3,2:T(8,128)(2,1)} fusion(f32[256]{0:T(256)S(1)} %copy-done.13, pred[4]{0:T(512)(128)(4,1)S(1)} %and_or_fusion, bf16[3,3,256,69]{2,3,1,0:T(8,128)(2,1)S(1)} %copy-done, bf16[8,69,2,1024]{1,0,3,2:T(8,128)(2,1)} %copy.99, bf16[8,69,2,1024]{1,0,3,2:T(8,128)(2,1)} %copy.94, bf16[8,69,2,1024]{1,0,3,2:T(8,128)(2,1)} %copy.97), kind=kOutput, calls=%fused_computation.8 | convolution fusion | flops 10504556544 | bytes 23879172 | tf_op jit(solution)/shard_map/conv_general_dilated | solution.py:34
  116.2 0.7 fusion.62
  116.9 22.9 %add_convert_fusion = bf16[8,69,2,1024]{1,0,3,2:T(8,128)(2,1)S(1)} fusion(bf16[8,69,2,1024]{1,0,3,2:T(8,128)(2,1)S(1)} %copy-done.3, f32[69]{0:T(128)S(1)} %copy-done.14, bf16[3,3,69,256]{3,2,1,0:T(8,128)(2,1)S(1)} %copy-done.12, bf16[8,256,4,1]{1,0,3,2:T(8,128)(2,1)S(1)} %get-tuple-element.8, bf16[8,256,4,1024]{1,0,3,2:T(8,128)(2,1)} %fusion.6, ...), kind=kOutput, calls=%fused_computation.23 | convolution fusion | flops 5230657536 | bytes 21650196 | tf_op jit(solution)/shard_map/conv_general_dilated | solution.py:34
  139.9 2.0 copy-done.4
  141.9 1.9 fusion.19
  143.8 7.5 %all_to_all.27 = f32[4,2,8,256]{3,2,1,0:T(8,128)S(1)} all-to-all(f32[4,2,8,256]{3,2,1,0:T(8,128)S(1)} %fusion.19), channel_id=1, replica_groups=mesh['y_lo'=2,'core'=2,'y_hi'=2,'x'=4,'z'=4] {'y_lo','core'}, dimensions={0} | all-to-all | bytes 131072 | tf_op jit(solution)/shard_map/all_to_all | solution.py:94
  151.3 0.2 fusion.40
  151.6 0.2 fusion.42
  151.8 10.8 %all-gather.7 = f32[4,2,1056]{2,1,0:T(2,128)S(1)} all-gather(f32[1,2,1056]{2,1,0:T(2,128)S(1)} %maximum_bitcast_fusion), channel_id=3, replica_groups=mesh['y_lo'=2,'core'=2,'y_hi'=2,'x'=4,'z'=4] {'z'}, dimensions={0}, use_global_device_ids=true | all-gather | bytes 42240 | tf_op jit(solution)/shard_map/all_gather | solution.py:113
  162.6 11.1 %all-gather.2 = f32[16,2,1056]{2,1,0:T(2,128)S(1)} all-gather(f32[4,2,1056]{2,1,0:T(2,128)S(1)} %all-gather.7), channel_id=4, replica_groups=mesh['y_lo'=2,'core'=2,'y_hi'=2,'x'=4,'z'=4] {'x'}, dimensions={0}, use_global_device_ids=true | all-gather | bytes 168960 | tf_op jit(solution)/shard_map/all_gather | solution.py:113
  173.8 8.4 %all-gather.3 = f32[8,4,2,1056]{3,1,2,0:T(4,128)S(1)} all-gather(f32[4,4,2,1056]{3,1,2,0:T(4,128)S(1)} %copy.106), channel_id=5, replica_groups=mesh['y_lo'=2,'core'=2,'y_hi'=2,'x'=4,'z'=4] {'y_hi'}, dimensions={0}, use_global_device_ids=true | all-gather | bytes 405504 | tf_op jit(solution)/shard_map/all_gather | solution.py:113
  182.2 9.5 %all-gather.4 = f32[4,4,4,2,1056]{4,2,3,1,0:T(4,128)} all-gather(f32[2,4,4,2,1056]{4,2,3,1,0:T(4,128)S(1)} %bitcast.102), channel_id=6, replica_groups=mesh['y_lo'=2,'core'=2,'y_hi'=2,'x'=4,'z'=4] {'core'}, dimensions={0}, use_global_device_ids=true | all-gather | bytes 811008 | tf_op jit(solution)/shard_map/all_gather | solution.py:113
  191.8 4.9 %copy.100 = bf16[8,69,2,1024]{1,0,2,3:T(8,128)(2,1)} copy(bf16[8,69,2,1024]{1,0,3,2:T(8,128)(2,1)} %copy-done.4) | data formatting | bytes 4521984 | tf_op jit(solution)/shard_map/convert_element_type | solution.py:73
  196.7 5.2 %all-to-all-start = ((bf16[8,69,2,1024]{1,0,2,3:T(8,128)(2,1)}), bf16[8,69,2,1024]{1,0,2,3:T(8,128)(2,1)}, u32[]{:S(2)}, u32[]{:S(2)}) async-start(bf16[8,69,2,1024]{1,0,2,3:T(8,128)(2,1)} %copy.100), calls=%async_computation | async-start | bytes 8388608 | tf_op jit(solution)/shard_map/all_to_all | solution.py:95
  201.9 23.8 %all-gather.10.cloned.1.call-done = f32[4,2,4,4,2,1056]{5,3,4,2,1,0:T(4,128)} async-done(((f32[2,2,4,4,2,1056]{5,3,4,2,1,0:T(4,128)}), f32[4,2,4,4,2,1056]{5,3,4,2,1,0:T(4,128)}) %all-gather.10.cloned.1.call-update) | async-done | bytes 1081360 | tf_op jit(solution)/shard_map/all_gather | solution.py:113
  225.8 1.9 copy.107
  227.6 0.8 reshape.72
  228.5 0.7 fusion.63
  229.3 0.3 fusion.37
  229.6 0.2 fusion.58
  230.0 0.2 fusion.36
  230.2 0.2 fusion.65
  230.3 0.2 fusion.64
  230.5 0.2 fusion.35
  231.0 0.2 fusion.34
  231.5 0.2 fusion.33
  232.0 0.2 fusion.32
  232.5 0.2 fusion.73
  232.8 27.5 %all-to-all-done = bf16[8,69,2,1024]{1,0,2,3:T(8,128)(2,1)} async-done(((bf16[8,69,2,1024]{1,0,2,3:T(8,128)(2,1)}), bf16[8,69,2,1024]{1,0,2,3:T(8,128)(2,1)}, u32[]{:S(2)}, u32[]{:S(2)}) %all-to-all-start) | async-done | bytes 2261024 | tf_op jit(solution)/shard_map/all_to_all | solution.py:95
  260.3 6.1 %copy.101 = bf16[8,69,2,1024]{3,0,2,1:T(8,128)(2,1)S(1)} copy(bf16[8,69,2,1024]{1,0,2,3:T(8,128)(2,1)} %all-to-all-done) | data formatting | bytes 4521984 | tf_op jit(solution)/shard_map/all_to_all | solution.py:95
  266.5 3.6 %reshape.83 = f32[8,69,2,4,256]{4,3,0,2,1:T(4,128)} reshape(bf16[8,69,2,1024]{3,0,2,1:T(8,128)(2,1)S(1)} %copy.101) | data formatting | bytes 6782976 | tf_op jit(solution)/shard_map/convert_element_type | solution.py:147
  270.1 1.8 convert_reduce_fusion
  271.9 7.0 %copy.120 = f32[4,8,69,2,256]{4,2,1,0,3:T(8,128)} copy(f32[4,8,69,2,256]{4,0,1,3,2:T(4,128)} %bitcast.98) | data formatting | bytes 9043968 | tf_op jit(solution)/shard_map/convert_element_type | solution.py:147
  279.0 5.1 %reshape.75 = f32[2,32,17664]{2,1,0:T(8,128)} reshape(f32[2,32,69,256]{3,2,1,0:T(8,128)} %bitcast.96) | data formatting | bytes 9043968 | tf_op jit(solution)/shard_map/convert_element_type | solution.py:147
  284.1 0.5 copy.121
  284.9 7.6 %convolution_add_fusion = f32[2,32,17664]{2,1,0:T(8,128)} fusion(f32[2,32,17664]{2,1,0:T(8,128)} %reshape.75, f32[2,17664]{1,0:T(2,128)S(1)} %bitcast.105, f32[2,32,32]{2,1,0:T(8,128)S(1)} %fusion.72, f32[2,32]{1,0:T(2,128)S(1)} %broadcast_divide_fusion.3, f32[2]{0:T(128)S(1)} %get-tuple-element.13), kind=kOutput, calls=%fused_computation.1 | convolution fusion | flops 436375552 | bytes 9193736 | tf_op jit(solution)/shard_map/pkm,pkc->pmc/dot_general | solution.py:150
  292.5 5.2 %reshape.74 = f32[2,32,69,256]{3,2,1,0:T(8,128)} reshape(f32[2,32,17664]{2,1,0:T(8,128)} %convolution_add_fusion) | data formatting | bytes 9043968 | tf_op jit(solution)/shard_map/reshape | solution.py:153
  297.7 7.9 %copy.111 = f32[32,69,2,256]{3,2,1,0:T(2,128)} copy(f32[32,69,2,256]{3,1,0,2:T(8,128)} %bitcast.97) | data formatting | bytes 9043968 | tf_op jit(solution)/shard_map/transpose | solution.py:153
  (61 shorter events, 2.4 us)
Async XLA Ops:
  6.5 69.8 %copy-start = (bf16[3,3,256,69]{2,3,1,0:T(8,128)(2,1)S(1)}, bf16[3,3,256,69]{2,3,1,0:T(8,128)(2,1)}, u32[]{:S(2)}) copy-start(bf16[3,3,256,69]{2,3,1,0:T(8,128)(2,1)} %param.11) | copy-start | bytes 953860
  6.5 11.0 %copy-start.2 = (bf16[8,69,2,1024]{3,2,1,0:T(2,128)(2,1)S(1)}, bf16[8,69,2,1024]{3,2,1,0:T(2,128)(2,1)}, u32[]{:S(2)}) copy-start(bf16[8,69,2,1024]{3,2,1,0:T(2,128)(2,1)} %param.10) | copy-start | bytes 6782980
  6.5 16.7 %copy-start.8 = (s32[2,256]{1,0:T(2,128)S(1)}, s32[2,256]{1,0:T(2,128)}, u32[]{:S(2)}) copy-start(s32[2,256]{1,0:T(2,128)} %param.15) | copy-start | bytes 6148
  6.5 219.2 %all-gather.10.cloned.1.call-start = ((), (), s32[]{:S(2)}) async-start(), calls=%async_computation.2 | async-start | bytes 1769472 | tf_op jit(solution)/shard_map/all_gather | solution.py:113
  10.4 52.5 %collective-permute-start = (bf16[8,69,2,1024]{3,0,2,1:T(8,128)(2,1)}, bf16[8,69,2,1024]{3,0,2,1:T(8,128)(2,1)}, u32[]{:S(2)}, u32[]{:S(2)}) collective-permute-start(bf16[8,69,2,1024]{3,0,2,1:T(8,128)(2,1)} %copy.95), channel_id=1, source_target_pairs={{0,1},{1,2},{2,3},{3,4},{4,5},{5,6},{6,7},{7,8},{8,9},{9,10},{10,1... | collective-permute-start | bytes 6782984 | tf_op jit(solution)/shard_map/ppermute | solution.py:24
  16.2 53.4 %collective-permute-start.1 = (bf16[8,69,2,1024]{3,0,2,1:T(8,128)(2,1)}, bf16[8,69,2,1024]{3,0,2,1:T(8,128)(2,1)}, u32[]{:S(2)}, u32[]{:S(2)}) collective-permute-start(bf16[8,69,2,1024]{3,0,2,1:T(8,128)(2,1)} %copy.95), channel_id=1, source_target_pairs={{1,0},{2,1},{3,2},{4,3},{5,4},{6,5},{7,6},{8,7},{9,8},{10,9},{11,1... | collective-permute-start | bytes 6782984 | tf_op jit(solution)/shard_map/ppermute | solution.py:26
  69.6 6.8 %copy-start.13 = (f32[256]{0:T(256)S(1)}, f32[256]{0:T(256)}, u32[]{:S(2)}) copy-start(f32[256]{0:T(256)} %param.12) | copy-start | bytes 3076
  76.3 40.6 %copy-start.3 = (bf16[8,69,2,1024]{1,0,3,2:T(8,128)(2,1)S(1)}, bf16[8,69,2,1024]{1,0,3,2:T(8,128)(2,1)}, u32[]{:S(2)}) copy-start(bf16[8,69,2,1024]{1,0,3,2:T(8,128)(2,1)} %copy.94) | copy-start | bytes 6782980
  76.3 40.6 %copy-start.12 = (bf16[3,3,69,256]{3,2,1,0:T(8,128)(2,1)S(1)}, bf16[3,3,69,256]{3,2,1,0:T(8,128)(2,1)}, u32[]{:S(2)}) copy-start(bf16[3,3,69,256]{3,2,1,0:T(8,128)(2,1)} %param.13) | copy-start | bytes 953860
  76.4 40.6 %copy-start.14 = (f32[69]{0:T(128)S(1)}, f32[69]{0:T(128)}, u32[]{:S(2)}) copy-start(f32[69]{0:T(128)} %param.14) | copy-start | bytes 832
  116.9 25.0 %copy-start.5 = (f32[4,2,69,256]{3,2,1,0:T(8,128)S(1)}, f32[4,2,69,256]{3,2,1,0:T(8,128)}, u32[]{:S(2)}) copy-start(f32[4,2,69,256]{3,2,1,0:T(8,128)} %fusion.39) | copy-start | bytes 1695748
  116.9 25.0 %copy-start.7 = (s32[4,2,256]{2,1,0:T(2,128)S(1)}, s32[4,2,256]{2,1,0:T(2,128)}, u32[]{:S(2)}) copy-start(s32[4,2,256]{2,1,0:T(2,128)} %get-tuple-element.9) | copy-start | bytes 24580
  139.9 2.0 copy-start.4
  139.9 11.4 %copy-start.6 = (f32[2,256]{1,0:T(2,128)S(1)}, f32[2,256]{1,0:T(2,128)}, u32[]{:S(2)}) copy-start(f32[2,256]{1,0:T(2,128)} %param.17) | copy-start | bytes 6148
  139.9 11.4 %copy-start.9 = (f32[2,256]{1,0:T(2,128)S(1)}, f32[2,256]{1,0:T(2,128)}, u32[]{:S(2)}) copy-start(f32[2,256]{1,0:T(2,128)} %param.16) | copy-start | bytes 6148
  141.9 49.8 %copy-start.10 = (f32[2,8]{1,0:T(2,128)S(1)}, f32[2,8]{1,0:T(2,128)}, u32[]{:S(2)}) copy-start(f32[2,8]{1,0:T(2,128)} %param.19) | copy-start | bytes 196
  141.9 49.8 %copy-start.11 = (s32[2,8]{1,0:T(2,128)S(1)}, s32[2,8]{1,0:T(2,128)}, u32[]{:S(2)}) copy-start(s32[2,8]{1,0:T(2,128)} %param.18) | copy-start | bytes 196
  196.7 63.6 %all-to-all-start = ((bf16[8,69,2,1024]{1,0,2,3:T(8,128)(2,1)}), bf16[8,69,2,1024]{1,0,2,3:T(8,128)(2,1)}, u32[]{:S(2)}, u32[]{:S(2)}) async-start(bf16[8,69,2,1024]{1,0,2,3:T(8,128)(2,1)} %copy.100), calls=%async_computation | async-start | bytes 8388608 | tf_op jit(solution)/shard_map/all_to_all | solution.py:95
  292.5 13.1 %copy-start.1 = (bf16[3,3,256,69]{2,3,1,0:T(8,128)(2,1)S(1)}, bf16[3,3,256,69]{2,3,1,0:T(8,128)(2,1)}, u32[]{:S(2)}) copy-start(bf16[3,3,256,69]{2,3,1,0:T(8,128)(2,1)} %param.11) | copy-start | bytes 953860
Sparse Core Ops, SparseCore 0:
  191.8 33.9 all-gather.9

commit v5 on v4

--- a/solution.py
+++ b/solution.py
@@ -92,10 +92,20 @@
         ).astype(jnp.float32)
         own_members = jnp.sum(by_column * channel_hot[:, :, :, None, :], axis=2)
         predicted = lax.all_to_all(own_members, GRP, split_axis=0, concat_axis=2, tiled=True)[0]
-        patch_block_slice = lax.all_to_all(
-            predicted_samples, GRP, split_axis=3, concat_axis=0, tiled=True
-        )
+        me = lax.axis_index(GRP)
+        blocks = predicted_samples.reshape(ensemble_part, channels, height, quarters, patch_width)
+        pieces = [lax.dynamic_index_in_dim(blocks, me, axis=3, keepdims=False)]
+        for step in range(1, quarters):
+            outgoing = lax.dynamic_index_in_dim(blocks, (me + step) % quarters, axis=3, keepdims=False)
+            pieces.append(
+                lax.ppermute(outgoing, GRP, [(j, (j + step) % quarters) for j in range(quarters)])
+            )
+        patch_block_slice = jnp.concatenate(pieces, axis=0)
         ensemble = patch_block_slice.shape[0]
+        source_member = (
+            ((me - jnp.arange(quarters, dtype=jnp.int32)) % quarters)[:, None] * ensemble_part
+            + jnp.arange(ensemble_part, dtype=jnp.int32)[None, :]
+        ).reshape(ensemble)
         predicted_mean = jnp.mean(predicted, axis=1)
         perturb = predicted - predicted_mean[:, None, :]
         innovation = obs_values - predicted_mean
@@ -141,16 +151,18 @@
         transform = (jnp.sqrt(ensemble - 1.0) / jnp.sqrt(norm_scale))[
             :, None, None
         ] * inverse_root + mean_weight[:, :, None]
-        realization_grid = jnp.transpose(patch_block_slice, (2, 0, 1, 3)).reshape(
-            height, ensemble, channels * patch_width
+        weights = transform + (1.0 - jnp.sum(transform, axis=1, keepdims=True)) / ensemble
+        weights = jnp.take(weights, source_member, axis=1)
+        patch_of = jnp.arange(height, dtype=jnp.int32)
+        spread_out = jnp.where(
+            (patch_of[:, None] == patch_of[None, :])[None, :, None, :, None],
+            patch_block_slice.astype(jnp.float32)[:, None],
+            0.0,
         )
-        field = realization_grid.astype(jnp.float32)
-        centre = jnp.mean(field, axis=1)
-        spread = field - centre[:, None, :]
-        analysed = centre[:, None, :] + jnp.einsum(
-            "pkm,pkc->pmc", transform, spread, precision=highest
+        analysed = jnp.einsum(
+            "ikm,kicjl->mcjl", weights, spread_out, precision=highest
         )
-        return analysed.reshape(height, ensemble, channels, patch_width).transpose(1, 2, 0, 3)
+        return analysed
 
     return on_device
 

time: 314 us -> 272 us (0.87)
  local copies, waits for them, and re-layouts: 69.4 us -> 45.8 us
  waiting for transfers between devices: 83.6 us -> 67.5 us
  blocking collectives: 53.2 us -> 46 us
  other arithmetic: 3.82 us -> 7.26 us
    ppermute x0 -> x3, waiting for transfers between devices: none -> 33.4 us  [on_device(): lax.ppermute(outgoing, GRP, [(j, (j + step) % quarters) for j in range(qu...]
    all_to_all x1, waiting for transfers between devices: 27.5 us -> 3.2 us  [on_device(): lax.all_to_all(own_members, GRP, split_axis=0, concat_axis=2, tiled=True)[0]]
    all_gather x1, waiting for transfers between devices: 23.8 us -> 0.01 us  [on_device(): packed = lax.all_gather(packed, axis, axis=0, tiled=False)]
    convert_element_type x4 -> x0, local copies, waits for them, and re-layouts: 20.6 us -> none  [the longest x3 15.8 us: on_device(): field = realization_grid.astype(jnp.float32)]
    transpose x1 -> x0, local copies, waits for them, and re-layouts: 7.94 us -> none  [on_device(): analysed.reshape(height, ensemble, channels, patch_width)]
    all_to_all x1 -> x0, blocking collectives: 7.45 us -> none  [on_device(): lax.all_to_all(own_members, GRP, split_axis=0, concat_axis=2, tiled=True)[0]]
    unnamed x34 -> x44, local copies, waits for them, and re-layouts: 12.2 us -> 18.9 us
    all_to_all x1 -> x0, local copies, waits for them, and re-layouts: 6.15 us -> none  [on_device(): lax.all_to_all(predicted_samples, GRP, split_axis=3, concat_axis=0, tiled...]
  transfers between devices with their start and end apart: 4 -> 7, of which waited for: 3 -> 5; matrix products, arithmetic and copies ran while one was open for 8% -> 11% of each run, Pallas kernels for 0% -> 0%
where the time goes in v5:
time: 272 us; the launch traced here: 271 us
  matrix products  77.2 us (28%)
  waiting for transfers between devices  67.5 us (25%)
  blocking collectives  46 us (17%)
  local copies, waits for them, and re-layouts  45.8 us (17%)
  between operations  13.9 us (5%)
  starting transfers between devices  13.6 us (5%)
  other arithmetic  7.26 us (3%)
    conv_general_dilated x2, matrix products, convolve(): lax.conv_general_dilated(wrapped, jnp.transpose(kernel, (2, 3, 0, 1)), wi...  62.7 us
    all_gather x4, blocking collectives, on_device(): packed = lax.all_gather(packed, axis, axis=0, tiled=False)  40.1 us
    ppermute x3, waiting for transfers between devices, on_device(): lax.ppermute(outgoing, GRP, [(j, (j + step) % quarters) for j in range(qu...  33.4 us
    ppermute x1, waiting for transfers between devices, padded_2(): lax.ppermute(tail, BAND, shift_pairs(band_size, 1))  30.8 us
    unnamed x44, local copies, waits for them, and re-layouts  18.9 us
    dot_general x1, matrix products, on_device(): jnp.einsum('ikm,kicjl->mcjl', weights, spread_out, precision=highest)  7.71 us
    ppermute x1, local copies, waits for them, and re-layouts, padded_2(): lax.ppermute(head, BAND, shift_pairs(band_size, -1))  6.77 us
    ppermute x1, local copies, waits for them, and re-layouts, padded_2(): lax.ppermute(tail, BAND, shift_pairs(band_size, 1))  6.7 us
  transfers between devices with their start and end apart: 7, of which 5 were waited for; matrix products, arithmetic and copies ran while one was open for 11% of the time, Pallas kernels for 0%

profile of v5, /device:TPU:1, one launch (start us, length us, event | category | flops | bytes accessed | tf_op | source)
XLA Modules:
  0.0 271.2 jit_solution(4583143686698539172)
XLA Ops:
  6.5 3.9 %copy.64 = bf16[8,69,2,1024]{3,0,2,1:T(8,128)(2,1)} copy(bf16[8,69,2,1024]{3,2,1,0:T(2,128)(2,1)} %param.10) | data formatting | bytes 4521984 | tf_op args[0]
  10.4 5.8 %collective-permute-start = (bf16[8,69,2,1024]{3,0,2,1:T(8,128)(2,1)}, bf16[8,69,2,1024]{3,0,2,1:T(8,128)(2,1)}, u32[]{:S(2)}, u32[]{:S(2)}) collective-permute-start(bf16[8,69,2,1024]{3,0,2,1:T(8,128)(2,1)} %copy.64), channel_id=1, source_target_pairs={{0,1},{1,2},{2,3},{3,4},{4,5},{5,6},{6,7},{7,8},{8,9},{9,10},{10,1... | collective-permute-start | bytes 6782984 | tf_op jit(solution)/shard_map/ppermute | solution.py:24
  16.2 1.3 collective-permute-start.1
  17.5 5.7 %copy.63 = bf16[8,69,2,1024]{1,0,3,2:T(8,128)(2,1)} copy(bf16[8,69,2,1024]{3,2,1,0:T(2,128)(2,1)S(1)} %copy-done.2) | data formatting | bytes 4521984 | tf_op args[0]
  23.4 5.9 %all-gather.6 = s32[4,2,256]{2,1,0:T(2,128)S(1)} all-gather(s32[1,2,256]{2,1,0:T(2,128)S(1)} %bitcast.108), channel_id=2, replica_groups=mesh['y_lo'=2,'core'=2,'y_hi'=2,'x'=4,'z'=4] {'y_lo','core'}, dimensions={0}, use_global_device_ids=true | all-gather | bytes 10240 | tf_op jit(solution)/shard_map/all_gather | solution.py:78
  29.3 0.6 fusion.62
  29.9 0.6 fusion.67
  30.5 0.6 and_select_fusion.1
  31.1 0.9 fusion.45
  32.1 30.8 %collective-permute-done = bf16[8,69,2,1024]{3,0,2,1:T(8,128)(2,1)} collective-permute-done((bf16[8,69,2,1024]{3,0,2,1:T(8,128)(2,1)}, bf16[8,69,2,1024]{3,0,2,1:T(8,128)(2,1)}, u32[]{:S(2)}, u32[]{:S(2)}) %collective-permute-start) | collective-permute-done | bytes 2261024 | tf_op jit(solution)/shard_map/ppermute | solution.py:24
  62.9 6.7 %copy.66 = bf16[8,69,2,1024]{1,0,3,2:T(8,128)(2,1)} copy(bf16[8,69,2,1024]{3,0,2,1:T(8,128)(2,1)} %collective-permute-done) | data formatting | bytes 4521984 | tf_op jit(solution)/shard_map/ppermute | solution.py:24
  69.6 6.8 %copy.68 = bf16[8,69,2,1024]{1,0,3,2:T(8,128)(2,1)} copy(bf16[8,69,2,1024]{3,0,2,1:T(8,128)(2,1)} %collective-permute-done.1) | data formatting | bytes 4521984 | tf_op jit(solution)/shard_map/ppermute | solution.py:26
  76.4 39.8 %fusion.6 = bf16[8,256,4,1024]{1,0,3,2:T(8,128)(2,1)} fusion(f32[256]{0:T(256)S(1)} %copy-done.17, pred[4]{0:T(512)(128)(4,1)S(1)} %and_or_fusion, bf16[3,3,256,69]{2,3,1,0:T(8,128)(2,1)S(1)} %copy-done, bf16[8,69,2,1024]{1,0,3,2:T(8,128)(2,1)} %copy.68, bf16[8,69,2,1024]{1,0,3,2:T(8,128)(2,1)} %copy.63, bf16[8,69,2,1024]{1,0,3,2:T(8,128)(2,1)} %copy.66), kind=kOutput, calls=%fused_computation.8 | convolution fusion | flops 10504556544 | bytes 23879172 | tf_op jit(solution)/shard_map/conv_general_dilated | solution.py:34
  116.2 0.7 fusion.71
  117.0 22.9 %add_convert_fusion = bf16[8,69,2,1024]{1,0,3,2:T(8,128)(2,1)S(1)} fusion(bf16[8,69,2,1024]{1,0,3,2:T(8,128)(2,1)S(1)} %copy-done.4, f32[69]{0:T(128)S(1)} %copy-done.18, bf16[3,3,69,256]{3,2,1,0:T(8,128)(2,1)S(1)} %copy-done.16, bf16[8,256,4,1]{1,0,3,2:T(8,128)(2,1)S(1)} %get-tuple-element.8, bf16[8,256,4,1024]{1,0,3,2:T(8,128)(2,1)} %fusion.6, ...), kind=kOutput, calls=%fused_computation.25 | convolution fusion | flops 5230657536 | bytes 21650196 | tf_op jit(solution)/shard_map/conv_general_dilated | solution.py:34
  140.0 2.0 copy-done.3
  142.0 2.5 fusion.21
  144.5 4.8 %all-to-all-start = ((f32[4,2,8,256]{3,2,1,0:T(8,128)}), f32[4,2,8,256]{3,2,1,0:T(8,128)S(1)}, u32[]{:S(2)}, u32[]{:S(2)}) async-start(f32[4,2,8,256]{3,2,1,0:T(8,128)} %fusion.21), calls=%async_computation | async-start | bytes 131072 | tf_op jit(solution)/shard_map/all_to_all | solution.py:94
  149.4 3.2 %all-to-all-done = f32[4,2,8,256]{3,2,1,0:T(8,128)S(1)} async-done(((f32[4,2,8,256]{3,2,1,0:T(8,128)}), f32[4,2,8,256]{3,2,1,0:T(8,128)S(1)}, u32[]{:S(2)}, u32[]{:S(2)}) %all-to-all-start) | async-done | bytes 65568 | tf_op jit(solution)/shard_map/all_to_all | solution.py:94
  152.6 0.2 fusion.46
  152.9 0.2 fusion.48
  153.1 10.8 %all-gather.7 = f32[4,2,1056]{2,1,0:T(2,128)S(1)} all-gather(f32[1,2,1056]{2,1,0:T(2,128)S(1)} %maximum_bitcast_fusion), channel_id=3, replica_groups=mesh['y_lo'=2,'core'=2,'y_hi'=2,'x'=4,'z'=4] {'z'}, dimensions={0}, use_global_device_ids=true | all-gather | bytes 42240 | tf_op jit(solution)/shard_map/all_gather | solution.py:123
  163.9 11.5 %all-gather.2 = f32[16,2,1056]{2,1,0:T(2,128)S(1)} all-gather(f32[4,2,1056]{2,1,0:T(2,128)S(1)} %all-gather.7), channel_id=4, replica_groups=mesh['y_lo'=2,'core'=2,'y_hi'=2,'x'=4,'z'=4] {'x'}, dimensions={0}, use_global_device_ids=true | all-gather | bytes 168960 | tf_op jit(solution)/shard_map/all_gather | solution.py:123
  175.4 8.3 %all-gather.3 = f32[8,4,2,1056]{3,1,2,0:T(4,128)S(1)} all-gather(f32[4,4,2,1056]{3,1,2,0:T(4,128)S(1)} %copy.71), channel_id=5, replica_groups=mesh['y_lo'=2,'core'=2,'y_hi'=2,'x'=4,'z'=4] {'y_hi'}, dimensions={0}, use_global_device_ids=true | all-gather | bytes 405504 | tf_op jit(solution)/shard_map/all_gather | solution.py:123
  183.7 9.5 %all-gather.4 = f32[4,4,4,2,1056]{4,2,3,1,0:T(4,128)} all-gather(f32[2,4,4,2,1056]{4,2,3,1,0:T(4,128)S(1)} %bitcast.99), channel_id=6, replica_groups=mesh['y_lo'=2,'core'=2,'y_hi'=2,'x'=4,'z'=4] {'core'}, dimensions={0}, use_global_device_ids=true | all-gather | bytes 811008 | tf_op jit(solution)/shard_map/all_gather | solution.py:123
  193.3 3.5 %constant_dynamic-slice_fusion.3 = (bf16[8,69,2,1,256]{1,0,4,3,2:T(8,128)(2,1)S(1)}, bf16[8,69,2,1,256]{1,0,4,3,2:T(8,128)(2,1)S(1)}, bf16[8,69,2,1,256]{1,0,4,3,2:T(8,128)(2,1)}, bf16[8,69,2,1,256]{1,0,4,3,2:T(8,128)(2,1)S(1)}) fusion(bf16[8,69,2,4,256]{1,0,4,3,2:T(8,128)(2,1)} %bitcast.96, s32[]{:T(128)S(6)} %select_n.84, s32[]{:T(128)S(6)} %select_n.88, ...), kind=kLoop, calls=%fused_computation.107 | loop fusion | bytes 4522000 | tf_op jit(solution)/shard_map/jit(dynamic_index_in_dim)/dynamic_slice | solution.py:97
  196.7 2.7 %copy.92 = bf16[8,69,2,1,256]{4,0,3,2,1:T(8,128)(2,1)} copy(bf16[8,69,2,1,256]{1,0,4,3,2:T(8,128)(2,1)} %get-tuple-element.11) | data formatting | bytes 1130496
  199.4 1.6 copy.93
  201.1 1.7 collective-permute-start.3
  202.8 1.6 copy.94
  204.7 1.2 copy.91
  205.9 12.3 %collective-permute-done.2 = bf16[8,69,2,256]{3,0,2,1:T(8,128)(2,1)} collective-permute-done((bf16[8,69,2,256]{3,0,2,1:T(8,128)(2,1)}, bf16[8,69,2,256]{3,0,2,1:T(8,128)(2,1)}, u32[]{:S(2)}, u32[]{:S(2)}) %collective-permute-start.2) | collective-permute-done | bytes 565280 | tf_op jit(solution)/shard_map/ppermute | solution.py:101
  218.2 19.2 %collective-permute-done.3 = bf16[8,69,2,256]{3,0,2,1:T(8,128)(2,1)S(1)} collective-permute-done((bf16[8,69,2,256]{3,0,2,1:T(8,128)(2,1)}, bf16[8,69,2,256]{3,0,2,1:T(8,128)(2,1)S(1)}, u32[]{:S(2)}, u32[]{:S(2)}) %collective-permute-start.3) | collective-permute-done | bytes 565280 | tf_op jit(solution)/shard_map/ppermute | solution.py:101
  237.4 1.9 collective-permute-done.4
  239.3 3.8 %maximum_convert_fusion = f32[32,69,2,256]{3,0,2,1:T(8,128)} fusion(bf16[8,69,2,256]{3,0,2,1:T(8,128)(2,1)} %collective-permute-done.4, bf16[8,69,2,256]{3,0,2,1:T(8,128)(2,1)S(1)} %collective-permute-done.3, bf16[8,69,2,256]{3,0,2,1:T(8,128)(2,1)} %collective-permute-done.2, bf16[8,69,2,256]{3,0,2,1:T(8,128)(2,1)S(1)} %bitcast.98), kind=kLoop, calls=%fused_computation.33 | loop fusion | flops 9043968 | bytes 6782976 | tf_op jit(solution)/shard_map/convert_element_type | solution.py:159
  243.1 1.9 copy.72
  244.9 0.8 reshape.160
  245.8 0.7 fusion.72
  246.6 0.2 fusion.43
  246.9 0.2 fusion.63
  247.3 0.2 fusion.42
  247.8 0.2 fusion.41
  248.3 0.2 fusion.40
  249.3 0.2 fusion.38
  249.8 0.2 fusion.82
  250.3 0.6 gather_fusion
  251.1 7.7 %fusion.29 = f32[32,69,2,256]{3,0,2,1:T(8,128)S(1)} fusion(f32[32,69,2,256]{3,0,2,1:T(8,128)} %maximum_convert_fusion, pred[2,2]{0,1:T(4,128)(4,1)S(1)} %iota_compare_fusion.4, f32[2,32,32,1,1]{2,0,1,4,3:T(2,128)S(1)} %select_bitcast_fusion), kind=kOutput, calls=%fused_computation.34 | convolution fusion | flops 870481920 | bytes 9052164 | tf_op jit(solution)/shard_map/ikm,kicjl->mcjl/dot_general | solution.py:162
  258.8 5.6 %copy.79 = f32[32,69,2,256]{3,2,1,0:T(2,128)} copy(f32[32,69,2,256]{3,0,2,1:T(8,128)S(1)} %fusion.29) | data formatting | bytes 9043968 | tf_op jit(solution)/shard_map/ikm,kicjl->mcjl/dot_general | solution.py:162
  (82 shorter events, 3.2 us)
Async XLA Ops:
  6.5 69.8 %copy-start = (bf16[3,3,256,69]{2,3,1,0:T(8,128)(2,1)S(1)}, bf16[3,3,256,69]{2,3,1,0:T(8,128)(2,1)}, u32[]{:S(2)}) copy-start(bf16[3,3,256,69]{2,3,1,0:T(8,128)(2,1)} %param.11) | copy-start | bytes 953860
  6.5 11.0 %copy-start.2 = (bf16[8,69,2,1024]{3,2,1,0:T(2,128)(2,1)S(1)}, bf16[8,69,2,1024]{3,2,1,0:T(2,128)(2,1)}, u32[]{:S(2)}) copy-start(bf16[8,69,2,1024]{3,2,1,0:T(2,128)(2,1)} %param.10) | copy-start | bytes 6782980
  6.5 16.9 %copy-start.11 = (s32[2,256]{1,0:T(2,128)S(1)}, s32[2,256]{1,0:T(2,128)}, u32[]{:S(2)}) copy-start(s32[2,256]{1,0:T(2,128)} %param.15) | copy-start | bytes 6148
  10.4 52.5 %collective-permute-start = (bf16[8,69,2,1024]{3,0,2,1:T(8,128)(2,1)}, bf16[8,69,2,1024]{3,0,2,1:T(8,128)(2,1)}, u32[]{:S(2)}, u32[]{:S(2)}) collective-permute-start(bf16[8,69,2,1024]{3,0,2,1:T(8,128)(2,1)} %copy.64), channel_id=1, source_target_pairs={{0,1},{1,2},{2,3},{3,4},{4,5},{5,6},{6,7},{7,8},{8,9},{9,10},{10,1... | collective-permute-start | bytes 6782984 | tf_op jit(solution)/shard_map/ppermute | solution.py:24
  16.2 53.4 %collective-permute-start.1 = (bf16[8,69,2,1024]{3,0,2,1:T(8,128)(2,1)}, bf16[8,69,2,1024]{3,0,2,1:T(8,128)(2,1)}, u32[]{:S(2)}, u32[]{:S(2)}) collective-permute-start(bf16[8,69,2,1024]{3,0,2,1:T(8,128)(2,1)} %copy.64), channel_id=1, source_target_pairs={{1,0},{2,1},{3,2},{4,3},{5,4},{6,5},{7,6},{8,7},{9,8},{10,9},{11,1... | collective-permute-start | bytes 6782984 | tf_op jit(solution)/shard_map/ppermute | solution.py:26
  23.3 53.0 %copy-start.7 = (s32[4,8]{1,0:T(4,128)}, s32[4,8]{1,0:T(4,128)S(1)}, u32[]{:S(2)}) copy-start(s32[4,8]{1,0:T(4,128)S(1)} %iota_add_fusion) | copy-start | bytes 388
  69.6 6.8 %copy-start.17 = (f32[256]{0:T(256)S(1)}, f32[256]{0:T(256)}, u32[]{:S(2)}) copy-start(f32[256]{0:T(256)} %param.12) | copy-start | bytes 3076
  76.4 40.6 %copy-start.4 = (bf16[8,69,2,1024]{1,0,3,2:T(8,128)(2,1)S(1)}, bf16[8,69,2,1024]{1,0,3,2:T(8,128)(2,1)}, u32[]{:S(2)}) copy-start(bf16[8,69,2,1024]{1,0,3,2:T(8,128)(2,1)} %copy.63) | copy-start | bytes 6782980
  76.4 40.6 %copy-start.16 = (bf16[3,3,69,256]{3,2,1,0:T(8,128)(2,1)S(1)}, bf16[3,3,69,256]{3,2,1,0:T(8,128)(2,1)}, u32[]{:S(2)}) copy-start(bf16[3,3,69,256]{3,2,1,0:T(8,128)(2,1)} %param.13) | copy-start | bytes 953860
  76.4 40.6 %copy-start.18 = (f32[69]{0:T(128)S(1)}, f32[69]{0:T(128)}, u32[]{:S(2)}) copy-start(f32[69]{0:T(128)} %param.14) | copy-start | bytes 832
  117.0 25.0 %copy-start.5 = (f32[4,2,69,256]{3,2,1,0:T(8,128)S(1)}, f32[4,2,69,256]{3,2,1,0:T(8,128)}, u32[]{:S(2)}) copy-start(f32[4,2,69,256]{3,2,1,0:T(8,128)} %fusion.45) | copy-start | bytes 1695748
  117.0 25.0 %copy-start.10 = (s32[4,2,256]{2,1,0:T(2,128)S(1)}, s32[4,2,256]{2,1,0:T(2,128)}, u32[]{:S(2)}) copy-start(s32[4,2,256]{2,1,0:T(2,128)} %get-tuple-element.13) | copy-start | bytes 24580
  139.9 2.0 copy-start.3
  140.0 9.3 %copy-start.15 = (s32[32]{0:T(128)S(1)}, s32[32]{0:T(128)}, u32[]{:S(2)}) copy-start(s32[32]{0:T(128)} %fusion.67) | copy-start | bytes 388
  140.0 12.6 %copy-start.9 = (f32[2,256]{1,0:T(2,128)S(1)}, f32[2,256]{1,0:T(2,128)}, u32[]{:S(2)}) copy-start(f32[2,256]{1,0:T(2,128)} %param.17) | copy-start | bytes 6148
  140.0 12.6 %copy-start.12 = (f32[2,256]{1,0:T(2,128)S(1)}, f32[2,256]{1,0:T(2,128)}, u32[]{:S(2)}) copy-start(f32[2,256]{1,0:T(2,128)} %param.16) | copy-start | bytes 6148
  144.5 8.1 %all-to-all-start = ((f32[4,2,8,256]{3,2,1,0:T(8,128)}), f32[4,2,8,256]{3,2,1,0:T(8,128)S(1)}, u32[]{:S(2)}, u32[]{:S(2)}) async-start(f32[4,2,8,256]{3,2,1,0:T(8,128)} %fusion.21), calls=%async_computation | async-start | bytes 131072 | tf_op jit(solution)/shard_map/all_to_all | solution.py:94
  149.3 93.8 %all-gather.10.cloned.1.call-start = ((), (), s32[]{:S(2)}) async-start(), calls=%async_computation.1 | async-start | bytes 1769472 | tf_op jit(solution)/shard_map/all_gather | solution.py:123
  193.2 11.2 %copy-start.8 = (s32[4,8]{1,0:T(4,128)S(1)}, s32[4,8]{1,0:T(4,128)}, u32[]{:S(2)}) copy-start(s32[4,8]{1,0:T(4,128)} %copy-done.7) | copy-start | bytes 388
  193.2 11.3 %copy-start.13 = (f32[2,8]{1,0:T(2,128)S(1)}, f32[2,8]{1,0:T(2,128)}, u32[]{:S(2)}) copy-start(f32[2,8]{1,0:T(2,128)} %param.19) | copy-start | bytes 196
  193.3 11.3 %copy-start.14 = (s32[2,8]{1,0:T(2,128)S(1)}, s32[2,8]{1,0:T(2,128)}, u32[]{:S(2)}) copy-start(s32[2,8]{1,0:T(2,128)} %param.18) | copy-start | bytes 196
  199.4 18.7 %collective-permute-start.2 = (bf16[8,69,2,256]{3,0,2,1:T(8,128)(2,1)}, bf16[8,69,2,256]{3,0,2,1:T(8,128)(2,1)}, u32[]{:S(2)}, u32[]{:S(2)}) collective-permute-start(bf16[8,69,2,256]{3,0,2,1:T(8,128)(2,1)} %bitcast.101), channel_id=1, source_target_pairs={{0,32},{32,64},{64,96},{96,0},{1,33},{33,65},{65,97},{97,1},{2,34}... | collective-permute-start | bytes 1695752 | tf_op jit(solution)/shard_map/ppermute | solution.py:101
  201.1 36.3 %collective-permute-start.3 = (bf16[8,69,2,256]{3,0,2,1:T(8,128)(2,1)}, bf16[8,69,2,256]{3,0,2,1:T(8,128)(2,1)S(1)}, u32[]{:S(2)}, u32[]{:S(2)}) collective-permute-start(bf16[8,69,2,256]{3,0,2,1:T(8,128)(2,1)} %bitcast.102), channel_id=1, source_target_pairs={{0,64},{32,96},{64,0},{96,32},{1,65},{33,97},{65,1},{97,33},{2,66}... | collective-permute-start | bytes 1695752 | tf_op jit(solution)/shard_map/ppermute | solution.py:101
  204.5 34.8 %collective-permute-start.4 = (bf16[8,69,2,256]{3,0,2,1:T(8,128)(2,1)}, bf16[8,69,2,256]{3,0,2,1:T(8,128)(2,1)}, u32[]{:S(2)}, u32[]{:S(2)}) collective-permute-start(bf16[8,69,2,256]{3,0,2,1:T(8,128)(2,1)} %bitcast.103), channel_id=1, source_target_pairs={{0,96},{32,0},{64,32},{96,64},{1,97},{33,1},{65,33},{97,65},{2,98}... | collective-permute-start | bytes 1695752 | tf_op jit(solution)/shard_map/ppermute | solution.py:101
  239.3 7.2 %copy-start.6 = (f32[32,32]{1,0:T(8,128)S(1)}, f32[32,32]{1,0:T(8,128)}, u32[]{:S(2)}) copy-start(f32[32,32]{1,0:T(8,128)} %fusion.62) | copy-start | bytes 12292
  251.1 13.3 %copy-start.1 = (bf16[3,3,256,69]{2,3,1,0:T(8,128)(2,1)S(1)}, bf16[3,3,256,69]{2,3,1,0:T(8,128)(2,1)}, u32[]{:S(2)}) copy-start(bf16[3,3,256,69]{2,3,1,0:T(8,128)(2,1)} %param.11) | copy-start | bytes 953860
Sparse Core Ops, SparseCore 0:
  193.4 36.5 all-gather.9

commit v6 on v5

--- a/solution.py
+++ b/solution.py
@@ -9,7 +9,7 @@
 
 GRP = ("y_lo", "core")
 BAND = ("y_hi", "x", "z")
-GATHER_ORDER = ("z", "x", "y_hi", "core", "y_lo")
+GATHER_ORDER = ("z", "x", "y_hi", "y_lo", "core")
 
 
 def shift_pairs(count, step):
@@ -123,8 +123,14 @@
             packed = lax.all_gather(packed, axis, axis=0, tiled=False)
         packed = packed.reshape(-1, ensemble * ensemble + ensemble)
         total_patches = packed.shape[0]
+        quarter_patches = total_patches // 4
+        gathered_row = (
+            (neighbours // quarter_patches) % 2 * (2 * quarter_patches)
+            + neighbours // (2 * quarter_patches) * quarter_patches
+            + neighbours % quarter_patches
+        )
         patch_ids = jnp.arange(total_patches, dtype=jnp.int32)
-        matches = (neighbours[:, :, None] == patch_ids[None, None, :]).astype(jnp.float32)
+        matches = (gathered_row[:, :, None] == patch_ids[None, None, :]).astype(jnp.float32)
         spread_weights = jnp.sum(loc_weight[:, :, None] * matches, axis=1)
         summed = jnp.einsum("pj,jf->pf", spread_weights, packed, precision=highest)
         gram_sum = summed[:, : ensemble * ensemble].reshape(count, ensemble, ensemble)

time: 272 us -> 266 us (0.978)
  waiting for transfers between devices: 67.5 us -> 53.6 us
  starting transfers between devices: 13.6 us -> 21.9 us
    ppermute x3, waiting for transfers between devices: 33.4 us -> 20.8 us  [on_device(): lax.ppermute(outgoing, GRP, [(j, (j + step) % quarters) for j in range(qu...]
    ppermute x3, starting transfers between devices: 1.73 us -> 10 us  [on_device(): lax.ppermute(outgoing, GRP, [(j, (j + step) % quarters) for j in range(qu...]
    unnamed x44 -> x48, local copies, waits for them, and re-layouts: 18.9 us -> 18.9 us
  transfers between devices with their start and end apart: 7 -> 7, of which waited for: 5 -> 5; matrix products, arithmetic and copies ran while one was open for 11% -> 12% of each run, Pallas kernels for 0% -> 0%
where the time goes in v6:
time: 266 us; the launch traced here: 265 us
  matrix products  77.2 us (29%)
  waiting for transfers between devices  53.6 us (20%)
  local copies, waits for them, and re-layouts  45.9 us (17%)
  blocking collectives  44.4 us (17%)
  starting transfers between devices  21.9 us (8%)
  between operations  13.9 us (5%)
  other arithmetic  8.47 us (3%)
    conv_general_dilated x2, matrix products, convolve(): lax.conv_general_dilated(wrapped, jnp.transpose(kernel, (2, 3, 0, 1)), wi...  62.8 us
    all_gather x4, blocking collectives, on_device(): packed = lax.all_gather(packed, axis, axis=0, tiled=False)  38.5 us
    ppermute x1, waiting for transfers between devices, padded_2(): lax.ppermute(tail, BAND, shift_pairs(band_size, 1))  29.6 us
    ppermute x3, waiting for transfers between devices, on_device(): lax.ppermute(outgoing, GRP, [(j, (j + step) % quarters) for j in range(qu...  20.8 us
    unnamed x48, local copies, waits for them, and re-layouts  18.9 us
    ppermute x3, starting transfers between devices, on_device(): lax.ppermute(outgoing, GRP, [(j, (j + step) % quarters) for j in range(qu...  10 us
    dot_general x1, matrix products, on_device(): jnp.einsum('ikm,kicjl->mcjl', weights, spread_out, precision=highest)  7.71 us
    ppermute x1, local copies, waits for them, and re-layouts, padded_2(): lax.ppermute(head, BAND, shift_pairs(band_size, -1))  6.76 us
  transfers between devices with their start and end apart: 7, of which 5 were waited for; matrix products, arithmetic and copies ran while one was open for 12% of the time, Pallas kernels for 0%

profile of v6, /device:TPU:1, one launch (start us, length us, event | category | flops | bytes accessed | tf_op | source)
XLA Modules:
  0.0 265.3 jit_solution(6488693129982418726)
XLA Ops:
  6.5 3.9 %copy.64 = bf16[8,69,2,1024]{3,0,2,1:T(8,128)(2,1)} copy(bf16[8,69,2,1024]{3,2,1,0:T(2,128)(2,1)} %param.10) | data formatting | bytes 4521984 | tf_op args[0]
  10.4 5.8 %collective-permute-start = (bf16[8,69,2,1024]{3,0,2,1:T(8,128)(2,1)}, bf16[8,69,2,1024]{3,0,2,1:T(8,128)(2,1)}, u32[]{:S(2)}, u32[]{:S(2)}) collective-permute-start(bf16[8,69,2,1024]{3,0,2,1:T(8,128)(2,1)} %copy.64), channel_id=1, source_target_pairs={{0,1},{1,2},{2,3},{3,4},{4,5},{5,6},{6,7},{7,8},{8,9},{9,10},{10,1... | collective-permute-start | bytes 6782984 | tf_op jit(solution)/shard_map/ppermute | solution.py:24
  16.2 1.3 collective-permute-start.1
  17.5 5.7 %copy.63 = bf16[8,69,2,1024]{1,0,3,2:T(8,128)(2,1)} copy(bf16[8,69,2,1024]{3,2,1,0:T(2,128)(2,1)S(1)} %copy-done.2) | data formatting | bytes 4521984 | tf_op args[0]
  23.4 5.9 %all-gather.6 = s32[4,2,256]{2,1,0:T(2,128)S(1)} all-gather(s32[1,2,256]{2,1,0:T(2,128)S(1)} %bitcast.108), channel_id=2, replica_groups=mesh['y_lo'=2,'core'=2,'y_hi'=2,'x'=4,'z'=4] {'y_lo','core'}, dimensions={0}, use_global_device_ids=true | all-gather | bytes 10240 | tf_op jit(solution)/shard_map/all_gather | solution.py:78
  29.3 0.6 fusion.62
  30.0 0.6 fusion.61
  30.6 0.6 fusion.60
  31.2 0.6 fusion.71
  31.8 0.6 and_select_fusion.1
  32.4 0.9 fusion.45
  33.3 29.6 %collective-permute-done = bf16[8,69,2,1024]{3,0,2,1:T(8,128)(2,1)} collective-permute-done((bf16[8,69,2,1024]{3,0,2,1:T(8,128)(2,1)}, bf16[8,69,2,1024]{3,0,2,1:T(8,128)(2,1)}, u32[]{:S(2)}, u32[]{:S(2)}) %collective-permute-start) | collective-permute-done | bytes 2261024 | tf_op jit(solution)/shard_map/ppermute | solution.py:24
  62.9 6.7 %copy.66 = bf16[8,69,2,1024]{1,0,3,2:T(8,128)(2,1)} copy(bf16[8,69,2,1024]{3,0,2,1:T(8,128)(2,1)} %collective-permute-done) | data formatting | bytes 4521984 | tf_op jit(solution)/shard_map/ppermute | solution.py:24
  69.6 6.8 %copy.68 = bf16[8,69,2,1024]{1,0,3,2:T(8,128)(2,1)} copy(bf16[8,69,2,1024]{3,0,2,1:T(8,128)(2,1)} %collective-permute-done.1) | data formatting | bytes 4521984 | tf_op jit(solution)/shard_map/ppermute | solution.py:26
  76.4 39.8 %fusion.6 = bf16[8,256,4,1024]{1,0,3,2:T(8,128)(2,1)} fusion(f32[256]{0:T(256)S(1)} %copy-done.19, pred[4]{0:T(512)(128)(4,1)S(1)} %and_or_fusion, bf16[3,3,256,69]{2,3,1,0:T(8,128)(2,1)S(1)} %copy-done, bf16[8,69,2,1024]{1,0,3,2:T(8,128)(2,1)} %copy.68, bf16[8,69,2,1024]{1,0,3,2:T(8,128)(2,1)} %copy.63, bf16[8,69,2,1024]{1,0,3,2:T(8,128)(2,1)} %copy.66), kind=kOutput, calls=%fused_computation.8 | convolution fusion | flops 10504556544 | bytes 23879172 | tf_op jit(solution)/shard_map/conv_general_dilated | solution.py:34
  116.3 0.7 fusion.75
  117.0 22.9 %add_convert_fusion = bf16[8,69,2,1024]{1,0,3,2:T(8,128)(2,1)S(1)} fusion(bf16[8,69,2,1024]{1,0,3,2:T(8,128)(2,1)S(1)} %copy-done.4, f32[69]{0:T(128)S(1)} %copy-done.20, bf16[3,3,69,256]{3,2,1,0:T(8,128)(2,1)S(1)} %copy-done.18, bf16[8,256,4,1]{1,0,3,2:T(8,128)(2,1)S(1)} %get-tuple-element.8, bf16[8,256,4,1024]{1,0,3,2:T(8,128)(2,1)} %fusion.6, ...), kind=kOutput, calls=%fused_computation.25 | convolution fusion | flops 5230657536 | bytes 21650196 | tf_op jit(solution)/shard_map/conv_general_dilated | solution.py:34
  140.0 2.0 copy-done.3
  142.0 2.5 fusion.21
  144.5 4.8 %all-to-all-start = ((f32[4,2,8,256]{3,2,1,0:T(8,128)}), f32[4,2,8,256]{3,2,1,0:T(8,128)S(1)}, u32[]{:S(2)}, u32[]{:S(2)}) async-start(f32[4,2,8,256]{3,2,1,0:T(8,128)} %fusion.21), calls=%async_computation | async-start | bytes 131072 | tf_op jit(solution)/shard_map/all_to_all | solution.py:94
  149.4 3.2 %all-to-all-done = f32[4,2,8,256]{3,2,1,0:T(8,128)S(1)} async-done(((f32[4,2,8,256]{3,2,1,0:T(8,128)}), f32[4,2,8,256]{3,2,1,0:T(8,128)S(1)}, u32[]{:S(2)}, u32[]{:S(2)}) %all-to-all-start) | async-done | bytes 65568 | tf_op jit(solution)/shard_map/all_to_all | solution.py:94
  152.7 0.2 fusion.46
  152.9 0.2 fusion.48
  153.1 10.8 %all-gather.7 = f32[4,2,1056]{2,1,0:T(2,128)S(1)} all-gather(f32[1,2,1056]{2,1,0:T(2,128)S(1)} %maximum_bitcast_fusion), channel_id=3, replica_groups=mesh['y_lo'=2,'core'=2,'y_hi'=2,'x'=4,'z'=4] {'z'}, dimensions={0}, use_global_device_ids=true | all-gather | bytes 42240 | tf_op jit(solution)/shard_map/all_gather | solution.py:123
  163.9 11.5 %all-gather.2 = f32[16,2,1056]{2,1,0:T(2,128)S(1)} all-gather(f32[4,2,1056]{2,1,0:T(2,128)S(1)} %all-gather.7), channel_id=4, replica_groups=mesh['y_lo'=2,'core'=2,'y_hi'=2,'x'=4,'z'=4] {'x'}, dimensions={0}, use_global_device_ids=true | all-gather | bytes 168960 | tf_op jit(solution)/shard_map/all_gather | solution.py:123
  175.4 8.3 %all-gather.3 = f32[8,4,2,1056]{3,1,2,0:T(4,128)S(1)} all-gather(f32[4,4,2,1056]{3,1,2,0:T(4,128)S(1)} %copy.71), channel_id=5, replica_groups=mesh['y_lo'=2,'core'=2,'y_hi'=2,'x'=4,'z'=4] {'y_hi'}, dimensions={0}, use_global_device_ids=true | all-gather | bytes 405504 | tf_op jit(solution)/shard_map/all_gather | solution.py:123
  183.8 7.9 %all-gather.4 = f32[4,4,4,2,1056]{4,2,3,1,0:T(4,128)} all-gather(f32[2,4,4,2,1056]{4,2,3,1,0:T(4,128)S(1)} %bitcast.99), channel_id=6, replica_groups=mesh['y_lo'=2,'core'=2,'y_hi'=2,'x'=4,'z'=4] {'y_lo'}, dimensions={0}, use_global_device_ids=true | all-gather | bytes 811008 | tf_op jit(solution)/shard_map/all_gather | solution.py:123
  191.7 3.5 %constant_dynamic-slice_fusion.3 = (bf16[8,69,2,1,256]{1,0,4,3,2:T(8,128)(2,1)S(1)}, bf16[8,69,2,1,256]{1,0,4,3,2:T(8,128)(2,1)S(1)}, bf16[8,69,2,1,256]{1,0,4,3,2:T(8,128)(2,1)}, bf16[8,69,2,1,256]{1,0,4,3,2:T(8,128)(2,1)S(1)}) fusion(bf16[8,69,2,4,256]{1,0,4,3,2:T(8,128)(2,1)} %bitcast.96, s32[]{:T(128)S(6)} %select_n.106, s32[]{:T(128)S(6)} %select_n.110, ...), kind=kLoop, calls=%fused_computation.122 | loop fusion | bytes 4522000 | tf_op jit(solution)/shard_map/jit(dynamic_index_in_dim)/dynamic_slice | solution.py:97
  195.2 2.7 %copy.92 = bf16[8,69,2,1,256]{4,0,3,2,1:T(8,128)(2,1)} copy(bf16[8,69,2,1,256]{1,0,4,3,2:T(8,128)(2,1)} %get-tuple-element.11) | data formatting | bytes 1130496
  197.9 8.2 %collective-permute-start.2 = (bf16[8,69,2,256]{3,0,2,1:T(8,128)(2,1)}, bf16[8,69,2,256]{3,0,2,1:T(8,128)(2,1)}, u32[]{:S(2)}, u32[]{:S(2)}) collective-permute-start(bf16[8,69,2,256]{3,0,2,1:T(8,128)(2,1)} %bitcast.101), channel_id=1, source_target_pairs={{0,32},{32,64},{64,96},{96,0},{1,33},{33,65},{65,97},{97,1},{2,34}... | collective-permute-start | bytes 1695752 | tf_op jit(solution)/shard_map/ppermute | solution.py:101
  206.1 1.7 copy.93
  207.8 1.8 collective-permute-start.3
  209.5 1.6 copy.94
  211.4 1.2 copy.91
  212.6 4.1 %collective-permute-done.2 = bf16[8,69,2,256]{3,0,2,1:T(8,128)(2,1)} collective-permute-done((bf16[8,69,2,256]{3,0,2,1:T(8,128)(2,1)}, bf16[8,69,2,256]{3,0,2,1:T(8,128)(2,1)}, u32[]{:S(2)}, u32[]{:S(2)}) %collective-permute-start.2) | collective-permute-done | bytes 565280 | tf_op jit(solution)/shard_map/ppermute | solution.py:101
  216.7 14.2 %collective-permute-done.3 = bf16[8,69,2,256]{3,0,2,1:T(8,128)(2,1)S(1)} collective-permute-done((bf16[8,69,2,256]{3,0,2,1:T(8,128)(2,1)}, bf16[8,69,2,256]{3,0,2,1:T(8,128)(2,1)S(1)}, u32[]{:S(2)}, u32[]{:S(2)}) %collective-permute-start.3) | collective-permute-done | bytes 565280 | tf_op jit(solution)/shard_map/ppermute | solution.py:101
  231.0 2.4 collective-permute-done.4
  233.4 3.8 %maximum_convert_fusion = f32[32,69,2,256]{3,0,2,1:T(8,128)} fusion(bf16[8,69,2,256]{3,0,2,1:T(8,128)(2,1)} %collective-permute-done.4, bf16[8,69,2,256]{3,0,2,1:T(8,128)(2,1)S(1)} %collective-permute-done.3, bf16[8,69,2,256]{3,0,2,1:T(8,128)(2,1)} %collective-permute-done.2, bf16[8,69,2,256]{3,0,2,1:T(8,128)(2,1)S(1)} %bitcast.98), kind=kLoop, calls=%fused_computation.33 | loop fusion | flops 9043968 | bytes 6782976 | tf_op jit(solution)/shard_map/convert_element_type | solution.py:165
  237.1 1.9 copy.72
  239.0 0.8 reshape.160
  239.9 0.7 fusion.76
  240.8 0.2 fusion.43
  241.0 0.2 fusion.63
  241.4 0.2 fusion.42
  243.9 0.2 fusion.86
  244.4 0.6 gather_fusion
  245.2 7.7 %fusion.29 = f32[32,69,2,256]{3,0,2,1:T(8,128)S(1)} fusion(f32[32,69,2,256]{3,0,2,1:T(8,128)} %maximum_convert_fusion, pred[2,2]{0,1:T(4,128)(4,1)S(1)} %iota_compare_fusion.4, f32[2,32,32,1,1]{2,0,1,4,3:T(2,128)S(1)} %select_bitcast_fusion), kind=kOutput, calls=%fused_computation.34 | convolution fusion | flops 870481920 | bytes 9052164 | tf_op jit(solution)/shard_map/ikm,kicjl->mcjl/dot_general | solution.py:168
  252.9 5.6 %copy.79 = f32[32,69,2,256]{3,2,1,0:T(2,128)} copy(f32[32,69,2,256]{3,0,2,1:T(8,128)S(1)} %fusion.29) | data formatting | bytes 9043968 | tf_op jit(solution)/shard_map/ikm,kicjl->mcjl/dot_general | solution.py:168
  (87 shorter events, 3.7 us)
Async XLA Ops:
  6.5 69.9 %copy-start = (bf16[3,3,256,69]{2,3,1,0:T(8,128)(2,1)S(1)}, bf16[3,3,256,69]{2,3,1,0:T(8,128)(2,1)}, u32[]{:S(2)}) copy-start(bf16[3,3,256,69]{2,3,1,0:T(8,128)(2,1)} %param.11) | copy-start | bytes 953860
  6.5 11.0 %copy-start.2 = (bf16[8,69,2,1024]{3,2,1,0:T(2,128)(2,1)S(1)}, bf16[8,69,2,1024]{3,2,1,0:T(2,128)(2,1)}, u32[]{:S(2)}) copy-start(bf16[8,69,2,1024]{3,2,1,0:T(2,128)(2,1)} %param.10) | copy-start | bytes 6782980
  6.5 16.9 %copy-start.13 = (s32[2,256]{1,0:T(2,128)S(1)}, s32[2,256]{1,0:T(2,128)}, u32[]{:S(2)}) copy-start(s32[2,256]{1,0:T(2,128)} %param.15) | copy-start | bytes 6148
  10.4 52.5 %collective-permute-start = (bf16[8,69,2,1024]{3,0,2,1:T(8,128)(2,1)}, bf16[8,69,2,1024]{3,0,2,1:T(8,128)(2,1)}, u32[]{:S(2)}, u32[]{:S(2)}) collective-permute-start(bf16[8,69,2,1024]{3,0,2,1:T(8,128)(2,1)} %copy.64), channel_id=1, source_target_pairs={{0,1},{1,2},{2,3},{3,4},{4,5},{5,6},{6,7},{7,8},{8,9},{9,10},{10,1... | collective-permute-start | bytes 6782984 | tf_op jit(solution)/shard_map/ppermute | solution.py:24
  16.2 53.4 %collective-permute-start.1 = (bf16[8,69,2,1024]{3,0,2,1:T(8,128)(2,1)}, bf16[8,69,2,1024]{3,0,2,1:T(8,128)(2,1)}, u32[]{:S(2)}, u32[]{:S(2)}) collective-permute-start(bf16[8,69,2,1024]{3,0,2,1:T(8,128)(2,1)} %copy.64), channel_id=1, source_target_pairs={{1,0},{2,1},{3,2},{4,3},{5,4},{6,5},{7,6},{8,7},{9,8},{10,9},{11,1... | collective-permute-start | bytes 6782984 | tf_op jit(solution)/shard_map/ppermute | solution.py:26
  23.4 53.0 %copy-start.9 = (s32[4,8]{1,0:T(4,128)}, s32[4,8]{1,0:T(4,128)S(1)}, u32[]{:S(2)}) copy-start(s32[4,8]{1,0:T(4,128)S(1)} %iota_add_fusion) | copy-start | bytes 388
  69.6 6.8 %copy-start.19 = (f32[256]{0:T(256)S(1)}, f32[256]{0:T(256)}, u32[]{:S(2)}) copy-start(f32[256]{0:T(256)} %param.12) | copy-start | bytes 3076
  76.4 40.6 %copy-start.4 = (bf16[8,69,2,1024]{1,0,3,2:T(8,128)(2,1)S(1)}, bf16[8,69,2,1024]{1,0,3,2:T(8,128)(2,1)}, u32[]{:S(2)}) copy-start(bf16[8,69,2,1024]{1,0,3,2:T(8,128)(2,1)} %copy.63) | copy-start | bytes 6782980
  76.4 40.6 %copy-start.18 = (bf16[3,3,69,256]{3,2,1,0:T(8,128)(2,1)S(1)}, bf16[3,3,69,256]{3,2,1,0:T(8,128)(2,1)}, u32[]{:S(2)}) copy-start(bf16[3,3,69,256]{3,2,1,0:T(8,128)(2,1)} %param.13) | copy-start | bytes 953860
  76.4 40.6 %copy-start.20 = (f32[69]{0:T(128)S(1)}, f32[69]{0:T(128)}, u32[]{:S(2)}) copy-start(f32[69]{0:T(128)} %param.14) | copy-start | bytes 832
  117.0 25.0 %copy-start.6 = (f32[4,2,69,256]{3,2,1,0:T(8,128)S(1)}, f32[4,2,69,256]{3,2,1,0:T(8,128)}, u32[]{:S(2)}) copy-start(f32[4,2,69,256]{3,2,1,0:T(8,128)} %fusion.45) | copy-start | bytes 1695748
  117.0 25.0 %copy-start.12 = (s32[4,2,256]{2,1,0:T(2,128)S(1)}, s32[4,2,256]{2,1,0:T(2,128)}, u32[]{:S(2)}) copy-start(s32[4,2,256]{2,1,0:T(2,128)} %get-tuple-element.13) | copy-start | bytes 24580
  140.0 2.0 copy-start.3
  140.0 9.4 %copy-start.17 = (s32[32]{0:T(128)S(1)}, s32[32]{0:T(128)}, u32[]{:S(2)}) copy-start(s32[32]{0:T(128)} %fusion.71) | copy-start | bytes 388
  140.0 12.6 %copy-start.11 = (f32[2,256]{1,0:T(2,128)S(1)}, f32[2,256]{1,0:T(2,128)}, u32[]{:S(2)}) copy-start(f32[2,256]{1,0:T(2,128)} %param.17) | copy-start | bytes 6148
  140.0 12.6 %copy-start.14 = (f32[2,256]{1,0:T(2,128)S(1)}, f32[2,256]{1,0:T(2,128)}, u32[]{:S(2)}) copy-start(f32[2,256]{1,0:T(2,128)} %param.16) | copy-start | bytes 6148
  144.5 8.1 %all-to-all-start = ((f32[4,2,8,256]{3,2,1,0:T(8,128)}), f32[4,2,8,256]{3,2,1,0:T(8,128)S(1)}, u32[]{:S(2)}, u32[]{:S(2)}) async-start(f32[4,2,8,256]{3,2,1,0:T(8,128)} %fusion.21), calls=%async_computation | async-start | bytes 131072 | tf_op jit(solution)/shard_map/all_to_all | solution.py:94
  149.3 87.8 %all-gather.10.cloned.1.call-start = ((), (), s32[]{:S(2)}) async-start(), calls=%async_computation.1 | async-start | bytes 1769472 | tf_op jit(solution)/shard_map/all_gather | solution.py:123
  191.7 19.5 %copy-start.10 = (s32[4,8]{1,0:T(4,128)S(1)}, s32[4,8]{1,0:T(4,128)}, u32[]{:S(2)}) copy-start(s32[4,8]{1,0:T(4,128)} %copy-done.9) | copy-start | bytes 388
  191.7 19.6 %copy-start.15 = (s32[2,8]{1,0:T(2,128)S(1)}, s32[2,8]{1,0:T(2,128)}, u32[]{:S(2)}) copy-start(s32[2,8]{1,0:T(2,128)} %param.18) | copy-start | bytes 196
  191.7 19.6 %copy-start.16 = (f32[2,8]{1,0:T(2,128)S(1)}, f32[2,8]{1,0:T(2,128)}, u32[]{:S(2)}) copy-start(f32[2,8]{1,0:T(2,128)} %param.19) | copy-start | bytes 196
  197.9 18.8 %collective-permute-start.2 = (bf16[8,69,2,256]{3,0,2,1:T(8,128)(2,1)}, bf16[8,69,2,256]{3,0,2,1:T(8,128)(2,1)}, u32[]{:S(2)}, u32[]{:S(2)}) collective-permute-start(bf16[8,69,2,256]{3,0,2,1:T(8,128)(2,1)} %bitcast.101), channel_id=1, source_target_pairs={{0,32},{32,64},{64,96},{96,0},{1,33},{33,65},{65,97},{97,1},{2,34}... | collective-permute-start | bytes 1695752 | tf_op jit(solution)/shard_map/ppermute | solution.py:101
  207.8 23.2 %collective-permute-start.3 = (bf16[8,69,2,256]{3,0,2,1:T(8,128)(2,1)}, bf16[8,69,2,256]{3,0,2,1:T(8,128)(2,1)S(1)}, u32[]{:S(2)}, u32[]{:S(2)}) collective-permute-start(bf16[8,69,2,256]{3,0,2,1:T(8,128)(2,1)} %bitcast.102), channel_id=1, source_target_pairs={{0,64},{32,96},{64,0},{96,32},{1,65},{33,97},{65,1},{97,33},{2,66}... | collective-permute-start | bytes 1695752 | tf_op jit(solution)/shard_map/ppermute | solution.py:101
  211.2 22.2 %collective-permute-start.4 = (bf16[8,69,2,256]{3,0,2,1:T(8,128)(2,1)}, bf16[8,69,2,256]{3,0,2,1:T(8,128)(2,1)}, u32[]{:S(2)}, u32[]{:S(2)}) collective-permute-start(bf16[8,69,2,256]{3,0,2,1:T(8,128)(2,1)} %bitcast.103), channel_id=1, source_target_pairs={{0,96},{32,0},{64,32},{96,64},{1,97},{33,1},{65,33},{97,65},{2,98}... | collective-permute-start | bytes 1695752 | tf_op jit(solution)/shard_map/ppermute | solution.py:101
  233.4 7.2 %copy-start.8 = (f32[32,32]{1,0:T(8,128)S(1)}, f32[32,32]{1,0:T(8,128)}, u32[]{:S(2)}) copy-start(f32[32,32]{1,0:T(8,128)} %fusion.62) | copy-start | bytes 12292
  237.1 3.6 %copy-start.5 = (f32[32,32]{1,0:T(8,128)S(1)}, f32[32,32]{1,0:T(8,128)}, u32[]{:S(2)}) copy-start(f32[32,32]{1,0:T(8,128)} %fusion.61) | copy-start | bytes 12292
  237.1 3.6 %copy-start.7 = (f32[32,32]{1,0:T(8,128)S(1)}, f32[32,32]{1,0:T(8,128)}, u32[]{:S(2)}) copy-start(f32[32,32]{1,0:T(8,128)} %fusion.60) | copy-start | bytes 12292
  245.2 13.3 %copy-start.1 = (bf16[3,3,256,69]{2,3,1,0:T(8,128)(2,1)S(1)}, bf16[3,3,256,69]{2,3,1,0:T(8,128)(2,1)}, u32[]{:S(2)}) copy-start(bf16[3,3,256,69]{2,3,1,0:T(8,128)(2,1)} %param.11) | copy-start | bytes 953860
Sparse Core Ops, SparseCore 0:
  191.8 17.5 all-gather.9

commit v7 on v6

--- a/solution.py
+++ b/solution.py
@@ -2,6 +2,7 @@
 import jax.numpy as jnp
 import numpy as np
 from jax import lax
+from jax.experimental.layout import Layout, with_layout_constraint
 from jax.sharding import Mesh
 from jax.sharding import PartitionSpec as P
 
@@ -16,27 +17,25 @@
     return [(i, i + step) for i in range(count) if 0 <= i + step < count]
 
 
-def padded_2(cells, band_size, width):
-    head = lax.slice_in_dim(cells, 0, width, axis=2)
-    tail = lax.slice_in_dim(cells, cells.shape[2] - width, cells.shape[2], axis=2)
+def padded_2(cells, band_size):
     return jnp.concatenate(
         [
-            lax.ppermute(tail, BAND, shift_pairs(band_size, 1)),
+            lax.ppermute(cells, BAND, shift_pairs(band_size, 1)),
             cells,
-            lax.ppermute(head, BAND, shift_pairs(band_size, -1)),
+            lax.ppermute(cells, BAND, shift_pairs(band_size, -1)),
         ],
-        axis=2,
+        axis=0,
     )
 
 
 def convolve(padded, kernel):
-    wrapped = jnp.concatenate([padded[..., -1:], padded, padded[..., :1]], axis=-1)
+    wrapped = jnp.concatenate([padded[:, -1:], padded, padded[:, :1]], axis=1)
     return lax.conv_general_dilated(
         wrapped,
-        jnp.transpose(kernel, (2, 3, 0, 1)),
+        kernel,
         window_strides=(1, 1),
         padding="VALID",
-        dimension_numbers=("NCHW", "OIHW", "NCHW"),
+        dimension_numbers=("HWNC", "HWOI", "HWNC"),
         preferred_element_type=jnp.float32,
     )
 
@@ -55,26 +54,28 @@
         loc_weight,
     ):
         highest = lax.Precision.HIGHEST
-        height = prior_samples.shape[2]
-        padded = padded_2(prior_samples, band_size, height)
+        rows_first = prior_samples
+        height = rows_first.shape[0]
+        padded = padded_2(rows_first, band_size)
         hidden_fields = jax.nn.silu(
-            convolve(padded, conv1_weight) + conv1_bias[None, :, None, None]
+            convolve(padded, conv1_weight) + conv1_bias
         ).astype(jnp.bfloat16)
         place = lax.axis_index(BAND)
-        row_ids = jnp.arange(height + 2, dtype=jnp.int32)[None, None, :, None]
+        row_ids = jnp.arange(height + 2, dtype=jnp.int32)[:, None, None, None]
         outside = ((place == 0) & (row_ids == 0)) | (
             (place == band_size - 1) & (row_ids == height + 1)
         )
         extended = jnp.where(outside, jnp.zeros_like(hidden_fields), hidden_fields)
-        predicted_samples = (
-            prior_samples.astype(jnp.float32)
+        forecast = (
+            rows_first.astype(jnp.float32)
             + convolve(extended, conv2_weight)
-            + conv2_bias[None, :, None, None]
+            + conv2_bias
         ).astype(jnp.bfloat16)
-        ensemble_part = predicted_samples.shape[0]
-        channels = predicted_samples.shape[1]
+        ensemble_part = forecast.shape[2]
+        channels = forecast.shape[3]
         quarters = lax.psum(1, GRP)
-        patch_width = predicted_samples.shape[3] // quarters
+        patch_width = forecast.shape[1] // quarters
+        blocks = forecast.reshape(height, quarters, patch_width, ensemble_part, channels)
         row_index = lax.all_gather(obs_index, GRP, axis=0, tiled=False)
         column = row_index % patch_width
         channel = row_index // patch_width
@@ -82,8 +83,8 @@
             column[..., None] == jnp.arange(patch_width, dtype=jnp.int32)
         ).astype(jnp.bfloat16)
         by_column = jnp.einsum(
-            "mciql,qiol->qicmo",
-            predicted_samples.reshape(ensemble_part, channels, height, quarters, patch_width),
+            "iqlmc,qiol->qicmo",
+            blocks,
             column_hot,
             preferred_element_type=jnp.float32,
         )
@@ -93,15 +94,14 @@
         own_members = jnp.sum(by_column * channel_hot[:, :, :, None, :], axis=2)
         predicted = lax.all_to_all(own_members, GRP, split_axis=0, concat_axis=2, tiled=True)[0]
         me = lax.axis_index(GRP)
-        blocks = predicted_samples.reshape(ensemble_part, channels, height, quarters, patch_width)
-        pieces = [lax.dynamic_index_in_dim(blocks, me, axis=3, keepdims=False)]
+        pieces = [lax.dynamic_index_in_dim(blocks, me, axis=1, keepdims=False)]
         for step in range(1, quarters):
-            outgoing = lax.dynamic_index_in_dim(blocks, (me + step) % quarters, axis=3, keepdims=False)
+            outgoing = lax.dynamic_index_in_dim(blocks, (me + step) % quarters, axis=1, keepdims=False)
             pieces.append(
                 lax.ppermute(outgoing, GRP, [(j, (j + step) % quarters) for j in range(quarters)])
             )
-        patch_block_slice = jnp.concatenate(pieces, axis=0)
-        ensemble = patch_block_slice.shape[0]
+        patch_block_slice = jnp.stack(pieces, axis=0)
+        ensemble = quarters * ensemble_part
         source_member = (
             ((me - jnp.arange(quarters, dtype=jnp.int32)) % quarters)[:, None] * ensemble_part
             + jnp.arange(ensemble_part, dtype=jnp.int32)[None, :]
@@ -158,15 +158,17 @@
             :, None, None
         ] * inverse_root + mean_weight[:, :, None]
         weights = transform + (1.0 - jnp.sum(transform, axis=1, keepdims=True)) / ensemble
-        weights = jnp.take(weights, source_member, axis=1)
+        weights = jnp.take(weights, source_member, axis=1).reshape(
+            height, quarters, ensemble_part, ensemble
+        )
         patch_of = jnp.arange(height, dtype=jnp.int32)
         spread_out = jnp.where(
-            (patch_of[:, None] == patch_of[None, :])[None, :, None, :, None],
+            (patch_of[:, None] == patch_of[None, :])[None, :, :, None, None, None],
             patch_block_slice.astype(jnp.float32)[:, None],
             0.0,
         )
         analysed = jnp.einsum(
-            "ikm,kicjl->mcjl", weights, spread_out, precision=highest
+            "ajnm,jailnc->mcil", weights, spread_out, precision=highest
         )
         return analysed
 
@@ -180,21 +182,29 @@
         GRP + BAND,
     )
     placed = (
-        P(GRP, None, BAND, None),
-        P(),
-        P(),
-        P(),
-        P(),
-        P(GRP + BAND, None),
-        P(GRP + BAND, None),
-        P(GRP + BAND, None),
-        P(GRP + BAND, None),
-        P(GRP + BAND, None),
-    )
-    return jax.shard_map(
+        P(BAND, None, GRP, None),
+        P(),
+        P(),
+        P(),
+        P(),
+        P(GRP + BAND, None),
+        P(GRP + BAND, None),
+        P(GRP + BAND, None),
+        P(GRP + BAND, None),
+        P(GRP + BAND, None),
+    )
+    mapped = jax.shard_map(
         make_on_device(band_size),
         mesh=fine,
         in_specs=placed,
         out_specs=P(None, None, BAND, GRP),
         check_vma=False,
     )
+
+    def run(prior_samples, *rest):
+        rows_first = with_layout_constraint(
+            jnp.transpose(prior_samples, (2, 3, 0, 1)), Layout((0, 1, 2, 3))
+        )
+        return mapped(rows_first, *rest)
+
+    return run

time: 266 us -> 253 us (0.951)
  waiting for transfers between devices: 53.6 us -> 43.7 us
  other arithmetic: 8.47 us -> 5.02 us
    ppermute x3, waiting for transfers between devices: 20.8 us -> 11.8 us  [on_device(): lax.ppermute(outgoing, GRP, [(j, (j + step) % quarters) for j in range(qu...]
    transpose x0 -> x2, local copies, waits for them, and re-layouts: none -> 7.97 us  [the longest x1 5.61 us: on_device(): jnp.einsum('ajnm,jailnc->mcil', weights, spread_out, precision=highest)]
    dot_general x1 -> x0, local copies, waits for them, and re-layouts: 5.61 us -> none  [on_device(): jnp.einsum('ikm,kicjl->mcjl', weights, spread_out, precision=highest)]
    convert_element_type x1 -> x0, other arithmetic: 3.75 us -> none  [on_device(): patch_block_slice.astype(jnp.float32)[:, None]]
    unnamed x48 -> x41, local copies, waits for them, and re-layouts: 18.9 us -> 16.6 us
  transfers between devices with their start and end apart: 7 -> 7, of which waited for: 5 -> 4; matrix products, arithmetic and copies ran while one was open for 12% -> 15% of each run, Pallas kernels for 0% -> 0%
where the time goes in v7:
time: 253 us; the launch traced here: 252 us
  matrix products  77.2 us (31%)
  local copies, waits for them, and re-layouts  45.9 us (18%)
  blocking collectives  44.5 us (18%)
  waiting for transfers between devices  43.7 us (17%)
  starting transfers between devices  21.9 us (9%)
  between operations  13.9 us (5%)
  other arithmetic  5.02 us (2%)
    conv_general_dilated x2, matrix products, convolve(): lax.conv_general_dilated(wrapped, kernel, window_strides=(1, 1), padding=...  62.7 us
    all_gather x4, blocking collectives, on_device(): packed = lax.all_gather(packed, axis, axis=0, tiled=False)  38.6 us
    ppermute x1, waiting for transfers between devices, padded_2(): lax.ppermute(cells, BAND, shift_pairs(band_size, 1))  28.7 us
    unnamed x41, local copies, waits for them, and re-layouts  16.6 us
    ppermute x3, waiting for transfers between devices, on_device(): lax.ppermute(outgoing, GRP, [(j, (j + step) % quarters) for j in range(qu...  11.8 us
    ppermute x3, starting transfers between devices, on_device(): lax.ppermute(outgoing, GRP, [(j, (j + step) % quarters) for j in range(qu...  10 us
    dot_general x1, matrix products, on_device(): jnp.einsum('ajnm,jailnc->mcil', weights, spread_out, precision=highest)  7.73 us
    ppermute x1, local copies, waits for them, and re-layouts, padded_2(): lax.ppermute(cells, BAND, shift_pairs(band_size, 1))  6.76 us
  transfers between devices with their start and end apart: 7, of which 4 were waited for; matrix products, arithmetic and copies ran while one was open for 15% of the time, Pallas kernels for 0%

profile of v7, /device:TPU:1, one launch (start us, length us, event | category | flops | bytes accessed | tf_op | source)
XLA Modules:
  0.0 252.0 jit_solution(8300522091741162253)
XLA Ops:
  6.5 2.4 copy.114
  8.9 5.8 %collective-permute-start = (bf16[2,1024,8,69]{1,2,3,0:T(8,128)(2,1)S(1)}, bf16[2,1024,8,69]{1,2,3,0:T(8,128)(2,1)}, u32[]{:S(2)}, u32[]{:S(2)}) collective-permute-start(bf16[2,1024,8,69]{1,2,3,0:T(8,128)(2,1)S(1)} %bitcast.115), channel_id=1, source_target_pairs={{0,1},{1,2},{2,3},{3,4},{4,5},{5,6},{6,7},{7,8},{8,9},{9,10},{10,1... | collective-permute-start | bytes 6782984 | tf_op jit(solution)/shard_map/ppermute | solution.py:23
  14.7 1.3 collective-permute-start.1
  16.0 7.1 %copy.57 = bf16[8,69,2,1024]{1,0,3,2:T(8,128)(2,1)} copy(bf16[8,69,2,1024]{3,2,1,0:T(2,128)(2,1)} %param.10) | data formatting | bytes 4521984 | tf_op args[0]
  23.1 0.6 copy-done.12
  23.8 5.9 %all-gather.6 = s32[4,2,256]{2,1,0:T(2,128)S(1)} all-gather(s32[1,2,256]{2,1,0:T(2,128)S(1)} %bitcast.127), channel_id=2, replica_groups=mesh['y_lo'=2,'core'=2,'y_hi'=2,'x'=4,'z'=4] {'y_lo','core'}, dimensions={0}, use_global_device_ids=true | all-gather | bytes 10240 | tf_op jit(solution)/shard_map/all_gather | solution.py:79
  29.7 0.6 fusion.63
  30.3 0.5 fusion.73
  30.8 0.6 and_select_fusion.1
  31.5 0.9 fusion.45
  32.4 28.7 %collective-permute-done = bf16[2,1024,8,69]{1,2,3,0:T(8,128)(2,1)} collective-permute-done((bf16[2,1024,8,69]{1,2,3,0:T(8,128)(2,1)S(1)}, bf16[2,1024,8,69]{1,2,3,0:T(8,128)(2,1)}, u32[]{:S(2)}, u32[]{:S(2)}) %collective-permute-start) | collective-permute-done | bytes 2261024 | tf_op jit(solution)/shard_map/ppermute | solution.py:23
  61.1 6.8 %copy.60 = bf16[2,1024,8,69]{3,2,1,0:T(8,128)(2,1)} copy(bf16[2,1024,8,69]{1,2,3,0:T(8,128)(2,1)} %collective-permute-done) | data formatting | bytes 4521984 | tf_op jit(solution)/shard_map/ppermute | solution.py:23
  67.9 6.7 %copy.61 = bf16[2,1024,8,69]{3,2,1,0:T(8,128)(2,1)} copy(bf16[2,1024,8,69]{1,2,3,0:T(8,128)(2,1)} %collective-permute-done.1) | data formatting | bytes 4521984 | tf_op jit(solution)/shard_map/ppermute | solution.py:25
  74.6 39.7 %fusion.6 = bf16[4,1024,8,256]{3,2,1,0:T(8,128)(2,1)} fusion(f32[256]{0:T(256)S(1)} %copy-done.16, pred[4]{0:T(512)(128)(4,1)S(1)} %and_or_fusion, bf16[3,3,256,69]{2,3,1,0:T(8,128)(2,1)S(1)} %copy-done, bf16[2,1024,8,69]{3,2,1,0:T(8,128)(2,1)} %copy.61, bf16[2,1024,8,69]{3,2,1,0:T(8,128)(2,1)} %bitcast.113, bf16[2,1024,8,69]{3,2,1,0:T(8,128)(2,1)} %copy.60), kind=kOutput, calls=%fused_computation.8 | convolution fusion | flops 10504556544 | bytes 23879172 | tf_op jit(solution)/shard_map/conv_general_dilated | solution.py:33
  114.3 0.7 fusion.78
  115.1 22.9 %add_convert_fusion = bf16[2,1024,8,69]{3,2,1,0:T(8,128)(2,1)S(1)} fusion(f32[69]{0:T(128)S(1)} %copy-done.17, bf16[3,3,69,256]{3,2,1,0:T(8,128)(2,1)S(1)} %copy-done.15, bf16[4,1,8,256]{3,2,1,0:T(8,128)(2,1)S(1)} %get-tuple-element.8, bf16[4,1024,8,256]{3,2,1,0:T(8,128)(2,1)} %fusion.6, bf16[4,1,8,256]{3,2,1,0:T(8,128)(2,1)S(1)} %get-tuple-element.7, ...), kind=kOutput, calls=%fused_computation.25 | convolution fusion | flops 5230657536 | bytes 21650196 | tf_op jit(solution)/shard_map/conv_general_dilated | solution.py:33
  138.1 1.9 copy-done.1
  140.1 2.5 %fusion.21 = f32[4,2,8,256]{3,2,1,0:T(8,128)} fusion(f32[4,2,69,256]{3,2,1,0:T(8,128)S(1)} %copy-done.3, bf16[2,4,256,8,69]{4,3,2,1,0:T(8,128)(2,1)S(1)} %bitcast.111, s32[4,2,256]{2,1,0:T(2,128)S(1)} %copy-done.7), kind=kOutput, calls=%fused_computation.27 | convolution fusion | flops 581582848 | bytes 2899968 | tf_op jit(solution)/shard_map/iqlmc,qiol->qicmo/dot_general | solution.py:85
  142.6 4.8 %all-to-all-start = ((f32[4,2,8,256]{3,2,1,0:T(8,128)}), f32[4,2,8,256]{3,2,1,0:T(8,128)S(1)}, u32[]{:S(2)}, u32[]{:S(2)}) async-start(f32[4,2,8,256]{3,2,1,0:T(8,128)} %fusion.21), calls=%async_computation | async-start | bytes 131072 | tf_op jit(solution)/shard_map/all_to_all | solution.py:95
  147.5 3.2 %all-to-all-done = f32[4,2,8,256]{3,2,1,0:T(8,128)S(1)} async-done(((f32[4,2,8,256]{3,2,1,0:T(8,128)}), f32[4,2,8,256]{3,2,1,0:T(8,128)S(1)}, u32[]{:S(2)}, u32[]{:S(2)}) %all-to-all-start) | async-done | bytes 65568 | tf_op jit(solution)/shard_map/all_to_all | solution.py:95
  150.7 0.2 fusion.46
  151.0 0.2 fusion.48
  151.2 10.9 %all-gather.7 = f32[4,2,1056]{2,1,0:T(2,128)S(1)} all-gather(f32[1,2,1056]{2,1,0:T(2,128)S(1)} %maximum_bitcast_fusion), channel_id=3, replica_groups=mesh['y_lo'=2,'core'=2,'y_hi'=2,'x'=4,'z'=4] {'z'}, dimensions={0}, use_global_device_ids=true | all-gather | bytes 42240 | tf_op jit(solution)/shard_map/all_gather | solution.py:123
  162.1 11.4 %all-gather.2 = f32[16,2,1056]{2,1,0:T(2,128)S(1)} all-gather(f32[4,2,1056]{2,1,0:T(2,128)S(1)} %all-gather.7), channel_id=4, replica_groups=mesh['y_lo'=2,'core'=2,'y_hi'=2,'x'=4,'z'=4] {'x'}, dimensions={0}, use_global_device_ids=true | all-gather | bytes 168960 | tf_op jit(solution)/shard_map/all_gather | solution.py:123
  173.6 8.4 %all-gather.3 = f32[8,4,2,1056]{3,1,2,0:T(4,128)S(1)} all-gather(f32[4,4,2,1056]{3,1,2,0:T(4,128)S(1)} %copy.69), channel_id=5, replica_groups=mesh['y_lo'=2,'core'=2,'y_hi'=2,'x'=4,'z'=4] {'y_hi'}, dimensions={0}, use_global_device_ids=true | all-gather | bytes 405504 | tf_op jit(solution)/shard_map/all_gather | solution.py:123
  181.9 7.9 %all-gather.4 = f32[4,4,4,2,1056]{4,2,3,1,0:T(4,128)} all-gather(f32[2,4,4,2,1056]{4,2,3,1,0:T(4,128)S(1)} %bitcast.117), channel_id=6, replica_groups=mesh['y_lo'=2,'core'=2,'y_hi'=2,'x'=4,'z'=4] {'y_lo'}, dimensions={0}, use_global_device_ids=true | all-gather | bytes 811008 | tf_op jit(solution)/shard_map/all_gather | solution.py:123
  189.8 0.5 iota_compare_fusion.4
  190.3 0.6 fusion.61
  191.1 0.6 compare_and_fusion
  191.7 3.4 %constant_dynamic-slice_fusion.3 = (bf16[2,1,256,8,69]{4,3,2,1,0:T(8,128)(2,1)S(1)}, bf16[2,1,256,8,69]{4,3,2,1,0:T(8,128)(2,1)S(1)}, bf16[2,1,256,8,69]{4,3,2,1,0:T(8,128)(2,1)S(1)}, bf16[2,1,256,8,69]{4,3,2,1,0:T(8,128)(2,1)}) fusion(bf16[2,4,256,8,69]{4,3,2,1,0:T(8,128)(2,1)} %bitcast.112, s32[]{:T(128)S(6)} %select_n.98, s32[]{:T(128)S(6)} %select_n.102, ...), kind=kLoop, calls=%fused_computation.124 | loop fusion | bytes 4522000 | tf_op jit(solution)/shard_map/jit(dynamic_index_in_dim)/dynamic_slice | solution.py:97
  195.1 2.7 %copy.88 = bf16[2,1,256,8,69]{2,3,4,1,0:T(8,128)(2,1)} copy(bf16[2,1,256,8,69]{4,3,2,1,0:T(8,128)(2,1)} %get-tuple-element.12) | data formatting | bytes 1130496
  197.8 8.7 %collective-permute-start.4 = (bf16[2,256,8,69]{1,2,3,0:T(8,128)(2,1)}, bf16[2,256,8,69]{1,2,3,0:T(8,128)(2,1)}, u32[]{:S(2)}, u32[]{:S(2)}) collective-permute-start(bf16[2,256,8,69]{1,2,3,0:T(8,128)(2,1)} %bitcast.119), channel_id=1, source_target_pairs={{0,96},{32,0},{64,32},{96,64},{1,97},{33,1},{65,33},{97,65},{2,98}... | collective-permute-start | bytes 1695752 | tf_op jit(solution)/shard_map/ppermute | solution.py:101
  206.5 1.7 copy.86
  208.2 1.6 copy.87
  209.8 1.4 collective-permute-start.3
  211.1 0.9 copy.85
  212.1 1.9 copy.70
  214.0 0.8 reshape.165
  214.8 0.7 fusion.79
  215.7 0.2 fusion.43
  216.0 0.2 fusion.65
  216.4 0.2 fusion.42
  218.9 0.2 fusion.89
  219.4 0.6 gather_fusion
  220.0 1.1 collective-permute-done.2
  221.2 10.7 %collective-permute-done.3 = bf16[2,256,8,69]{1,2,3,0:T(8,128)(2,1)} collective-permute-done((bf16[2,256,8,69]{1,2,3,0:T(8,128)(2,1)}, bf16[2,256,8,69]{1,2,3,0:T(8,128)(2,1)}, u32[]{:S(2)}, u32[]{:S(2)}) %collective-permute-start.3) | collective-permute-done | bytes 565280 | tf_op jit(solution)/shard_map/ppermute | solution.py:101
  231.8 7.7 %fusion.29 = f32[32,69,2,256]{3,0,1,2:T(8,128)S(1)} fusion(pred[2,2]{0,1:T(4,128)(4,1)} %iota_compare_fusion.4, f32[2,4,8,32]{3,0,2,1:T(2,128)S(1)} %bitcast.122, pred[4,8]{1,0:T(4,128)(4,1)} %compare_and_fusion, bf16[1,2,256,8,69]{2,3,4,1,0:T(8,128)(2,1)} %bitcast.10, bf16[1,2,256,8,69]{2,3,4,1,0:T(8,128)(2,1)} %bitcast.8, ...), kind=kOutput, calls=%fused_computation.35 | convolution fusion | flops 875005952 | bytes 6791204 | tf_op jit(solution)/shard_map/ajnm,jailnc->mcil/dot_general | solution.py:170
  239.6 5.6 %copy.73 = f32[32,69,2,256]{3,2,1,0:T(2,128)} copy(f32[32,69,2,256]{3,0,1,2:T(8,128)S(1)} %fusion.29) | data formatting | bytes 9043968 | tf_op jit(solution)/shard_map/ajnm,jailnc->mcil/transpose | solution.py:170
  (78 shorter events, 3.5 us)
Async XLA Ops:
  6.5 68.0 %copy-start = (bf16[3,3,256,69]{2,3,1,0:T(8,128)(2,1)S(1)}, bf16[3,3,256,69]{2,3,1,0:T(8,128)(2,1)}, u32[]{:S(2)}) copy-start(bf16[3,3,256,69]{2,3,1,0:T(8,128)(2,1)} %param.11) | copy-start | bytes 953860
  6.5 17.3 %copy-start.8 = (s32[2,256]{1,0:T(2,128)S(1)}, s32[2,256]{1,0:T(2,128)}, u32[]{:S(2)}) copy-start(s32[2,256]{1,0:T(2,128)} %param.15) | copy-start | bytes 6148
  8.9 52.2 %collective-permute-start = (bf16[2,1024,8,69]{1,2,3,0:T(8,128)(2,1)S(1)}, bf16[2,1024,8,69]{1,2,3,0:T(8,128)(2,1)}, u32[]{:S(2)}, u32[]{:S(2)}) collective-permute-start(bf16[2,1024,8,69]{1,2,3,0:T(8,128)(2,1)S(1)} %bitcast.115), channel_id=1, source_target_pairs={{0,1},{1,2},{2,3},{3,4},{4,5},{5,6},{6,7},{7,8},{8,9},{9,10},{10,1... | collective-permute-start | bytes 6782984 | tf_op jit(solution)/shard_map/ppermute | solution.py:23
  14.7 53.2 %collective-permute-start.1 = (bf16[2,1024,8,69]{1,2,3,0:T(8,128)(2,1)S(1)}, bf16[2,1024,8,69]{1,2,3,0:T(8,128)(2,1)}, u32[]{:S(2)}, u32[]{:S(2)}) collective-permute-start(bf16[2,1024,8,69]{1,2,3,0:T(8,128)(2,1)S(1)} %bitcast.116), channel_id=1, source_target_pairs={{1,0},{2,1},{3,2},{4,3},{5,4},{6,5},{7,6},{8,7},{9,8},{10,9},{11,1... | collective-permute-start | bytes 6782984 | tf_op jit(solution)/shard_map/ppermute | solution.py:25
  23.0 51.5 %copy-start.16 = (f32[256]{0:T(256)S(1)}, f32[256]{0:T(256)}, u32[]{:S(2)}) copy-start(f32[256]{0:T(256)} %param.12) | copy-start | bytes 3076
  23.1 0.6 copy-start.12
  74.6 40.5 %copy-start.2 = (bf16[8,69,2,1024]{1,0,3,2:T(8,128)(2,1)S(1)}, bf16[8,69,2,1024]{1,0,3,2:T(8,128)(2,1)}, u32[]{:S(2)}) copy-start(bf16[8,69,2,1024]{1,0,3,2:T(8,128)(2,1)} %copy.57) | copy-start | bytes 6782980
  74.6 40.5 %copy-start.15 = (bf16[3,3,69,256]{3,2,1,0:T(8,128)(2,1)S(1)}, bf16[3,3,69,256]{3,2,1,0:T(8,128)(2,1)}, u32[]{:S(2)}) copy-start(bf16[3,3,69,256]{3,2,1,0:T(8,128)(2,1)} %param.13) | copy-start | bytes 953860
  74.6 40.5 %copy-start.17 = (f32[69]{0:T(128)S(1)}, f32[69]{0:T(128)}, u32[]{:S(2)}) copy-start(f32[69]{0:T(128)} %param.14) | copy-start | bytes 832
  115.1 25.0 %copy-start.3 = (f32[4,2,69,256]{3,2,1,0:T(8,128)S(1)}, f32[4,2,69,256]{3,2,1,0:T(8,128)}, u32[]{:S(2)}) copy-start(f32[4,2,69,256]{3,2,1,0:T(8,128)} %fusion.45) | copy-start | bytes 1695748
  115.1 25.0 %copy-start.7 = (s32[4,2,256]{2,1,0:T(2,128)S(1)}, s32[4,2,256]{2,1,0:T(2,128)}, u32[]{:S(2)}) copy-start(s32[4,2,256]{2,1,0:T(2,128)} %get-tuple-element.13) | copy-start | bytes 24580
  138.0 2.0 copy-start.1
  138.0 9.4 %copy-start.14 = (s32[32]{0:T(128)S(1)}, s32[32]{0:T(128)}, u32[]{:S(2)}) copy-start(s32[32]{0:T(128)} %fusion.73) | copy-start | bytes 388
  138.1 12.6 %copy-start.6 = (f32[2,256]{1,0:T(2,128)S(1)}, f32[2,256]{1,0:T(2,128)}, u32[]{:S(2)}) copy-start(f32[2,256]{1,0:T(2,128)} %param.17) | copy-start | bytes 6148
  138.1 12.6 %copy-start.9 = (f32[2,256]{1,0:T(2,128)S(1)}, f32[2,256]{1,0:T(2,128)}, u32[]{:S(2)}) copy-start(f32[2,256]{1,0:T(2,128)} %param.16) | copy-start | bytes 6148
  138.1 52.9 %copy-start.10 = (s32[2,8]{1,0:T(2,128)S(1)}, s32[2,8]{1,0:T(2,128)}, u32[]{:S(2)}) copy-start(s32[2,8]{1,0:T(2,128)} %param.18) | copy-start | bytes 196
  138.1 52.9 %copy-start.11 = (f32[2,8]{1,0:T(2,128)S(1)}, f32[2,8]{1,0:T(2,128)}, u32[]{:S(2)}) copy-start(f32[2,8]{1,0:T(2,128)} %param.19) | copy-start | bytes 196
  138.1 53.0 %copy-start.13 = (s32[4]{0:T(128)S(1)}, s32[4]{0:T(128)}, u32[]{:S(2)}) copy-start(s32[4]{0:T(128)} %copy-done.12) | copy-start | bytes 52
  142.6 8.1 %all-to-all-start = ((f32[4,2,8,256]{3,2,1,0:T(8,128)}), f32[4,2,8,256]{3,2,1,0:T(8,128)S(1)}, u32[]{:S(2)}, u32[]{:S(2)}) async-start(f32[4,2,8,256]{3,2,1,0:T(8,128)} %fusion.21), calls=%async_computation | async-start | bytes 131072 | tf_op jit(solution)/shard_map/all_to_all | solution.py:95
  147.4 64.7 %all-gather.10.cloned.1.call-start = ((), (), s32[]{:S(2)}) async-start(), calls=%async_computation.1 | async-start | bytes 1769472 | tf_op jit(solution)/shard_map/all_gather | solution.py:123
  191.7 23.9 %copy-start.4 = (f32[32,32]{1,0:T(8,128)S(1)}, f32[32,32]{1,0:T(8,128)}, u32[]{:S(2)}) copy-start(f32[32,32]{1,0:T(8,128)} %fusion.63) | copy-start | bytes 12292
  197.8 22.2 %collective-permute-start.4 = (bf16[2,256,8,69]{1,2,3,0:T(8,128)(2,1)}, bf16[2,256,8,69]{1,2,3,0:T(8,128)(2,1)}, u32[]{:S(2)}, u32[]{:S(2)}) collective-permute-start(bf16[2,256,8,69]{1,2,3,0:T(8,128)(2,1)} %bitcast.119), channel_id=1, source_target_pairs={{0,96},{32,0},{64,32},{96,64},{1,97},{33,1},{65,33},{97,65},{2,98}... | collective-permute-start | bytes 1695752 | tf_op jit(solution)/shard_map/ppermute | solution.py:101
  208.1 7.6 %copy-start.5 = (f32[32,32]{1,0:T(8,128)S(1)}, f32[32,32]{1,0:T(8,128)}, u32[]{:S(2)}) copy-start(f32[32,32]{1,0:T(8,128)} %fusion.61) | copy-start | bytes 12292
  208.1 13.0 %collective-permute-start.2 = (bf16[2,256,8,69]{1,2,3,0:T(8,128)(2,1)}, bf16[2,256,8,69]{1,2,3,0:T(8,128)(2,1)}, u32[]{:S(2)}, u32[]{:S(2)}) collective-permute-start(bf16[2,256,8,69]{1,2,3,0:T(8,128)(2,1)} %bitcast.121), channel_id=1, source_target_pairs={{0,32},{32,64},{64,96},{96,0},{1,33},{33,65},{65,97},{97,1},{2,34}... | collective-permute-start | bytes 1695752 | tf_op jit(solution)/shard_map/ppermute | solution.py:101
  209.8 22.0 %collective-permute-start.3 = (bf16[2,256,8,69]{1,2,3,0:T(8,128)(2,1)}, bf16[2,256,8,69]{1,2,3,0:T(8,128)(2,1)}, u32[]{:S(2)}, u32[]{:S(2)}) collective-permute-start(bf16[2,256,8,69]{1,2,3,0:T(8,128)(2,1)} %bitcast.7), channel_id=1, source_target_pairs={{0,64},{32,96},{64,0},{96,32},{1,65},{33,97},{65,1},{97,33},{2,66}... | collective-permute-start | bytes 1695752 | tf_op jit(solution)/shard_map/ppermute | solution.py:101
Sparse Core Ops, SparseCore 0:
  190.0 17.5 all-gather.9

commit v8 on v7

--- a/solution.py
+++ b/solution.py
@@ -10,7 +10,6 @@
 
 GRP = ("y_lo", "core")
 BAND = ("y_hi", "x", "z")
-GATHER_ORDER = ("z", "x", "y_hi", "y_lo", "core")
 
 
 def shift_pairs(count, step):
@@ -119,18 +118,15 @@
         packed = jnp.concatenate(
             [gram_local.reshape(count, ensemble * ensemble), pull_vec], axis=1
         )
-        for axis in GATHER_ORDER:
-            packed = lax.all_gather(packed, axis, axis=0, tiled=False)
+        devices = lax.psum(1, GRP + BAND)
+        packed = lax.all_to_all(
+            jnp.broadcast_to(packed[None], (devices,) + packed.shape),
+            GRP + BAND, split_axis=0, concat_axis=0, tiled=True,
+        )
         packed = packed.reshape(-1, ensemble * ensemble + ensemble)
         total_patches = packed.shape[0]
-        quarter_patches = total_patches // 4
-        gathered_row = (
-            (neighbours // quarter_patches) % 2 * (2 * quarter_patches)
-            + neighbours // (2 * quarter_patches) * quarter_patches
-            + neighbours % quarter_patches
-        )
         patch_ids = jnp.arange(total_patches, dtype=jnp.int32)
-        matches = (gathered_row[:, :, None] == patch_ids[None, None, :]).astype(jnp.float32)
+        matches = (neighbours[:, :, None] == patch_ids[None, None, :]).astype(jnp.float32)
         spread_weights = jnp.sum(loc_weight[:, :, None] * matches, axis=1)
         summed = jnp.einsum("pj,jf->pf", spread_weights, packed, precision=highest)
         gram_sum = summed[:, : ensemble * ensemble].reshape(count, ensemble, ensemble)

time: 253 us -> 210 us (0.83)
  blocking collectives: 44.5 us -> 5.9 us
  between operations: 13.9 us -> 0.43 us
  waiting for transfers between devices: 43.7 us -> 48.7 us
  starting transfers between devices: 21.9 us -> 26.6 us
  other arithmetic: 5.02 us -> 2.29 us
    all_gather x4 -> x0, blocking collectives: 38.6 us -> none  [on_device(): packed = lax.all_gather(packed, axis, axis=0, tiled=False)]
    all_to_all x0 -> x1, starting transfers between devices: none -> 11.5 us  [on_device(): lax.all_to_all(jnp.broadcast_to(packed[None], (devices,) + packed.shape),...]
    ppermute x3, starting transfers between devices: 10 us -> 3.2 us  [on_device(): lax.ppermute(outgoing, GRP, [(j, (j + step) % quarters) for j in range(qu...]
    all_to_all x0 -> x1, waiting for transfers between devices: none -> 3.21 us  [on_device(): lax.all_to_all(jnp.broadcast_to(packed[None], (devices,) + packed.shape),...]
    unnamed x41 -> x37, local copies, waits for them, and re-layouts: 16.6 us -> 18.7 us
  transfers between devices with their start and end apart: 7 -> 7, of which waited for: 4 -> 6; matrix products, arithmetic and copies ran while one was open for 15% -> 17% of each run, Pallas kernels for 0% -> 0%
where the time goes in v8:
time: 210 us
  matrix products  77.3 us (37%)
  waiting for transfers between devices  48.7 us (23%)
  local copies, waits for them, and re-layouts  48.4 us (23%)
  starting transfers between devices  26.6 us (13%)
  blocking collectives  5.9 us (3%)
  other arithmetic  2.29 us (1%)
    conv_general_dilated x2, matrix products, convolve(): lax.conv_general_dilated(wrapped, kernel, window_strides=(1, 1), padding=...  62.8 us
    ppermute x1, waiting for transfers between devices, padded_2(): lax.ppermute(cells, BAND, shift_pairs(band_size, 1))  29.2 us
    unnamed x37, local copies, waits for them, and re-layouts  18.7 us
    ppermute x3, waiting for transfers between devices, on_device(): lax.ppermute(outgoing, GRP, [(j, (j + step) % quarters) for j in range(qu...  13 us
    all_to_all x1, starting transfers between devices, on_device(): lax.all_to_all(jnp.broadcast_to(packed[None], (devices,) + packed.shape),...  11.5 us
    dot_general x1, matrix products, on_device(): jnp.einsum('ajnm,jailnc->mcil', weights, spread_out, precision=highest)  7.75 us
    ppermute x1, local copies, waits for them, and re-layouts, padded_2(): lax.ppermute(cells, BAND, shift_pairs(band_size, 1))  6.78 us
    ppermute x1, local copies, waits for them, and re-layouts, padded_2(): lax.ppermute(cells, BAND, shift_pairs(band_size, -1))  6.7 us
  transfers between devices with their start and end apart: 7, of which 6 were waited for; matrix products, arithmetic and copies ran while one was open for 17% of the time, Pallas kernels for 0%

profile of v8, /device:TPU:1, one launch (start us, length us, event | category | flops | bytes accessed | tf_op | source)
XLA Modules:
  0.0 209.6 jit_solution(4923577957203350791)
XLA Ops:
  0.0 2.4 %copy.108 = bf16[8,69,2,1024]{3,0,1,2:T(8,128)(2,1)S(1)} copy(bf16[8,69,2,1024]{3,2,1,0:T(2,128)(2,1)} %param.10) | data formatting | bytes 4521984 | tf_op jit(solution)/transpose | solution.py:202
  2.4 5.8 %collective-permute-start = (bf16[2,1024,8,69]{1,2,3,0:T(8,128)(2,1)S(1)}, bf16[2,1024,8,69]{1,2,3,0:T(8,128)(2,1)}, u32[]{:S(2)}, u32[]{:S(2)}) collective-permute-start(bf16[2,1024,8,69]{1,2,3,0:T(8,128)(2,1)S(1)} %bitcast.109), channel_id=1, source_target_pairs={{0,1},{1,2},{2,3},{3,4},{4,5},{5,6},{6,7},{7,8},{8,9},{9,10},{10,1... | collective-permute-start | bytes 6782984 | tf_op jit(solution)/shard_map/ppermute | solution.py:22
  8.1 1.3 collective-permute-start.1
  9.4 7.1 %copy.53 = bf16[8,69,2,1024]{1,0,3,2:T(8,128)(2,1)} copy(bf16[8,69,2,1024]{3,2,1,0:T(2,128)(2,1)} %param.10) | data formatting | bytes 4521984 | tf_op args[0]
  16.6 0.5 copy-done.10
  17.2 0.7 add.188
  17.8 5.9 %all-gather.1 = s32[4,2,256]{2,1,0:T(2,128)S(1)} all-gather(s32[1,2,256]{2,1,0:T(2,128)S(1)} %bitcast.120), channel_id=2, replica_groups=mesh['y_lo'=2,'core'=2,'y_hi'=2,'x'=4,'z'=4] {'y_lo','core'}, dimensions={0}, use_global_device_ids=true | all-gather | bytes 10240 | tf_op jit(solution)/shard_map/all_gather | solution.py:78
  23.8 0.6 and_select_fusion.1
  24.4 0.9 fusion.45
  25.3 29.2 %collective-permute-done = bf16[2,1024,8,69]{1,2,3,0:T(8,128)(2,1)} collective-permute-done((bf16[2,1024,8,69]{1,2,3,0:T(8,128)(2,1)S(1)}, bf16[2,1024,8,69]{1,2,3,0:T(8,128)(2,1)}, u32[]{:S(2)}, u32[]{:S(2)}) %collective-permute-start) | collective-permute-done | bytes 2261024 | tf_op jit(solution)/shard_map/ppermute | solution.py:22
  54.5 6.8 %copy.56 = bf16[2,1024,8,69]{3,2,1,0:T(8,128)(2,1)} copy(bf16[2,1024,8,69]{1,2,3,0:T(8,128)(2,1)} %collective-permute-done) | data formatting | bytes 4521984 | tf_op jit(solution)/shard_map/ppermute | solution.py:22
  61.3 6.7 %copy.57 = bf16[2,1024,8,69]{3,2,1,0:T(8,128)(2,1)} copy(bf16[2,1024,8,69]{1,2,3,0:T(8,128)(2,1)} %collective-permute-done.1) | data formatting | bytes 4521984 | tf_op jit(solution)/shard_map/ppermute | solution.py:24
  68.1 39.8 %fusion.6 = bf16[4,1024,8,256]{3,2,1,0:T(8,128)(2,1)} fusion(f32[256]{0:T(256)S(1)} %copy-done.14, pred[4]{0:T(512)(128)(4,1)S(1)} %and_or_fusion, bf16[3,3,256,69]{2,3,1,0:T(8,128)(2,1)S(1)} %copy-done, bf16[2,1024,8,69]{3,2,1,0:T(8,128)(2,1)} %copy.57, bf16[2,1024,8,69]{3,2,1,0:T(8,128)(2,1)} %bitcast.108, bf16[2,1024,8,69]{3,2,1,0:T(8,128)(2,1)} %copy.56), kind=kOutput, calls=%fused_computation.8 | convolution fusion | flops 10504556544 | bytes 23879172 | tf_op jit(solution)/shard_map/conv_general_dilated | solution.py:32
  107.9 0.7 fusion.74
  108.7 22.9 %add_convert_fusion = bf16[2,1024,8,69]{3,2,1,0:T(8,128)(2,1)S(1)} fusion(f32[69]{0:T(128)S(1)} %copy-done.15, bf16[3,3,69,256]{3,2,1,0:T(8,128)(2,1)S(1)} %copy-done.13, bf16[4,1,8,256]{3,2,1,0:T(8,128)(2,1)S(1)} %get-tuple-element.8, bf16[4,1024,8,256]{3,2,1,0:T(8,128)(2,1)} %fusion.6, bf16[4,1,8,256]{3,2,1,0:T(8,128)(2,1)S(1)} %get-tuple-element.7, ...), kind=kOutput, calls=%fused_computation.25 | convolution fusion | flops 5230657536 | bytes 21650196 | tf_op jit(solution)/shard_map/conv_general_dilated | solution.py:32
  131.7 1.9 copy-done.1
  133.6 2.5 %fusion.21 = f32[4,2,8,256]{3,2,1,0:T(8,128)} fusion(f32[4,2,69,256]{3,2,1,0:T(8,128)S(1)} %copy-done.3, bf16[2,4,256,8,69]{4,3,2,1,0:T(8,128)(2,1)S(1)} %bitcast.106, s32[4,2,256]{2,1,0:T(2,128)S(1)} %copy-done.5), kind=kOutput, calls=%fused_computation.27 | convolution fusion | flops 581582848 | bytes 2899968 | tf_op jit(solution)/shard_map/iqlmc,qiol->qicmo/dot_general | solution.py:84
  136.2 4.8 %all-to-all-start = ((f32[4,2,8,256]{3,2,1,0:T(8,128)}), f32[4,2,8,256]{3,2,1,0:T(8,128)S(1)}, u32[]{:S(2)}, u32[]{:S(2)}) async-start(f32[4,2,8,256]{3,2,1,0:T(8,128)} %fusion.21), calls=%async_computation | async-start | bytes 131072 | tf_op jit(solution)/shard_map/all_to_all | solution.py:94
  141.0 3.3 %all-to-all-done = f32[4,2,8,256]{3,2,1,0:T(8,128)S(1)} async-done(((f32[4,2,8,256]{3,2,1,0:T(8,128)}), f32[4,2,8,256]{3,2,1,0:T(8,128)S(1)}, u32[]{:S(2)}, u32[]{:S(2)}) %all-to-all-start) | async-done | bytes 65568 | tf_op jit(solution)/shard_map/all_to_all | solution.py:94
  144.3 0.2 fusion.46
  144.6 0.2 fusion.48
  144.7 1.3 broadcast_in_dim.96
  146.1 11.5 %all-to-all-start.1 = ((f32[128,2,1056]{2,1,0:T(2,128)}), f32[128,2,1056]{2,1,0:T(2,128)S(1)}, u32[]{:S(2)}, u32[]{:S(2)}) async-start(f32[128,2,1056]{2,1,0:T(2,128)} %broadcast_in_dim.96), calls=%async_computation.1 | async-start | bytes 2359296 | tf_op jit(solution)/shard_map/all_to_all | solution.py:122
  157.9 3.9 %constant_dynamic-slice_fusion.3 = (bf16[2,1,256,8,69]{4,3,2,1,0:T(8,128)(2,1)S(1)}, bf16[2,1,256,8,69]{4,3,2,1,0:T(8,128)(2,1)}, bf16[2,1,256,8,69]{4,3,2,1,0:T(8,128)(2,1)}, bf16[2,1,256,8,69]{4,3,2,1,0:T(8,128)(2,1)}) fusion(bf16[2,4,256,8,69]{4,3,2,1,0:T(8,128)(2,1)} %bitcast.107, s32[]{:T(128)S(6)} %select_n.80, s32[]{:T(128)S(6)} %select_n.84, ...), kind=kLoop, calls=%fused_computation.109 | loop fusion | bytes 4522000 | tf_op jit(solution)/shard_map/jit(dynamic_index_in_dim)/dynamic_slice | solution.py:96
  161.8 2.0 copy.82
  163.8 1.1 collective-permute-start.4
  164.9 2.7 %copy.80 = bf16[2,1,256,8,69]{2,3,4,1,0:T(8,128)(2,1)} copy(bf16[2,1,256,8,69]{4,3,2,1,0:T(8,128)(2,1)} %get-tuple-element.11) | data formatting | bytes 1130496
  167.6 0.7 collective-permute-start.2
  168.3 2.7 %copy.81 = bf16[2,1,256,8,69]{2,3,4,1,0:T(8,128)(2,1)} copy(bf16[2,1,256,8,69]{4,3,2,1,0:T(8,128)(2,1)} %get-tuple-element.10) | data formatting | bytes 1130496
  171.0 1.4 collective-permute-start.3
  172.4 1.7 copy.79
  174.0 3.2 %all-to-all-done.1 = f32[128,2,1056]{2,1,0:T(2,128)S(1)} async-done(((f32[128,2,1056]{2,1,0:T(2,128)}), f32[128,2,1056]{2,1,0:T(2,128)S(1)}, u32[]{:S(2)}, u32[]{:S(2)}) %all-to-all-start.1) | async-done | bytes 1081376 | tf_op jit(solution)/shard_map/all_to_all | solution.py:122
  177.2 0.8 reshape.166
  178.0 0.7 fusion.75
  178.9 0.3 fusion.43
  179.2 0.2 fusion.65
  179.6 0.2 fusion.42
  180.1 0.2 fusion.41
  180.6 0.2 fusion.40
  181.1 0.2 fusion.39
  181.6 0.2 fusion.38
  181.8 0.2 fusion.84
  182.1 0.2 fusion.85
  182.6 0.6 gather_fusion
  183.2 0.2 collective-permute-done.4
  183.6 12.7 %collective-permute-done.3 = bf16[2,256,8,69]{1,2,3,0:T(8,128)(2,1)} collective-permute-done((bf16[2,256,8,69]{1,2,3,0:T(8,128)(2,1)}, bf16[2,256,8,69]{1,2,3,0:T(8,128)(2,1)}, u32[]{:S(2)}, u32[]{:S(2)}) %collective-permute-start.3) | collective-permute-done | bytes 565280 | tf_op jit(solution)/shard_map/ppermute | solution.py:100
  196.3 7.8 %fusion.29 = f32[32,69,2,256]{3,0,1,2:T(8,128)S(1)} fusion(pred[2,2]{0,1:T(4,128)(4,1)S(1)} %iota_compare_fusion.4, f32[2,4,8,32]{3,0,2,1:T(2,128)S(1)} %bitcast.115, pred[4,8]{1,0:T(4,128)(4,1)S(1)} %compare_and_fusion, bf16[1,2,256,8,69]{2,3,4,1,0:T(8,128)(2,1)} %bitcast.10, bf16[1,2,256,8,69]{2,3,4,1,0:T(8,128)(2,1)} %bitcast.8, ...), kind=kOutput, calls=%fused_computation.35 | convolution fusion | flops 875005952 | bytes 6791204 | tf_op jit(solution)/shard_map/ajnm,jailnc->mcil/dot_general | solution.py:166
  204.0 5.6 %copy.67 = f32[32,69,2,256]{3,2,1,0:T(2,128)} copy(f32[32,69,2,256]{3,0,1,2:T(8,128)S(1)} %fusion.29) | data formatting | bytes 9043968 | tf_op jit(solution)/shard_map/ajnm,jailnc->mcil/transpose | solution.py:166
  (67 shorter events, 2.8 us)
Async XLA Ops:
  0.0 68.0 %copy-start = (bf16[3,3,256,69]{2,3,1,0:T(8,128)(2,1)S(1)}, bf16[3,3,256,69]{2,3,1,0:T(8,128)(2,1)}, u32[]{:S(2)}) copy-start(bf16[3,3,256,69]{2,3,1,0:T(8,128)(2,1)} %param.11) | copy-start | bytes 953860
  0.0 17.8 %copy-start.6 = (s32[2,256]{1,0:T(2,128)S(1)}, s32[2,256]{1,0:T(2,128)}, u32[]{:S(2)}) copy-start(s32[2,256]{1,0:T(2,128)} %param.15) | copy-start | bytes 6148
  2.4 52.2 %collective-permute-start = (bf16[2,1024,8,69]{1,2,3,0:T(8,128)(2,1)S(1)}, bf16[2,1024,8,69]{1,2,3,0:T(8,128)(2,1)}, u32[]{:S(2)}, u32[]{:S(2)}) collective-permute-start(bf16[2,1024,8,69]{1,2,3,0:T(8,128)(2,1)S(1)} %bitcast.109), channel_id=1, source_target_pairs={{0,1},{1,2},{2,3},{3,4},{4,5},{5,6},{6,7},{7,8},{8,9},{9,10},{10,1... | collective-permute-start | bytes 6782984 | tf_op jit(solution)/shard_map/ppermute | solution.py:22
  8.1 53.2 %collective-permute-start.1 = (bf16[2,1024,8,69]{1,2,3,0:T(8,128)(2,1)S(1)}, bf16[2,1024,8,69]{1,2,3,0:T(8,128)(2,1)}, u32[]{:S(2)}, u32[]{:S(2)}) collective-permute-start(bf16[2,1024,8,69]{1,2,3,0:T(8,128)(2,1)S(1)} %bitcast.110), channel_id=1, source_target_pairs={{1,0},{2,1},{3,2},{4,3},{5,4},{6,5},{7,6},{8,7},{9,8},{10,9},{11,1... | collective-permute-start | bytes 6782984 | tf_op jit(solution)/shard_map/ppermute | solution.py:24
  16.5 51.5 %copy-start.14 = (f32[256]{0:T(256)S(1)}, f32[256]{0:T(256)}, u32[]{:S(2)}) copy-start(f32[256]{0:T(256)} %param.12) | copy-start | bytes 3076
  16.6 0.5 copy-start.10
  68.0 40.6 %copy-start.2 = (bf16[8,69,2,1024]{1,0,3,2:T(8,128)(2,1)S(1)}, bf16[8,69,2,1024]{1,0,3,2:T(8,128)(2,1)}, u32[]{:S(2)}) copy-start(bf16[8,69,2,1024]{1,0,3,2:T(8,128)(2,1)} %copy.53) | copy-start | bytes 6782980
  68.0 40.6 %copy-start.13 = (bf16[3,3,69,256]{3,2,1,0:T(8,128)(2,1)S(1)}, bf16[3,3,69,256]{3,2,1,0:T(8,128)(2,1)}, u32[]{:S(2)}) copy-start(bf16[3,3,69,256]{3,2,1,0:T(8,128)(2,1)} %param.13) | copy-start | bytes 953860
  68.1 40.6 %copy-start.15 = (f32[69]{0:T(128)S(1)}, f32[69]{0:T(128)}, u32[]{:S(2)}) copy-start(f32[69]{0:T(128)} %param.14) | copy-start | bytes 832
  108.6 25.0 %copy-start.3 = (f32[4,2,69,256]{3,2,1,0:T(8,128)S(1)}, f32[4,2,69,256]{3,2,1,0:T(8,128)}, u32[]{:S(2)}) copy-start(f32[4,2,69,256]{3,2,1,0:T(8,128)} %fusion.45) | copy-start | bytes 1695748
  108.7 25.0 %copy-start.5 = (s32[4,2,256]{2,1,0:T(2,128)S(1)}, s32[4,2,256]{2,1,0:T(2,128)}, u32[]{:S(2)}) copy-start(s32[4,2,256]{2,1,0:T(2,128)} %get-tuple-element.13) | copy-start | bytes 24580
  131.6 2.0 copy-start.1
  131.6 9.3 %copy-start.12 = (s32[32,1]{0,1:T(1,128)S(1)}, s32[32,1]{0,1:T(1,128)}, u32[]{:S(2)}) copy-start(s32[32,1]{0,1:T(1,128)} %add.188) | copy-start | bytes 388
  131.6 12.6 %copy-start.4 = (f32[2,256]{1,0:T(2,128)S(1)}, f32[2,256]{1,0:T(2,128)}, u32[]{:S(2)}) copy-start(f32[2,256]{1,0:T(2,128)} %param.17) | copy-start | bytes 6148
  131.6 12.6 %copy-start.7 = (f32[2,256]{1,0:T(2,128)S(1)}, f32[2,256]{1,0:T(2,128)}, u32[]{:S(2)}) copy-start(f32[2,256]{1,0:T(2,128)} %param.16) | copy-start | bytes 6148
  131.7 26.0 %copy-start.8 = (f32[2,8]{1,0:T(2,128)S(1)}, f32[2,8]{1,0:T(2,128)}, u32[]{:S(2)}) copy-start(f32[2,8]{1,0:T(2,128)} %param.19) | copy-start | bytes 196
  131.7 26.0 %copy-start.9 = (s32[2,8]{1,0:T(2,128)S(1)}, s32[2,8]{1,0:T(2,128)}, u32[]{:S(2)}) copy-start(s32[2,8]{1,0:T(2,128)} %param.18) | copy-start | bytes 196
  131.7 26.1 %copy-start.11 = (s32[4]{0:T(128)S(1)}, s32[4]{0:T(128)}, u32[]{:S(2)}) copy-start(s32[4]{0:T(128)} %copy-done.10) | copy-start | bytes 52
  136.2 8.1 %all-to-all-start = ((f32[4,2,8,256]{3,2,1,0:T(8,128)}), f32[4,2,8,256]{3,2,1,0:T(8,128)S(1)}, u32[]{:S(2)}, u32[]{:S(2)}) async-start(f32[4,2,8,256]{3,2,1,0:T(8,128)} %fusion.21), calls=%async_computation | async-start | bytes 131072 | tf_op jit(solution)/shard_map/all_to_all | solution.py:94
  146.1 31.1 %all-to-all-start.1 = ((f32[128,2,1056]{2,1,0:T(2,128)}), f32[128,2,1056]{2,1,0:T(2,128)S(1)}, u32[]{:S(2)}, u32[]{:S(2)}) async-start(f32[128,2,1056]{2,1,0:T(2,128)} %broadcast_in_dim.96), calls=%async_computation.1 | async-start | bytes 2359296 | tf_op jit(solution)/shard_map/all_to_all | solution.py:122
  163.8 19.6 %collective-permute-start.4 = (bf16[2,256,8,69]{1,2,3,0:T(8,128)(2,1)S(1)}, bf16[2,256,8,69]{1,2,3,0:T(8,128)(2,1)}, u32[]{:S(2)}, u32[]{:S(2)}) collective-permute-start(bf16[2,256,8,69]{1,2,3,0:T(8,128)(2,1)S(1)} %bitcast.111), channel_id=1, source_target_pairs={{0,96},{32,0},{64,32},{96,64},{1,97},{33,1},{65,33},{97,65},{2,98}... | collective-permute-start | bytes 1695752 | tf_op jit(solution)/shard_map/ppermute | solution.py:100
  167.6 16.0 %collective-permute-start.2 = (bf16[2,256,8,69]{1,2,3,0:T(8,128)(2,1)}, bf16[2,256,8,69]{1,2,3,0:T(8,128)(2,1)}, u32[]{:S(2)}, u32[]{:S(2)}) collective-permute-start(bf16[2,256,8,69]{1,2,3,0:T(8,128)(2,1)} %bitcast.113), channel_id=1, source_target_pairs={{0,32},{32,64},{64,96},{96,0},{1,33},{33,65},{65,97},{97,1},{2,34}... | collective-permute-start | bytes 1695752 | tf_op jit(solution)/shard_map/ppermute | solution.py:100
  171.0 25.3 %collective-permute-start.3 = (bf16[2,256,8,69]{1,2,3,0:T(8,128)(2,1)}, bf16[2,256,8,69]{1,2,3,0:T(8,128)(2,1)}, u32[]{:S(2)}, u32[]{:S(2)}) collective-permute-start(bf16[2,256,8,69]{1,2,3,0:T(8,128)(2,1)} %bitcast.114), channel_id=1, source_target_pairs={{0,64},{32,96},{64,0},{96,32},{1,65},{33,97},{65,1},{97,33},{2,66}... | collective-permute-start | bytes 1695752 | tf_op jit(solution)/shard_map/ppermute | solution.py:100

commit v9 on v8

--- a/solution.py
+++ b/solution.py
@@ -32,6 +32,23 @@
     return lax.conv_general_dilated(
         wrapped,
         kernel,
+        window_strides=(1, 1),
+        padding="VALID",
+        dimension_numbers=("HWNC", "HWOI", "HWNC"),
+        preferred_element_type=jnp.float32,
+    )
+
+
+def convolve_stacked(padded, kernel):
+    stacked = jnp.concatenate(
+        [jnp.roll(padded, 1, axis=1), padded, jnp.roll(padded, -1, axis=1)], axis=3
+    )
+    rows_kernel = jnp.transpose(kernel, (0, 2, 1, 3)).reshape(
+        kernel.shape[0], 1, kernel.shape[2], kernel.shape[1] * kernel.shape[3]
+    )
+    return lax.conv_general_dilated(
+        stacked,
+        rows_kernel,
         window_strides=(1, 1),
         padding="VALID",
         dimension_numbers=("HWNC", "HWOI", "HWNC"),
@@ -57,7 +74,7 @@
         height = rows_first.shape[0]
         padded = padded_2(rows_first, band_size)
         hidden_fields = jax.nn.silu(
-            convolve(padded, conv1_weight) + conv1_bias
+            convolve_stacked(padded, conv1_weight) + conv1_bias
         ).astype(jnp.bfloat16)
         place = lax.axis_index(BAND)
         row_ids = jnp.arange(height + 2, dtype=jnp.int32)[:, None, None, None]

time: 210 us -> 284 us (1.35)
  matrix products: 77.3 us -> 126 us
  local copies, waits for them, and re-layouts: 48.4 us -> 66.9 us
  other arithmetic: 2.29 us -> 9.4 us
    conv_general_dilated x0 -> x1, matrix products: none -> 88.7 us  [convolve_stacked(): lax.conv_general_dilated(stacked, rows_kernel, window_strides=(1, 1), pad...]
    conv_general_dilated x2 -> x1, matrix products: 62.8 us -> 22.9 us  [convolve(): lax.conv_general_dilated(wrapped, kernel, window_strides=(1, 1), padding=...]
    slice x0 -> x1, local copies, waits for them, and re-layouts: none -> 12.4 us  [convolve_stacked(): jnp.roll(padded, 1, axis=1)]
    concatenate x0 -> x1, other arithmetic: none -> 7.16 us  [padded_2(): jnp.concatenate([lax.ppermute(cells, BAND, shift_pairs(band_size, 1)), ce...]
    unnamed x37 -> x39, local copies, waits for them, and re-layouts: 18.7 us -> 24.5 us
  transfers between devices with their start and end apart: 7 -> 7, of which waited for: 6 -> 5; matrix products, arithmetic and copies ran while one was open for 17% -> 13% of each run, Pallas kernels for 0% -> 0%
where the time goes in v9:
time: 284 us; the launch traced here: 283 us
  matrix products  126 us (44%)
  local copies, waits for them, and re-layouts  66.9 us (24%)
  waiting for transfers between devices  47.5 us (17%)
  starting transfers between devices  26.6 us (9%)
  other arithmetic  9.4 us (3%)
  blocking collectives  6.03 us (2%)
    conv_general_dilated x1, matrix products, convolve_stacked(): lax.conv_general_dilated(stacked, rows_kernel, window_strides=(1, 1), pad...  88.7 us
    ppermute x1, waiting for transfers between devices, padded_2(): lax.ppermute(cells, BAND, shift_pairs(band_size, 1))  28 us
    unnamed x39, local copies, waits for them, and re-layouts  24.5 us
    conv_general_dilated x1, matrix products, convolve(): lax.conv_general_dilated(wrapped, kernel, window_strides=(1, 1), padding=...  22.9 us
    ppermute x3, waiting for transfers between devices, on_device(): lax.ppermute(outgoing, GRP, [(j, (j + step) % quarters) for j in range(qu...  13 us
    slice x1, local copies, waits for them, and re-layouts, convolve_stacked(): jnp.roll(padded, 1, axis=1)  12.4 us
    all_to_all x1, starting transfers between devices, on_device(): lax.all_to_all(jnp.broadcast_to(packed[None], (devices,) + packed.shape),...  11.5 us
    dot_general x1, matrix products, on_device(): jnp.einsum('ajnm,jailnc->mcil', weights, spread_out, precision=highest)  7.76 us
  transfers between devices with their start and end apart: 7, of which 5 were waited for; matrix products, arithmetic and copies ran while one was open for 13% of the time, Pallas kernels for 0%

profile of v9, /device:TPU:1, one launch (start us, length us, event | category | flops | bytes accessed | tf_op | source)
XLA Modules:
  0.0 283.1 jit_solution(3531424386427412718)
XLA Ops:
  0.0 2.4 copy.113
  2.4 5.8 %collective-permute-start = (bf16[2,1024,8,69]{1,2,3,0:T(8,128)(2,1)S(1)}, bf16[2,1024,8,69]{1,2,3,0:T(8,128)(2,1)}, u32[]{:S(2)}, u32[]{:S(2)}) collective-permute-start(bf16[2,1024,8,69]{1,2,3,0:T(8,128)(2,1)S(1)} %bitcast.116), channel_id=1, source_target_pairs={{0,1},{1,2},{2,3},{3,4},{4,5},{5,6},{6,7},{7,8},{8,9},{9,10},{10,1... | collective-permute-start | bytes 6782984 | tf_op jit(solution)/shard_map/ppermute | solution.py:22
  8.1 1.3 collective-permute-start.1
  9.4 7.2 %copy.57 = bf16[8,69,2,1024]{1,0,3,2:T(8,128)(2,1)} copy(bf16[8,69,2,1024]{3,2,1,0:T(2,128)(2,1)} %param.10) | data formatting | bytes 4521984 | tf_op args[0]
  16.6 1.1 reshape.167
  17.7 0.6 copy-done.11
  18.3 0.7 add.188
  19.0 6.0 %all-gather.1 = s32[4,2,256]{2,1,0:T(2,128)S(1)} all-gather(s32[1,2,256]{2,1,0:T(2,128)} %bitcast.128), channel_id=2, replica_groups=mesh['y_lo'=2,'core'=2,'y_hi'=2,'x'=4,'z'=4] {'y_lo','core'}, dimensions={0}, use_global_device_ids=true | all-gather | bytes 10240 | tf_op jit(solution)/shard_map/all_gather | solution.py:95
  25.0 0.6 and_select_fusion.1
  25.6 0.9 fusion.51
  26.5 28.0 %collective-permute-done = bf16[2,1024,8,69]{1,2,3,0:T(8,128)(2,1)} collective-permute-done((bf16[2,1024,8,69]{1,2,3,0:T(8,128)(2,1)S(1)}, bf16[2,1024,8,69]{1,2,3,0:T(8,128)(2,1)}, u32[]{:S(2)}, u32[]{:S(2)}) %collective-permute-start) | collective-permute-done | bytes 2261024 | tf_op jit(solution)/shard_map/ppermute | solution.py:22
  54.5 6.8 %copy.60 = bf16[2,1024,8,69]{3,2,1,0:T(8,128)(2,1)} copy(bf16[2,1024,8,69]{1,2,3,0:T(8,128)(2,1)} %collective-permute-done) | data formatting | bytes 4521984 | tf_op jit(solution)/shard_map/ppermute | solution.py:22
  61.3 6.7 %copy.61 = bf16[2,1024,8,69]{3,2,1,0:T(8,128)(2,1)} copy(bf16[2,1024,8,69]{1,2,3,0:T(8,128)(2,1)} %collective-permute-done.1) | data formatting | bytes 4521984 | tf_op jit(solution)/shard_map/ppermute | solution.py:24
  68.0 7.2 %pad_maximum_fusion.6 = bf16[6,1024,8,69]{3,2,1,0:T(8,128)(2,1)S(1)} fusion(bf16[2,1024,8,69]{3,2,1,0:T(8,128)(2,1)} %copy.61, bf16[2,1024,8,69]{3,2,1,0:T(8,128)(2,1)} %bitcast.112, bf16[2,1024,8,69]{3,2,1,0:T(8,128)(2,1)} %copy.60), kind=kLoop, calls=%fused_computation.27 | loop fusion | flops 6782976 | bytes 13565952 | tf_op jit(solution)/shard_map/concatenate | solution.py:20
  75.2 12.4 %fusion.82 = (bf16[6,1023,8,69]{3,2,1,0:T(8,128)(2,1)}, bf16[6,1023,8,69]{3,2,1,0:T(8,128)(2,1)}) fusion(bf16[6,1024,8,69]{3,2,1,0:T(8,128)(2,1)S(1)} %pad_maximum_fusion.6), kind=kLoop, calls=%fused_computation.127 | loop fusion | bytes 27105408 | tf_op jit(solution)/shard_map/jit(_roll_static)/slice | solution.py:44
  87.6 88.7 %fusion.22 = bf16[4,1024,8,256]{3,2,1,0:T(8,128)(2,1)S(1)} fusion(f32[256]{0:T(256)S(1)} %copy-done.15, pred[4]{0:T(512)(128)(4,1)S(1)} %and_or_fusion, bf16[2,1024,8,69]{3,2,1,0:T(8,128)(2,1)S(1)} %copy-done.3, bf16[2,1024,8,69]{3,2,1,0:T(8,128)(2,1)S(1)} %bitcast.113, bf16[2,1024,8,69]{3,2,1,0:T(8,128)(2,1)S(1)} %copy-done.2, ...), kind=kOutput, calls=%fused_computation.26 | convolution fusion | flops 10701209600 | bytes 37431876 | tf_op jit(solution)/shard_map/conv_general_dilated | solution.py:49
  176.4 5.7 %copy-done.14 = bf16[4,1024,8,256]{3,2,1,0:T(8,128)(2,1)} copy-done((bf16[4,1024,8,256]{3,2,1,0:T(8,128)(2,1)}, bf16[4,1024,8,256]{3,2,1,0:T(8,128)(2,1)S(1)}, u32[]{:S(2)}) %copy-start.14) | copy-done | bytes 16777240
  182.1 22.9 %add_convert_fusion = bf16[2,1024,8,69]{3,2,1,0:T(8,128)(2,1)S(1)} fusion(f32[69]{0:T(128)S(1)} %copy-done.16, bf16[3,3,69,256]{3,2,1,0:T(8,128)(2,1)S(1)} %copy-done, bf16[4,1,8,256]{3,2,1,0:T(8,128)(2,1)S(1)} %get-tuple-element.8, bf16[4,1024,8,256]{3,2,1,0:T(8,128)(2,1)} %copy-done.14, bf16[4,1,8,256]{3,2,1,0:T(8,128)(2,1)S(1)} %get-tuple-element.7, ...), kind=kOutput, calls=%fused_computation.30 | convolution fusion | flops 5230657536 | bytes 21650196 | tf_op jit(solution)/shard_map/conv_general_dilated | solution.py:32
  205.1 2.0 copy-done.4
  207.1 2.6 fusion.25
  209.6 4.8 %all-to-all-start = ((f32[4,2,8,256]{3,2,1,0:T(8,128)}), f32[4,2,8,256]{3,2,1,0:T(8,128)S(1)}, u32[]{:S(2)}, u32[]{:S(2)}) async-start(f32[4,2,8,256]{3,2,1,0:T(8,128)} %fusion.25), calls=%async_computation | async-start | bytes 131072 | tf_op jit(solution)/shard_map/all_to_all | solution.py:111
  214.4 3.3 %all-to-all-done = f32[4,2,8,256]{3,2,1,0:T(8,128)S(1)} async-done(((f32[4,2,8,256]{3,2,1,0:T(8,128)}), f32[4,2,8,256]{3,2,1,0:T(8,128)S(1)}, u32[]{:S(2)}, u32[]{:S(2)}) %all-to-all-start) | async-done | bytes 65568 | tf_op jit(solution)/shard_map/all_to_all | solution.py:111
  217.7 0.2 fusion.53
  218.0 0.2 fusion.55
  218.2 1.4 broadcast_in_dim.96
  219.6 11.5 %all-to-all-start.1 = ((f32[128,2,1056]{2,1,0:T(2,128)}), f32[128,2,1056]{2,1,0:T(2,128)S(1)}, u32[]{:S(2)}, u32[]{:S(2)}) async-start(f32[128,2,1056]{2,1,0:T(2,128)} %broadcast_in_dim.96), calls=%async_computation.1 | async-start | bytes 2359296 | tf_op jit(solution)/shard_map/all_to_all | solution.py:139
  231.4 3.9 %constant_dynamic-slice_fusion.3 = (bf16[2,1,256,8,69]{4,3,2,1,0:T(8,128)(2,1)S(1)}, bf16[2,1,256,8,69]{4,3,2,1,0:T(8,128)(2,1)}, bf16[2,1,256,8,69]{4,3,2,1,0:T(8,128)(2,1)}, bf16[2,1,256,8,69]{4,3,2,1,0:T(8,128)(2,1)}) fusion(bf16[2,4,256,8,69]{4,3,2,1,0:T(8,128)(2,1)} %bitcast.115, s32[]{:T(128)S(6)} %select_n.80, s32[]{:T(128)S(6)} %select_n.84, ...), kind=kLoop, calls=%fused_computation.115 | loop fusion | bytes 4522000 | tf_op jit(solution)/shard_map/jit(dynamic_index_in_dim)/dynamic_slice | solution.py:113
  235.2 2.0 copy.86
  237.2 1.5 collective-permute-start.3
  238.7 2.7 copy.87
  241.4 0.6 collective-permute-start.4
  242.0 2.7 copy.85
  244.7 1.1 collective-permute-start.2
  245.8 1.6 copy.84
  247.5 3.2 %all-to-all-done.1 = f32[128,2,1056]{2,1,0:T(2,128)S(1)} async-done(((f32[128,2,1056]{2,1,0:T(2,128)}), f32[128,2,1056]{2,1,0:T(2,128)S(1)}, u32[]{:S(2)}, u32[]{:S(2)}) %all-to-all-start.1) | async-done | bytes 1081376 | tf_op jit(solution)/shard_map/all_to_all | solution.py:139
  250.7 0.8 reshape.170
  251.6 0.7 fusion.83
  252.4 0.3 fusion.49
  252.7 0.2 fusion.72
  253.1 0.2 fusion.48
  253.6 0.2 fusion.47
  254.1 0.2 fusion.46
  255.6 0.2 fusion.93
  256.1 0.6 gather_fusion
  256.7 0.8 collective-permute-done.3
  257.5 12.2 %collective-permute-done.4 = bf16[2,256,8,69]{1,2,3,0:T(8,128)(2,1)} collective-permute-done((bf16[2,256,8,69]{1,2,3,0:T(8,128)(2,1)}, bf16[2,256,8,69]{1,2,3,0:T(8,128)(2,1)}, u32[]{:S(2)}, u32[]{:S(2)}) %collective-permute-start.4) | collective-permute-done | bytes 565280 | tf_op jit(solution)/shard_map/ppermute | solution.py:117
  269.8 7.8 %fusion.33 = f32[32,69,2,256]{3,0,1,2:T(8,128)S(1)} fusion(pred[2,2]{0,1:T(4,128)(4,1)S(1)} %iota_compare_fusion.4, f32[2,4,8,32]{3,0,2,1:T(2,128)S(1)} %bitcast.123, pred[4,8]{1,0:T(4,128)(4,1)S(1)} %compare_and_fusion, bf16[1,2,256,8,69]{2,3,4,1,0:T(8,128)(2,1)} %bitcast.12, bf16[1,2,256,8,69]{2,3,4,1,0:T(8,128)(2,1)} %bitcast.10, ...), kind=kOutput, calls=%fused_computation.40 | convolution fusion | flops 875005952 | bytes 6791204 | tf_op jit(solution)/shard_map/ajnm,jailnc->mcil/dot_general | solution.py:183
  277.5 5.6 %copy.72 = f32[32,69,2,256]{3,2,1,0:T(2,128)} copy(f32[32,69,2,256]{3,0,1,2:T(8,128)S(1)} %fusion.33) | data formatting | bytes 9043968 | tf_op jit(solution)/shard_map/ajnm,jailnc->mcil/transpose | solution.py:183
  (72 shorter events, 3.1 us)
Async XLA Ops:
  0.0 182.1 %copy-start = (bf16[3,3,69,256]{3,2,1,0:T(8,128)(2,1)S(1)}, bf16[3,3,69,256]{3,2,1,0:T(8,128)(2,1)}, u32[]{:S(2)}) copy-start(bf16[3,3,69,256]{3,2,1,0:T(8,128)(2,1)} %param.13) | copy-start | bytes 953860
  2.4 52.2 %collective-permute-start = (bf16[2,1024,8,69]{1,2,3,0:T(8,128)(2,1)S(1)}, bf16[2,1024,8,69]{1,2,3,0:T(8,128)(2,1)}, u32[]{:S(2)}, u32[]{:S(2)}) collective-permute-start(bf16[2,1024,8,69]{1,2,3,0:T(8,128)(2,1)S(1)} %bitcast.116), channel_id=1, source_target_pairs={{0,1},{1,2},{2,3},{3,4},{4,5},{5,6},{6,7},{7,8},{8,9},{9,10},{10,1... | collective-permute-start | bytes 6782984 | tf_op jit(solution)/shard_map/ppermute | solution.py:22
  8.1 53.2 %collective-permute-start.1 = (bf16[2,1024,8,69]{1,2,3,0:T(8,128)(2,1)S(1)}, bf16[2,1024,8,69]{1,2,3,0:T(8,128)(2,1)}, u32[]{:S(2)}, u32[]{:S(2)}) collective-permute-start(bf16[2,1024,8,69]{1,2,3,0:T(8,128)(2,1)S(1)} %bitcast.117), channel_id=1, source_target_pairs={{1,0},{2,1},{3,2},{4,3},{5,4},{6,5},{7,6},{8,7},{9,8},{10,9},{11,1... | collective-permute-start | bytes 6782984 | tf_op jit(solution)/shard_map/ppermute | solution.py:24
  17.6 0.6 copy-start.11
  75.2 12.4 %copy-start.1 = (bf16[8,69,2,1024]{1,0,3,2:T(8,128)(2,1)S(1)}, bf16[8,69,2,1024]{1,0,3,2:T(8,128)(2,1)}, u32[]{:S(2)}) copy-start(bf16[8,69,2,1024]{1,0,3,2:T(8,128)(2,1)} %copy.57) | copy-start | bytes 6782980
  75.2 12.4 %copy-start.2 = (bf16[2,1024,8,69]{3,2,1,0:T(8,128)(2,1)S(1)}, bf16[2,1024,8,69]{3,2,1,0:T(8,128)(2,1)}, u32[]{:S(2)}) copy-start(bf16[2,1024,8,69]{3,2,1,0:T(8,128)(2,1)} %copy.60) | copy-start | bytes 6782980
  75.2 12.4 %copy-start.3 = (bf16[2,1024,8,69]{3,2,1,0:T(8,128)(2,1)S(1)}, bf16[2,1024,8,69]{3,2,1,0:T(8,128)(2,1)}, u32[]{:S(2)}) copy-start(bf16[2,1024,8,69]{3,2,1,0:T(8,128)(2,1)} %copy.61) | copy-start | bytes 6782980
  75.2 12.4 %copy-start.15 = (f32[256]{0:T(256)S(1)}, f32[256]{0:T(256)}, u32[]{:S(2)}) copy-start(f32[256]{0:T(256)} %param.12) | copy-start | bytes 3076
  87.6 94.5 %copy-start.16 = (f32[69]{0:T(128)S(1)}, f32[69]{0:T(128)}, u32[]{:S(2)}) copy-start(f32[69]{0:T(128)} %param.14) | copy-start | bytes 832
  176.3 5.7 %copy-start.14 = (bf16[4,1024,8,256]{3,2,1,0:T(8,128)(2,1)}, bf16[4,1024,8,256]{3,2,1,0:T(8,128)(2,1)S(1)}, u32[]{:S(2)}) copy-start(bf16[4,1024,8,256]{3,2,1,0:T(8,128)(2,1)S(1)} %fusion.22) | copy-start | bytes 50331652
  182.1 25.0 %copy-start.5 = (f32[4,2,69,256]{3,2,1,0:T(8,128)S(1)}, f32[4,2,69,256]{3,2,1,0:T(8,128)}, u32[]{:S(2)}) copy-start(f32[4,2,69,256]{3,2,1,0:T(8,128)} %fusion.51) | copy-start | bytes 1695748
  182.1 25.0 %copy-start.7 = (s32[4,2,256]{2,1,0:T(2,128)S(1)}, s32[4,2,256]{2,1,0:T(2,128)}, u32[]{:S(2)}) copy-start(s32[4,2,256]{2,1,0:T(2,128)} %get-tuple-element.15) | copy-start | bytes 24580
  182.1 32.3 %copy-start.13 = (s32[32,1]{0,1:T(1,128)S(1)}, s32[32,1]{0,1:T(1,128)}, u32[]{:S(2)}) copy-start(s32[32,1]{0,1:T(1,128)} %add.188) | copy-start | bytes 388
  182.1 35.6 %copy-start.6 = (f32[2,256]{1,0:T(2,128)S(1)}, f32[2,256]{1,0:T(2,128)}, u32[]{:S(2)}) copy-start(f32[2,256]{1,0:T(2,128)} %param.17) | copy-start | bytes 6148
  182.1 35.6 %copy-start.8 = (f32[2,256]{1,0:T(2,128)S(1)}, f32[2,256]{1,0:T(2,128)}, u32[]{:S(2)}) copy-start(f32[2,256]{1,0:T(2,128)} %param.16) | copy-start | bytes 6148
  205.1 2.0 copy-start.4
  205.1 26.1 %copy-start.9 = (f32[2,8]{1,0:T(2,128)S(1)}, f32[2,8]{1,0:T(2,128)}, u32[]{:S(2)}) copy-start(f32[2,8]{1,0:T(2,128)} %param.19) | copy-start | bytes 196
  205.1 26.1 %copy-start.10 = (s32[2,8]{1,0:T(2,128)S(1)}, s32[2,8]{1,0:T(2,128)}, u32[]{:S(2)}) copy-start(s32[2,8]{1,0:T(2,128)} %param.18) | copy-start | bytes 196
  205.1 26.2 %copy-start.12 = (s32[4]{0:T(128)S(1)}, s32[4]{0:T(128)}, u32[]{:S(2)}) copy-start(s32[4]{0:T(128)} %copy-done.11) | copy-start | bytes 52
  209.6 8.1 %all-to-all-start = ((f32[4,2,8,256]{3,2,1,0:T(8,128)}), f32[4,2,8,256]{3,2,1,0:T(8,128)S(1)}, u32[]{:S(2)}, u32[]{:S(2)}) async-start(f32[4,2,8,256]{3,2,1,0:T(8,128)} %fusion.25), calls=%async_computation | async-start | bytes 131072 | tf_op jit(solution)/shard_map/all_to_all | solution.py:111
  219.6 31.2 %all-to-all-start.1 = ((f32[128,2,1056]{2,1,0:T(2,128)}), f32[128,2,1056]{2,1,0:T(2,128)S(1)}, u32[]{:S(2)}, u32[]{:S(2)}) async-start(f32[128,2,1056]{2,1,0:T(2,128)} %broadcast_in_dim.96), calls=%async_computation.1 | async-start | bytes 2359296 | tf_op jit(solution)/shard_map/all_to_all | solution.py:139
  237.2 20.3 %collective-permute-start.3 = (bf16[2,256,8,69]{1,2,3,0:T(8,128)(2,1)S(1)}, bf16[2,256,8,69]{1,2,3,0:T(8,128)(2,1)}, u32[]{:S(2)}, u32[]{:S(2)}) collective-permute-start(bf16[2,256,8,69]{1,2,3,0:T(8,128)(2,1)S(1)} %bitcast.118), channel_id=1, source_target_pairs={{0,64},{32,96},{64,0},{96,32},{1,65},{33,97},{65,1},{97,33},{2,66}... | collective-permute-start | bytes 1695752 | tf_op jit(solution)/shard_map/ppermute | solution.py:117
  241.4 28.4 %collective-permute-start.4 = (bf16[2,256,8,69]{1,2,3,0:T(8,128)(2,1)}, bf16[2,256,8,69]{1,2,3,0:T(8,128)(2,1)}, u32[]{:S(2)}, u32[]{:S(2)}) collective-permute-start(bf16[2,256,8,69]{1,2,3,0:T(8,128)(2,1)} %bitcast.120), channel_id=1, source_target_pairs={{0,96},{32,0},{64,32},{96,64},{1,97},{33,1},{65,33},{97,65},{2,98}... | collective-permute-start | bytes 1695752 | tf_op jit(solution)/shard_map/ppermute | solution.py:117
  244.7 25.0 %collective-permute-start.2 = (bf16[2,256,8,69]{1,2,3,0:T(8,128)(2,1)}, bf16[2,256,8,69]{1,2,3,0:T(8,128)(2,1)}, u32[]{:S(2)}, u32[]{:S(2)}) collective-permute-start(bf16[2,256,8,69]{1,2,3,0:T(8,128)(2,1)} %bitcast.121), channel_id=1, source_target_pairs={{0,32},{32,64},{64,96},{96,0},{1,33},{33,65},{65,97},{97,1},{2,34}... | collective-permute-start | bytes 1695752 | tf_op jit(solution)/shard_map/ppermute | solution.py:117

commit v10 on v8

--- a/solution.py
+++ b/solution.py
@@ -115,22 +115,28 @@
             "pmo,po->pm", perturb, obs_prec * innovation, precision=highest
         )
         count = gram_local.shape[0]
+        upper_rows, upper_cols = np.triu_indices(ensemble)
+        upper = upper_rows * ensemble + upper_cols
+        triangle = upper.shape[0]
+        place_of = np.zeros((ensemble, ensemble), np.int32)
+        place_of[upper_rows, upper_cols] = np.arange(triangle)
+        place_of[upper_cols, upper_rows] = np.arange(triangle)
         packed = jnp.concatenate(
-            [gram_local.reshape(count, ensemble * ensemble), pull_vec], axis=1
+            [gram_local.reshape(count, ensemble * ensemble)[:, upper], pull_vec], axis=1
         )
         devices = lax.psum(1, GRP + BAND)
         packed = lax.all_to_all(
             jnp.broadcast_to(packed[None], (devices,) + packed.shape),
             GRP + BAND, split_axis=0, concat_axis=0, tiled=True,
         )
-        packed = packed.reshape(-1, ensemble * ensemble + ensemble)
+        packed = packed.reshape(-1, triangle + ensemble)
         total_patches = packed.shape[0]
         patch_ids = jnp.arange(total_patches, dtype=jnp.int32)
         matches = (neighbours[:, :, None] == patch_ids[None, None, :]).astype(jnp.float32)
         spread_weights = jnp.sum(loc_weight[:, :, None] * matches, axis=1)
         summed = jnp.einsum("pj,jf->pf", spread_weights, packed, precision=highest)
-        gram_sum = summed[:, : ensemble * ensemble].reshape(count, ensemble, ensemble)
-        pull_sum = summed[:, ensemble * ensemble :]
+        gram_sum = summed[:, place_of.reshape(-1)].reshape(count, ensemble, ensemble)
+        pull_sum = summed[:, triangle:]
         identity = jnp.broadcast_to(
             jnp.eye(ensemble, dtype=jnp.float32), (height, ensemble, ensemble)
         )

time: 210 us -> 209 us (level)
  waiting for transfers between devices: 48.7 us -> 39.9 us
  other arithmetic: 2.29 us -> 7.77 us
    gather x0 -> x3, local copies, waits for them, and re-layouts: none -> 4.52 us  [the longest x1 2.81 us: on_device(): summed[:, place_of.reshape(-1)].reshape(count, ensemble, ensemble)]
    unnamed x37 -> x43, local copies, waits for them, and re-layouts: 18.7 us -> 15.3 us
    ppermute x3, waiting for transfers between devices: 13 us -> 9.93 us  [on_device(): lax.ppermute(outgoing, GRP, [(j, (j + step) % quarters) for j in range(qu...]
    all_to_all x1, waiting for transfers between devices: 3.21 us -> 0.48 us  [on_device(): lax.all_to_all(jnp.broadcast_to(packed[None], (devices,) + packed.shape),...]
    ppermute x1, waiting for transfers between devices: 29.2 us -> 26.8 us  [padded_2(): lax.ppermute(cells, BAND, shift_pairs(band_size, 1))]
  transfers between devices with their start and end apart: 7 -> 7, of which waited for: 6 -> 4; matrix products, arithmetic and copies ran while one was open for 17% -> 19% of each run, Pallas kernels for 0% -> 0%
where the time goes in v10:
time: 209 us; the launch traced here: 208 us
  matrix products  77 us (37%)
  local copies, waits for them, and re-layouts  49.6 us (24%)
  waiting for transfers between devices  39.9 us (19%)
  starting transfers between devices  27 us (13%)
  other arithmetic  7.77 us (4%)
  blocking collectives  5.9 us (3%)
    conv_general_dilated x2, matrix products, convolve(): lax.conv_general_dilated(wrapped, kernel, window_strides=(1, 1), padding=...  62.7 us
    ppermute x1, waiting for transfers between devices, padded_2(): lax.ppermute(cells, BAND, shift_pairs(band_size, 1))  26.8 us
    unnamed x43, local copies, waits for them, and re-layouts  15.3 us
    all_to_all x1, starting transfers between devices, on_device(): lax.all_to_all(jnp.broadcast_to(packed[None], (devices,) + packed.shape),...  11.9 us
    ppermute x3, waiting for transfers between devices, on_device(): lax.ppermute(outgoing, GRP, [(j, (j + step) % quarters) for j in range(qu...  9.93 us
    dot_general x1, matrix products, on_device(): jnp.einsum('ajnm,jailnc->mcil', weights, spread_out, precision=highest)  7.73 us
    ppermute x1, local copies, waits for them, and re-layouts, padded_2(): lax.ppermute(cells, BAND, shift_pairs(band_size, 1))  6.76 us
    ppermute x1, local copies, waits for them, and re-layouts, padded_2(): lax.ppermute(cells, BAND, shift_pairs(band_size, -1))  6.7 us
  transfers between devices with their start and end apart: 7, of which 4 were waited for; matrix products, arithmetic and copies ran while one was open for 19% of the time, Pallas kernels for 0%

profile of v10, /device:TPU:1, one launch (start us, length us, event | category | flops | bytes accessed | tf_op | source)
XLA Modules:
  0.0 207.6 jit_solution(2633009516469307652)
XLA Ops:
  0.0 2.4 %copy.136 = bf16[8,69,2,1024]{3,0,1,2:T(8,128)(2,1)S(1)} copy(bf16[8,69,2,1024]{3,2,1,0:T(2,128)(2,1)} %param.14) | data formatting | bytes 4521984 | tf_op jit(solution)/transpose | solution.py:208
  2.4 5.8 %collective-permute-start = (bf16[2,1024,8,69]{1,2,3,0:T(8,128)(2,1)S(1)}, bf16[2,1024,8,69]{1,2,3,0:T(8,128)(2,1)}, u32[]{:S(2)}, u32[]{:S(2)}) collective-permute-start(bf16[2,1024,8,69]{1,2,3,0:T(8,128)(2,1)S(1)} %bitcast.114), channel_id=1, source_target_pairs={{0,1},{1,2},{2,3},{3,4},{4,5},{5,6},{6,7},{7,8},{8,9},{9,10},{10,1... | collective-permute-start | bytes 6782984 | tf_op jit(solution)/shard_map/ppermute | solution.py:22
  8.2 1.3 collective-permute-start.1
  9.4 7.1 %copy.75 = bf16[8,69,2,1024]{1,0,3,2:T(8,128)(2,1)} copy(bf16[8,69,2,1024]{3,2,1,0:T(2,128)(2,1)} %param.14) | data formatting | bytes 4521984 | tf_op args[0]
  16.7 5.9 %all-gather.1 = s32[4,2,256]{2,1,0:T(2,128)S(1)} all-gather(s32[1,2,256]{2,1,0:T(2,128)S(1)} %bitcast.128), channel_id=2, replica_groups=mesh['y_lo'=2,'core'=2,'y_hi'=2,'x'=4,'z'=4] {'y_lo','core'}, dimensions={0}, use_global_device_ids=true | all-gather | bytes 10240 | tf_op jit(solution)/shard_map/all_gather | solution.py:78
  22.6 0.6 pad_clamp_fusion.1
  23.2 0.6 fusion.63
  23.8 0.6 fusion.62
  24.4 0.6 fusion.61
  25.0 0.6 compare_and_fusion
  25.6 0.6 fusion.69
  26.2 0.6 and_select_fusion.1
  26.8 0.9 fusion.45
  27.7 26.8 %collective-permute-done = bf16[2,1024,8,69]{1,2,3,0:T(8,128)(2,1)} collective-permute-done((bf16[2,1024,8,69]{1,2,3,0:T(8,128)(2,1)S(1)}, bf16[2,1024,8,69]{1,2,3,0:T(8,128)(2,1)}, u32[]{:S(2)}, u32[]{:S(2)}) %collective-permute-start) | collective-permute-done | bytes 2261024 | tf_op jit(solution)/shard_map/ppermute | solution.py:22
  54.6 6.8 %copy.78 = bf16[2,1024,8,69]{3,2,1,0:T(8,128)(2,1)} copy(bf16[2,1024,8,69]{1,2,3,0:T(8,128)(2,1)} %collective-permute-done) | data formatting | bytes 4521984 | tf_op jit(solution)/shard_map/ppermute | solution.py:22
  61.3 6.7 %copy.79 = bf16[2,1024,8,69]{3,2,1,0:T(8,128)(2,1)} copy(bf16[2,1024,8,69]{1,2,3,0:T(8,128)(2,1)} %collective-permute-done.1) | data formatting | bytes 4521984 | tf_op jit(solution)/shard_map/ppermute | solution.py:24
  68.1 39.8 %fusion.6 = bf16[4,1024,8,256]{3,2,1,0:T(8,128)(2,1)} fusion(f32[256]{0:T(256)S(1)} %copy-done.17, pred[4]{0:T(512)(128)(4,1)S(1)} %and_or_fusion, bf16[3,3,256,69]{2,3,1,0:T(8,128)(2,1)S(1)} %copy-done, bf16[2,1024,8,69]{3,2,1,0:T(8,128)(2,1)} %copy.79, bf16[2,1024,8,69]{3,2,1,0:T(8,128)(2,1)} %bitcast.113, bf16[2,1024,8,69]{3,2,1,0:T(8,128)(2,1)} %copy.78), kind=kOutput, calls=%fused_computation.10 | convolution fusion | flops 10504556544 | bytes 23879172 | tf_op jit(solution)/shard_map/conv_general_dilated | solution.py:32
  107.9 0.7 fusion.74
  108.7 22.9 %add_convert_fusion = bf16[2,1024,8,69]{3,2,1,0:T(8,128)(2,1)S(1)} fusion(f32[69]{0:T(128)S(1)} %copy-done.18, bf16[3,3,69,256]{3,2,1,0:T(8,128)(2,1)S(1)} %copy-done.16, bf16[4,1,8,256]{3,2,1,0:T(8,128)(2,1)S(1)} %get-tuple-element.8, bf16[4,1024,8,256]{3,2,1,0:T(8,128)(2,1)} %fusion.6, bf16[4,1,8,256]{3,2,1,0:T(8,128)(2,1)S(1)} %get-tuple-element.7, ...), kind=kOutput, calls=%fused_computation.27 | convolution fusion | flops 5230657536 | bytes 21650196 | tf_op jit(solution)/shard_map/conv_general_dilated | solution.py:32
  131.7 1.9 copy-done.1
  133.6 2.5 %fusion.21 = f32[4,2,8,256]{3,2,1,0:T(8,128)} fusion(f32[4,2,69,256]{3,2,1,0:T(8,128)S(1)} %copy-done.4, bf16[2,4,256,8,69]{4,3,2,1,0:T(8,128)(2,1)S(1)} %bitcast.111, s32[4,2,256]{2,1,0:T(2,128)S(1)} %copy-done.8), kind=kOutput, calls=%fused_computation.29 | convolution fusion | flops 581582848 | bytes 2899968 | tf_op jit(solution)/shard_map/iqlmc,qiol->qicmo/dot_general | solution.py:84
  136.2 4.8 %all-to-all-start = ((f32[4,2,8,256]{3,2,1,0:T(8,128)}), f32[4,2,8,256]{3,2,1,0:T(8,128)S(1)}, u32[]{:S(2)}, u32[]{:S(2)}) async-start(f32[4,2,8,256]{3,2,1,0:T(8,128)} %fusion.21), calls=%async_computation | async-start | bytes 131072 | tf_op jit(solution)/shard_map/all_to_all | solution.py:94
  141.0 0.6 pad_clamp_fusion
  141.5 2.7 %all-to-all-done = f32[4,2,8,256]{3,2,1,0:T(8,128)S(1)} async-done(((f32[4,2,8,256]{3,2,1,0:T(8,128)}), f32[4,2,8,256]{3,2,1,0:T(8,128)S(1)}, u32[]{:S(2)}, u32[]{:S(2)}) %all-to-all-start) | async-done | bytes 65568 | tf_op jit(solution)/shard_map/all_to_all | solution.py:94
  144.5 0.3 copy.105
  144.7 1.6 gather_fusion
  146.7 1.0 broadcast_in_dim.103
  147.8 11.9 %all-to-all-start.1 = ((f32[128,2,560]{2,1,0:T(2,128)}), f32[128,2,560]{2,1,0:T(2,128)}, u32[]{:S(2)}, u32[]{:S(2)}) async-start(f32[128,2,560]{2,1,0:T(2,128)} %broadcast_in_dim.103), calls=%async_computation.1 | async-start | bytes 1310720 | tf_op jit(solution)/shard_map/all_to_all | solution.py:128
  159.7 0.6 iota_compare_fusion.4
  160.4 3.5 %constant_dynamic-slice_fusion.3 = (bf16[2,1,256,8,69]{4,3,2,1,0:T(8,128)(2,1)S(1)}, bf16[2,1,256,8,69]{4,3,2,1,0:T(8,128)(2,1)S(1)}, bf16[2,1,256,8,69]{4,3,2,1,0:T(8,128)(2,1)S(1)}, bf16[2,1,256,8,69]{4,3,2,1,0:T(8,128)(2,1)}) fusion(bf16[2,4,256,8,69]{4,3,2,1,0:T(8,128)(2,1)} %bitcast.112, s32[]{:T(128)S(6)} %select_n.86, s32[]{:T(128)S(6)} %select_n.90, ...), kind=kLoop, calls=%fused_computation.113 | loop fusion | bytes 4522000 | tf_op jit(solution)/shard_map/jit(dynamic_index_in_dim)/dynamic_slice | solution.py:96
  163.9 2.7 %copy.110 = bf16[2,1,256,8,69]{2,3,4,1,0:T(8,128)(2,1)} copy(bf16[2,1,256,8,69]{4,3,2,1,0:T(8,128)(2,1)} %get-tuple-element.12) | data formatting | bytes 1130496
  166.6 1.1 collective-permute-start.4
  167.7 1.6 copy.108
  169.3 0.6 collective-permute-start.2
  169.9 0.9 copy.109
  170.9 1.5 collective-permute-start.3
  172.4 0.9 copy.107
  173.3 0.5 all-to-all-done.1
  173.8 1.5 reshape.166
  175.3 0.4 fusion.75
  176.0 2.8 %gather_fusion.1 = f32[1024,2]{1,0:T(8,128)S(1)} fusion(f32[2,560]{0,1:T(8,128)S(1)} %copy.89, s32[1024]{0:T(1024)S(1)} %broadcast_clamp_fusion), kind=kCustom, calls=%fused_computation.1 | custom fusion | bytes 20480 | tf_op jit(solution)/shard_map/gather | solution.py:138
  178.8 0.3 copy.106
  179.1 0.8 multiply_reduce_fusion
  179.9 0.2 fusion.43
  183.6 0.7 gather_fusion.2
  184.4 9.9 %collective-permute-done.3 = bf16[2,256,8,69]{1,2,3,0:T(8,128)(2,1)} collective-permute-done((bf16[2,256,8,69]{1,2,3,0:T(8,128)(2,1)S(1)}, bf16[2,256,8,69]{1,2,3,0:T(8,128)(2,1)}, u32[]{:S(2)}, u32[]{:S(2)}) %collective-permute-start.3) | collective-permute-done | bytes 565280 | tf_op jit(solution)/shard_map/ppermute | solution.py:100
  194.3 7.7 %fusion.29 = f32[32,69,2,256]{3,0,1,2:T(8,128)S(1)} fusion(pred[2,2]{0,1:T(4,128)(4,1)} %iota_compare_fusion.4, f32[2,4,8,32]{3,0,2,1:T(2,128)S(1)} %bitcast.123, pred[4,8]{1,0:T(4,128)(4,1)} %compare_and_fusion, bf16[1,2,256,8,69]{2,3,4,1,0:T(8,128)(2,1)} %bitcast.10, bf16[1,2,256,8,69]{2,3,4,1,0:T(8,128)(2,1)} %bitcast.8, ...), kind=kOutput, calls=%fused_computation.37 | convolution fusion | flops 875005952 | bytes 6791204 | tf_op jit(solution)/shard_map/ajnm,jailnc->mcil/dot_general | solution.py:172
  202.0 5.6 %copy.93 = f32[32,69,2,256]{3,2,1,0:T(2,128)} copy(f32[32,69,2,256]{3,0,1,2:T(8,128)S(1)} %fusion.29) | data formatting | bytes 9043968 | tf_op jit(solution)/shard_map/ajnm,jailnc->mcil/transpose | solution.py:172
  (78 shorter events, 4.5 us)
Async XLA Ops:
  0.0 68.0 %copy-start = (bf16[3,3,256,69]{2,3,1,0:T(8,128)(2,1)S(1)}, bf16[3,3,256,69]{2,3,1,0:T(8,128)(2,1)}, u32[]{:S(2)}) copy-start(bf16[3,3,256,69]{2,3,1,0:T(8,128)(2,1)} %param.15) | copy-start | bytes 953860
  0.0 22.6 %copy-start.10 = (s32[528]{0:T(1024)S(1)}, s32[528]{0:T(1024)}, u32[]{:S(2)}) copy-start(s32[528]{0:T(1024)} %constant.160) | copy-start | bytes 6340
  0.0 16.7 %copy-start.11 = (s32[2,256]{1,0:T(2,128)S(1)}, s32[2,256]{1,0:T(2,128)}, u32[]{:S(2)}) copy-start(s32[2,256]{1,0:T(2,128)} %param.19) | copy-start | bytes 6148
  2.4 52.2 %collective-permute-start = (bf16[2,1024,8,69]{1,2,3,0:T(8,128)(2,1)S(1)}, bf16[2,1024,8,69]{1,2,3,0:T(8,128)(2,1)}, u32[]{:S(2)}, u32[]{:S(2)}) collective-permute-start(bf16[2,1024,8,69]{1,2,3,0:T(8,128)(2,1)S(1)} %bitcast.114), channel_id=1, source_target_pairs={{0,1},{1,2},{2,3},{3,4},{4,5},{5,6},{6,7},{7,8},{8,9},{9,10},{10,1... | collective-permute-start | bytes 6782984 | tf_op jit(solution)/shard_map/ppermute | solution.py:22
  8.2 53.2 %collective-permute-start.1 = (bf16[2,1024,8,69]{1,2,3,0:T(8,128)(2,1)S(1)}, bf16[2,1024,8,69]{1,2,3,0:T(8,128)(2,1)}, u32[]{:S(2)}, u32[]{:S(2)}) collective-permute-start(bf16[2,1024,8,69]{1,2,3,0:T(8,128)(2,1)S(1)} %bitcast.115), channel_id=1, source_target_pairs={{1,0},{2,1},{3,2},{4,3},{5,4},{6,5},{7,6},{8,7},{9,8},{10,9},{11,1... | collective-permute-start | bytes 6782984 | tf_op jit(solution)/shard_map/ppermute | solution.py:24
  16.5 51.5 %copy-start.17 = (f32[256]{0:T(256)S(1)}, f32[256]{0:T(256)}, u32[]{:S(2)}) copy-start(f32[256]{0:T(256)} %param.16) | copy-start | bytes 3076
  68.0 40.6 %copy-start.2 = (bf16[8,69,2,1024]{1,0,3,2:T(8,128)(2,1)S(1)}, bf16[8,69,2,1024]{1,0,3,2:T(8,128)(2,1)}, u32[]{:S(2)}) copy-start(bf16[8,69,2,1024]{1,0,3,2:T(8,128)(2,1)} %copy.75) | copy-start | bytes 6782980
  68.0 40.6 %copy-start.16 = (bf16[3,3,69,256]{3,2,1,0:T(8,128)(2,1)S(1)}, bf16[3,3,69,256]{3,2,1,0:T(8,128)(2,1)}, u32[]{:S(2)}) copy-start(bf16[3,3,69,256]{3,2,1,0:T(8,128)(2,1)} %param.17) | copy-start | bytes 953860
  68.1 40.6 %copy-start.18 = (f32[69]{0:T(128)S(1)}, f32[69]{0:T(128)}, u32[]{:S(2)}) copy-start(f32[69]{0:T(128)} %param.18) | copy-start | bytes 832
  108.6 25.0 %copy-start.4 = (f32[4,2,69,256]{3,2,1,0:T(8,128)S(1)}, f32[4,2,69,256]{3,2,1,0:T(8,128)}, u32[]{:S(2)}) copy-start(f32[4,2,69,256]{3,2,1,0:T(8,128)} %fusion.45) | copy-start | bytes 1695748
  108.6 25.0 %copy-start.8 = (s32[4,2,256]{2,1,0:T(2,128)S(1)}, s32[4,2,256]{2,1,0:T(2,128)}, u32[]{:S(2)}) copy-start(s32[4,2,256]{2,1,0:T(2,128)} %get-tuple-element.13) | copy-start | bytes 24580
  131.6 2.0 copy-start.1
  131.6 9.4 %copy-start.15 = (s32[32]{0:T(128)S(1)}, s32[32]{0:T(128)}, u32[]{:S(2)}) copy-start(s32[32]{0:T(128)} %fusion.69) | copy-start | bytes 388
  131.6 12.6 %copy-start.7 = (f32[2,256]{1,0:T(2,128)S(1)}, f32[2,256]{1,0:T(2,128)}, u32[]{:S(2)}) copy-start(f32[2,256]{1,0:T(2,128)} %param.21) | copy-start | bytes 6148
  131.6 12.6 %copy-start.12 = (f32[2,256]{1,0:T(2,128)S(1)}, f32[2,256]{1,0:T(2,128)}, u32[]{:S(2)}) copy-start(f32[2,256]{1,0:T(2,128)} %param.20) | copy-start | bytes 6148
  131.6 13.1 %copy-start.6 = (s32[1024]{0:T(1024)S(1)}, s32[1024]{0:T(1024)}, u32[]{:S(2)}) copy-start(s32[1024]{0:T(1024)} %pad_clamp_fusion.1) | copy-start | bytes 12292
  131.6 28.6 %copy-start.13 = (f32[2,8]{1,0:T(2,128)S(1)}, f32[2,8]{1,0:T(2,128)}, u32[]{:S(2)}) copy-start(f32[2,8]{1,0:T(2,128)} %param.23) | copy-start | bytes 196
  131.7 28.6 %copy-start.14 = (s32[2,8]{1,0:T(2,128)S(1)}, s32[2,8]{1,0:T(2,128)}, u32[]{:S(2)}) copy-start(s32[2,8]{1,0:T(2,128)} %param.22) | copy-start | bytes 196
  131.7 28.7 %copy-start.9 = (s32[1024]{0:T(1024)S(1)}, s32[1024]{0:T(1024)}, u32[]{:S(2)}) copy-start(s32[1024]{0:T(1024)} %constant.161) | copy-start | bytes 12292
  136.2 8.1 %all-to-all-start = ((f32[4,2,8,256]{3,2,1,0:T(8,128)}), f32[4,2,8,256]{3,2,1,0:T(8,128)S(1)}, u32[]{:S(2)}, u32[]{:S(2)}) async-start(f32[4,2,8,256]{3,2,1,0:T(8,128)} %fusion.21), calls=%async_computation | async-start | bytes 131072 | tf_op jit(solution)/shard_map/all_to_all | solution.py:94
  147.8 26.0 %all-to-all-start.1 = ((f32[128,2,560]{2,1,0:T(2,128)}), f32[128,2,560]{2,1,0:T(2,128)}, u32[]{:S(2)}, u32[]{:S(2)}) async-start(f32[128,2,560]{2,1,0:T(2,128)} %broadcast_in_dim.103), calls=%async_computation.1 | async-start | bytes 1310720 | tf_op jit(solution)/shard_map/all_to_all | solution.py:128
  160.4 19.6 %copy-start.3 = (f32[32,32]{1,0:T(8,128)S(1)}, f32[32,32]{1,0:T(8,128)}, u32[]{:S(2)}) copy-start(f32[32,32]{1,0:T(8,128)} %fusion.62) | copy-start | bytes 12292
  160.4 19.5 %copy-start.5 = (f32[32,32]{1,0:T(8,128)S(1)}, f32[32,32]{1,0:T(8,128)}, u32[]{:S(2)}) copy-start(f32[32,32]{1,0:T(8,128)} %fusion.61) | copy-start | bytes 12292
  166.6 17.8 %collective-permute-start.4 = (bf16[2,256,8,69]{1,2,3,0:T(8,128)(2,1)}, bf16[2,256,8,69]{1,2,3,0:T(8,128)(2,1)}, u32[]{:S(2)}, u32[]{:S(2)}) collective-permute-start(bf16[2,256,8,69]{1,2,3,0:T(8,128)(2,1)} %bitcast.117), channel_id=1, source_target_pairs={{0,96},{32,0},{64,32},{96,64},{1,97},{33,1},{65,33},{97,65},{2,98}... | collective-permute-start | bytes 1695752 | tf_op jit(solution)/shard_map/ppermute | solution.py:100
  169.3 15.0 %collective-permute-start.2 = (bf16[2,256,8,69]{1,2,3,0:T(8,128)(2,1)}, bf16[2,256,8,69]{1,2,3,0:T(8,128)(2,1)}, u32[]{:S(2)}, u32[]{:S(2)}) collective-permute-start(bf16[2,256,8,69]{1,2,3,0:T(8,128)(2,1)} %bitcast.119), channel_id=1, source_target_pairs={{0,32},{32,64},{64,96},{96,0},{1,33},{33,65},{65,97},{97,1},{2,34}... | collective-permute-start | bytes 1695752 | tf_op jit(solution)/shard_map/ppermute | solution.py:100
  170.9 23.4 %collective-permute-start.3 = (bf16[2,256,8,69]{1,2,3,0:T(8,128)(2,1)S(1)}, bf16[2,256,8,69]{1,2,3,0:T(8,128)(2,1)}, u32[]{:S(2)}, u32[]{:S(2)}) collective-permute-start(bf16[2,256,8,69]{1,2,3,0:T(8,128)(2,1)S(1)} %bitcast.120), channel_id=1, source_target_pairs={{0,64},{32,96},{64,0},{96,32},{1,65},{33,97},{65,1},{97,33},{2,66}... | collective-permute-start | bytes 1695752 | tf_op jit(solution)/shard_map/ppermute | solution.py:100

commit v11 on v10

--- a/solution.py
+++ b/solution.py
@@ -75,6 +75,17 @@
         quarters = lax.psum(1, GRP)
         patch_width = forecast.shape[1] // quarters
         blocks = forecast.reshape(height, quarters, patch_width, ensemble_part, channels)
+        me = lax.axis_index(GRP)
+        outgoing = [
+            lax.dynamic_index_in_dim(blocks, (me + step) % quarters, axis=1, keepdims=False)
+            for step in range(quarters)
+        ]
+        outgoing, blocks = lax.optimization_barrier((outgoing, blocks))
+        pieces = [outgoing[0]] + [
+            lax.ppermute(outgoing[step], GRP, [(j, (j + step) % quarters) for j in range(quarters)])
+            for step in range(1, quarters)
+        ]
+        patch_block_slice = jnp.stack(pieces, axis=0)
         row_index = lax.all_gather(obs_index, GRP, axis=0, tiled=False)
         column = row_index % patch_width
         channel = row_index // patch_width
@@ -91,15 +102,20 @@
             channel[:, :, None, :] == jnp.arange(channels, dtype=jnp.int32)[None, None, :, None]
         ).astype(jnp.float32)
         own_members = jnp.sum(by_column * channel_hot[:, :, :, None, :], axis=2)
-        predicted = lax.all_to_all(own_members, GRP, split_axis=0, concat_axis=2, tiled=True)[0]
-        me = lax.axis_index(GRP)
-        pieces = [lax.dynamic_index_in_dim(blocks, me, axis=1, keepdims=False)]
-        for step in range(1, quarters):
-            outgoing = lax.dynamic_index_in_dim(blocks, (me + step) % quarters, axis=1, keepdims=False)
-            pieces.append(
-                lax.ppermute(outgoing, GRP, [(j, (j + step) % quarters) for j in range(quarters)])
+        got = [lax.dynamic_index_in_dim(own_members, me, axis=0, keepdims=False)] + [
+            lax.ppermute(
+                lax.dynamic_index_in_dim(own_members, (me + step) % quarters, axis=0, keepdims=False),
+                GRP,
+                [(j, (j + step) % quarters) for j in range(quarters)],
             )
-        patch_block_slice = jnp.stack(pieces, axis=0)
+            for step in range(1, quarters)
+        ]
+        member_ids = jnp.arange(quarters * ensemble_part, dtype=jnp.int32)
+        in_order = (
+            (me - member_ids // ensemble_part) % quarters * ensemble_part
+            + member_ids % ensemble_part
+        )
+        predicted = jnp.take(jnp.concatenate(got, axis=1), in_order, axis=1)
         ensemble = quarters * ensemble_part
         source_member = (
             ((me - jnp.arange(quarters, dtype=jnp.int32)) % quarters)[:, None] * ensemble_part

time: 209 us -> 215 us (1.029)
  waiting for transfers between devices: 39.9 us -> 49.9 us
  starting transfers between devices: 27 us -> 24.4 us
    all_to_all x1, waiting for transfers between devices: 0.48 us -> 11 us  [on_device(): lax.all_to_all(jnp.broadcast_to(packed[None], (devices,) + packed.shape),...]
    all_to_all x1 -> x0, starting transfers between devices: 4.79 us -> none  [on_device(): lax.all_to_all(own_members, GRP, split_axis=0, concat_axis=2, tiled=True)[0]]
    ppermute x3 -> x6, starting transfers between devices: 3.21 us -> 6.57 us  [the longest x3 3.35 us: on_device(): lax.ppermute(lax.dynamic_index_in_dim(own_members, (me + step) % quarters...]
    ppermute x3 -> x6, waiting for transfers between devices: 9.93 us -> 12.8 us  [the longest x3 9.9 us: on_device(): lax.ppermute(outgoing[step], GRP, [(j, (j + step) % quarters) for j in ra...]
    all_to_all x1 -> x0, waiting for transfers between devices: 2.68 us -> none  [on_device(): lax.all_to_all(own_members, GRP, split_axis=0, concat_axis=2, tiled=True)[0]]
    unnamed x43 -> x49, local copies, waits for them, and re-layouts: 15.3 us -> 17.4 us
  transfers between devices with their start and end apart: 7 -> 9, of which waited for: 4 -> 6; matrix products, arithmetic and copies ran while one was open for 19% -> 13% of each run, Pallas kernels for 0% -> 0%
where the time goes in v11:
time: 215 us
  matrix products  78.5 us (37%)
  waiting for transfers between devices  49.9 us (23%)
  local copies, waits for them, and re-layouts  49.2 us (23%)
  starting transfers between devices  24.4 us (11%)
  other arithmetic  6.28 us (3%)
  blocking collectives  5.9 us (3%)
    conv_general_dilated x2, matrix products, convolve(): lax.conv_general_dilated(wrapped, kernel, window_strides=(1, 1), padding=...  62.8 us
    ppermute x1, waiting for transfers between devices, padded_2(): lax.ppermute(cells, BAND, shift_pairs(band_size, 1))  26.1 us
    unnamed x49, local copies, waits for them, and re-layouts  17.4 us
    all_to_all x1, waiting for transfers between devices, on_device(): lax.all_to_all(jnp.broadcast_to(packed[None], (devices,) + packed.shape),...  11 us
    all_to_all x1, starting transfers between devices, on_device(): lax.all_to_all(jnp.broadcast_to(packed[None], (devices,) + packed.shape),...  10.8 us
    ppermute x3, waiting for transfers between devices, on_device(): lax.ppermute(outgoing[step], GRP, [(j, (j + step) % quarters) for j in ra...  9.9 us
    dot_general x1, matrix products, on_device(): jnp.einsum('ajnm,jailnc->mcil', weights, spread_out, precision=highest)  7.66 us
    ppermute x1, local copies, waits for them, and re-layouts, padded_2(): lax.ppermute(cells, BAND, shift_pairs(band_size, 1))  6.77 us
  transfers between devices with their start and end apart: 9, of which 6 were waited for; matrix products, arithmetic and copies ran while one was open for 13% of the time, Pallas kernels for 0%

profile of v11, /device:TPU:1, one launch (start us, length us, event | category | flops | bytes accessed | tf_op | source)
XLA Modules:
  0.0 214.6 jit_solution(3346631500443040955)
XLA Ops:
  0.0 2.4 %copy.129 = bf16[8,69,2,1024]{3,0,1,2:T(8,128)(2,1)S(1)} copy(bf16[8,69,2,1024]{3,2,1,0:T(2,128)(2,1)} %param.14) | data formatting | bytes 4521984 | tf_op jit(solution)/transpose | solution.py:224
  2.4 5.8 %collective-permute-start = (bf16[2,1024,8,69]{1,2,3,0:T(8,128)(2,1)S(1)}, bf16[2,1024,8,69]{1,2,3,0:T(8,128)(2,1)}, u32[]{:S(2)}, u32[]{:S(2)}) collective-permute-start(bf16[2,1024,8,69]{1,2,3,0:T(8,128)(2,1)S(1)} %bitcast.122), channel_id=1, source_target_pairs={{0,1},{1,2},{2,3},{3,4},{4,5},{5,6},{6,7},{7,8},{8,9},{9,10},{10,1... | collective-permute-start | bytes 6782984 | tf_op jit(solution)/shard_map/ppermute | solution.py:22
  8.2 1.3 collective-permute-start.1
  9.5 7.1 %copy.64 = bf16[8,69,2,1024]{1,0,3,2:T(8,128)(2,1)} copy(bf16[8,69,2,1024]{3,2,1,0:T(2,128)(2,1)} %param.14) | data formatting | bytes 4521984 | tf_op args[0]
  16.6 0.5 copy-done.17
  17.3 5.9 %all-gather.1 = s32[4,2,256]{2,1,0:T(2,128)S(1)} all-gather(s32[1,2,256]{2,1,0:T(2,128)S(1)} %bitcast.138), channel_id=2, replica_groups=mesh['y_lo'=2,'core'=2,'y_hi'=2,'x'=4,'z'=4] {'y_lo','core'}, dimensions={0}, use_global_device_ids=true | all-gather | bytes 10240 | tf_op jit(solution)/shard_map/all_gather | solution.py:89
  23.3 0.6 pad_clamp_fusion.2
  23.9 0.6 pad_clamp_fusion.1
  24.4 0.6 pad_clamp_fusion
  25.0 0.6 fusion.60
  25.7 0.6 fusion.59
  26.3 0.6 fusion.58
  26.9 0.6 and_select_fusion.1
  27.5 0.9 fusion.45
  28.4 26.1 %collective-permute-done = bf16[2,1024,8,69]{1,2,3,0:T(8,128)(2,1)} collective-permute-done((bf16[2,1024,8,69]{1,2,3,0:T(8,128)(2,1)S(1)}, bf16[2,1024,8,69]{1,2,3,0:T(8,128)(2,1)}, u32[]{:S(2)}, u32[]{:S(2)}) %collective-permute-start) | collective-permute-done | bytes 2261024 | tf_op jit(solution)/shard_map/ppermute | solution.py:22
  54.6 6.8 %copy.67 = bf16[2,1024,8,69]{3,2,1,0:T(8,128)(2,1)} copy(bf16[2,1024,8,69]{1,2,3,0:T(8,128)(2,1)} %collective-permute-done) | data formatting | bytes 4521984 | tf_op jit(solution)/shard_map/ppermute | solution.py:22
  61.3 6.7 %copy.68 = bf16[2,1024,8,69]{3,2,1,0:T(8,128)(2,1)} copy(bf16[2,1024,8,69]{1,2,3,0:T(8,128)(2,1)} %collective-permute-done.1) | data formatting | bytes 4521984 | tf_op jit(solution)/shard_map/ppermute | solution.py:24
  68.1 39.8 %fusion.6 = bf16[4,1024,8,256]{3,2,1,0:T(8,128)(2,1)} fusion(f32[256]{0:T(256)S(1)} %copy-done.20, pred[4]{0:T(512)(128)(4,1)S(1)} %and_or_fusion, bf16[3,3,256,69]{2,3,1,0:T(8,128)(2,1)S(1)} %copy-done, bf16[2,1024,8,69]{3,2,1,0:T(8,128)(2,1)} %copy.68, bf16[2,1024,8,69]{3,2,1,0:T(8,128)(2,1)} %bitcast.121, bf16[2,1024,8,69]{3,2,1,0:T(8,128)(2,1)} %copy.67), kind=kOutput, calls=%fused_computation.11 | convolution fusion | flops 10504556544 | bytes 23879172 | tf_op jit(solution)/shard_map/conv_general_dilated | solution.py:32
  107.9 0.7 fusion.80
  108.7 22.9 %add_convert_fusion = bf16[2,1024,8,69]{3,2,1,0:T(8,128)(2,1)S(1)} fusion(f32[69]{0:T(128)S(1)} %copy-done.21, bf16[3,3,69,256]{3,2,1,0:T(8,128)(2,1)S(1)} %copy-done.19, bf16[4,1,8,256]{3,2,1,0:T(8,128)(2,1)S(1)} %get-tuple-element.20, bf16[4,1024,8,256]{3,2,1,0:T(8,128)(2,1)} %fusion.6, bf16[4,1,8,256]{3,2,1,0:T(8,128)(2,1)S(1)} %get-tuple-element.19, ...), kind=kOutput, calls=%fused_computation.28 | convolution fusion | flops 5230657536 | bytes 21650196 | tf_op jit(solution)/shard_map/conv_general_dilated | solution.py:32
  131.6 2.0 copy-done.1
  133.6 1.3 constant_dynamic-slice_fusion.4
  134.9 2.7 %copy.101 = bf16[2,1,256,8,69]{2,3,4,1,0:T(8,128)(2,1)} copy(bf16[2,1,256,8,69]{4,3,2,1,0:T(8,128)(2,1)} %get-tuple-element.24) | data formatting | bytes 1130496
  137.7 1.6 copy.102
  139.3 1.6 copy.103
  141.0 1.6 copy.104
  142.6 4.0 %fusion.21 = f32[4,2,8,256]{3,2,1,0:T(8,128)S(1)} fusion(f32[4,2,69,256]{3,2,1,0:T(8,128)} %fusion.45, bf16[2,4,256,8,69]{4,3,2,1,0:T(8,128)(2,1)} %bitcast.120, s32[4,2,256]{2,1,0:T(2,128)S(1)} %copy-done.10), kind=kOutput, calls=%fused_computation.30 | convolution fusion | flops 581582848 | bytes 2899968 | tf_op jit(solution)/shard_map/iqlmc,qiol->qicmo/dot_general | solution.py:95
  146.7 2.8 %collective-permute-start.5 = (f32[2,8,256]{2,0,1:T(2,128)S(1)}, f32[2,8,256]{2,0,1:T(2,128)S(1)}, u32[]{:S(2)}, u32[]{:S(2)}) collective-permute-start(f32[2,8,256]{2,0,1:T(2,128)S(1)} %bitcast.131), channel_id=1, source_target_pairs={{0,32},{32,64},{64,96},{96,0},{1,33},{33,65},{65,97},{97,1},{2,34}... | collective-permute-start | bytes 49160 | tf_op jit(solution)/shard_map/ppermute | solution.py:106
  149.8 0.3 collective-permute-start.7
  150.4 1.8 collective-permute-done.6
  152.2 0.8 collective-permute-done.7
  153.0 0.8 gather_fusion
  154.2 0.3 copy.99
  154.5 1.6 gather_fusion.1
  156.5 1.0 broadcast_in_dim.115
  157.5 10.8 %all-to-all-start = ((f32[128,2,560]{2,1,0:T(2,128)}), f32[128,2,560]{2,1,0:T(2,128)S(1)}, u32[]{:S(2)}, u32[]{:S(2)}) async-start(f32[128,2,560]{2,1,0:T(2,128)} %broadcast_in_dim.115), calls=%async_computation | async-start | bytes 1310720 | tf_op jit(solution)/shard_map/all_to_all | solution.py:144
  168.5 1.5 collective-permute-start.3
  170.0 0.6 collective-permute-start.4
  170.6 1.1 collective-permute-start.2
  171.7 11.0 %all-to-all-done = f32[128,2,560]{2,1,0:T(2,128)S(1)} async-done(((f32[128,2,560]{2,1,0:T(2,128)}), f32[128,2,560]{2,1,0:T(2,128)S(1)}, u32[]{:S(2)}, u32[]{:S(2)}) %all-to-all-start) | async-done | bytes 573472 | tf_op jit(solution)/shard_map/all_to_all | solution.py:144
  182.7 0.5 reshape.269
  183.2 0.4 fusion.81
  183.8 2.8 %gather_fusion.2 = f32[1024,2]{1,0:T(8,128)S(1)} fusion(f32[2,560]{0,1:T(8,128)S(1)} %copy.83, s32[1024]{0:T(1024)S(1)} %broadcast_clamp_fusion), kind=kCustom, calls=%fused_computation.2 | custom fusion | bytes 20480 | tf_op jit(solution)/shard_map/gather | solution.py:154
  186.6 0.3 copy.100
  190.7 0.7 gather_fusion.3
  191.5 9.9 %collective-permute-done.4 = bf16[2,256,8,69]{1,2,3,0:T(8,128)(2,1)} collective-permute-done((bf16[2,256,8,69]{1,2,3,0:T(8,128)(2,1)}, bf16[2,256,8,69]{1,2,3,0:T(8,128)(2,1)}, u32[]{:S(2)}, u32[]{:S(2)}) %collective-permute-start.4) | collective-permute-done | bytes 565280 | tf_op jit(solution)/shard_map/ppermute | solution.py:85
  201.4 7.7 %fusion.29 = f32[32,69,2,256]{3,0,1,2:T(8,128)S(1)} fusion(pred[2,2]{0,1:T(4,128)(4,1)S(1)} %iota_compare_fusion.4, f32[2,4,8,32]{3,0,2,1:T(2,128)S(1)} %bitcast.130, pred[4,8]{1,0:T(4,128)(4,1)S(1)} %compare_and_fusion.1, bf16[1,2,256,8,69]{2,3,4,1,0:T(8,128)(2,1)} %bitcast.11, bf16[1,2,256,8,69]{2,3,4,1,0:T(8,128)(2,1)} %bitcast.10, ...), kind=kOutput, calls=%fused_computation.38 | convolution fusion | flops 875005952 | bytes 6791204 | tf_op jit(solution)/shard_map/ajnm,jailnc->mcil/dot_general | solution.py:188
  209.0 5.6 %copy.87 = f32[32,69,2,256]{3,2,1,0:T(2,128)} copy(f32[32,69,2,256]{3,0,1,2:T(8,128)S(1)} %fusion.29) | data formatting | bytes 9043968 | tf_op jit(solution)/shard_map/ajnm,jailnc->mcil/transpose | solution.py:188
  (99 shorter events, 5.7 us)
Async XLA Ops:
  0.0 68.0 %copy-start = (bf16[3,3,256,69]{2,3,1,0:T(8,128)(2,1)S(1)}, bf16[3,3,256,69]{2,3,1,0:T(8,128)(2,1)}, u32[]{:S(2)}) copy-start(bf16[3,3,256,69]{2,3,1,0:T(8,128)(2,1)} %param.15) | copy-start | bytes 953860
  0.0 23.8 %copy-start.12 = (s32[528]{0:T(1024)S(1)}, s32[528]{0:T(1024)}, u32[]{:S(2)}) copy-start(s32[528]{0:T(1024)} %constant.231) | copy-start | bytes 6340
  0.0 17.3 %copy-start.13 = (s32[2,256]{1,0:T(2,128)S(1)}, s32[2,256]{1,0:T(2,128)}, u32[]{:S(2)}) copy-start(s32[2,256]{1,0:T(2,128)} %param.19) | copy-start | bytes 6148
  2.4 52.2 %collective-permute-start = (bf16[2,1024,8,69]{1,2,3,0:T(8,128)(2,1)S(1)}, bf16[2,1024,8,69]{1,2,3,0:T(8,128)(2,1)}, u32[]{:S(2)}, u32[]{:S(2)}) collective-permute-start(bf16[2,1024,8,69]{1,2,3,0:T(8,128)(2,1)S(1)} %bitcast.122), channel_id=1, source_target_pairs={{0,1},{1,2},{2,3},{3,4},{4,5},{5,6},{6,7},{7,8},{8,9},{9,10},{10,1... | collective-permute-start | bytes 6782984 | tf_op jit(solution)/shard_map/ppermute | solution.py:22
  8.2 53.2 %collective-permute-start.1 = (bf16[2,1024,8,69]{1,2,3,0:T(8,128)(2,1)S(1)}, bf16[2,1024,8,69]{1,2,3,0:T(8,128)(2,1)}, u32[]{:S(2)}, u32[]{:S(2)}) collective-permute-start(bf16[2,1024,8,69]{1,2,3,0:T(8,128)(2,1)S(1)} %bitcast.123), channel_id=1, source_target_pairs={{1,0},{2,1},{3,2},{4,3},{5,4},{6,5},{7,6},{8,7},{9,8},{10,9},{11,1... | collective-permute-start | bytes 6782984 | tf_op jit(solution)/shard_map/ppermute | solution.py:24
  16.6 51.4 %copy-start.20 = (f32[256]{0:T(256)S(1)}, f32[256]{0:T(256)}, u32[]{:S(2)}) copy-start(f32[256]{0:T(256)} %param.16) | copy-start | bytes 3076
  16.6 0.5 copy-start.17
  68.0 40.6 %copy-start.2 = (bf16[8,69,2,1024]{1,0,3,2:T(8,128)(2,1)S(1)}, bf16[8,69,2,1024]{1,0,3,2:T(8,128)(2,1)}, u32[]{:S(2)}) copy-start(bf16[8,69,2,1024]{1,0,3,2:T(8,128)(2,1)} %copy.64) | copy-start | bytes 6782980
  68.1 40.6 %copy-start.19 = (bf16[3,3,69,256]{3,2,1,0:T(8,128)(2,1)S(1)}, bf16[3,3,69,256]{3,2,1,0:T(8,128)(2,1)}, u32[]{:S(2)}) copy-start(bf16[3,3,69,256]{3,2,1,0:T(8,128)(2,1)} %param.17) | copy-start | bytes 953860
  68.1 40.6 %copy-start.21 = (f32[69]{0:T(128)S(1)}, f32[69]{0:T(128)}, u32[]{:S(2)}) copy-start(f32[69]{0:T(128)} %param.18) | copy-start | bytes 832
  131.6 2.0 copy-start.1
  131.6 11.0 %copy-start.10 = (s32[4,2,256]{2,1,0:T(2,128)S(1)}, s32[4,2,256]{2,1,0:T(2,128)}, u32[]{:S(2)}) copy-start(s32[4,2,256]{2,1,0:T(2,128)} %get-tuple-element.29) | copy-start | bytes 24580
  134.9 19.0 %copy-start.9 = (f32[2,256]{1,0:T(2,128)S(1)}, f32[2,256]{1,0:T(2,128)}, u32[]{:S(2)}) copy-start(f32[2,256]{1,0:T(2,128)} %param.21) | copy-start | bytes 6148
  134.9 19.0 %copy-start.14 = (f32[2,256]{1,0:T(2,128)S(1)}, f32[2,256]{1,0:T(2,128)}, u32[]{:S(2)}) copy-start(f32[2,256]{1,0:T(2,128)} %param.20) | copy-start | bytes 6148
  134.9 19.6 %copy-start.8 = (s32[1024]{0:T(1024)S(1)}, s32[1024]{0:T(1024)}, u32[]{:S(2)}) copy-start(s32[1024]{0:T(1024)} %pad_clamp_fusion.1) | copy-start | bytes 12292
  137.7 30.7 %copy-start.15 = (f32[2,8]{1,0:T(2,128)S(1)}, f32[2,8]{1,0:T(2,128)}, u32[]{:S(2)}) copy-start(f32[2,8]{1,0:T(2,128)} %param.23) | copy-start | bytes 196
  137.7 30.7 %copy-start.16 = (s32[2,8]{1,0:T(2,128)S(1)}, s32[2,8]{1,0:T(2,128)}, u32[]{:S(2)}) copy-start(s32[2,8]{1,0:T(2,128)} %param.22) | copy-start | bytes 196
  137.7 30.8 %copy-start.18 = (s32[4]{0:T(128)S(1)}, s32[4]{0:T(128)}, u32[]{:S(2)}) copy-start(s32[4]{0:T(128)} %copy-done.17) | copy-start | bytes 52
  137.7 30.8 %copy-start.11 = (s32[1024]{0:T(1024)S(1)}, s32[1024]{0:T(1024)}, u32[]{:S(2)}) copy-start(s32[1024]{0:T(1024)} %constant.232) | copy-start | bytes 12292
  139.3 31.3 %copy-start.5 = (bf16[2,1,256,8,69]{2,3,4,1,0:T(8,128)(2,1)S(1)}, bf16[2,1,256,8,69]{2,3,4,1,0:T(8,128)(2,1)}, u32[]{:S(2)}) copy-start(bf16[2,1,256,8,69]{2,3,4,1,0:T(8,128)(2,1)} %copy.102) | copy-start | bytes 1695748
  141.0 45.9 %copy-start.7 = (f32[32,32]{1,0:T(8,128)S(1)}, f32[32,32]{1,0:T(8,128)}, u32[]{:S(2)}) copy-start(f32[32,32]{1,0:T(8,128)} %fusion.60) | copy-start | bytes 12292
  141.0 46.1 %copy-start.3 = (f32[32,32]{1,0:T(8,128)S(1)}, f32[32,32]{1,0:T(8,128)}, u32[]{:S(2)}) copy-start(f32[32,32]{1,0:T(8,128)} %fusion.59) | copy-start | bytes 12292
  141.0 46.1 %copy-start.6 = (f32[32,32]{1,0:T(8,128)S(1)}, f32[32,32]{1,0:T(8,128)}, u32[]{:S(2)}) copy-start(f32[32,32]{1,0:T(8,128)} %fusion.58) | copy-start | bytes 12292
  142.6 58.8 %copy-start.4 = (bf16[2,1,256,8,69]{2,3,4,1,0:T(8,128)(2,1)S(1)}, bf16[2,1,256,8,69]{2,3,4,1,0:T(8,128)(2,1)}, u32[]{:S(2)}) copy-start(bf16[2,1,256,8,69]{2,3,4,1,0:T(8,128)(2,1)} %copy.101) | copy-start | bytes 1695748
  146.7 3.7 %collective-permute-start.5 = (f32[2,8,256]{2,0,1:T(2,128)S(1)}, f32[2,8,256]{2,0,1:T(2,128)S(1)}, u32[]{:S(2)}, u32[]{:S(2)}) collective-permute-start(f32[2,8,256]{2,0,1:T(2,128)S(1)} %bitcast.131), channel_id=1, source_target_pairs={{0,32},{32,64},{64,96},{96,0},{1,33},{33,65},{65,97},{97,1},{2,34}... | collective-permute-start | bytes 49160 | tf_op jit(solution)/shard_map/ppermute | solution.py:106
  149.5 2.7 %collective-permute-start.6 = (f32[2,8,256]{2,0,1:T(2,128)S(1)}, f32[2,8,256]{2,0,1:T(2,128)S(1)}, u32[]{:S(2)}, u32[]{:S(2)}) collective-permute-start(f32[2,8,256]{2,0,1:T(2,128)S(1)} %bitcast.132), channel_id=1, source_target_pairs={{0,64},{32,96},{64,0},{96,32},{1,65},{33,97},{65,1},{97,33},{2,66}... | collective-permute-start | bytes 49160 | tf_op jit(solution)/shard_map/ppermute | solution.py:106
  149.8 3.2 %collective-permute-start.7 = (f32[2,8,256]{2,0,1:T(2,128)S(1)}, f32[2,8,256]{2,0,1:T(2,128)S(1)}, u32[]{:S(2)}, u32[]{:S(2)}) collective-permute-start(f32[2,8,256]{2,0,1:T(2,128)S(1)} %bitcast.133), channel_id=1, source_target_pairs={{0,96},{32,0},{64,32},{96,64},{1,97},{33,1},{65,33},{97,65},{2,98}... | collective-permute-start | bytes 49160 | tf_op jit(solution)/shard_map/ppermute | solution.py:106
  157.5 25.2 %all-to-all-start = ((f32[128,2,560]{2,1,0:T(2,128)}), f32[128,2,560]{2,1,0:T(2,128)S(1)}, u32[]{:S(2)}, u32[]{:S(2)}) async-start(f32[128,2,560]{2,1,0:T(2,128)} %broadcast_in_dim.115), calls=%async_computation | async-start | bytes 1310720 | tf_op jit(solution)/shard_map/all_to_all | solution.py:144
  168.5 23.0 %collective-permute-start.3 = (bf16[2,256,8,69]{1,2,3,0:T(8,128)(2,1)}, bf16[2,256,8,69]{1,2,3,0:T(8,128)(2,1)}, u32[]{:S(2)}, u32[]{:S(2)}) collective-permute-start(bf16[2,256,8,69]{1,2,3,0:T(8,128)(2,1)} %bitcast.6), channel_id=1, source_target_pairs={{0,64},{32,96},{64,0},{96,32},{1,65},{33,97},{65,1},{97,33},{2,66}... | collective-permute-start | bytes 1695752 | tf_op jit(solution)/shard_map/ppermute | solution.py:85
  170.0 31.4 %collective-permute-start.4 = (bf16[2,256,8,69]{1,2,3,0:T(8,128)(2,1)}, bf16[2,256,8,69]{1,2,3,0:T(8,128)(2,1)}, u32[]{:S(2)}, u32[]{:S(2)}) collective-permute-start(bf16[2,256,8,69]{1,2,3,0:T(8,128)(2,1)} %bitcast.7), channel_id=1, source_target_pairs={{0,96},{32,0},{64,32},{96,64},{1,97},{33,1},{65,33},{97,65},{2,98}... | collective-permute-start | bytes 1695752 | tf_op jit(solution)/shard_map/ppermute | solution.py:85
  170.6 30.7 %collective-permute-start.2 = (bf16[2,256,8,69]{1,2,3,0:T(8,128)(2,1)S(1)}, bf16[2,256,8,69]{1,2,3,0:T(8,128)(2,1)}, u32[]{:S(2)}, u32[]{:S(2)}) collective-permute-start(bf16[2,256,8,69]{1,2,3,0:T(8,128)(2,1)S(1)} %bitcast.126), channel_id=1, source_target_pairs={{0,32},{32,64},{64,96},{96,0},{1,33},{33,65},{65,97},{97,1},{2,34}... | collective-permute-start | bytes 1695752 | tf_op jit(solution)/shard_map/ppermute | solution.py:85

commit v12 on v10

--- a/solution.py
+++ b/solution.py
@@ -149,8 +149,14 @@
             half_step = 1.5 * identity - 0.5 * jnp.einsum(
                 "pab,pbc->pac", inverse_root, sqrt_iter, precision=highest
             )
-            sqrt_iter = jnp.einsum("pab,pbc->pac", sqrt_iter, half_step, precision=highest)
-            inverse_root = jnp.einsum("pab,pbc->pac", half_step, inverse_root, precision=highest)
+            both = jnp.einsum(
+                "pab,pbc->pac",
+                half_step,
+                jnp.concatenate([sqrt_iter, inverse_root], axis=2),
+                precision=highest,
+            )
+            sqrt_iter = both[:, :, :ensemble]
+            inverse_root = both[:, :, ensemble:]
         once_applied = jnp.einsum("pab,pb->pa", inverse_root, pulled, precision=highest)
         mean_weight = (
             jnp.einsum("pab,pb->pa", inverse_root, once_applied, precision=highest)

time: 209 us -> 209 us (level)
  transfers between devices with their start and end apart: 7 -> 7, of which waited for: 4 -> 4; matrix products, arithmetic and copies ran while one was open for 19% -> 20% of each run, Pallas kernels for 0% -> 0%
where the time goes in v12:
time: 209 us; the launch traced here: 208 us
  matrix products  77.3 us (37%)
  local copies, waits for them, and re-layouts  50.3 us (24%)
  waiting for transfers between devices  39.6 us (19%)
  starting transfers between devices  27 us (13%)
  other arithmetic  7.12 us (3%)
  blocking collectives  5.9 us (3%)
    conv_general_dilated x2, matrix products, convolve(): lax.conv_general_dilated(wrapped, kernel, window_strides=(1, 1), padding=...  62.8 us
    ppermute x1, waiting for transfers between devices, padded_2(): lax.ppermute(cells, BAND, shift_pairs(band_size, 1))  26.8 us
    unnamed x43, local copies, waits for them, and re-layouts  15.3 us
    all_to_all x1, starting transfers between devices, on_device(): lax.all_to_all(jnp.broadcast_to(packed[None], (devices,) + packed.shape),...  11.9 us
    ppermute x3, waiting for transfers between devices, on_device(): lax.ppermute(outgoing, GRP, [(j, (j + step) % quarters) for j in range(qu...  9.58 us
    dot_general x1, matrix products, on_device(): jnp.einsum('ajnm,jailnc->mcil', weights, spread_out, precision=highest)  7.73 us
    ppermute x1, local copies, waits for them, and re-layouts, padded_2(): lax.ppermute(cells, BAND, shift_pairs(band_size, 1))  6.77 us
    ppermute x1, local copies, waits for them, and re-layouts, padded_2(): lax.ppermute(cells, BAND, shift_pairs(band_size, -1))  6.7 us
  transfers between devices with their start and end apart: 7, of which 4 were waited for; matrix products, arithmetic and copies ran while one was open for 20% of the time, Pallas kernels for 0%

profile of v12, /device:TPU:1, one launch (start us, length us, event | category | flops | bytes accessed | tf_op | source)
XLA Modules:
  0.0 207.6 jit_solution(6949044128184680884)
XLA Ops:
  0.0 2.4 %copy.136 = bf16[8,69,2,1024]{3,0,1,2:T(8,128)(2,1)S(1)} copy(bf16[8,69,2,1024]{3,2,1,0:T(2,128)(2,1)} %param.14) | data formatting | bytes 4521984 | tf_op jit(solution)/transpose | solution.py:214
  2.4 5.8 %collective-permute-start = (bf16[2,1024,8,69]{1,2,3,0:T(8,128)(2,1)S(1)}, bf16[2,1024,8,69]{1,2,3,0:T(8,128)(2,1)}, u32[]{:S(2)}, u32[]{:S(2)}) collective-permute-start(bf16[2,1024,8,69]{1,2,3,0:T(8,128)(2,1)S(1)} %bitcast.95), channel_id=1, source_target_pairs={{0,1},{1,2},{2,3},{3,4},{4,5},{5,6},{6,7},{7,8},{8,9},{9,10},{10,1... | collective-permute-start | bytes 6782984 | tf_op jit(solution)/shard_map/ppermute | solution.py:22
  8.2 1.3 collective-permute-start.1
  9.4 7.1 %copy.75 = bf16[8,69,2,1024]{1,0,3,2:T(8,128)(2,1)} copy(bf16[8,69,2,1024]{3,2,1,0:T(2,128)(2,1)} %param.14) | data formatting | bytes 4521984 | tf_op args[0]
  16.7 5.9 %all-gather.1 = s32[4,2,256]{2,1,0:T(2,128)S(1)} all-gather(s32[1,2,256]{2,1,0:T(2,128)S(1)} %bitcast.109), channel_id=2, replica_groups=mesh['y_lo'=2,'core'=2,'y_hi'=2,'x'=4,'z'=4] {'y_lo','core'}, dimensions={0}, use_global_device_ids=true | all-gather | bytes 10240 | tf_op jit(solution)/shard_map/all_gather | solution.py:78
  22.6 0.6 pad_clamp_fusion.1
  23.2 0.6 fusion.77
  23.8 0.6 fusion.76
  24.4 0.6 fusion.75
  25.0 0.7 compare_and_fusion
  25.7 0.5 fusion.82
  26.2 0.6 and_select_fusion.1
  26.8 0.9 fusion.45
  27.8 26.8 %collective-permute-done = bf16[2,1024,8,69]{1,2,3,0:T(8,128)(2,1)} collective-permute-done((bf16[2,1024,8,69]{1,2,3,0:T(8,128)(2,1)S(1)}, bf16[2,1024,8,69]{1,2,3,0:T(8,128)(2,1)}, u32[]{:S(2)}, u32[]{:S(2)}) %collective-permute-start) | collective-permute-done | bytes 2261024 | tf_op jit(solution)/shard_map/ppermute | solution.py:22
  54.6 6.8 %copy.78 = bf16[2,1024,8,69]{3,2,1,0:T(8,128)(2,1)} copy(bf16[2,1024,8,69]{1,2,3,0:T(8,128)(2,1)} %collective-permute-done) | data formatting | bytes 4521984 | tf_op jit(solution)/shard_map/ppermute | solution.py:22
  61.3 6.7 %copy.79 = bf16[2,1024,8,69]{3,2,1,0:T(8,128)(2,1)} copy(bf16[2,1024,8,69]{1,2,3,0:T(8,128)(2,1)} %collective-permute-done.1) | data formatting | bytes 4521984 | tf_op jit(solution)/shard_map/ppermute | solution.py:24
  68.1 39.8 %fusion.6 = bf16[4,1024,8,256]{3,2,1,0:T(8,128)(2,1)} fusion(f32[256]{0:T(256)S(1)} %copy-done.17, pred[4]{0:T(512)(128)(4,1)S(1)} %and_or_fusion, bf16[3,3,256,69]{2,3,1,0:T(8,128)(2,1)S(1)} %copy-done, bf16[2,1024,8,69]{3,2,1,0:T(8,128)(2,1)} %copy.79, bf16[2,1024,8,69]{3,2,1,0:T(8,128)(2,1)} %bitcast.94, bf16[2,1024,8,69]{3,2,1,0:T(8,128)(2,1)} %copy.78), kind=kOutput, calls=%fused_computation.10 | convolution fusion | flops 10504556544 | bytes 23879172 | tf_op jit(solution)/shard_map/conv_general_dilated | solution.py:32
  107.9 0.7 fusion.88
  108.7 22.9 %add_convert_fusion = bf16[2,1024,8,69]{3,2,1,0:T(8,128)(2,1)S(1)} fusion(f32[69]{0:T(128)S(1)} %copy-done.18, bf16[3,3,69,256]{3,2,1,0:T(8,128)(2,1)S(1)} %copy-done.16, bf16[4,1,8,256]{3,2,1,0:T(8,128)(2,1)S(1)} %get-tuple-element.6, bf16[4,1024,8,256]{3,2,1,0:T(8,128)(2,1)} %fusion.6, bf16[4,1,8,256]{3,2,1,0:T(8,128)(2,1)S(1)} %get-tuple-element.5, ...), kind=kOutput, calls=%fused_computation.27 | convolution fusion | flops 5230657536 | bytes 21650196 | tf_op jit(solution)/shard_map/conv_general_dilated | solution.py:32
  131.7 1.9 copy-done.1
  133.6 2.6 %fusion.21 = f32[4,2,8,256]{3,2,1,0:T(8,128)} fusion(f32[4,2,69,256]{3,2,1,0:T(8,128)S(1)} %copy-done.4, bf16[2,4,256,8,69]{4,3,2,1,0:T(8,128)(2,1)S(1)} %bitcast.92, s32[4,2,256]{2,1,0:T(2,128)S(1)} %copy-done.8), kind=kOutput, calls=%fused_computation.29 | convolution fusion | flops 581582848 | bytes 2899968 | tf_op jit(solution)/shard_map/iqlmc,qiol->qicmo/dot_general | solution.py:84
  136.2 4.8 %all-to-all-start = ((f32[4,2,8,256]{3,2,1,0:T(8,128)}), f32[4,2,8,256]{3,2,1,0:T(8,128)S(1)}, u32[]{:S(2)}, u32[]{:S(2)}) async-start(f32[4,2,8,256]{3,2,1,0:T(8,128)} %fusion.21), calls=%async_computation | async-start | bytes 131072 | tf_op jit(solution)/shard_map/all_to_all | solution.py:94
  141.0 0.6 pad_clamp_fusion
  141.6 2.7 %all-to-all-done = f32[4,2,8,256]{3,2,1,0:T(8,128)S(1)} async-done(((f32[4,2,8,256]{3,2,1,0:T(8,128)}), f32[4,2,8,256]{3,2,1,0:T(8,128)S(1)}, u32[]{:S(2)}, u32[]{:S(2)}) %all-to-all-start) | async-done | bytes 65568 | tf_op jit(solution)/shard_map/all_to_all | solution.py:94
  144.5 0.3 copy.105
  144.8 1.6 gather_fusion
  146.8 1.0 broadcast_in_dim.103
  147.8 11.9 %all-to-all-start.1 = ((f32[128,2,560]{2,1,0:T(2,128)}), f32[128,2,560]{2,1,0:T(2,128)}, u32[]{:S(2)}, u32[]{:S(2)}) async-start(f32[128,2,560]{2,1,0:T(2,128)} %broadcast_in_dim.103), calls=%async_computation.1 | async-start | bytes 1310720 | tf_op jit(solution)/shard_map/all_to_all | solution.py:128
  159.7 0.5 iota_compare_fusion.4
  160.4 3.5 %constant_dynamic-slice_fusion.3 = (bf16[2,1,256,8,69]{4,3,2,1,0:T(8,128)(2,1)S(1)}, bf16[2,1,256,8,69]{4,3,2,1,0:T(8,128)(2,1)S(1)}, bf16[2,1,256,8,69]{4,3,2,1,0:T(8,128)(2,1)S(1)}, bf16[2,1,256,8,69]{4,3,2,1,0:T(8,128)(2,1)}) fusion(bf16[2,4,256,8,69]{4,3,2,1,0:T(8,128)(2,1)} %bitcast.93, s32[]{:T(128)S(6)} %select_n.86, s32[]{:T(128)S(6)} %select_n.90, ...), kind=kLoop, calls=%fused_computation.126 | loop fusion | bytes 4522000 | tf_op jit(solution)/shard_map/jit(dynamic_index_in_dim)/dynamic_slice | solution.py:96
  163.8 2.7 %copy.110 = bf16[2,1,256,8,69]{2,3,4,1,0:T(8,128)(2,1)} copy(bf16[2,1,256,8,69]{4,3,2,1,0:T(8,128)(2,1)} %get-tuple-element.10) | data formatting | bytes 1130496
  166.5 1.1 collective-permute-start.4
  167.7 1.6 copy.108
  169.3 0.6 collective-permute-start.2
  169.9 0.9 copy.109
  170.9 1.5 collective-permute-start.3
  172.3 0.9 copy.107
  173.3 0.5 all-to-all-done.1
  173.8 1.5 reshape.166
  175.4 0.4 fusion.89
  176.0 2.8 %gather_fusion.1 = f32[1024,2]{1,0:T(8,128)S(1)} fusion(f32[2,560]{0,1:T(8,128)S(1)} %copy.89, s32[1024]{0:T(1024)S(1)} %broadcast_clamp_fusion), kind=kCustom, calls=%fused_computation.1 | custom fusion | bytes 20480 | tf_op jit(solution)/shard_map/gather | solution.py:138
  178.8 0.3 copy.106
  179.3 0.9 fusion.43
  180.2 0.7 broadcast_in_dim.106
  184.0 0.7 gather_fusion.2
  184.7 9.6 %collective-permute-done.3 = bf16[2,256,8,69]{1,2,3,0:T(8,128)(2,1)} collective-permute-done((bf16[2,256,8,69]{1,2,3,0:T(8,128)(2,1)S(1)}, bf16[2,256,8,69]{1,2,3,0:T(8,128)(2,1)}, u32[]{:S(2)}, u32[]{:S(2)}) %collective-permute-start.3) | collective-permute-done | bytes 565280 | tf_op jit(solution)/shard_map/ppermute | solution.py:100
  194.3 7.7 %fusion.29 = f32[32,69,2,256]{3,0,1,2:T(8,128)S(1)} fusion(pred[2,2]{0,1:T(4,128)(4,1)} %iota_compare_fusion.4, f32[2,4,8,32]{3,0,2,1:T(2,128)S(1)} %bitcast.104, pred[4,8]{1,0:T(4,128)(4,1)} %compare_and_fusion, bf16[1,2,256,8,69]{2,3,4,1,0:T(8,128)(2,1)} %bitcast.10, bf16[1,2,256,8,69]{2,3,4,1,0:T(8,128)(2,1)} %bitcast.8, ...), kind=kOutput, calls=%fused_computation.37 | convolution fusion | flops 875005952 | bytes 6791204 | tf_op jit(solution)/shard_map/ajnm,jailnc->mcil/dot_general | solution.py:178
  202.0 5.6 %copy.93 = f32[32,69,2,256]{3,2,1,0:T(2,128)} copy(f32[32,69,2,256]{3,0,1,2:T(8,128)S(1)} %fusion.29) | data formatting | bytes 9043968 | tf_op jit(solution)/shard_map/ajnm,jailnc->mcil/transpose | solution.py:178
  (75 shorter events, 4.3 us)
Async XLA Ops:
  0.0 68.0 %copy-start = (bf16[3,3,256,69]{2,3,1,0:T(8,128)(2,1)S(1)}, bf16[3,3,256,69]{2,3,1,0:T(8,128)(2,1)}, u32[]{:S(2)}) copy-start(bf16[3,3,256,69]{2,3,1,0:T(8,128)(2,1)} %param.15) | copy-start | bytes 953860
  0.0 22.6 %copy-start.10 = (s32[528]{0:T(1024)S(1)}, s32[528]{0:T(1024)}, u32[]{:S(2)}) copy-start(s32[528]{0:T(1024)} %constant.160) | copy-start | bytes 6340
  0.0 16.7 %copy-start.11 = (s32[2,256]{1,0:T(2,128)S(1)}, s32[2,256]{1,0:T(2,128)}, u32[]{:S(2)}) copy-start(s32[2,256]{1,0:T(2,128)} %param.19) | copy-start | bytes 6148
  2.4 52.2 %collective-permute-start = (bf16[2,1024,8,69]{1,2,3,0:T(8,128)(2,1)S(1)}, bf16[2,1024,8,69]{1,2,3,0:T(8,128)(2,1)}, u32[]{:S(2)}, u32[]{:S(2)}) collective-permute-start(bf16[2,1024,8,69]{1,2,3,0:T(8,128)(2,1)S(1)} %bitcast.95), channel_id=1, source_target_pairs={{0,1},{1,2},{2,3},{3,4},{4,5},{5,6},{6,7},{7,8},{8,9},{9,10},{10,1... | collective-permute-start | bytes 6782984 | tf_op jit(solution)/shard_map/ppermute | solution.py:22
  8.2 53.2 %collective-permute-start.1 = (bf16[2,1024,8,69]{1,2,3,0:T(8,128)(2,1)S(1)}, bf16[2,1024,8,69]{1,2,3,0:T(8,128)(2,1)}, u32[]{:S(2)}, u32[]{:S(2)}) collective-permute-start(bf16[2,1024,8,69]{1,2,3,0:T(8,128)(2,1)S(1)} %bitcast.96), channel_id=1, source_target_pairs={{1,0},{2,1},{3,2},{4,3},{5,4},{6,5},{7,6},{8,7},{9,8},{10,9},{11,1... | collective-permute-start | bytes 6782984 | tf_op jit(solution)/shard_map/ppermute | solution.py:24
  16.5 51.5 %copy-start.17 = (f32[256]{0:T(256)S(1)}, f32[256]{0:T(256)}, u32[]{:S(2)}) copy-start(f32[256]{0:T(256)} %param.16) | copy-start | bytes 3076
  68.1 40.6 %copy-start.2 = (bf16[8,69,2,1024]{1,0,3,2:T(8,128)(2,1)S(1)}, bf16[8,69,2,1024]{1,0,3,2:T(8,128)(2,1)}, u32[]{:S(2)}) copy-start(bf16[8,69,2,1024]{1,0,3,2:T(8,128)(2,1)} %copy.75) | copy-start | bytes 6782980
  68.1 40.6 %copy-start.16 = (bf16[3,3,69,256]{3,2,1,0:T(8,128)(2,1)S(1)}, bf16[3,3,69,256]{3,2,1,0:T(8,128)(2,1)}, u32[]{:S(2)}) copy-start(bf16[3,3,69,256]{3,2,1,0:T(8,128)(2,1)} %param.17) | copy-start | bytes 953860
  68.1 40.6 %copy-start.18 = (f32[69]{0:T(128)S(1)}, f32[69]{0:T(128)}, u32[]{:S(2)}) copy-start(f32[69]{0:T(128)} %param.18) | copy-start | bytes 832
  108.7 25.0 %copy-start.4 = (f32[4,2,69,256]{3,2,1,0:T(8,128)S(1)}, f32[4,2,69,256]{3,2,1,0:T(8,128)}, u32[]{:S(2)}) copy-start(f32[4,2,69,256]{3,2,1,0:T(8,128)} %fusion.45) | copy-start | bytes 1695748
  108.7 25.0 %copy-start.8 = (s32[4,2,256]{2,1,0:T(2,128)S(1)}, s32[4,2,256]{2,1,0:T(2,128)}, u32[]{:S(2)}) copy-start(s32[4,2,256]{2,1,0:T(2,128)} %get-tuple-element.11) | copy-start | bytes 24580
  131.6 2.0 copy-start.1
  131.6 9.4 %copy-start.15 = (s32[32]{0:T(128)S(1)}, s32[32]{0:T(128)}, u32[]{:S(2)}) copy-start(s32[32]{0:T(128)} %fusion.82) | copy-start | bytes 388
  131.6 12.6 %copy-start.7 = (f32[2,256]{1,0:T(2,128)S(1)}, f32[2,256]{1,0:T(2,128)}, u32[]{:S(2)}) copy-start(f32[2,256]{1,0:T(2,128)} %param.21) | copy-start | bytes 6148
  131.7 12.6 %copy-start.12 = (f32[2,256]{1,0:T(2,128)S(1)}, f32[2,256]{1,0:T(2,128)}, u32[]{:S(2)}) copy-start(f32[2,256]{1,0:T(2,128)} %param.20) | copy-start | bytes 6148
  131.7 13.1 %copy-start.6 = (s32[1024]{0:T(1024)S(1)}, s32[1024]{0:T(1024)}, u32[]{:S(2)}) copy-start(s32[1024]{0:T(1024)} %pad_clamp_fusion.1) | copy-start | bytes 12292
  131.7 28.6 %copy-start.13 = (f32[2,8]{1,0:T(2,128)S(1)}, f32[2,8]{1,0:T(2,128)}, u32[]{:S(2)}) copy-start(f32[2,8]{1,0:T(2,128)} %param.23) | copy-start | bytes 196
  131.7 28.6 %copy-start.14 = (s32[2,8]{1,0:T(2,128)S(1)}, s32[2,8]{1,0:T(2,128)}, u32[]{:S(2)}) copy-start(s32[2,8]{1,0:T(2,128)} %param.22) | copy-start | bytes 196
  131.7 28.6 %copy-start.9 = (s32[1024]{0:T(1024)S(1)}, s32[1024]{0:T(1024)}, u32[]{:S(2)}) copy-start(s32[1024]{0:T(1024)} %constant.161) | copy-start | bytes 12292
  136.2 8.1 %all-to-all-start = ((f32[4,2,8,256]{3,2,1,0:T(8,128)}), f32[4,2,8,256]{3,2,1,0:T(8,128)S(1)}, u32[]{:S(2)}, u32[]{:S(2)}) async-start(f32[4,2,8,256]{3,2,1,0:T(8,128)} %fusion.21), calls=%async_computation | async-start | bytes 131072 | tf_op jit(solution)/shard_map/all_to_all | solution.py:94
  147.8 26.0 %all-to-all-start.1 = ((f32[128,2,560]{2,1,0:T(2,128)}), f32[128,2,560]{2,1,0:T(2,128)}, u32[]{:S(2)}, u32[]{:S(2)}) async-start(f32[128,2,560]{2,1,0:T(2,128)} %broadcast_in_dim.103), calls=%async_computation.1 | async-start | bytes 1310720 | tf_op jit(solution)/shard_map/all_to_all | solution.py:128
  160.3 18.8 %copy-start.5 = (f32[32,32]{1,0:T(8,128)S(1)}, f32[32,32]{1,0:T(8,128)}, u32[]{:S(2)}) copy-start(f32[32,32]{1,0:T(8,128)} %fusion.77) | copy-start | bytes 12292
  160.4 19.0 %copy-start.3 = (f32[32,32]{1,0:T(8,128)S(1)}, f32[32,32]{1,0:T(8,128)}, u32[]{:S(2)}) copy-start(f32[32,32]{1,0:T(8,128)} %fusion.76) | copy-start | bytes 12292
  166.5 18.2 %collective-permute-start.4 = (bf16[2,256,8,69]{1,2,3,0:T(8,128)(2,1)}, bf16[2,256,8,69]{1,2,3,0:T(8,128)(2,1)}, u32[]{:S(2)}, u32[]{:S(2)}) collective-permute-start(bf16[2,256,8,69]{1,2,3,0:T(8,128)(2,1)} %bitcast.98), channel_id=1, source_target_pairs={{0,96},{32,0},{64,32},{96,64},{1,97},{33,1},{65,33},{97,65},{2,98}... | collective-permute-start | bytes 1695752 | tf_op jit(solution)/shard_map/ppermute | solution.py:100
  169.3 15.4 %collective-permute-start.2 = (bf16[2,256,8,69]{1,2,3,0:T(8,128)(2,1)}, bf16[2,256,8,69]{1,2,3,0:T(8,128)(2,1)}, u32[]{:S(2)}, u32[]{:S(2)}) collective-permute-start(bf16[2,256,8,69]{1,2,3,0:T(8,128)(2,1)} %bitcast.100), channel_id=1, source_target_pairs={{0,32},{32,64},{64,96},{96,0},{1,33},{33,65},{65,97},{97,1},{2,34}... | collective-permute-start | bytes 1695752 | tf_op jit(solution)/shard_map/ppermute | solution.py:100
  170.9 23.4 %collective-permute-start.3 = (bf16[2,256,8,69]{1,2,3,0:T(8,128)(2,1)S(1)}, bf16[2,256,8,69]{1,2,3,0:T(8,128)(2,1)}, u32[]{:S(2)}, u32[]{:S(2)}) collective-permute-start(bf16[2,256,8,69]{1,2,3,0:T(8,128)(2,1)S(1)} %bitcast.101), channel_id=1, source_target_pairs={{0,64},{32,96},{64,0},{96,32},{1,65},{33,97},{65,1},{97,33},{2,66}... | collective-permute-start | bytes 1695752 | tf_op jit(solution)/shard_map/ppermute | solution.py:100

commit v13 on v10

--- a/solution.py
+++ b/solution.py
@@ -163,14 +163,17 @@
         weights = jnp.take(weights, source_member, axis=1).reshape(
             height, quarters, ensemble_part, ensemble
         )
-        patch_of = jnp.arange(height, dtype=jnp.int32)
-        spread_out = jnp.where(
-            (patch_of[:, None] == patch_of[None, :])[None, :, :, None, None, None],
-            patch_block_slice.astype(jnp.float32)[:, None],
-            0.0,
-        )
-        analysed = jnp.einsum(
-            "ajnm,jailnc->mcil", weights, spread_out, precision=highest
+        analysed = jnp.stack(
+            [
+                jnp.einsum(
+                    "jnm,jlnc->mcl",
+                    weights[row],
+                    patch_block_slice[:, row].astype(jnp.float32),
+                    precision=highest,
+                )
+                for row in range(height)
+            ],
+            axis=2,
         )
         return analysed
 

time: 209 us -> 212 us (1.014)
  waiting for transfers between devices: 39.9 us -> 46.4 us
  matrix products: 77 us -> 72.6 us
  local copies, waits for them, and re-layouts: 49.6 us -> 51.9 us
    unnamed x43 -> x49, local copies, waits for them, and re-layouts: 15.3 us -> 8.69 us
    all_to_all x1, waiting for transfers between devices: 0.48 us -> 6.64 us  [on_device(): lax.all_to_all(jnp.broadcast_to(packed[None], (devices,) + packed.shape),...]
    dynamic_slice x0 -> x3, local copies, waits for them, and re-layouts: none -> 6.03 us  [on_device(): lax.dynamic_index_in_dim(blocks, (me + step) % quarters, axis=1, keepdims...]
    another operation x0 -> x1, local copies, waits for them, and re-layouts: none -> 5.61 us  [on_device(): jnp.stack([jnp.einsum('jnm,jlnc->mcl', weights[row], patch_block_slice[:,...]
    transpose x1 -> x0, local copies, waits for them, and re-layouts: 5.61 us -> none  [on_device(): jnp.einsum('ajnm,jailnc->mcil', weights, spread_out, precision=highest)]
    dot_general x1 -> x2, matrix products: 7.73 us -> 2.23 us  [on_device(): jnp.einsum('jnm,jlnc->mcl', weights[row], patch_block_slice[:, row].astyp...]
    all_to_all x1, waiting for transfers between devices: 2.68 us -> 0.01 us  [on_device(): lax.all_to_all(own_members, GRP, split_axis=0, concat_axis=2, tiled=True)[0]]
    another operation x0 -> x2, other arithmetic: none -> 2.45 us  [the longest x1 1.86 us: on_device(): patch_block_slice = jnp.stack(pieces, axis=0)]
  transfers between devices with their start and end apart: 7 -> 7, of which waited for: 4 -> 3; matrix products, arithmetic and copies ran while one was open for 19% -> 16% of each run, Pallas kernels for 0% -> 0%
where the time goes in v13:
time: 212 us; the launch traced here: 211 us
  matrix products  72.6 us (34%)
  local copies, waits for them, and re-layouts  51.9 us (24%)
  waiting for transfers between devices  46.4 us (22%)
  starting transfers between devices  25.6 us (12%)
  other arithmetic  8.4 us (4%)
  blocking collectives  5.9 us (3%)
    conv_general_dilated x2, matrix products, convolve(): lax.conv_general_dilated(wrapped, kernel, window_strides=(1, 1), padding=...  62.8 us
    ppermute x1, waiting for transfers between devices, padded_2(): lax.ppermute(cells, BAND, shift_pairs(band_size, 1))  28.4 us
    ppermute x3, waiting for transfers between devices, on_device(): lax.ppermute(outgoing, GRP, [(j, (j + step) % quarters) for j in range(qu...  11.4 us
    all_to_all x1, starting transfers between devices, on_device(): lax.all_to_all(jnp.broadcast_to(packed[None], (devices,) + packed.shape),...  10.7 us
    unnamed x49, local copies, waits for them, and re-layouts  8.69 us
    ppermute x1, local copies, waits for them, and re-layouts, padded_2(): lax.ppermute(cells, BAND, shift_pairs(band_size, 1))  6.77 us
    ppermute x1, local copies, waits for them, and re-layouts, padded_2(): lax.ppermute(cells, BAND, shift_pairs(band_size, -1))  6.71 us
    all_to_all x1, waiting for transfers between devices, on_device(): lax.all_to_all(jnp.broadcast_to(packed[None], (devices,) + packed.shape),...  6.64 us
  transfers between devices with their start and end apart: 7, of which 3 were waited for; matrix products, arithmetic and copies ran while one was open for 16% of the time, Pallas kernels for 0%

profile of v13, /device:TPU:1, one launch (start us, length us, event | category | flops | bytes accessed | tf_op | source)
XLA Modules:
  0.0 211.4 jit_solution(8090289634301401963)
XLA Ops:
  0.0 3.8 %copy.121 = bf16[8,69,2,1024]{3,0,1,2:T(8,128)(2,1)} copy(bf16[8,69,2,1024]{3,2,1,0:T(2,128)(2,1)} %param.14) | data formatting | bytes 4521984 | tf_op jit(solution)/transpose | solution.py:211
  3.9 5.8 %collective-permute-start = (bf16[2,1024,8,69]{1,2,3,0:T(8,128)(2,1)}, bf16[2,1024,8,69]{1,2,3,0:T(8,128)(2,1)}, u32[]{:S(2)}, u32[]{:S(2)}) collective-permute-start(bf16[2,1024,8,69]{1,2,3,0:T(8,128)(2,1)} %bitcast.126), channel_id=1, source_target_pairs={{0,1},{1,2},{2,3},{3,4},{4,5},{5,6},{6,7},{7,8},{8,9},{9,10},{10,1... | collective-permute-start | bytes 6782984 | tf_op jit(solution)/shard_map/ppermute | solution.py:22
  9.6 1.3 collective-permute-start.1
  11.0 5.8 %copy.73 = bf16[8,69,2,1024]{1,0,3,2:T(8,128)(2,1)} copy(bf16[8,69,2,1024]{3,2,1,0:T(2,128)(2,1)S(1)} %copy-done.2) | data formatting | bytes 4521984 | tf_op args[0]
  17.0 5.9 %all-gather.1 = s32[4,2,256]{2,1,0:T(2,128)S(1)} all-gather(s32[1,2,256]{2,1,0:T(2,128)S(1)} %bitcast.143), channel_id=2, replica_groups=mesh['y_lo'=2,'core'=2,'y_hi'=2,'x'=4,'z'=4] {'y_lo','core'}, dimensions={0}, use_global_device_ids=true | all-gather | bytes 10240 | tf_op jit(solution)/shard_map/all_gather | solution.py:78
  22.9 0.6 pad_clamp_fusion.1
  23.5 0.6 fusion.53
  24.1 0.6 fusion.52
  24.7 0.6 fusion.51
  25.3 0.5 fusion.58
  25.8 0.6 compare_and_fusion
  26.4 0.6 and_select_fusion.1
  27.0 0.9 fusion.37
  28.0 28.4 %collective-permute-done = bf16[2,1024,8,69]{1,2,3,0:T(8,128)(2,1)} collective-permute-done((bf16[2,1024,8,69]{1,2,3,0:T(8,128)(2,1)}, bf16[2,1024,8,69]{1,2,3,0:T(8,128)(2,1)}, u32[]{:S(2)}, u32[]{:S(2)}) %collective-permute-start) | collective-permute-done | bytes 2261024 | tf_op jit(solution)/shard_map/ppermute | solution.py:22
  56.3 6.8 %copy.76 = bf16[2,1024,8,69]{3,2,1,0:T(8,128)(2,1)} copy(bf16[2,1024,8,69]{1,2,3,0:T(8,128)(2,1)} %collective-permute-done) | data formatting | bytes 4521984 | tf_op jit(solution)/shard_map/ppermute | solution.py:22
  63.1 6.7 %copy.77 = bf16[2,1024,8,69]{3,2,1,0:T(8,128)(2,1)} copy(bf16[2,1024,8,69]{1,2,3,0:T(8,128)(2,1)} %collective-permute-done.1) | data formatting | bytes 4521984 | tf_op jit(solution)/shard_map/ppermute | solution.py:24
  69.9 39.8 %fusion.6 = bf16[4,1024,8,256]{3,2,1,0:T(8,128)(2,1)} fusion(f32[256]{0:T(256)S(1)} %copy-done.22, pred[4]{0:T(512)(128)(4,1)S(1)} %and_or_fusion, bf16[3,3,256,69]{2,3,1,0:T(8,128)(2,1)S(1)} %copy-done, bf16[2,1024,8,69]{3,2,1,0:T(8,128)(2,1)} %copy.77, bf16[2,1024,8,69]{3,2,1,0:T(8,128)(2,1)} %bitcast.129, bf16[2,1024,8,69]{3,2,1,0:T(8,128)(2,1)} %copy.76), kind=kOutput, calls=%fused_computation.10 | convolution fusion | flops 10504556544 | bytes 23879172 | tf_op jit(solution)/shard_map/conv_general_dilated | solution.py:32
  109.7 0.7 fusion.61
  110.5 22.9 %add_convert_fusion = bf16[2,1024,8,69]{3,2,1,0:T(8,128)(2,1)S(1)} fusion(f32[69]{0:T(128)S(1)} %copy-done.23, bf16[3,3,69,256]{3,2,1,0:T(8,128)(2,1)S(1)} %copy-done.21, bf16[4,1,8,256]{3,2,1,0:T(8,128)(2,1)S(1)} %get-tuple-element.8, bf16[4,1024,8,256]{3,2,1,0:T(8,128)(2,1)} %fusion.6, bf16[4,1,8,256]{3,2,1,0:T(8,128)(2,1)S(1)} %get-tuple-element.7, ...), kind=kOutput, calls=%fused_computation.25 | convolution fusion | flops 5230657536 | bytes 21650196 | tf_op jit(solution)/shard_map/conv_general_dilated | solution.py:32
  133.4 2.0 copy-done.3
  135.4 2.5 %fusion.19 = f32[4,2,8,256]{3,2,1,0:T(8,128)} fusion(f32[4,2,69,256]{3,2,1,0:T(8,128)S(1)} %copy-done.6, bf16[2,4,256,8,69]{4,3,2,1,0:T(8,128)(2,1)S(1)} %bitcast.127, s32[4,2,256]{2,1,0:T(2,128)S(1)} %copy-done.12), kind=kOutput, calls=%fused_computation.27 | convolution fusion | flops 581582848 | bytes 2899968 | tf_op jit(solution)/shard_map/iqlmc,qiol->qicmo/dot_general | solution.py:84
  138.0 4.8 %all-to-all-start = ((f32[4,2,8,256]{3,2,1,0:T(8,128)}), f32[4,2,8,256]{3,2,1,0:T(8,128)S(1)}, u32[]{:S(2)}, u32[]{:S(2)}) async-start(f32[4,2,8,256]{3,2,1,0:T(8,128)} %fusion.19), calls=%async_computation | async-start | bytes 131072 | tf_op jit(solution)/shard_map/all_to_all | solution.py:94
  142.8 3.5 %constant_dynamic-slice_fusion.3 = (bf16[2,1,256,8,69]{4,3,2,1,0:T(8,128)(2,1)S(1)}, bf16[2,1,256,8,69]{4,3,2,1,0:T(8,128)(2,1)}, bf16[2,1,256,8,69]{4,3,2,1,0:T(8,128)(2,1)S(1)}, bf16[2,1,256,8,69]{4,3,2,1,0:T(8,128)(2,1)S(1)}) fusion(bf16[2,4,256,8,69]{4,3,2,1,0:T(8,128)(2,1)} %bitcast.128, s32[]{:T(128)S(6)} %select_n.80, s32[]{:T(128)S(6)} %select_n.86, ...), kind=kLoop, calls=%fused_computation.109 | loop fusion | bytes 4522000 | tf_op jit(solution)/shard_map/jit(dynamic_index_in_dim)/dynamic_slice | solution.py:96
  146.3 2.7 %copy.81 = bf16[2,1,256,8,69]{2,3,4,0,1:T(8,128)(2,1)} copy(bf16[2,1,256,8,69]{4,3,2,1,0:T(8,128)(2,1)} %get-tuple-element.10) | data formatting | bytes 1130496 | tf_op jit(solution)/shard_map/jit(dynamic_index_in_dim)/dynamic_slice | solution.py:98
  149.1 1.6 copy.79
  150.7 1.7 collective-permute-start.2
  152.4 1.7 copy.80
  154.1 1.4 collective-permute-start.3
  155.9 0.3 copy.101
  156.2 1.6 gather_fusion
  158.0 1.0 broadcast_in_dim.76
  159.0 10.7 %all-to-all-start.1 = ((f32[128,2,560]{2,1,0:T(2,128)}), f32[128,2,560]{2,1,0:T(2,128)S(1)}, u32[]{:S(2)}, u32[]{:S(2)}) async-start(f32[128,2,560]{2,1,0:T(2,128)} %broadcast_in_dim.76), calls=%async_computation.1 | async-start | bytes 1310720 | tf_op jit(solution)/shard_map/all_to_all | solution.py:128
  169.9 1.6 copy.78
  171.5 11.4 %collective-permute-done.3 = bf16[2,256,8,69]{1,2,3,0:T(8,128)(2,1)S(1)} collective-permute-done((bf16[2,256,8,69]{1,2,3,0:T(8,128)(2,1)}, bf16[2,256,8,69]{1,2,3,0:T(8,128)(2,1)S(1)}, u32[]{:S(2)}, u32[]{:S(2)}) %collective-permute-start.3) | collective-permute-done | bytes 565280 | tf_op jit(solution)/shard_map/ppermute | solution.py:100
  182.9 0.8 copy-done.7
  183.7 1.9 pad_maximum_fusion.7
  185.6 6.6 %all-to-all-done.1 = f32[128,2,560]{2,1,0:T(2,128)S(1)} async-done(((f32[128,2,560]{2,1,0:T(2,128)}), f32[128,2,560]{2,1,0:T(2,128)S(1)}, u32[]{:S(2)}, u32[]{:S(2)}) %all-to-all-start.1) | async-done | bytes 573472 | tf_op jit(solution)/shard_map/all_to_all | solution.py:128
  192.2 1.3 reshape.123
  193.5 1.5 fusion.63
  195.2 2.8 %gather_fusion.1 = f32[1024,2]{1,0:T(8,128)S(1)} fusion(f32[2,560]{0,1:T(8,128)S(1)} %copy.86, s32[1024]{0:T(1024)S(1)} %broadcast_clamp_fusion), kind=kCustom, calls=%fused_computation.1 | custom fusion | bytes 20480 | tf_op jit(solution)/shard_map/gather | solution.py:138
  198.0 0.3 copy.102
  198.5 0.2 fusion.35
  198.7 0.2 fusion.54
  202.1 0.6 gather_fusion.2
  202.9 1.1 convolution_bitcast_fusion.1
  204.0 1.1 convolution_bitcast_fusion
  205.2 0.6 pad_maximum_fusion.6
  205.8 5.6 %copy.89 = f32[32,69,2,256]{3,2,1,0:T(2,128)} copy(f32[32,69,2,256]{3,0,1,2:T(8,128)S(1)} %pad_maximum_fusion.6) | data formatting | bytes 9043968 | tf_op jit(solution)/shard_map/stack | solution.py:166
  (93 shorter events, 4.7 us)
Async XLA Ops:
  0.0 69.8 %copy-start = (bf16[3,3,256,69]{2,3,1,0:T(8,128)(2,1)S(1)}, bf16[3,3,256,69]{2,3,1,0:T(8,128)(2,1)}, u32[]{:S(2)}) copy-start(bf16[3,3,256,69]{2,3,1,0:T(8,128)(2,1)} %param.15) | copy-start | bytes 953860
  0.0 22.9 %copy-start.14 = (s32[528]{0:T(1024)S(1)}, s32[528]{0:T(1024)}, u32[]{:S(2)}) copy-start(s32[528]{0:T(1024)} %constant.160) | copy-start | bytes 6340
  0.0 10.9 %copy-start.2 = (bf16[8,69,2,1024]{3,2,1,0:T(2,128)(2,1)S(1)}, bf16[8,69,2,1024]{3,2,1,0:T(2,128)(2,1)}, u32[]{:S(2)}) copy-start(bf16[8,69,2,1024]{3,2,1,0:T(2,128)(2,1)} %param.14) | copy-start | bytes 6782980
  0.0 17.0 %copy-start.15 = (s32[2,256]{1,0:T(2,128)S(1)}, s32[2,256]{1,0:T(2,128)}, u32[]{:S(2)}) copy-start(s32[2,256]{1,0:T(2,128)} %param.19) | copy-start | bytes 6148
  3.9 52.5 %collective-permute-start = (bf16[2,1024,8,69]{1,2,3,0:T(8,128)(2,1)}, bf16[2,1024,8,69]{1,2,3,0:T(8,128)(2,1)}, u32[]{:S(2)}, u32[]{:S(2)}) collective-permute-start(bf16[2,1024,8,69]{1,2,3,0:T(8,128)(2,1)} %bitcast.126), channel_id=1, source_target_pairs={{0,1},{1,2},{2,3},{3,4},{4,5},{5,6},{6,7},{7,8},{8,9},{9,10},{10,1... | collective-permute-start | bytes 6782984 | tf_op jit(solution)/shard_map/ppermute | solution.py:22
  9.6 53.5 %collective-permute-start.1 = (bf16[2,1024,8,69]{1,2,3,0:T(8,128)(2,1)}, bf16[2,1024,8,69]{1,2,3,0:T(8,128)(2,1)}, u32[]{:S(2)}, u32[]{:S(2)}) collective-permute-start(bf16[2,1024,8,69]{1,2,3,0:T(8,128)(2,1)} %bitcast.126), channel_id=1, source_target_pairs={{1,0},{2,1},{3,2},{4,3},{5,4},{6,5},{7,6},{8,7},{9,8},{10,9},{11,1... | collective-permute-start | bytes 6782984 | tf_op jit(solution)/shard_map/ppermute | solution.py:24
  63.1 6.7 %copy-start.22 = (f32[256]{0:T(256)S(1)}, f32[256]{0:T(256)}, u32[]{:S(2)}) copy-start(f32[256]{0:T(256)} %param.16) | copy-start | bytes 3076
  69.8 40.6 %copy-start.4 = (bf16[8,69,2,1024]{1,0,3,2:T(8,128)(2,1)S(1)}, bf16[8,69,2,1024]{1,0,3,2:T(8,128)(2,1)}, u32[]{:S(2)}) copy-start(bf16[8,69,2,1024]{1,0,3,2:T(8,128)(2,1)} %copy.73) | copy-start | bytes 6782980
  69.8 40.6 %copy-start.21 = (bf16[3,3,69,256]{3,2,1,0:T(8,128)(2,1)S(1)}, bf16[3,3,69,256]{3,2,1,0:T(8,128)(2,1)}, u32[]{:S(2)}) copy-start(bf16[3,3,69,256]{3,2,1,0:T(8,128)(2,1)} %param.17) | copy-start | bytes 953860
  69.8 40.6 %copy-start.23 = (f32[69]{0:T(128)S(1)}, f32[69]{0:T(128)}, u32[]{:S(2)}) copy-start(f32[69]{0:T(128)} %param.18) | copy-start | bytes 832
  110.4 25.0 %copy-start.6 = (f32[4,2,69,256]{3,2,1,0:T(8,128)S(1)}, f32[4,2,69,256]{3,2,1,0:T(8,128)}, u32[]{:S(2)}) copy-start(f32[4,2,69,256]{3,2,1,0:T(8,128)} %fusion.37) | copy-start | bytes 1695748
  110.5 25.0 %copy-start.12 = (s32[4,2,256]{2,1,0:T(2,128)S(1)}, s32[4,2,256]{2,1,0:T(2,128)}, u32[]{:S(2)}) copy-start(s32[4,2,256]{2,1,0:T(2,128)} %get-tuple-element.15) | copy-start | bytes 24580
  133.4 2.0 copy-start.3
  138.0 17.5 %all-to-all-start = ((f32[4,2,8,256]{3,2,1,0:T(8,128)}), f32[4,2,8,256]{3,2,1,0:T(8,128)S(1)}, u32[]{:S(2)}, u32[]{:S(2)}) async-start(f32[4,2,8,256]{3,2,1,0:T(8,128)} %fusion.19), calls=%async_computation | async-start | bytes 131072 | tf_op jit(solution)/shard_map/all_to_all | solution.py:94
  146.2 9.2 %copy-start.11 = (f32[2,256]{1,0:T(2,128)S(1)}, f32[2,256]{1,0:T(2,128)}, u32[]{:S(2)}) copy-start(f32[2,256]{1,0:T(2,128)} %param.21) | copy-start | bytes 6148
  146.2 9.2 %copy-start.16 = (f32[2,256]{1,0:T(2,128)S(1)}, f32[2,256]{1,0:T(2,128)}, u32[]{:S(2)}) copy-start(f32[2,256]{1,0:T(2,128)} %param.20) | copy-start | bytes 6148
  146.2 9.9 %copy-start.10 = (s32[1024]{0:T(1024)S(1)}, s32[1024]{0:T(1024)}, u32[]{:S(2)}) copy-start(s32[1024]{0:T(1024)} %pad_clamp_fusion.1) | copy-start | bytes 12292
  146.2 23.4 %copy-start.20 = (s32[32]{0:T(128)S(1)}, s32[32]{0:T(128)}, u32[]{:S(2)}) copy-start(s32[32]{0:T(128)} %fusion.58) | copy-start | bytes 388
  146.2 23.5 %copy-start.17 = (f32[2,8]{1,0:T(2,128)S(1)}, f32[2,8]{1,0:T(2,128)}, u32[]{:S(2)}) copy-start(f32[2,8]{1,0:T(2,128)} %param.23) | copy-start | bytes 196
  146.3 23.5 %copy-start.18 = (s32[2,8]{1,0:T(2,128)S(1)}, s32[2,8]{1,0:T(2,128)}, u32[]{:S(2)}) copy-start(s32[2,8]{1,0:T(2,128)} %param.22) | copy-start | bytes 196
  146.3 23.5 %copy-start.13 = (s32[1024]{0:T(1024)S(1)}, s32[1024]{0:T(1024)}, u32[]{:S(2)}) copy-start(s32[1024]{0:T(1024)} %constant.161) | copy-start | bytes 12292
  149.0 22.5 %collective-permute-start.4 = (bf16[2,256,8,69]{1,2,3,0:T(8,128)(2,1)}, bf16[2,256,8,69]{1,2,3,0:T(8,128)(2,1)}, u32[]{:S(2)}, u32[]{:S(2)}) collective-permute-start(bf16[2,256,8,69]{1,2,3,0:T(8,128)(2,1)} %bitcast.133), channel_id=1, source_target_pairs={{0,96},{32,0},{64,32},{96,64},{1,97},{33,1},{65,33},{97,65},{2,98}... | collective-permute-start | bytes 1695752 | tf_op jit(solution)/shard_map/ppermute | solution.py:100
  150.7 20.8 %collective-permute-start.2 = (bf16[2,256,8,69]{1,2,3,0:T(8,128)(2,1)}, bf16[2,256,8,69]{1,2,3,0:T(8,128)(2,1)}, u32[]{:S(2)}, u32[]{:S(2)}) collective-permute-start(bf16[2,256,8,69]{1,2,3,0:T(8,128)(2,1)} %bitcast.134), channel_id=1, source_target_pairs={{0,32},{32,64},{64,96},{96,0},{1,33},{33,65},{65,97},{97,1},{2,34}... | collective-permute-start | bytes 1695752 | tf_op jit(solution)/shard_map/ppermute | solution.py:100
  154.1 28.8 %collective-permute-start.3 = (bf16[2,256,8,69]{1,2,3,0:T(8,128)(2,1)}, bf16[2,256,8,69]{1,2,3,0:T(8,128)(2,1)S(1)}, u32[]{:S(2)}, u32[]{:S(2)}) collective-permute-start(bf16[2,256,8,69]{1,2,3,0:T(8,128)(2,1)} %bitcast.7), channel_id=1, source_target_pairs={{0,64},{32,96},{64,0},{96,32},{1,65},{33,97},{65,1},{97,33},{2,66}... | collective-permute-start | bytes 1695752 | tf_op jit(solution)/shard_map/ppermute | solution.py:100
  159.0 33.2 %all-to-all-start.1 = ((f32[128,2,560]{2,1,0:T(2,128)}), f32[128,2,560]{2,1,0:T(2,128)S(1)}, u32[]{:S(2)}, u32[]{:S(2)}) async-start(f32[128,2,560]{2,1,0:T(2,128)} %broadcast_in_dim.76), calls=%async_computation.1 | async-start | bytes 1310720 | tf_op jit(solution)/shard_map/all_to_all | solution.py:128
  169.8 28.5 %copy-start.9 = (f32[32,32]{1,0:T(8,128)S(1)}, f32[32,32]{1,0:T(8,128)}, u32[]{:S(2)}) copy-start(f32[32,32]{1,0:T(8,128)} %fusion.53) | copy-start | bytes 12292
  169.8 28.6 %copy-start.5 = (f32[32,32]{1,0:T(8,128)S(1)}, f32[32,32]{1,0:T(8,128)}, u32[]{:S(2)}) copy-start(f32[32,32]{1,0:T(8,128)} %fusion.52) | copy-start | bytes 12292
  169.8 28.6 %copy-start.8 = (f32[32,32]{1,0:T(8,128)S(1)}, f32[32,32]{1,0:T(8,128)}, u32[]{:S(2)}) copy-start(f32[32,32]{1,0:T(8,128)} %fusion.51) | copy-start | bytes 12292
  182.9 0.8 copy-start.7
  183.7 19.1 %copy-start.19 = (pred[32]{0:T(512)(128)(4,1)S(1)}, pred[32]{0:T(512)(128)(4,1)}, u32[]{:S(2)}) copy-start(pred[32]{0:T(512)(128)(4,1)} %compare_and_fusion) | copy-start | bytes 100
  205.1 6.2 %copy-start.1 = (bf16[3,3,256,69]{2,3,1,0:T(8,128)(2,1)S(1)}, bf16[3,3,256,69]{2,3,1,0:T(8,128)(2,1)}, u32[]{:S(2)}) copy-start(bf16[3,3,256,69]{2,3,1,0:T(8,128)(2,1)} %param.15) | copy-start | bytes 953860

commit v14 on v10

--- a/solution.py
+++ b/solution.py
@@ -56,8 +56,13 @@
         rows_first = prior_samples
         height = rows_first.shape[0]
         padded = padded_2(rows_first, band_size)
+        channels_in = padded.shape[3]
         hidden_fields = jax.nn.silu(
-            convolve(padded, conv1_weight) + conv1_bias
+            convolve(
+                jnp.pad(padded, ((0, 0), (0, 0), (0, 0), (0, 128 - channels_in))),
+                jnp.pad(conv1_weight, ((0, 0), (0, 0), (0, 0), (0, 128 - channels_in))),
+            )
+            + conv1_bias
         ).astype(jnp.bfloat16)
         place = lax.axis_index(BAND)
         row_ids = jnp.arange(height + 2, dtype=jnp.int32)[:, None, None, None]

time: 209 us -> 211 us (level)
  matrix products: 77 us -> 67.1 us
  other arithmetic: 7.77 us -> 15.7 us
  local copies, waits for them, and re-layouts: 49.6 us -> 54.4 us
    conv_general_dilated x2, matrix products: 62.7 us -> 52.8 us  [convolve(): lax.conv_general_dilated(wrapped, kernel, window_strides=(1, 1), padding=...]
    concatenate x0 -> x1, other arithmetic: none -> 8.07 us  [padded_2(): jnp.concatenate([lax.ppermute(cells, BAND, shift_pairs(band_size, 1)), ce...]
    unnamed x43 -> x46, local copies, waits for them, and re-layouts: 15.3 us -> 20.2 us
where the time goes in v14:
time: 211 us; the launch traced here: 210 us
  matrix products  67.1 us (32%)
  local copies, waits for them, and re-layouts  54.4 us (26%)
  waiting for transfers between devices  39.6 us (19%)
  starting transfers between devices  27.1 us (13%)
  other arithmetic  15.7 us (7%)
  blocking collectives  5.9 us (3%)
    conv_general_dilated x2, matrix products, convolve(): lax.conv_general_dilated(wrapped, kernel, window_strides=(1, 1), padding=...  52.8 us
    ppermute x1, waiting for transfers between devices, padded_2(): lax.ppermute(cells, BAND, shift_pairs(band_size, 1))  26.4 us
    unnamed x46, local copies, waits for them, and re-layouts  20.2 us
    all_to_all x1, starting transfers between devices, on_device(): lax.all_to_all(jnp.broadcast_to(packed[None], (devices,) + packed.shape),...  11.9 us
    ppermute x3, waiting for transfers between devices, on_device(): lax.ppermute(outgoing, GRP, [(j, (j + step) % quarters) for j in range(qu...  9.9 us
    concatenate x1, other arithmetic, padded_2(): jnp.concatenate([lax.ppermute(cells, BAND, shift_pairs(band_size, 1)), ce...  8.07 us
    dot_general x1, matrix products, on_device(): jnp.einsum('ajnm,jailnc->mcil', weights, spread_out, precision=highest)  7.73 us
    ppermute x1, local copies, waits for them, and re-layouts, padded_2(): lax.ppermute(cells, BAND, shift_pairs(band_size, -1))  6.7 us
  transfers between devices with their start and end apart: 7, of which 4 were waited for; matrix products, arithmetic and copies ran while one was open for 19% of the time, Pallas kernels for 0%

profile of v14, /device:TPU:1, one launch (start us, length us, event | category | flops | bytes accessed | tf_op | source)
XLA Modules:
  0.0 210.2 jit_solution(8320090650924615627)
XLA Ops:
  0.0 2.4 %copy.141 = bf16[8,69,2,1024]{3,0,1,2:T(8,128)(2,1)S(1)} copy(bf16[8,69,2,1024]{3,2,1,0:T(2,128)(2,1)} %param.14) | data formatting | bytes 4521984 | tf_op jit(solution)/transpose | solution.py:213
  2.4 5.8 %collective-permute-start = (bf16[2,1024,8,69]{1,2,3,0:T(8,128)(2,1)S(1)}, bf16[2,1024,8,69]{1,2,3,0:T(8,128)(2,1)}, u32[]{:S(2)}, u32[]{:S(2)}) collective-permute-start(bf16[2,1024,8,69]{1,2,3,0:T(8,128)(2,1)S(1)} %bitcast.113), channel_id=1, source_target_pairs={{0,1},{1,2},{2,3},{3,4},{4,5},{5,6},{6,7},{7,8},{8,9},{9,10},{10,1... | collective-permute-start | bytes 6782984 | tf_op jit(solution)/shard_map/ppermute | solution.py:22
  8.2 1.3 collective-permute-start.1
  9.5 7.1 %copy.79 = bf16[8,69,2,1024]{1,0,3,2:T(8,128)(2,1)} copy(bf16[8,69,2,1024]{3,2,1,0:T(2,128)(2,1)} %param.14) | data formatting | bytes 4521984 | tf_op args[0]
  16.7 0.3 copy.84
  17.2 5.9 %all-gather.1 = s32[4,2,256]{2,1,0:T(2,128)S(1)} all-gather(s32[1,2,256]{2,1,0:T(2,128)S(1)} %bitcast.127), channel_id=2, replica_groups=mesh['y_lo'=2,'core'=2,'y_hi'=2,'x'=4,'z'=4] {'y_lo','core'}, dimensions={0}, use_global_device_ids=true | all-gather | bytes 10240 | tf_op jit(solution)/shard_map/all_gather | solution.py:83
  23.1 0.6 pad_clamp_fusion.1
  23.7 0.6 fusion.63
  24.3 0.6 fusion.62
  24.9 0.6 fusion.61
  25.5 0.6 compare_and_fusion
  26.1 0.5 fusion.69
  26.7 0.6 and_select_fusion.1
  27.3 0.9 fusion.45
  28.1 26.4 %collective-permute-done = bf16[2,1024,8,69]{1,2,3,0:T(8,128)(2,1)} collective-permute-done((bf16[2,1024,8,69]{1,2,3,0:T(8,128)(2,1)S(1)}, bf16[2,1024,8,69]{1,2,3,0:T(8,128)(2,1)}, u32[]{:S(2)}, u32[]{:S(2)}) %collective-permute-start) | collective-permute-done | bytes 2261024 | tf_op jit(solution)/shard_map/ppermute | solution.py:22
  54.6 6.7 %copy.82 = bf16[2,1024,8,69]{3,2,1,0:T(8,128)(2,1)} copy(bf16[2,1024,8,69]{1,2,3,0:T(8,128)(2,1)} %collective-permute-done) | data formatting | bytes 4521984 | tf_op jit(solution)/shard_map/ppermute | solution.py:22
  61.3 6.7 %copy.83 = bf16[2,1024,8,69]{3,2,1,0:T(8,128)(2,1)} copy(bf16[2,1024,8,69]{1,2,3,0:T(8,128)(2,1)} %collective-permute-done.1) | data formatting | bytes 4521984 | tf_op jit(solution)/shard_map/ppermute | solution.py:24
  68.0 8.1 %fusion.17 = bf16[6,1024,8,128]{3,2,1,0:T(8,128)(2,1)S(1)} fusion(bf16[2,1024,8,69]{3,2,1,0:T(8,128)(2,1)} %copy.83, bf16[2,1024,8,69]{3,2,1,0:T(8,128)(2,1)} %bitcast.110, bf16[2,1024,8,69]{3,2,1,0:T(8,128)(2,1)} %copy.82), kind=kLoop, calls=%fused_computation.22 | loop fusion | flops 62914560 | bytes 19365888 | tf_op jit(solution)/shard_map/concatenate | solution.py:20
  76.1 4.5 %copy-done.2 = bf16[6,1024,8,128]{3,2,1,0:T(8,128)(2,1)} copy-done((bf16[6,1024,8,128]{3,2,1,0:T(8,128)(2,1)}, bf16[6,1024,8,128]{3,2,1,0:T(8,128)(2,1)S(1)}, u32[]{:S(2)}) %copy-start.2) | copy-done | bytes 12582936
  80.6 29.9 %fusion.9 = bf16[4,1024,8,256]{3,2,1,0:T(8,128)(2,1)} fusion(f32[256]{0:T(256)S(1)} %copy-done.18, pred[4]{0:T(512)(128)(4,1)S(1)} %and_or_fusion, bf16[3,3,256,69]{3,2,1,0:T(8,128)(2,1)S(1)} %copy.84, bf16[6,1,8,128]{3,2,1,0:T(8,128)(2,1)S(1)} %get-tuple-element.10, bf16[6,1024,8,128]{3,2,1,0:T(8,128)(2,1)} %copy-done.2, ...), kind=kOutput, calls=%fused_computation.14 | convolution fusion | flops 19398680576 | bytes 29703684 | tf_op jit(solution)/shard_map/conv_general_dilated | solution.py:32
  110.5 0.7 fusion.75
  111.3 22.9 %add_convert_fusion = bf16[2,1024,8,69]{3,2,1,0:T(8,128)(2,1)S(1)} fusion(f32[69]{0:T(128)S(1)} %copy-done.19, bf16[3,3,69,256]{3,2,1,0:T(8,128)(2,1)S(1)} %copy-done, bf16[4,1,8,256]{3,2,1,0:T(8,128)(2,1)S(1)} %get-tuple-element.8, bf16[4,1024,8,256]{3,2,1,0:T(8,128)(2,1)} %fusion.9, bf16[4,1,8,256]{3,2,1,0:T(8,128)(2,1)S(1)} %get-tuple-element.7, ...), kind=kOutput, calls=%fused_computation.25 | convolution fusion | flops 5230657536 | bytes 21650196 | tf_op jit(solution)/shard_map/conv_general_dilated | solution.py:32
  134.3 2.0 copy-done.3
  136.2 2.5 %fusion.20 = f32[4,2,8,256]{3,2,1,0:T(8,128)} fusion(f32[4,2,69,256]{3,2,1,0:T(8,128)S(1)} %copy-done.5, bf16[2,4,256,8,69]{4,3,2,1,0:T(8,128)(2,1)S(1)} %bitcast.111, s32[4,2,256]{2,1,0:T(2,128)S(1)} %copy-done.10), kind=kOutput, calls=%fused_computation.27 | convolution fusion | flops 581582848 | bytes 2899968 | tf_op jit(solution)/shard_map/iqlmc,qiol->qicmo/dot_general | solution.py:89
  138.8 4.8 %all-to-all-start = ((f32[4,2,8,256]{3,2,1,0:T(8,128)}), f32[4,2,8,256]{3,2,1,0:T(8,128)S(1)}, u32[]{:S(2)}, u32[]{:S(2)}) async-start(f32[4,2,8,256]{3,2,1,0:T(8,128)} %fusion.20), calls=%async_computation | async-start | bytes 131072 | tf_op jit(solution)/shard_map/all_to_all | solution.py:99
  143.6 0.6 pad_clamp_fusion
  144.2 2.7 %all-to-all-done = f32[4,2,8,256]{3,2,1,0:T(8,128)S(1)} async-done(((f32[4,2,8,256]{3,2,1,0:T(8,128)}), f32[4,2,8,256]{3,2,1,0:T(8,128)S(1)}, u32[]{:S(2)}, u32[]{:S(2)}) %all-to-all-start) | async-done | bytes 65568 | tf_op jit(solution)/shard_map/all_to_all | solution.py:99
  147.4 1.6 gather_fusion
  149.3 1.0 broadcast_in_dim.103
  150.4 11.9 %all-to-all-start.1 = ((f32[128,2,560]{2,1,0:T(2,128)}), f32[128,2,560]{2,1,0:T(2,128)}, u32[]{:S(2)}, u32[]{:S(2)}) async-start(f32[128,2,560]{2,1,0:T(2,128)} %broadcast_in_dim.103), calls=%async_computation.1 | async-start | bytes 1310720 | tf_op jit(solution)/shard_map/all_to_all | solution.py:133
  162.3 0.5 iota_compare_fusion.5
  162.9 3.5 %constant_dynamic-slice_fusion.3 = (bf16[2,1,256,8,69]{4,3,2,1,0:T(8,128)(2,1)S(1)}, bf16[2,1,256,8,69]{4,3,2,1,0:T(8,128)(2,1)S(1)}, bf16[2,1,256,8,69]{4,3,2,1,0:T(8,128)(2,1)S(1)}, bf16[2,1,256,8,69]{4,3,2,1,0:T(8,128)(2,1)}) fusion(bf16[2,4,256,8,69]{4,3,2,1,0:T(8,128)(2,1)} %bitcast.112, s32[]{:T(128)S(6)} %select_n.86, s32[]{:T(128)S(6)} %select_n.90, ...), kind=kLoop, calls=%fused_computation.112 | loop fusion | bytes 4522000 | tf_op jit(solution)/shard_map/jit(dynamic_index_in_dim)/dynamic_slice | solution.py:101
  166.4 2.7 %copy.115 = bf16[2,1,256,8,69]{2,3,4,1,0:T(8,128)(2,1)} copy(bf16[2,1,256,8,69]{4,3,2,1,0:T(8,128)(2,1)} %get-tuple-element.14) | data formatting | bytes 1130496
  169.1 1.1 collective-permute-start.4
  170.2 1.6 copy.113
  171.9 0.6 collective-permute-start.2
  172.5 0.9 copy.114
  173.4 1.5 collective-permute-start.3
  174.9 0.9 copy.112
  175.8 0.6 all-to-all-done.1
  176.4 1.5 reshape.166
  177.9 0.4 fusion.77
  178.6 2.8 %gather_fusion.1 = f32[1024,2]{1,0:T(8,128)S(1)} fusion(f32[2,560]{0,1:T(8,128)S(1)} %copy.94, s32[1024]{0:T(1024)S(1)} %broadcast_clamp_fusion), kind=kCustom, calls=%fused_computation.1 | custom fusion | bytes 20480 | tf_op jit(solution)/shard_map/gather | solution.py:143
  181.7 0.8 multiply_reduce_fusion
  186.2 0.7 gather_fusion.2
  187.0 9.9 %collective-permute-done.3 = bf16[2,256,8,69]{1,2,3,0:T(8,128)(2,1)} collective-permute-done((bf16[2,256,8,69]{1,2,3,0:T(8,128)(2,1)S(1)}, bf16[2,256,8,69]{1,2,3,0:T(8,128)(2,1)}, u32[]{:S(2)}, u32[]{:S(2)}) %collective-permute-start.3) | collective-permute-done | bytes 565280 | tf_op jit(solution)/shard_map/ppermute | solution.py:105
  196.9 7.7 %fusion.28 = f32[32,69,2,256]{3,0,1,2:T(8,128)S(1)} fusion(pred[2,2]{0,1:T(4,128)(4,1)} %iota_compare_fusion.5, f32[2,4,8,32]{3,0,2,1:T(2,128)S(1)} %bitcast.122, pred[4,8]{1,0:T(4,128)(4,1)} %compare_and_fusion, bf16[1,2,256,8,69]{2,3,4,1,0:T(8,128)(2,1)} %bitcast.10, bf16[1,2,256,8,69]{2,3,4,1,0:T(8,128)(2,1)} %bitcast.8, ...), kind=kOutput, calls=%fused_computation.35 | convolution fusion | flops 875005952 | bytes 6791204 | tf_op jit(solution)/shard_map/ajnm,jailnc->mcil/dot_general | solution.py:177
  204.6 5.6 %copy.98 = f32[32,69,2,256]{3,2,1,0:T(2,128)} copy(f32[32,69,2,256]{3,0,1,2:T(8,128)S(1)} %fusion.28) | data formatting | bytes 9043968 | tf_op jit(solution)/shard_map/ajnm,jailnc->mcil/transpose | solution.py:177
  (83 shorter events, 5.3 us)
Async XLA Ops:
  0.0 111.2 %copy-start = (bf16[3,3,69,256]{3,2,1,0:T(8,128)(2,1)S(1)}, bf16[3,3,69,256]{3,2,1,0:T(8,128)(2,1)}, u32[]{:S(2)}) copy-start(bf16[3,3,69,256]{3,2,1,0:T(8,128)(2,1)} %param.17) | copy-start | bytes 953860
  0.0 23.1 %copy-start.12 = (s32[528]{0:T(1024)S(1)}, s32[528]{0:T(1024)}, u32[]{:S(2)}) copy-start(s32[528]{0:T(1024)} %constant.165) | copy-start | bytes 6340
  0.0 16.7 %copy-start.6 = (bf16[3,3,256,69]{2,3,1,0:T(8,128)(2,1)S(1)}, bf16[3,3,256,69]{2,3,1,0:T(8,128)(2,1)}, u32[]{:S(2)}) copy-start(bf16[3,3,256,69]{2,3,1,0:T(8,128)(2,1)} %param.15) | copy-start | bytes 953860
  0.0 17.2 %copy-start.13 = (s32[2,256]{1,0:T(2,128)S(1)}, s32[2,256]{1,0:T(2,128)}, u32[]{:S(2)}) copy-start(s32[2,256]{1,0:T(2,128)} %param.19) | copy-start | bytes 6148
  2.4 52.2 %collective-permute-start = (bf16[2,1024,8,69]{1,2,3,0:T(8,128)(2,1)S(1)}, bf16[2,1024,8,69]{1,2,3,0:T(8,128)(2,1)}, u32[]{:S(2)}, u32[]{:S(2)}) collective-permute-start(bf16[2,1024,8,69]{1,2,3,0:T(8,128)(2,1)S(1)} %bitcast.113), channel_id=1, source_target_pairs={{0,1},{1,2},{2,3},{3,4},{4,5},{5,6},{6,7},{7,8},{8,9},{9,10},{10,1... | collective-permute-start | bytes 6782984 | tf_op jit(solution)/shard_map/ppermute | solution.py:22
  8.2 53.0 %collective-permute-start.1 = (bf16[2,1024,8,69]{1,2,3,0:T(8,128)(2,1)S(1)}, bf16[2,1024,8,69]{1,2,3,0:T(8,128)(2,1)}, u32[]{:S(2)}, u32[]{:S(2)}) collective-permute-start(bf16[2,1024,8,69]{1,2,3,0:T(8,128)(2,1)S(1)} %bitcast.114), channel_id=1, source_target_pairs={{1,0},{2,1},{3,2},{4,3},{5,4},{6,5},{7,6},{8,7},{9,8},{10,9},{11,1... | collective-permute-start | bytes 6782984 | tf_op jit(solution)/shard_map/ppermute | solution.py:24
  68.0 12.6 %copy-start.18 = (f32[256]{0:T(256)S(1)}, f32[256]{0:T(256)}, u32[]{:S(2)}) copy-start(f32[256]{0:T(256)} %param.16) | copy-start | bytes 3076
  76.0 4.5 %copy-start.2 = (bf16[6,1024,8,128]{3,2,1,0:T(8,128)(2,1)}, bf16[6,1024,8,128]{3,2,1,0:T(8,128)(2,1)S(1)}, u32[]{:S(2)}) copy-start(bf16[6,1024,8,128]{3,2,1,0:T(8,128)(2,1)S(1)} %fusion.17) | copy-start | bytes 37748740
  80.6 30.7 %copy-start.1 = (bf16[8,69,2,1024]{1,0,3,2:T(8,128)(2,1)S(1)}, bf16[8,69,2,1024]{1,0,3,2:T(8,128)(2,1)}, u32[]{:S(2)}) copy-start(bf16[8,69,2,1024]{1,0,3,2:T(8,128)(2,1)} %copy.79) | copy-start | bytes 6782980
  80.6 30.7 %copy-start.19 = (f32[69]{0:T(128)S(1)}, f32[69]{0:T(128)}, u32[]{:S(2)}) copy-start(f32[69]{0:T(128)} %param.18) | copy-start | bytes 832
  111.2 25.0 %copy-start.5 = (f32[4,2,69,256]{3,2,1,0:T(8,128)S(1)}, f32[4,2,69,256]{3,2,1,0:T(8,128)}, u32[]{:S(2)}) copy-start(f32[4,2,69,256]{3,2,1,0:T(8,128)} %fusion.45) | copy-start | bytes 1695748
  111.3 25.0 %copy-start.10 = (s32[4,2,256]{2,1,0:T(2,128)S(1)}, s32[4,2,256]{2,1,0:T(2,128)}, u32[]{:S(2)}) copy-start(s32[4,2,256]{2,1,0:T(2,128)} %get-tuple-element.15) | copy-start | bytes 24580
  111.3 32.3 %copy-start.17 = (s32[32]{0:T(128)S(1)}, s32[32]{0:T(128)}, u32[]{:S(2)}) copy-start(s32[32]{0:T(128)} %fusion.69) | copy-start | bytes 388
  111.3 35.6 %copy-start.9 = (f32[2,256]{1,0:T(2,128)S(1)}, f32[2,256]{1,0:T(2,128)}, u32[]{:S(2)}) copy-start(f32[2,256]{1,0:T(2,128)} %param.21) | copy-start | bytes 6148
  111.3 35.6 %copy-start.14 = (f32[2,256]{1,0:T(2,128)S(1)}, f32[2,256]{1,0:T(2,128)}, u32[]{:S(2)}) copy-start(f32[2,256]{1,0:T(2,128)} %param.20) | copy-start | bytes 6148
  134.2 2.0 copy-start.3
  134.2 13.1 %copy-start.8 = (s32[1024]{0:T(1024)S(1)}, s32[1024]{0:T(1024)}, u32[]{:S(2)}) copy-start(s32[1024]{0:T(1024)} %pad_clamp_fusion.1) | copy-start | bytes 12292
  134.2 28.6 %copy-start.15 = (f32[2,8]{1,0:T(2,128)S(1)}, f32[2,8]{1,0:T(2,128)}, u32[]{:S(2)}) copy-start(f32[2,8]{1,0:T(2,128)} %param.23) | copy-start | bytes 196
  134.2 28.6 %copy-start.16 = (s32[2,8]{1,0:T(2,128)S(1)}, s32[2,8]{1,0:T(2,128)}, u32[]{:S(2)}) copy-start(s32[2,8]{1,0:T(2,128)} %param.22) | copy-start | bytes 196
  134.2 28.7 %copy-start.11 = (s32[1024]{0:T(1024)S(1)}, s32[1024]{0:T(1024)}, u32[]{:S(2)}) copy-start(s32[1024]{0:T(1024)} %constant.166) | copy-start | bytes 12292
  138.8 8.1 %all-to-all-start = ((f32[4,2,8,256]{3,2,1,0:T(8,128)}), f32[4,2,8,256]{3,2,1,0:T(8,128)S(1)}, u32[]{:S(2)}, u32[]{:S(2)}) async-start(f32[4,2,8,256]{3,2,1,0:T(8,128)} %fusion.20), calls=%async_computation | async-start | bytes 131072 | tf_op jit(solution)/shard_map/all_to_all | solution.py:99
  150.4 26.0 %all-to-all-start.1 = ((f32[128,2,560]{2,1,0:T(2,128)}), f32[128,2,560]{2,1,0:T(2,128)}, u32[]{:S(2)}, u32[]{:S(2)}) async-start(f32[128,2,560]{2,1,0:T(2,128)} %broadcast_in_dim.103), calls=%async_computation.1 | async-start | bytes 1310720 | tf_op jit(solution)/shard_map/all_to_all | solution.py:133
  162.3 20.2 %copy-start.4 = (f32[32,32]{1,0:T(8,128)S(1)}, f32[32,32]{1,0:T(8,128)}, u32[]{:S(2)}) copy-start(f32[32,32]{1,0:T(8,128)} %fusion.62) | copy-start | bytes 12292
  162.3 20.2 %copy-start.7 = (f32[32,32]{1,0:T(8,128)S(1)}, f32[32,32]{1,0:T(8,128)}, u32[]{:S(2)}) copy-start(f32[32,32]{1,0:T(8,128)} %fusion.61) | copy-start | bytes 12292
  169.1 17.9 %collective-permute-start.4 = (bf16[2,256,8,69]{1,2,3,0:T(8,128)(2,1)}, bf16[2,256,8,69]{1,2,3,0:T(8,128)(2,1)}, u32[]{:S(2)}, u32[]{:S(2)}) collective-permute-start(bf16[2,256,8,69]{1,2,3,0:T(8,128)(2,1)} %bitcast.116), channel_id=1, source_target_pairs={{0,96},{32,0},{64,32},{96,64},{1,97},{33,1},{65,33},{97,65},{2,98}... | collective-permute-start | bytes 1695752 | tf_op jit(solution)/shard_map/ppermute | solution.py:105
  171.9 15.1 %collective-permute-start.2 = (bf16[2,256,8,69]{1,2,3,0:T(8,128)(2,1)}, bf16[2,256,8,69]{1,2,3,0:T(8,128)(2,1)}, u32[]{:S(2)}, u32[]{:S(2)}) collective-permute-start(bf16[2,256,8,69]{1,2,3,0:T(8,128)(2,1)} %bitcast.118), channel_id=1, source_target_pairs={{0,32},{32,64},{64,96},{96,0},{1,33},{33,65},{65,97},{97,1},{2,34}... | collective-permute-start | bytes 1695752 | tf_op jit(solution)/shard_map/ppermute | solution.py:105
  173.4 23.5 %collective-permute-start.3 = (bf16[2,256,8,69]{1,2,3,0:T(8,128)(2,1)S(1)}, bf16[2,256,8,69]{1,2,3,0:T(8,128)(2,1)}, u32[]{:S(2)}, u32[]{:S(2)}) collective-permute-start(bf16[2,256,8,69]{1,2,3,0:T(8,128)(2,1)S(1)} %bitcast.119), channel_id=1, source_target_pairs={{0,64},{32,96},{64,0},{96,32},{1,65},{33,97},{65,1},{97,33},{2,66}... | collective-permute-start | bytes 1695752 | tf_op jit(solution)/shard_map/ppermute | solution.py:105

commit v15 on v10

--- a/solution.py
+++ b/solution.py
@@ -56,6 +56,7 @@
         rows_first = prior_samples
         height = rows_first.shape[0]
         padded = padded_2(rows_first, band_size)
+        channels = rows_first.shape[3]
         hidden_fields = jax.nn.silu(
             convolve(padded, conv1_weight) + conv1_bias
         ).astype(jnp.bfloat16)
@@ -67,7 +68,10 @@
         extended = jnp.where(outside, jnp.zeros_like(hidden_fields), hidden_fields)
         forecast = (
             rows_first.astype(jnp.float32)
-            + convolve(extended, conv2_weight)
+            + convolve(
+                extended,
+                jnp.pad(conv2_weight, ((0, 0), (0, 0), (0, 128 - channels), (0, 0))),
+            )[..., :channels]
             + conv2_bias
         ).astype(jnp.bfloat16)
         ensemble_part = forecast.shape[2]

time: 209 us -> 209 us (level)
  no operation moved by 1% of the time
where the time goes in v15:
time: 209 us; the launch traced here: 208 us
  matrix products  77 us (37%)
  local copies, waits for them, and re-layouts  49.6 us (24%)
  waiting for transfers between devices  39.9 us (19%)
  starting transfers between devices  27 us (13%)
  other arithmetic  7.77 us (4%)
  blocking collectives  5.9 us (3%)
    conv_general_dilated x2, matrix products, convolve(): lax.conv_general_dilated(wrapped, kernel, window_strides=(1, 1), padding=...  62.7 us
    ppermute x1, waiting for transfers between devices, padded_2(): lax.ppermute(cells, BAND, shift_pairs(band_size, 1))  26.8 us
    unnamed x43, local copies, waits for them, and re-layouts  15.3 us
    all_to_all x1, starting transfers between devices, on_device(): lax.all_to_all(jnp.broadcast_to(packed[None], (devices,) + packed.shape),...  11.9 us
    ppermute x3, waiting for transfers between devices, on_device(): lax.ppermute(outgoing, GRP, [(j, (j + step) % quarters) for j in range(qu...  9.93 us
    dot_general x1, matrix products, on_device(): jnp.einsum('ajnm,jailnc->mcil', weights, spread_out, precision=highest)  7.73 us
    ppermute x1, local copies, waits for them, and re-layouts, padded_2(): lax.ppermute(cells, BAND, shift_pairs(band_size, 1))  6.76 us
    ppermute x1, local copies, waits for them, and re-layouts, padded_2(): lax.ppermute(cells, BAND, shift_pairs(band_size, -1))  6.7 us
  transfers between devices with their start and end apart: 7, of which 4 were waited for; matrix products, arithmetic and copies ran while one was open for 19% of the time, Pallas kernels for 0%

profile of v15, /device:TPU:1, one launch (start us, length us, event | category | flops | bytes accessed | tf_op | source)
XLA Modules:
  0.0 207.6 jit_solution(2633009516469307652)
XLA Ops:
  0.0 2.4 %copy.136 = bf16[8,69,2,1024]{3,0,1,2:T(8,128)(2,1)S(1)} copy(bf16[8,69,2,1024]{3,2,1,0:T(2,128)(2,1)} %param.14) | data formatting | bytes 4521984 | tf_op jit(solution)/transpose | solution.py:212
  2.4 5.8 %collective-permute-start = (bf16[2,1024,8,69]{1,2,3,0:T(8,128)(2,1)S(1)}, bf16[2,1024,8,69]{1,2,3,0:T(8,128)(2,1)}, u32[]{:S(2)}, u32[]{:S(2)}) collective-permute-start(bf16[2,1024,8,69]{1,2,3,0:T(8,128)(2,1)S(1)} %bitcast.114), channel_id=1, source_target_pairs={{0,1},{1,2},{2,3},{3,4},{4,5},{5,6},{6,7},{7,8},{8,9},{9,10},{10,1... | collective-permute-start | bytes 6782984 | tf_op jit(solution)/shard_map/ppermute | solution.py:22
  8.2 1.3 collective-permute-start.1
  9.4 7.1 %copy.75 = bf16[8,69,2,1024]{1,0,3,2:T(8,128)(2,1)} copy(bf16[8,69,2,1024]{3,2,1,0:T(2,128)(2,1)} %param.14) | data formatting | bytes 4521984 | tf_op args[0]
  16.7 5.9 %all-gather.1 = s32[4,2,256]{2,1,0:T(2,128)S(1)} all-gather(s32[1,2,256]{2,1,0:T(2,128)S(1)} %bitcast.128), channel_id=2, replica_groups=mesh['y_lo'=2,'core'=2,'y_hi'=2,'x'=4,'z'=4] {'y_lo','core'}, dimensions={0}, use_global_device_ids=true | all-gather | bytes 10240 | tf_op jit(solution)/shard_map/all_gather | solution.py:82
  22.6 0.6 pad_clamp_fusion.1
  23.2 0.6 fusion.63
  23.8 0.6 fusion.62
  24.4 0.6 fusion.61
  25.0 0.6 compare_and_fusion
  25.6 0.6 fusion.69
  26.2 0.6 and_select_fusion.1
  26.8 0.9 fusion.45
  27.7 26.8 %collective-permute-done = bf16[2,1024,8,69]{1,2,3,0:T(8,128)(2,1)} collective-permute-done((bf16[2,1024,8,69]{1,2,3,0:T(8,128)(2,1)S(1)}, bf16[2,1024,8,69]{1,2,3,0:T(8,128)(2,1)}, u32[]{:S(2)}, u32[]{:S(2)}) %collective-permute-start) | collective-permute-done | bytes 2261024 | tf_op jit(solution)/shard_map/ppermute | solution.py:22
  54.6 6.8 %copy.78 = bf16[2,1024,8,69]{3,2,1,0:T(8,128)(2,1)} copy(bf16[2,1024,8,69]{1,2,3,0:T(8,128)(2,1)} %collective-permute-done) | data formatting | bytes 4521984 | tf_op jit(solution)/shard_map/ppermute | solution.py:22
  61.3 6.7 %copy.79 = bf16[2,1024,8,69]{3,2,1,0:T(8,128)(2,1)} copy(bf16[2,1024,8,69]{1,2,3,0:T(8,128)(2,1)} %collective-permute-done.1) | data formatting | bytes 4521984 | tf_op jit(solution)/shard_map/ppermute | solution.py:24
  68.1 39.8 %fusion.6 = bf16[4,1024,8,256]{3,2,1,0:T(8,128)(2,1)} fusion(f32[256]{0:T(256)S(1)} %copy-done.17, pred[4]{0:T(512)(128)(4,1)S(1)} %and_or_fusion, bf16[3,3,256,69]{2,3,1,0:T(8,128)(2,1)S(1)} %copy-done, bf16[2,1024,8,69]{3,2,1,0:T(8,128)(2,1)} %copy.79, bf16[2,1024,8,69]{3,2,1,0:T(8,128)(2,1)} %bitcast.113, bf16[2,1024,8,69]{3,2,1,0:T(8,128)(2,1)} %copy.78), kind=kOutput, calls=%fused_computation.10 | convolution fusion | flops 10504556544 | bytes 23879172 | tf_op jit(solution)/shard_map/conv_general_dilated | solution.py:32
  107.9 0.7 fusion.74
  108.7 22.9 %add_convert_fusion = bf16[2,1024,8,69]{3,2,1,0:T(8,128)(2,1)S(1)} fusion(f32[69]{0:T(128)S(1)} %copy-done.18, bf16[3,3,69,256]{3,2,1,0:T(8,128)(2,1)S(1)} %copy-done.16, bf16[4,1,8,256]{3,2,1,0:T(8,128)(2,1)S(1)} %get-tuple-element.8, bf16[4,1024,8,256]{3,2,1,0:T(8,128)(2,1)} %fusion.6, bf16[4,1,8,256]{3,2,1,0:T(8,128)(2,1)S(1)} %get-tuple-element.7, ...), kind=kOutput, calls=%fused_computation.27 | convolution fusion | flops 5230657536 | bytes 21650196 | tf_op jit(solution)/shard_map/conv_general_dilated | solution.py:32
  131.7 1.9 copy-done.1
  133.6 2.5 %fusion.21 = f32[4,2,8,256]{3,2,1,0:T(8,128)} fusion(f32[4,2,69,256]{3,2,1,0:T(8,128)S(1)} %copy-done.4, bf16[2,4,256,8,69]{4,3,2,1,0:T(8,128)(2,1)S(1)} %bitcast.111, s32[4,2,256]{2,1,0:T(2,128)S(1)} %copy-done.8), kind=kOutput, calls=%fused_computation.29 | convolution fusion | flops 581582848 | bytes 2899968 | tf_op jit(solution)/shard_map/iqlmc,qiol->qicmo/dot_general | solution.py:88
  136.2 4.8 %all-to-all-start = ((f32[4,2,8,256]{3,2,1,0:T(8,128)}), f32[4,2,8,256]{3,2,1,0:T(8,128)S(1)}, u32[]{:S(2)}, u32[]{:S(2)}) async-start(f32[4,2,8,256]{3,2,1,0:T(8,128)} %fusion.21), calls=%async_computation | async-start | bytes 131072 | tf_op jit(solution)/shard_map/all_to_all | solution.py:98
  141.0 0.6 pad_clamp_fusion
  141.5 2.7 %all-to-all-done = f32[4,2,8,256]{3,2,1,0:T(8,128)S(1)} async-done(((f32[4,2,8,256]{3,2,1,0:T(8,128)}), f32[4,2,8,256]{3,2,1,0:T(8,128)S(1)}, u32[]{:S(2)}, u32[]{:S(2)}) %all-to-all-start) | async-done | bytes 65568 | tf_op jit(solution)/shard_map/all_to_all | solution.py:98
  144.5 0.3 copy.105
  144.7 1.6 gather_fusion
  146.7 1.0 broadcast_in_dim.103
  147.8 11.9 %all-to-all-start.1 = ((f32[128,2,560]{2,1,0:T(2,128)}), f32[128,2,560]{2,1,0:T(2,128)}, u32[]{:S(2)}, u32[]{:S(2)}) async-start(f32[128,2,560]{2,1,0:T(2,128)} %broadcast_in_dim.103), calls=%async_computation.1 | async-start | bytes 1310720 | tf_op jit(solution)/shard_map/all_to_all | solution.py:132
  159.7 0.6 iota_compare_fusion.4
  160.4 3.5 %constant_dynamic-slice_fusion.3 = (bf16[2,1,256,8,69]{4,3,2,1,0:T(8,128)(2,1)S(1)}, bf16[2,1,256,8,69]{4,3,2,1,0:T(8,128)(2,1)S(1)}, bf16[2,1,256,8,69]{4,3,2,1,0:T(8,128)(2,1)S(1)}, bf16[2,1,256,8,69]{4,3,2,1,0:T(8,128)(2,1)}) fusion(bf16[2,4,256,8,69]{4,3,2,1,0:T(8,128)(2,1)} %bitcast.112, s32[]{:T(128)S(6)} %select_n.86, s32[]{:T(128)S(6)} %select_n.90, ...), kind=kLoop, calls=%fused_computation.113 | loop fusion | bytes 4522000 | tf_op jit(solution)/shard_map/jit(dynamic_index_in_dim)/dynamic_slice | solution.py:100
  163.9 2.7 %copy.110 = bf16[2,1,256,8,69]{2,3,4,1,0:T(8,128)(2,1)} copy(bf16[2,1,256,8,69]{4,3,2,1,0:T(8,128)(2,1)} %get-tuple-element.12) | data formatting | bytes 1130496
  166.6 1.1 collective-permute-start.4
  167.7 1.6 copy.108
  169.3 0.6 collective-permute-start.2
  169.9 0.9 copy.109
  170.9 1.5 collective-permute-start.3
  172.4 0.9 copy.107
  173.3 0.5 all-to-all-done.1
  173.8 1.5 reshape.166
  175.3 0.4 fusion.75
  176.0 2.8 %gather_fusion.1 = f32[1024,2]{1,0:T(8,128)S(1)} fusion(f32[2,560]{0,1:T(8,128)S(1)} %copy.89, s32[1024]{0:T(1024)S(1)} %broadcast_clamp_fusion), kind=kCustom, calls=%fused_computation.1 | custom fusion | bytes 20480 | tf_op jit(solution)/shard_map/gather | solution.py:142
  178.8 0.3 copy.106
  179.1 0.8 multiply_reduce_fusion
  179.9 0.2 fusion.43
  183.6 0.7 gather_fusion.2
  184.4 9.9 %collective-permute-done.3 = bf16[2,256,8,69]{1,2,3,0:T(8,128)(2,1)} collective-permute-done((bf16[2,256,8,69]{1,2,3,0:T(8,128)(2,1)S(1)}, bf16[2,256,8,69]{1,2,3,0:T(8,128)(2,1)}, u32[]{:S(2)}, u32[]{:S(2)}) %collective-permute-start.3) | collective-permute-done | bytes 565280 | tf_op jit(solution)/shard_map/ppermute | solution.py:104
  194.3 7.7 %fusion.29 = f32[32,69,2,256]{3,0,1,2:T(8,128)S(1)} fusion(pred[2,2]{0,1:T(4,128)(4,1)} %iota_compare_fusion.4, f32[2,4,8,32]{3,0,2,1:T(2,128)S(1)} %bitcast.123, pred[4,8]{1,0:T(4,128)(4,1)} %compare_and_fusion, bf16[1,2,256,8,69]{2,3,4,1,0:T(8,128)(2,1)} %bitcast.10, bf16[1,2,256,8,69]{2,3,4,1,0:T(8,128)(2,1)} %bitcast.8, ...), kind=kOutput, calls=%fused_computation.37 | convolution fusion | flops 875005952 | bytes 6791204 | tf_op jit(solution)/shard_map/ajnm,jailnc->mcil/dot_general | solution.py:176
  202.0 5.6 %copy.93 = f32[32,69,2,256]{3,2,1,0:T(2,128)} copy(f32[32,69,2,256]{3,0,1,2:T(8,128)S(1)} %fusion.29) | data formatting | bytes 9043968 | tf_op jit(solution)/shard_map/ajnm,jailnc->mcil/transpose | solution.py:176
  (78 shorter events, 4.5 us)
Async XLA Ops:
  0.0 68.0 %copy-start = (bf16[3,3,256,69]{2,3,1,0:T(8,128)(2,1)S(1)}, bf16[3,3,256,69]{2,3,1,0:T(8,128)(2,1)}, u32[]{:S(2)}) copy-start(bf16[3,3,256,69]{2,3,1,0:T(8,128)(2,1)} %param.15) | copy-start | bytes 953860
  0.0 22.6 %copy-start.10 = (s32[528]{0:T(1024)S(1)}, s32[528]{0:T(1024)}, u32[]{:S(2)}) copy-start(s32[528]{0:T(1024)} %constant.160) | copy-start | bytes 6340
  0.0 16.7 %copy-start.11 = (s32[2,256]{1,0:T(2,128)S(1)}, s32[2,256]{1,0:T(2,128)}, u32[]{:S(2)}) copy-start(s32[2,256]{1,0:T(2,128)} %param.19) | copy-start | bytes 6148
  2.4 52.2 %collective-permute-start = (bf16[2,1024,8,69]{1,2,3,0:T(8,128)(2,1)S(1)}, bf16[2,1024,8,69]{1,2,3,0:T(8,128)(2,1)}, u32[]{:S(2)}, u32[]{:S(2)}) collective-permute-start(bf16[2,1024,8,69]{1,2,3,0:T(8,128)(2,1)S(1)} %bitcast.114), channel_id=1, source_target_pairs={{0,1},{1,2},{2,3},{3,4},{4,5},{5,6},{6,7},{7,8},{8,9},{9,10},{10,1... | collective-permute-start | bytes 6782984 | tf_op jit(solution)/shard_map/ppermute | solution.py:22
  8.2 53.2 %collective-permute-start.1 = (bf16[2,1024,8,69]{1,2,3,0:T(8,128)(2,1)S(1)}, bf16[2,1024,8,69]{1,2,3,0:T(8,128)(2,1)}, u32[]{:S(2)}, u32[]{:S(2)}) collective-permute-start(bf16[2,1024,8,69]{1,2,3,0:T(8,128)(2,1)S(1)} %bitcast.115), channel_id=1, source_target_pairs={{1,0},{2,1},{3,2},{4,3},{5,4},{6,5},{7,6},{8,7},{9,8},{10,9},{11,1... | collective-permute-start | bytes 6782984 | tf_op jit(solution)/shard_map/ppermute | solution.py:24
  16.5 51.5 %copy-start.17 = (f32[256]{0:T(256)S(1)}, f32[256]{0:T(256)}, u32[]{:S(2)}) copy-start(f32[256]{0:T(256)} %param.16) | copy-start | bytes 3076
  68.0 40.6 %copy-start.2 = (bf16[8,69,2,1024]{1,0,3,2:T(8,128)(2,1)S(1)}, bf16[8,69,2,1024]{1,0,3,2:T(8,128)(2,1)}, u32[]{:S(2)}) copy-start(bf16[8,69,2,1024]{1,0,3,2:T(8,128)(2,1)} %copy.75) | copy-start | bytes 6782980
  68.0 40.6 %copy-start.16 = (bf16[3,3,69,256]{3,2,1,0:T(8,128)(2,1)S(1)}, bf16[3,3,69,256]{3,2,1,0:T(8,128)(2,1)}, u32[]{:S(2)}) copy-start(bf16[3,3,69,256]{3,2,1,0:T(8,128)(2,1)} %param.17) | copy-start | bytes 953860
  68.1 40.6 %copy-start.18 = (f32[69]{0:T(128)S(1)}, f32[69]{0:T(128)}, u32[]{:S(2)}) copy-start(f32[69]{0:T(128)} %param.18) | copy-start | bytes 832
  108.6 25.0 %copy-start.4 = (f32[4,2,69,256]{3,2,1,0:T(8,128)S(1)}, f32[4,2,69,256]{3,2,1,0:T(8,128)}, u32[]{:S(2)}) copy-start(f32[4,2,69,256]{3,2,1,0:T(8,128)} %fusion.45) | copy-start | bytes 1695748
  108.6 25.0 %copy-start.8 = (s32[4,2,256]{2,1,0:T(2,128)S(1)}, s32[4,2,256]{2,1,0:T(2,128)}, u32[]{:S(2)}) copy-start(s32[4,2,256]{2,1,0:T(2,128)} %get-tuple-element.13) | copy-start | bytes 24580
  131.6 2.0 copy-start.1
  131.6 9.4 %copy-start.15 = (s32[32]{0:T(128)S(1)}, s32[32]{0:T(128)}, u32[]{:S(2)}) copy-start(s32[32]{0:T(128)} %fusion.69) | copy-start | bytes 388
  131.6 12.6 %copy-start.7 = (f32[2,256]{1,0:T(2,128)S(1)}, f32[2,256]{1,0:T(2,128)}, u32[]{:S(2)}) copy-start(f32[2,256]{1,0:T(2,128)} %param.21) | copy-start | bytes 6148
  131.6 12.6 %copy-start.12 = (f32[2,256]{1,0:T(2,128)S(1)}, f32[2,256]{1,0:T(2,128)}, u32[]{:S(2)}) copy-start(f32[2,256]{1,0:T(2,128)} %param.20) | copy-start | bytes 6148
  131.6 13.1 %copy-start.6 = (s32[1024]{0:T(1024)S(1)}, s32[1024]{0:T(1024)}, u32[]{:S(2)}) copy-start(s32[1024]{0:T(1024)} %pad_clamp_fusion.1) | copy-start | bytes 12292
  131.6 28.6 %copy-start.13 = (f32[2,8]{1,0:T(2,128)S(1)}, f32[2,8]{1,0:T(2,128)}, u32[]{:S(2)}) copy-start(f32[2,8]{1,0:T(2,128)} %param.23) | copy-start | bytes 196
  131.7 28.6 %copy-start.14 = (s32[2,8]{1,0:T(2,128)S(1)}, s32[2,8]{1,0:T(2,128)}, u32[]{:S(2)}) copy-start(s32[2,8]{1,0:T(2,128)} %param.22) | copy-start | bytes 196
  131.7 28.7 %copy-start.9 = (s32[1024]{0:T(1024)S(1)}, s32[1024]{0:T(1024)}, u32[]{:S(2)}) copy-start(s32[1024]{0:T(1024)} %constant.161) | copy-start | bytes 12292
  136.2 8.1 %all-to-all-start = ((f32[4,2,8,256]{3,2,1,0:T(8,128)}), f32[4,2,8,256]{3,2,1,0:T(8,128)S(1)}, u32[]{:S(2)}, u32[]{:S(2)}) async-start(f32[4,2,8,256]{3,2,1,0:T(8,128)} %fusion.21), calls=%async_computation | async-start | bytes 131072 | tf_op jit(solution)/shard_map/all_to_all | solution.py:98
  147.8 26.0 %all-to-all-start.1 = ((f32[128,2,560]{2,1,0:T(2,128)}), f32[128,2,560]{2,1,0:T(2,128)}, u32[]{:S(2)}, u32[]{:S(2)}) async-start(f32[128,2,560]{2,1,0:T(2,128)} %broadcast_in_dim.103), calls=%async_computation.1 | async-start | bytes 1310720 | tf_op jit(solution)/shard_map/all_to_all | solution.py:132
  160.4 19.6 %copy-start.3 = (f32[32,32]{1,0:T(8,128)S(1)}, f32[32,32]{1,0:T(8,128)}, u32[]{:S(2)}) copy-start(f32[32,32]{1,0:T(8,128)} %fusion.62) | copy-start | bytes 12292
  160.4 19.5 %copy-start.5 = (f32[32,32]{1,0:T(8,128)S(1)}, f32[32,32]{1,0:T(8,128)}, u32[]{:S(2)}) copy-start(f32[32,32]{1,0:T(8,128)} %fusion.61) | copy-start | bytes 12292
  166.6 17.8 %collective-permute-start.4 = (bf16[2,256,8,69]{1,2,3,0:T(8,128)(2,1)}, bf16[2,256,8,69]{1,2,3,0:T(8,128)(2,1)}, u32[]{:S(2)}, u32[]{:S(2)}) collective-permute-start(bf16[2,256,8,69]{1,2,3,0:T(8,128)(2,1)} %bitcast.117), channel_id=1, source_target_pairs={{0,96},{32,0},{64,32},{96,64},{1,97},{33,1},{65,33},{97,65},{2,98}... | collective-permute-start | bytes 1695752 | tf_op jit(solution)/shard_map/ppermute | solution.py:104
  169.3 15.0 %collective-permute-start.2 = (bf16[2,256,8,69]{1,2,3,0:T(8,128)(2,1)}, bf16[2,256,8,69]{1,2,3,0:T(8,128)(2,1)}, u32[]{:S(2)}, u32[]{:S(2)}) collective-permute-start(bf16[2,256,8,69]{1,2,3,0:T(8,128)(2,1)} %bitcast.119), channel_id=1, source_target_pairs={{0,32},{32,64},{64,96},{96,0},{1,33},{33,65},{65,97},{97,1},{2,34}... | collective-permute-start | bytes 1695752 | tf_op jit(solution)/shard_map/ppermute | solution.py:104
  170.9 23.4 %collective-permute-start.3 = (bf16[2,256,8,69]{1,2,3,0:T(8,128)(2,1)S(1)}, bf16[2,256,8,69]{1,2,3,0:T(8,128)(2,1)}, u32[]{:S(2)}, u32[]{:S(2)}) collective-permute-start(bf16[2,256,8,69]{1,2,3,0:T(8,128)(2,1)S(1)} %bitcast.120), channel_id=1, source_target_pairs={{0,64},{32,96},{64,0},{96,32},{1,65},{33,97},{65,1},{97,33},{2,66}... | collective-permute-start | bytes 1695752 | tf_op jit(solution)/shard_map/ppermute | solution.py:104

commit v16 on v12

--- a/solution.py
+++ b/solution.py
@@ -56,6 +56,7 @@
         rows_first = prior_samples
         height = rows_first.shape[0]
         padded = padded_2(rows_first, band_size)
+        channels = rows_first.shape[3]
         hidden_fields = jax.nn.silu(
             convolve(padded, conv1_weight) + conv1_bias
         ).astype(jnp.bfloat16)
@@ -67,7 +68,10 @@
         extended = jnp.where(outside, jnp.zeros_like(hidden_fields), hidden_fields)
         forecast = (
             rows_first.astype(jnp.float32)
-            + convolve(extended, conv2_weight)
+            + convolve(
+                extended,
+                jnp.pad(conv2_weight, ((0, 0), (0, 0), (0, 128 - channels), (0, 0))),
+            )[..., :channels]
             + conv2_bias
         ).astype(jnp.bfloat16)
         ensemble_part = forecast.shape[2]

time: 209 us -> 209 us (level)
  no operation moved by 1% of the time
where the time goes in v16:
time: 209 us; the launch traced here: 208 us
  matrix products  77.3 us (37%)
  local copies, waits for them, and re-layouts  50.3 us (24%)
  waiting for transfers between devices  39.6 us (19%)
  starting transfers between devices  27 us (13%)
  other arithmetic  7.12 us (3%)
  blocking collectives  5.9 us (3%)
    conv_general_dilated x2, matrix products, convolve(): lax.conv_general_dilated(wrapped, kernel, window_strides=(1, 1), padding=...  62.8 us
    ppermute x1, waiting for transfers between devices, padded_2(): lax.ppermute(cells, BAND, shift_pairs(band_size, 1))  26.8 us
    unnamed x43, local copies, waits for them, and re-layouts  15.3 us
    all_to_all x1, starting transfers between devices, on_device(): lax.all_to_all(jnp.broadcast_to(packed[None], (devices,) + packed.shape),...  11.9 us
    ppermute x3, waiting for transfers between devices, on_device(): lax.ppermute(outgoing, GRP, [(j, (j + step) % quarters) for j in range(qu...  9.58 us
    dot_general x1, matrix products, on_device(): jnp.einsum('ajnm,jailnc->mcil', weights, spread_out, precision=highest)  7.73 us
    ppermute x1, local copies, waits for them, and re-layouts, padded_2(): lax.ppermute(cells, BAND, shift_pairs(band_size, 1))  6.77 us
    ppermute x1, local copies, waits for them, and re-layouts, padded_2(): lax.ppermute(cells, BAND, shift_pairs(band_size, -1))  6.7 us
  transfers between devices with their start and end apart: 7, of which 4 were waited for; matrix products, arithmetic and copies ran while one was open for 20% of the time, Pallas kernels for 0%

profile of v16, /device:TPU:1, one launch (start us, length us, event | category | flops | bytes accessed | tf_op | source)
XLA Modules:
  0.0 207.6 jit_solution(6949044128184680884)
XLA Ops:
  0.0 2.4 %copy.136 = bf16[8,69,2,1024]{3,0,1,2:T(8,128)(2,1)S(1)} copy(bf16[8,69,2,1024]{3,2,1,0:T(2,128)(2,1)} %param.14) | data formatting | bytes 4521984 | tf_op jit(solution)/transpose | solution.py:218
  2.4 5.8 %collective-permute-start = (bf16[2,1024,8,69]{1,2,3,0:T(8,128)(2,1)S(1)}, bf16[2,1024,8,69]{1,2,3,0:T(8,128)(2,1)}, u32[]{:S(2)}, u32[]{:S(2)}) collective-permute-start(bf16[2,1024,8,69]{1,2,3,0:T(8,128)(2,1)S(1)} %bitcast.95), channel_id=1, source_target_pairs={{0,1},{1,2},{2,3},{3,4},{4,5},{5,6},{6,7},{7,8},{8,9},{9,10},{10,1... | collective-permute-start | bytes 6782984 | tf_op jit(solution)/shard_map/ppermute | solution.py:22
  8.2 1.3 collective-permute-start.1
  9.4 7.1 %copy.75 = bf16[8,69,2,1024]{1,0,3,2:T(8,128)(2,1)} copy(bf16[8,69,2,1024]{3,2,1,0:T(2,128)(2,1)} %param.14) | data formatting | bytes 4521984 | tf_op args[0]
  16.7 5.9 %all-gather.1 = s32[4,2,256]{2,1,0:T(2,128)S(1)} all-gather(s32[1,2,256]{2,1,0:T(2,128)S(1)} %bitcast.109), channel_id=2, replica_groups=mesh['y_lo'=2,'core'=2,'y_hi'=2,'x'=4,'z'=4] {'y_lo','core'}, dimensions={0}, use_global_device_ids=true | all-gather | bytes 10240 | tf_op jit(solution)/shard_map/all_gather | solution.py:82
  22.6 0.6 pad_clamp_fusion.1
  23.2 0.6 fusion.77
  23.8 0.6 fusion.76
  24.4 0.6 fusion.75
  25.0 0.7 compare_and_fusion
  25.7 0.5 fusion.82
  26.2 0.6 and_select_fusion.1
  26.8 0.9 fusion.45
  27.8 26.8 %collective-permute-done = bf16[2,1024,8,69]{1,2,3,0:T(8,128)(2,1)} collective-permute-done((bf16[2,1024,8,69]{1,2,3,0:T(8,128)(2,1)S(1)}, bf16[2,1024,8,69]{1,2,3,0:T(8,128)(2,1)}, u32[]{:S(2)}, u32[]{:S(2)}) %collective-permute-start) | collective-permute-done | bytes 2261024 | tf_op jit(solution)/shard_map/ppermute | solution.py:22
  54.6 6.8 %copy.78 = bf16[2,1024,8,69]{3,2,1,0:T(8,128)(2,1)} copy(bf16[2,1024,8,69]{1,2,3,0:T(8,128)(2,1)} %collective-permute-done) | data formatting | bytes 4521984 | tf_op jit(solution)/shard_map/ppermute | solution.py:22
  61.3 6.7 %copy.79 = bf16[2,1024,8,69]{3,2,1,0:T(8,128)(2,1)} copy(bf16[2,1024,8,69]{1,2,3,0:T(8,128)(2,1)} %collective-permute-done.1) | data formatting | bytes 4521984 | tf_op jit(solution)/shard_map/ppermute | solution.py:24
  68.1 39.8 %fusion.6 = bf16[4,1024,8,256]{3,2,1,0:T(8,128)(2,1)} fusion(f32[256]{0:T(256)S(1)} %copy-done.17, pred[4]{0:T(512)(128)(4,1)S(1)} %and_or_fusion, bf16[3,3,256,69]{2,3,1,0:T(8,128)(2,1)S(1)} %copy-done, bf16[2,1024,8,69]{3,2,1,0:T(8,128)(2,1)} %copy.79, bf16[2,1024,8,69]{3,2,1,0:T(8,128)(2,1)} %bitcast.94, bf16[2,1024,8,69]{3,2,1,0:T(8,128)(2,1)} %copy.78), kind=kOutput, calls=%fused_computation.10 | convolution fusion | flops 10504556544 | bytes 23879172 | tf_op jit(solution)/shard_map/conv_general_dilated | solution.py:32
  107.9 0.7 fusion.88
  108.7 22.9 %add_convert_fusion = bf16[2,1024,8,69]{3,2,1,0:T(8,128)(2,1)S(1)} fusion(f32[69]{0:T(128)S(1)} %copy-done.18, bf16[3,3,69,256]{3,2,1,0:T(8,128)(2,1)S(1)} %copy-done.16, bf16[4,1,8,256]{3,2,1,0:T(8,128)(2,1)S(1)} %get-tuple-element.6, bf16[4,1024,8,256]{3,2,1,0:T(8,128)(2,1)} %fusion.6, bf16[4,1,8,256]{3,2,1,0:T(8,128)(2,1)S(1)} %get-tuple-element.5, ...), kind=kOutput, calls=%fused_computation.27 | convolution fusion | flops 5230657536 | bytes 21650196 | tf_op jit(solution)/shard_map/conv_general_dilated | solution.py:32
  131.7 1.9 copy-done.1
  133.6 2.6 %fusion.21 = f32[4,2,8,256]{3,2,1,0:T(8,128)} fusion(f32[4,2,69,256]{3,2,1,0:T(8,128)S(1)} %copy-done.4, bf16[2,4,256,8,69]{4,3,2,1,0:T(8,128)(2,1)S(1)} %bitcast.92, s32[4,2,256]{2,1,0:T(2,128)S(1)} %copy-done.8), kind=kOutput, calls=%fused_computation.29 | convolution fusion | flops 581582848 | bytes 2899968 | tf_op jit(solution)/shard_map/iqlmc,qiol->qicmo/dot_general | solution.py:88
  136.2 4.8 %all-to-all-start = ((f32[4,2,8,256]{3,2,1,0:T(8,128)}), f32[4,2,8,256]{3,2,1,0:T(8,128)S(1)}, u32[]{:S(2)}, u32[]{:S(2)}) async-start(f32[4,2,8,256]{3,2,1,0:T(8,128)} %fusion.21), calls=%async_computation | async-start | bytes 131072 | tf_op jit(solution)/shard_map/all_to_all | solution.py:98
  141.0 0.6 pad_clamp_fusion
  141.6 2.7 %all-to-all-done = f32[4,2,8,256]{3,2,1,0:T(8,128)S(1)} async-done(((f32[4,2,8,256]{3,2,1,0:T(8,128)}), f32[4,2,8,256]{3,2,1,0:T(8,128)S(1)}, u32[]{:S(2)}, u32[]{:S(2)}) %all-to-all-start) | async-done | bytes 65568 | tf_op jit(solution)/shard_map/all_to_all | solution.py:98
  144.5 0.3 copy.105
  144.8 1.6 gather_fusion
  146.8 1.0 broadcast_in_dim.103
  147.8 11.9 %all-to-all-start.1 = ((f32[128,2,560]{2,1,0:T(2,128)}), f32[128,2,560]{2,1,0:T(2,128)}, u32[]{:S(2)}, u32[]{:S(2)}) async-start(f32[128,2,560]{2,1,0:T(2,128)} %broadcast_in_dim.103), calls=%async_computation.1 | async-start | bytes 1310720 | tf_op jit(solution)/shard_map/all_to_all | solution.py:132
  159.7 0.5 iota_compare_fusion.4
  160.4 3.5 %constant_dynamic-slice_fusion.3 = (bf16[2,1,256,8,69]{4,3,2,1,0:T(8,128)(2,1)S(1)}, bf16[2,1,256,8,69]{4,3,2,1,0:T(8,128)(2,1)S(1)}, bf16[2,1,256,8,69]{4,3,2,1,0:T(8,128)(2,1)S(1)}, bf16[2,1,256,8,69]{4,3,2,1,0:T(8,128)(2,1)}) fusion(bf16[2,4,256,8,69]{4,3,2,1,0:T(8,128)(2,1)} %bitcast.93, s32[]{:T(128)S(6)} %select_n.86, s32[]{:T(128)S(6)} %select_n.90, ...), kind=kLoop, calls=%fused_computation.126 | loop fusion | bytes 4522000 | tf_op jit(solution)/shard_map/jit(dynamic_index_in_dim)/dynamic_slice | solution.py:100
  163.8 2.7 %copy.110 = bf16[2,1,256,8,69]{2,3,4,1,0:T(8,128)(2,1)} copy(bf16[2,1,256,8,69]{4,3,2,1,0:T(8,128)(2,1)} %get-tuple-element.10) | data formatting | bytes 1130496
  166.5 1.1 collective-permute-start.4
  167.7 1.6 copy.108
  169.3 0.6 collective-permute-start.2
  169.9 0.9 copy.109
  170.9 1.5 collective-permute-start.3
  172.3 0.9 copy.107
  173.3 0.5 all-to-all-done.1
  173.8 1.5 reshape.166
  175.4 0.4 fusion.89
  176.0 2.8 %gather_fusion.1 = f32[1024,2]{1,0:T(8,128)S(1)} fusion(f32[2,560]{0,1:T(8,128)S(1)} %copy.89, s32[1024]{0:T(1024)S(1)} %broadcast_clamp_fusion), kind=kCustom, calls=%fused_computation.1 | custom fusion | bytes 20480 | tf_op jit(solution)/shard_map/gather | solution.py:142
  178.8 0.3 copy.106
  179.3 0.9 fusion.43
  180.2 0.7 broadcast_in_dim.106
  184.0 0.7 gather_fusion.2
  184.7 9.6 %collective-permute-done.3 = bf16[2,256,8,69]{1,2,3,0:T(8,128)(2,1)} collective-permute-done((bf16[2,256,8,69]{1,2,3,0:T(8,128)(2,1)S(1)}, bf16[2,256,8,69]{1,2,3,0:T(8,128)(2,1)}, u32[]{:S(2)}, u32[]{:S(2)}) %collective-permute-start.3) | collective-permute-done | bytes 565280 | tf_op jit(solution)/shard_map/ppermute | solution.py:104
  194.3 7.7 %fusion.29 = f32[32,69,2,256]{3,0,1,2:T(8,128)S(1)} fusion(pred[2,2]{0,1:T(4,128)(4,1)} %iota_compare_fusion.4, f32[2,4,8,32]{3,0,2,1:T(2,128)S(1)} %bitcast.104, pred[4,8]{1,0:T(4,128)(4,1)} %compare_and_fusion, bf16[1,2,256,8,69]{2,3,4,1,0:T(8,128)(2,1)} %bitcast.10, bf16[1,2,256,8,69]{2,3,4,1,0:T(8,128)(2,1)} %bitcast.8, ...), kind=kOutput, calls=%fused_computation.37 | convolution fusion | flops 875005952 | bytes 6791204 | tf_op jit(solution)/shard_map/ajnm,jailnc->mcil/dot_general | solution.py:182
  202.0 5.6 %copy.93 = f32[32,69,2,256]{3,2,1,0:T(2,128)} copy(f32[32,69,2,256]{3,0,1,2:T(8,128)S(1)} %fusion.29) | data formatting | bytes 9043968 | tf_op jit(solution)/shard_map/ajnm,jailnc->mcil/transpose | solution.py:182
  (75 shorter events, 4.3 us)
Async XLA Ops:
  0.0 68.0 %copy-start = (bf16[3,3,256,69]{2,3,1,0:T(8,128)(2,1)S(1)}, bf16[3,3,256,69]{2,3,1,0:T(8,128)(2,1)}, u32[]{:S(2)}) copy-start(bf16[3,3,256,69]{2,3,1,0:T(8,128)(2,1)} %param.15) | copy-start | bytes 953860
  0.0 22.6 %copy-start.10 = (s32[528]{0:T(1024)S(1)}, s32[528]{0:T(1024)}, u32[]{:S(2)}) copy-start(s32[528]{0:T(1024)} %constant.160) | copy-start | bytes 6340
  0.0 16.7 %copy-start.11 = (s32[2,256]{1,0:T(2,128)S(1)}, s32[2,256]{1,0:T(2,128)}, u32[]{:S(2)}) copy-start(s32[2,256]{1,0:T(2,128)} %param.19) | copy-start | bytes 6148
  2.4 52.2 %collective-permute-start = (bf16[2,1024,8,69]{1,2,3,0:T(8,128)(2,1)S(1)}, bf16[2,1024,8,69]{1,2,3,0:T(8,128)(2,1)}, u32[]{:S(2)}, u32[]{:S(2)}) collective-permute-start(bf16[2,1024,8,69]{1,2,3,0:T(8,128)(2,1)S(1)} %bitcast.95), channel_id=1, source_target_pairs={{0,1},{1,2},{2,3},{3,4},{4,5},{5,6},{6,7},{7,8},{8,9},{9,10},{10,1... | collective-permute-start | bytes 6782984 | tf_op jit(solution)/shard_map/ppermute | solution.py:22
  8.2 53.2 %collective-permute-start.1 = (bf16[2,1024,8,69]{1,2,3,0:T(8,128)(2,1)S(1)}, bf16[2,1024,8,69]{1,2,3,0:T(8,128)(2,1)}, u32[]{:S(2)}, u32[]{:S(2)}) collective-permute-start(bf16[2,1024,8,69]{1,2,3,0:T(8,128)(2,1)S(1)} %bitcast.96), channel_id=1, source_target_pairs={{1,0},{2,1},{3,2},{4,3},{5,4},{6,5},{7,6},{8,7},{9,8},{10,9},{11,1... | collective-permute-start | bytes 6782984 | tf_op jit(solution)/shard_map/ppermute | solution.py:24
  16.5 51.5 %copy-start.17 = (f32[256]{0:T(256)S(1)}, f32[256]{0:T(256)}, u32[]{:S(2)}) copy-start(f32[256]{0:T(256)} %param.16) | copy-start | bytes 3076
  68.1 40.6 %copy-start.2 = (bf16[8,69,2,1024]{1,0,3,2:T(8,128)(2,1)S(1)}, bf16[8,69,2,1024]{1,0,3,2:T(8,128)(2,1)}, u32[]{:S(2)}) copy-start(bf16[8,69,2,1024]{1,0,3,2:T(8,128)(2,1)} %copy.75) | copy-start | bytes 6782980
  68.1 40.6 %copy-start.16 = (bf16[3,3,69,256]{3,2,1,0:T(8,128)(2,1)S(1)}, bf16[3,3,69,256]{3,2,1,0:T(8,128)(2,1)}, u32[]{:S(2)}) copy-start(bf16[3,3,69,256]{3,2,1,0:T(8,128)(2,1)} %param.17) | copy-start | bytes 953860
  68.1 40.6 %copy-start.18 = (f32[69]{0:T(128)S(1)}, f32[69]{0:T(128)}, u32[]{:S(2)}) copy-start(f32[69]{0:T(128)} %param.18) | copy-start | bytes 832
  108.7 25.0 %copy-start.4 = (f32[4,2,69,256]{3,2,1,0:T(8,128)S(1)}, f32[4,2,69,256]{3,2,1,0:T(8,128)}, u32[]{:S(2)}) copy-start(f32[4,2,69,256]{3,2,1,0:T(8,128)} %fusion.45) | copy-start | bytes 1695748
  108.7 25.0 %copy-start.8 = (s32[4,2,256]{2,1,0:T(2,128)S(1)}, s32[4,2,256]{2,1,0:T(2,128)}, u32[]{:S(2)}) copy-start(s32[4,2,256]{2,1,0:T(2,128)} %get-tuple-element.11) | copy-start | bytes 24580
  131.6 2.0 copy-start.1
  131.6 9.4 %copy-start.15 = (s32[32]{0:T(128)S(1)}, s32[32]{0:T(128)}, u32[]{:S(2)}) copy-start(s32[32]{0:T(128)} %fusion.82) | copy-start | bytes 388
  131.6 12.6 %copy-start.7 = (f32[2,256]{1,0:T(2,128)S(1)}, f32[2,256]{1,0:T(2,128)}, u32[]{:S(2)}) copy-start(f32[2,256]{1,0:T(2,128)} %param.21) | copy-start | bytes 6148
  131.7 12.6 %copy-start.12 = (f32[2,256]{1,0:T(2,128)S(1)}, f32[2,256]{1,0:T(2,128)}, u32[]{:S(2)}) copy-start(f32[2,256]{1,0:T(2,128)} %param.20) | copy-start | bytes 6148
  131.7 13.1 %copy-start.6 = (s32[1024]{0:T(1024)S(1)}, s32[1024]{0:T(1024)}, u32[]{:S(2)}) copy-start(s32[1024]{0:T(1024)} %pad_clamp_fusion.1) | copy-start | bytes 12292
  131.7 28.6 %copy-start.13 = (f32[2,8]{1,0:T(2,128)S(1)}, f32[2,8]{1,0:T(2,128)}, u32[]{:S(2)}) copy-start(f32[2,8]{1,0:T(2,128)} %param.23) | copy-start | bytes 196
  131.7 28.6 %copy-start.14 = (s32[2,8]{1,0:T(2,128)S(1)}, s32[2,8]{1,0:T(2,128)}, u32[]{:S(2)}) copy-start(s32[2,8]{1,0:T(2,128)} %param.22) | copy-start | bytes 196
  131.7 28.6 %copy-start.9 = (s32[1024]{0:T(1024)S(1)}, s32[1024]{0:T(1024)}, u32[]{:S(2)}) copy-start(s32[1024]{0:T(1024)} %constant.161) | copy-start | bytes 12292
  136.2 8.1 %all-to-all-start = ((f32[4,2,8,256]{3,2,1,0:T(8,128)}), f32[4,2,8,256]{3,2,1,0:T(8,128)S(1)}, u32[]{:S(2)}, u32[]{:S(2)}) async-start(f32[4,2,8,256]{3,2,1,0:T(8,128)} %fusion.21), calls=%async_computation | async-start | bytes 131072 | tf_op jit(solution)/shard_map/all_to_all | solution.py:98
  147.8 26.0 %all-to-all-start.1 = ((f32[128,2,560]{2,1,0:T(2,128)}), f32[128,2,560]{2,1,0:T(2,128)}, u32[]{:S(2)}, u32[]{:S(2)}) async-start(f32[128,2,560]{2,1,0:T(2,128)} %broadcast_in_dim.103), calls=%async_computation.1 | async-start | bytes 1310720 | tf_op jit(solution)/shard_map/all_to_all | solution.py:132
  160.3 18.8 %copy-start.5 = (f32[32,32]{1,0:T(8,128)S(1)}, f32[32,32]{1,0:T(8,128)}, u32[]{:S(2)}) copy-start(f32[32,32]{1,0:T(8,128)} %fusion.77) | copy-start | bytes 12292
  160.4 19.0 %copy-start.3 = (f32[32,32]{1,0:T(8,128)S(1)}, f32[32,32]{1,0:T(8,128)}, u32[]{:S(2)}) copy-start(f32[32,32]{1,0:T(8,128)} %fusion.76) | copy-start | bytes 12292
  166.5 18.2 %collective-permute-start.4 = (bf16[2,256,8,69]{1,2,3,0:T(8,128)(2,1)}, bf16[2,256,8,69]{1,2,3,0:T(8,128)(2,1)}, u32[]{:S(2)}, u32[]{:S(2)}) collective-permute-start(bf16[2,256,8,69]{1,2,3,0:T(8,128)(2,1)} %bitcast.98), channel_id=1, source_target_pairs={{0,96},{32,0},{64,32},{96,64},{1,97},{33,1},{65,33},{97,65},{2,98}... | collective-permute-start | bytes 1695752 | tf_op jit(solution)/shard_map/ppermute | solution.py:104
  169.3 15.4 %collective-permute-start.2 = (bf16[2,256,8,69]{1,2,3,0:T(8,128)(2,1)}, bf16[2,256,8,69]{1,2,3,0:T(8,128)(2,1)}, u32[]{:S(2)}, u32[]{:S(2)}) collective-permute-start(bf16[2,256,8,69]{1,2,3,0:T(8,128)(2,1)} %bitcast.100), channel_id=1, source_target_pairs={{0,32},{32,64},{64,96},{96,0},{1,33},{33,65},{65,97},{97,1},{2,34}... | collective-permute-start | bytes 1695752 | tf_op jit(solution)/shard_map/ppermute | solution.py:104
  170.9 23.4 %collective-permute-start.3 = (bf16[2,256,8,69]{1,2,3,0:T(8,128)(2,1)S(1)}, bf16[2,256,8,69]{1,2,3,0:T(8,128)(2,1)}, u32[]{:S(2)}, u32[]{:S(2)}) collective-permute-start(bf16[2,256,8,69]{1,2,3,0:T(8,128)(2,1)S(1)} %bitcast.101), channel_id=1, source_target_pairs={{0,64},{32,96},{64,0},{96,32},{1,65},{33,97},{65,1},{97,33},{2,66}... | collective-permute-start | bytes 1695752 | tf_op jit(solution)/shard_map/ppermute | solution.py:104

commit v17 on v10

--- a/solution.py
+++ b/solution.py
@@ -170,7 +170,7 @@
             0.0,
         )
         analysed = jnp.einsum(
-            "ajnm,jailnc->mcil", weights, spread_out, precision=highest
+            "ajnm,jailnc->mcil", weights, spread_out, precision=lax.Precision.HIGH
         )
         return analysed
 

time: 209 us -> 205 us (0.981)
  matrix products: 77 us -> 73.2 us
    dot_general x1, matrix products: 7.73 us -> 3.91 us  [on_device(): jnp.einsum('ajnm,jailnc->mcil', weights, spread_out, precision=lax.Precis...]
  transfers between devices with their start and end apart: 7 -> 7, of which waited for: 4 -> 4; matrix products, arithmetic and copies ran while one was open for 19% -> 20% of each run, Pallas kernels for 0% -> 0%
where the time goes in v17:
time: 205 us; the launch traced here: 204 us
  matrix products  73.2 us (36%)
  local copies, waits for them, and re-layouts  49.6 us (24%)
  waiting for transfers between devices  39.9 us (19%)
  starting transfers between devices  27 us (13%)
  other arithmetic  7.77 us (4%)
  blocking collectives  5.9 us (3%)
    conv_general_dilated x2, matrix products, convolve(): lax.conv_general_dilated(wrapped, kernel, window_strides=(1, 1), padding=...  62.7 us
    ppermute x1, waiting for transfers between devices, padded_2(): lax.ppermute(cells, BAND, shift_pairs(band_size, 1))  26.8 us
    unnamed x43, local copies, waits for them, and re-layouts  15.3 us
    all_to_all x1, starting transfers between devices, on_device(): lax.all_to_all(jnp.broadcast_to(packed[None], (devices,) + packed.shape),...  11.9 us
    ppermute x3, waiting for transfers between devices, on_device(): lax.ppermute(outgoing, GRP, [(j, (j + step) % quarters) for j in range(qu...  9.93 us
    ppermute x1, local copies, waits for them, and re-layouts, padded_2(): lax.ppermute(cells, BAND, shift_pairs(band_size, 1))  6.76 us
    ppermute x1, local copies, waits for them, and re-layouts, padded_2(): lax.ppermute(cells, BAND, shift_pairs(band_size, -1))  6.7 us
    all_gather x1, blocking collectives, on_device(): row_index = lax.all_gather(obs_index, GRP, axis=0, tiled=False)  5.9 us
  transfers between devices with their start and end apart: 7, of which 4 were waited for; matrix products, arithmetic and copies ran while one was open for 20% of the time, Pallas kernels for 0%

profile of v17, /device:TPU:1, one launch (start us, length us, event | category | flops | bytes accessed | tf_op | source)
XLA Modules:
  0.0 203.8 jit_solution(1856137423397304332)
XLA Ops:
  0.0 2.4 %copy.136 = bf16[8,69,2,1024]{3,0,1,2:T(8,128)(2,1)S(1)} copy(bf16[8,69,2,1024]{3,2,1,0:T(2,128)(2,1)} %param.14) | data formatting | bytes 4521984 | tf_op jit(solution)/transpose | solution.py:208
  2.4 5.8 %collective-permute-start = (bf16[2,1024,8,69]{1,2,3,0:T(8,128)(2,1)S(1)}, bf16[2,1024,8,69]{1,2,3,0:T(8,128)(2,1)}, u32[]{:S(2)}, u32[]{:S(2)}) collective-permute-start(bf16[2,1024,8,69]{1,2,3,0:T(8,128)(2,1)S(1)} %bitcast.114), channel_id=1, source_target_pairs={{0,1},{1,2},{2,3},{3,4},{4,5},{5,6},{6,7},{7,8},{8,9},{9,10},{10,1... | collective-permute-start | bytes 6782984 | tf_op jit(solution)/shard_map/ppermute | solution.py:22
  8.2 1.3 collective-permute-start.1
  9.4 7.1 %copy.75 = bf16[8,69,2,1024]{1,0,3,2:T(8,128)(2,1)} copy(bf16[8,69,2,1024]{3,2,1,0:T(2,128)(2,1)} %param.14) | data formatting | bytes 4521984 | tf_op args[0]
  16.7 5.9 %all-gather.1 = s32[4,2,256]{2,1,0:T(2,128)S(1)} all-gather(s32[1,2,256]{2,1,0:T(2,128)S(1)} %bitcast.128), channel_id=2, replica_groups=mesh['y_lo'=2,'core'=2,'y_hi'=2,'x'=4,'z'=4] {'y_lo','core'}, dimensions={0}, use_global_device_ids=true | all-gather | bytes 10240 | tf_op jit(solution)/shard_map/all_gather | solution.py:78
  22.6 0.6 pad_clamp_fusion.1
  23.2 0.6 fusion.63
  23.8 0.6 fusion.62
  24.4 0.6 fusion.61
  25.0 0.6 compare_and_fusion
  25.6 0.6 fusion.69
  26.2 0.6 and_select_fusion.1
  26.8 0.9 fusion.45
  27.7 26.8 %collective-permute-done = bf16[2,1024,8,69]{1,2,3,0:T(8,128)(2,1)} collective-permute-done((bf16[2,1024,8,69]{1,2,3,0:T(8,128)(2,1)S(1)}, bf16[2,1024,8,69]{1,2,3,0:T(8,128)(2,1)}, u32[]{:S(2)}, u32[]{:S(2)}) %collective-permute-start) | collective-permute-done | bytes 2261024 | tf_op jit(solution)/shard_map/ppermute | solution.py:22
  54.6 6.8 %copy.78 = bf16[2,1024,8,69]{3,2,1,0:T(8,128)(2,1)} copy(bf16[2,1024,8,69]{1,2,3,0:T(8,128)(2,1)} %collective-permute-done) | data formatting | bytes 4521984 | tf_op jit(solution)/shard_map/ppermute | solution.py:22
  61.3 6.7 %copy.79 = bf16[2,1024,8,69]{3,2,1,0:T(8,128)(2,1)} copy(bf16[2,1024,8,69]{1,2,3,0:T(8,128)(2,1)} %collective-permute-done.1) | data formatting | bytes 4521984 | tf_op jit(solution)/shard_map/ppermute | solution.py:24
  68.1 39.8 %fusion.6 = bf16[4,1024,8,256]{3,2,1,0:T(8,128)(2,1)} fusion(f32[256]{0:T(256)S(1)} %copy-done.17, pred[4]{0:T(512)(128)(4,1)S(1)} %and_or_fusion, bf16[3,3,256,69]{2,3,1,0:T(8,128)(2,1)S(1)} %copy-done, bf16[2,1024,8,69]{3,2,1,0:T(8,128)(2,1)} %copy.79, bf16[2,1024,8,69]{3,2,1,0:T(8,128)(2,1)} %bitcast.113, bf16[2,1024,8,69]{3,2,1,0:T(8,128)(2,1)} %copy.78), kind=kOutput, calls=%fused_computation.10 | convolution fusion | flops 10504556544 | bytes 23879172 | tf_op jit(solution)/shard_map/conv_general_dilated | solution.py:32
  107.9 0.7 fusion.74
  108.7 22.9 %add_convert_fusion = bf16[2,1024,8,69]{3,2,1,0:T(8,128)(2,1)S(1)} fusion(f32[69]{0:T(128)S(1)} %copy-done.18, bf16[3,3,69,256]{3,2,1,0:T(8,128)(2,1)S(1)} %copy-done.16, bf16[4,1,8,256]{3,2,1,0:T(8,128)(2,1)S(1)} %get-tuple-element.8, bf16[4,1024,8,256]{3,2,1,0:T(8,128)(2,1)} %fusion.6, bf16[4,1,8,256]{3,2,1,0:T(8,128)(2,1)S(1)} %get-tuple-element.7, ...), kind=kOutput, calls=%fused_computation.27 | convolution fusion | flops 5230657536 | bytes 21650196 | tf_op jit(solution)/shard_map/conv_general_dilated | solution.py:32
  131.7 1.9 copy-done.1
  133.6 2.5 %fusion.21 = f32[4,2,8,256]{3,2,1,0:T(8,128)} fusion(f32[4,2,69,256]{3,2,1,0:T(8,128)S(1)} %copy-done.4, bf16[2,4,256,8,69]{4,3,2,1,0:T(8,128)(2,1)S(1)} %bitcast.111, s32[4,2,256]{2,1,0:T(2,128)S(1)} %copy-done.8), kind=kOutput, calls=%fused_computation.29 | convolution fusion | flops 581582848 | bytes 2899968 | tf_op jit(solution)/shard_map/iqlmc,qiol->qicmo/dot_general | solution.py:84
  136.2 4.8 %all-to-all-start = ((f32[4,2,8,256]{3,2,1,0:T(8,128)}), f32[4,2,8,256]{3,2,1,0:T(8,128)S(1)}, u32[]{:S(2)}, u32[]{:S(2)}) async-start(f32[4,2,8,256]{3,2,1,0:T(8,128)} %fusion.21), calls=%async_computation | async-start | bytes 131072 | tf_op jit(solution)/shard_map/all_to_all | solution.py:94
  141.0 0.6 pad_clamp_fusion
  141.5 2.7 %all-to-all-done = f32[4,2,8,256]{3,2,1,0:T(8,128)S(1)} async-done(((f32[4,2,8,256]{3,2,1,0:T(8,128)}), f32[4,2,8,256]{3,2,1,0:T(8,128)S(1)}, u32[]{:S(2)}, u32[]{:S(2)}) %all-to-all-start) | async-done | bytes 65568 | tf_op jit(solution)/shard_map/all_to_all | solution.py:94
  144.5 0.3 copy.105
  144.7 1.6 gather_fusion
  146.7 1.0 broadcast_in_dim.103
  147.8 11.9 %all-to-all-start.1 = ((f32[128,2,560]{2,1,0:T(2,128)}), f32[128,2,560]{2,1,0:T(2,128)}, u32[]{:S(2)}, u32[]{:S(2)}) async-start(f32[128,2,560]{2,1,0:T(2,128)} %broadcast_in_dim.103), calls=%async_computation.1 | async-start | bytes 1310720 | tf_op jit(solution)/shard_map/all_to_all | solution.py:128
  159.7 0.6 iota_compare_fusion.4
  160.4 3.5 %constant_dynamic-slice_fusion.3 = (bf16[2,1,256,8,69]{4,3,2,1,0:T(8,128)(2,1)S(1)}, bf16[2,1,256,8,69]{4,3,2,1,0:T(8,128)(2,1)S(1)}, bf16[2,1,256,8,69]{4,3,2,1,0:T(8,128)(2,1)S(1)}, bf16[2,1,256,8,69]{4,3,2,1,0:T(8,128)(2,1)}) fusion(bf16[2,4,256,8,69]{4,3,2,1,0:T(8,128)(2,1)} %bitcast.112, s32[]{:T(128)S(6)} %select_n.86, s32[]{:T(128)S(6)} %select_n.90, ...), kind=kLoop, calls=%fused_computation.113 | loop fusion | bytes 4522000 | tf_op jit(solution)/shard_map/jit(dynamic_index_in_dim)/dynamic_slice | solution.py:96
  163.9 2.7 %copy.110 = bf16[2,1,256,8,69]{2,3,4,1,0:T(8,128)(2,1)} copy(bf16[2,1,256,8,69]{4,3,2,1,0:T(8,128)(2,1)} %get-tuple-element.12) | data formatting | bytes 1130496
  166.6 1.1 collective-permute-start.4
  167.7 1.6 copy.108
  169.3 0.6 collective-permute-start.2
  169.9 0.9 copy.109
  170.9 1.5 collective-permute-start.3
  172.4 0.9 copy.107
  173.3 0.5 all-to-all-done.1
  173.8 1.5 reshape.166
  175.3 0.4 fusion.75
  176.0 2.8 %gather_fusion.1 = f32[1024,2]{1,0:T(8,128)S(1)} fusion(f32[2,560]{0,1:T(8,128)S(1)} %copy.89, s32[1024]{0:T(1024)S(1)} %broadcast_clamp_fusion), kind=kCustom, calls=%fused_computation.1 | custom fusion | bytes 20480 | tf_op jit(solution)/shard_map/gather | solution.py:138
  178.8 0.3 copy.106
  179.1 0.8 multiply_reduce_fusion
  179.9 0.2 fusion.43
  183.6 0.7 gather_fusion.2
  184.4 9.9 %collective-permute-done.3 = bf16[2,256,8,69]{1,2,3,0:T(8,128)(2,1)} collective-permute-done((bf16[2,256,8,69]{1,2,3,0:T(8,128)(2,1)S(1)}, bf16[2,256,8,69]{1,2,3,0:T(8,128)(2,1)}, u32[]{:S(2)}, u32[]{:S(2)}) %collective-permute-start.3) | collective-permute-done | bytes 565280 | tf_op jit(solution)/shard_map/ppermute | solution.py:100
  194.3 3.9 %fusion.29 = f32[32,69,2,256]{3,0,1,2:T(8,128)S(1)} fusion(pred[2,2]{0,1:T(4,128)(4,1)} %iota_compare_fusion.4, f32[2,4,8,32]{3,0,2,1:T(2,128)S(1)} %bitcast.123, pred[4,8]{1,0:T(4,128)(4,1)} %compare_and_fusion, bf16[1,2,256,8,69]{2,3,4,1,0:T(8,128)(2,1)} %bitcast.10, bf16[1,2,256,8,69]{2,3,4,1,0:T(8,128)(2,1)} %bitcast.8, ...), kind=kOutput, calls=%fused_computation.37 | convolution fusion | flops 440895488 | bytes 6791204 | tf_op jit(solution)/shard_map/ajnm,jailnc->mcil/dot_general | solution.py:172
  198.2 5.6 %copy.93 = f32[32,69,2,256]{3,2,1,0:T(2,128)} copy(f32[32,69,2,256]{3,0,1,2:T(8,128)S(1)} %fusion.29) | data formatting | bytes 9043968 | tf_op jit(solution)/shard_map/ajnm,jailnc->mcil/transpose | solution.py:172
  (78 shorter events, 4.5 us)
Async XLA Ops:
  0.0 68.0 %copy-start = (bf16[3,3,256,69]{2,3,1,0:T(8,128)(2,1)S(1)}, bf16[3,3,256,69]{2,3,1,0:T(8,128)(2,1)}, u32[]{:S(2)}) copy-start(bf16[3,3,256,69]{2,3,1,0:T(8,128)(2,1)} %param.15) | copy-start | bytes 953860
  0.0 22.6 %copy-start.10 = (s32[528]{0:T(1024)S(1)}, s32[528]{0:T(1024)}, u32[]{:S(2)}) copy-start(s32[528]{0:T(1024)} %constant.160) | copy-start | bytes 6340
  0.0 16.7 %copy-start.11 = (s32[2,256]{1,0:T(2,128)S(1)}, s32[2,256]{1,0:T(2,128)}, u32[]{:S(2)}) copy-start(s32[2,256]{1,0:T(2,128)} %param.19) | copy-start | bytes 6148
  2.4 52.2 %collective-permute-start = (bf16[2,1024,8,69]{1,2,3,0:T(8,128)(2,1)S(1)}, bf16[2,1024,8,69]{1,2,3,0:T(8,128)(2,1)}, u32[]{:S(2)}, u32[]{:S(2)}) collective-permute-start(bf16[2,1024,8,69]{1,2,3,0:T(8,128)(2,1)S(1)} %bitcast.114), channel_id=1, source_target_pairs={{0,1},{1,2},{2,3},{3,4},{4,5},{5,6},{6,7},{7,8},{8,9},{9,10},{10,1... | collective-permute-start | bytes 6782984 | tf_op jit(solution)/shard_map/ppermute | solution.py:22
  8.2 53.2 %collective-permute-start.1 = (bf16[2,1024,8,69]{1,2,3,0:T(8,128)(2,1)S(1)}, bf16[2,1024,8,69]{1,2,3,0:T(8,128)(2,1)}, u32[]{:S(2)}, u32[]{:S(2)}) collective-permute-start(bf16[2,1024,8,69]{1,2,3,0:T(8,128)(2,1)S(1)} %bitcast.115), channel_id=1, source_target_pairs={{1,0},{2,1},{3,2},{4,3},{5,4},{6,5},{7,6},{8,7},{9,8},{10,9},{11,1... | collective-permute-start | bytes 6782984 | tf_op jit(solution)/shard_map/ppermute | solution.py:24
  16.5 51.5 %copy-start.17 = (f32[256]{0:T(256)S(1)}, f32[256]{0:T(256)}, u32[]{:S(2)}) copy-start(f32[256]{0:T(256)} %param.16) | copy-start | bytes 3076
  68.0 40.6 %copy-start.2 = (bf16[8,69,2,1024]{1,0,3,2:T(8,128)(2,1)S(1)}, bf16[8,69,2,1024]{1,0,3,2:T(8,128)(2,1)}, u32[]{:S(2)}) copy-start(bf16[8,69,2,1024]{1,0,3,2:T(8,128)(2,1)} %copy.75) | copy-start | bytes 6782980
  68.0 40.6 %copy-start.16 = (bf16[3,3,69,256]{3,2,1,0:T(8,128)(2,1)S(1)}, bf16[3,3,69,256]{3,2,1,0:T(8,128)(2,1)}, u32[]{:S(2)}) copy-start(bf16[3,3,69,256]{3,2,1,0:T(8,128)(2,1)} %param.17) | copy-start | bytes 953860
  68.1 40.6 %copy-start.18 = (f32[69]{0:T(128)S(1)}, f32[69]{0:T(128)}, u32[]{:S(2)}) copy-start(f32[69]{0:T(128)} %param.18) | copy-start | bytes 832
  108.6 25.0 %copy-start.4 = (f32[4,2,69,256]{3,2,1,0:T(8,128)S(1)}, f32[4,2,69,256]{3,2,1,0:T(8,128)}, u32[]{:S(2)}) copy-start(f32[4,2,69,256]{3,2,1,0:T(8,128)} %fusion.45) | copy-start | bytes 1695748
  108.6 25.0 %copy-start.8 = (s32[4,2,256]{2,1,0:T(2,128)S(1)}, s32[4,2,256]{2,1,0:T(2,128)}, u32[]{:S(2)}) copy-start(s32[4,2,256]{2,1,0:T(2,128)} %get-tuple-element.13) | copy-start | bytes 24580
  131.6 2.0 copy-start.1
  131.6 9.4 %copy-start.15 = (s32[32]{0:T(128)S(1)}, s32[32]{0:T(128)}, u32[]{:S(2)}) copy-start(s32[32]{0:T(128)} %fusion.69) | copy-start | bytes 388
  131.6 12.6 %copy-start.7 = (f32[2,256]{1,0:T(2,128)S(1)}, f32[2,256]{1,0:T(2,128)}, u32[]{:S(2)}) copy-start(f32[2,256]{1,0:T(2,128)} %param.21) | copy-start | bytes 6148
  131.6 12.6 %copy-start.12 = (f32[2,256]{1,0:T(2,128)S(1)}, f32[2,256]{1,0:T(2,128)}, u32[]{:S(2)}) copy-start(f32[2,256]{1,0:T(2,128)} %param.20) | copy-start | bytes 6148
  131.6 13.1 %copy-start.6 = (s32[1024]{0:T(1024)S(1)}, s32[1024]{0:T(1024)}, u32[]{:S(2)}) copy-start(s32[1024]{0:T(1024)} %pad_clamp_fusion.1) | copy-start | bytes 12292
  131.6 28.6 %copy-start.13 = (f32[2,8]{1,0:T(2,128)S(1)}, f32[2,8]{1,0:T(2,128)}, u32[]{:S(2)}) copy-start(f32[2,8]{1,0:T(2,128)} %param.23) | copy-start | bytes 196
  131.7 28.6 %copy-start.14 = (s32[2,8]{1,0:T(2,128)S(1)}, s32[2,8]{1,0:T(2,128)}, u32[]{:S(2)}) copy-start(s32[2,8]{1,0:T(2,128)} %param.22) | copy-start | bytes 196
  131.7 28.7 %copy-start.9 = (s32[1024]{0:T(1024)S(1)}, s32[1024]{0:T(1024)}, u32[]{:S(2)}) copy-start(s32[1024]{0:T(1024)} %constant.161) | copy-start | bytes 12292
  136.2 8.1 %all-to-all-start = ((f32[4,2,8,256]{3,2,1,0:T(8,128)}), f32[4,2,8,256]{3,2,1,0:T(8,128)S(1)}, u32[]{:S(2)}, u32[]{:S(2)}) async-start(f32[4,2,8,256]{3,2,1,0:T(8,128)} %fusion.21), calls=%async_computation | async-start | bytes 131072 | tf_op jit(solution)/shard_map/all_to_all | solution.py:94
  147.8 26.0 %all-to-all-start.1 = ((f32[128,2,560]{2,1,0:T(2,128)}), f32[128,2,560]{2,1,0:T(2,128)}, u32[]{:S(2)}, u32[]{:S(2)}) async-start(f32[128,2,560]{2,1,0:T(2,128)} %broadcast_in_dim.103), calls=%async_computation.1 | async-start | bytes 1310720 | tf_op jit(solution)/shard_map/all_to_all | solution.py:128
  160.4 19.6 %copy-start.3 = (f32[32,32]{1,0:T(8,128)S(1)}, f32[32,32]{1,0:T(8,128)}, u32[]{:S(2)}) copy-start(f32[32,32]{1,0:T(8,128)} %fusion.62) | copy-start | bytes 12292
  160.4 19.5 %copy-start.5 = (f32[32,32]{1,0:T(8,128)S(1)}, f32[32,32]{1,0:T(8,128)}, u32[]{:S(2)}) copy-start(f32[32,32]{1,0:T(8,128)} %fusion.61) | copy-start | bytes 12292
  166.6 17.8 %collective-permute-start.4 = (bf16[2,256,8,69]{1,2,3,0:T(8,128)(2,1)}, bf16[2,256,8,69]{1,2,3,0:T(8,128)(2,1)}, u32[]{:S(2)}, u32[]{:S(2)}) collective-permute-start(bf16[2,256,8,69]{1,2,3,0:T(8,128)(2,1)} %bitcast.117), channel_id=1, source_target_pairs={{0,96},{32,0},{64,32},{96,64},{1,97},{33,1},{65,33},{97,65},{2,98}... | collective-permute-start | bytes 1695752 | tf_op jit(solution)/shard_map/ppermute | solution.py:100
  169.3 15.0 %collective-permute-start.2 = (bf16[2,256,8,69]{1,2,3,0:T(8,128)(2,1)}, bf16[2,256,8,69]{1,2,3,0:T(8,128)(2,1)}, u32[]{:S(2)}, u32[]{:S(2)}) collective-permute-start(bf16[2,256,8,69]{1,2,3,0:T(8,128)(2,1)} %bitcast.119), channel_id=1, source_target_pairs={{0,32},{32,64},{64,96},{96,0},{1,33},{33,65},{65,97},{97,1},{2,34}... | collective-permute-start | bytes 1695752 | tf_op jit(solution)/shard_map/ppermute | solution.py:100
  170.9 23.4 %collective-permute-start.3 = (bf16[2,256,8,69]{1,2,3,0:T(8,128)(2,1)S(1)}, bf16[2,256,8,69]{1,2,3,0:T(8,128)(2,1)}, u32[]{:S(2)}, u32[]{:S(2)}) collective-permute-start(bf16[2,256,8,69]{1,2,3,0:T(8,128)(2,1)S(1)} %bitcast.120), channel_id=1, source_target_pairs={{0,64},{32,96},{64,0},{96,32},{1,65},{33,97},{65,1},{97,33},{2,66}... | collective-permute-start | bytes 1695752 | tf_op jit(solution)/shard_map/ppermute | solution.py:100

commit v18 on v17

--- a/solution.py
+++ b/solution.py
@@ -52,7 +52,7 @@
         neighbours,
         loc_weight,
     ):
-        highest = lax.Precision.HIGHEST
+        highest = lax.Precision.HIGH
         rows_first = prior_samples
         height = rows_first.shape[0]
         padded = padded_2(rows_first, band_size)

time: 205 us -> 205 us (level)
  no operation moved by 1% of the time
where the time goes in v18:
time: 205 us; the launch traced here: 204 us
  matrix products  72.5 us (35%)
  local copies, waits for them, and re-layouts  49.6 us (24%)
  waiting for transfers between devices  40.6 us (20%)
  starting transfers between devices  27 us (13%)
  other arithmetic  7.76 us (4%)
  blocking collectives  5.9 us (3%)
    conv_general_dilated x2, matrix products, convolve(): lax.conv_general_dilated(wrapped, kernel, window_strides=(1, 1), padding=...  62.7 us
    ppermute x1, waiting for transfers between devices, padded_2(): lax.ppermute(cells, BAND, shift_pairs(band_size, 1))  26.8 us
    unnamed x43, local copies, waits for them, and re-layouts  15.3 us
    all_to_all x1, starting transfers between devices, on_device(): lax.all_to_all(jnp.broadcast_to(packed[None], (devices,) + packed.shape),...  11.9 us
    ppermute x3, waiting for transfers between devices, on_device(): lax.ppermute(outgoing, GRP, [(j, (j + step) % quarters) for j in range(qu...  10.6 us
    ppermute x1, local copies, waits for them, and re-layouts, padded_2(): lax.ppermute(cells, BAND, shift_pairs(band_size, 1))  6.76 us
    ppermute x1, local copies, waits for them, and re-layouts, padded_2(): lax.ppermute(cells, BAND, shift_pairs(band_size, -1))  6.7 us
    all_gather x1, blocking collectives, on_device(): row_index = lax.all_gather(obs_index, GRP, axis=0, tiled=False)  5.9 us
  transfers between devices with their start and end apart: 7, of which 4 were waited for; matrix products, arithmetic and copies ran while one was open for 20% of the time, Pallas kernels for 0%

profile of v18, /device:TPU:1, one launch (start us, length us, event | category | flops | bytes accessed | tf_op | source)
XLA Modules:
  0.0 203.8 jit_solution(11577029568538490792)
XLA Ops:
  0.0 2.4 %copy.136 = bf16[8,69,2,1024]{3,0,1,2:T(8,128)(2,1)S(1)} copy(bf16[8,69,2,1024]{3,2,1,0:T(2,128)(2,1)} %param.14) | data formatting | bytes 4521984 | tf_op jit(solution)/transpose | solution.py:208
  2.4 5.8 %collective-permute-start = (bf16[2,1024,8,69]{1,2,3,0:T(8,128)(2,1)S(1)}, bf16[2,1024,8,69]{1,2,3,0:T(8,128)(2,1)}, u32[]{:S(2)}, u32[]{:S(2)}) collective-permute-start(bf16[2,1024,8,69]{1,2,3,0:T(8,128)(2,1)S(1)} %bitcast.114), channel_id=1, source_target_pairs={{0,1},{1,2},{2,3},{3,4},{4,5},{5,6},{6,7},{7,8},{8,9},{9,10},{10,1... | collective-permute-start | bytes 6782984 | tf_op jit(solution)/shard_map/ppermute | solution.py:22
  8.2 1.3 collective-permute-start.1
  9.4 7.1 %copy.75 = bf16[8,69,2,1024]{1,0,3,2:T(8,128)(2,1)} copy(bf16[8,69,2,1024]{3,2,1,0:T(2,128)(2,1)} %param.14) | data formatting | bytes 4521984 | tf_op args[0]
  16.7 5.9 %all-gather.1 = s32[4,2,256]{2,1,0:T(2,128)S(1)} all-gather(s32[1,2,256]{2,1,0:T(2,128)S(1)} %bitcast.128), channel_id=2, replica_groups=mesh['y_lo'=2,'core'=2,'y_hi'=2,'x'=4,'z'=4] {'y_lo','core'}, dimensions={0}, use_global_device_ids=true | all-gather | bytes 10240 | tf_op jit(solution)/shard_map/all_gather | solution.py:78
  22.6 0.6 pad_clamp_fusion.1
  23.2 0.6 fusion.63
  23.8 0.6 fusion.62
  24.4 0.6 fusion.61
  25.0 0.6 compare_and_fusion
  25.6 0.6 fusion.69
  26.2 0.6 and_select_fusion.1
  26.8 0.9 fusion.45
  27.7 26.8 %collective-permute-done = bf16[2,1024,8,69]{1,2,3,0:T(8,128)(2,1)} collective-permute-done((bf16[2,1024,8,69]{1,2,3,0:T(8,128)(2,1)S(1)}, bf16[2,1024,8,69]{1,2,3,0:T(8,128)(2,1)}, u32[]{:S(2)}, u32[]{:S(2)}) %collective-permute-start) | collective-permute-done | bytes 2261024 | tf_op jit(solution)/shard_map/ppermute | solution.py:22
  54.6 6.8 %copy.78 = bf16[2,1024,8,69]{3,2,1,0:T(8,128)(2,1)} copy(bf16[2,1024,8,69]{1,2,3,0:T(8,128)(2,1)} %collective-permute-done) | data formatting | bytes 4521984 | tf_op jit(solution)/shard_map/ppermute | solution.py:22
  61.3 6.7 %copy.79 = bf16[2,1024,8,69]{3,2,1,0:T(8,128)(2,1)} copy(bf16[2,1024,8,69]{1,2,3,0:T(8,128)(2,1)} %collective-permute-done.1) | data formatting | bytes 4521984 | tf_op jit(solution)/shard_map/ppermute | solution.py:24
  68.1 39.8 %fusion.6 = bf16[4,1024,8,256]{3,2,1,0:T(8,128)(2,1)} fusion(f32[256]{0:T(256)S(1)} %copy-done.17, pred[4]{0:T(512)(128)(4,1)S(1)} %and_or_fusion, bf16[3,3,256,69]{2,3,1,0:T(8,128)(2,1)S(1)} %copy-done, bf16[2,1024,8,69]{3,2,1,0:T(8,128)(2,1)} %copy.79, bf16[2,1024,8,69]{3,2,1,0:T(8,128)(2,1)} %bitcast.113, bf16[2,1024,8,69]{3,2,1,0:T(8,128)(2,1)} %copy.78), kind=kOutput, calls=%fused_computation.10 | convolution fusion | flops 10504556544 | bytes 23879172 | tf_op jit(solution)/shard_map/conv_general_dilated | solution.py:32
  107.9 0.7 fusion.74
  108.7 22.9 %add_convert_fusion = bf16[2,1024,8,69]{3,2,1,0:T(8,128)(2,1)S(1)} fusion(f32[69]{0:T(128)S(1)} %copy-done.18, bf16[3,3,69,256]{3,2,1,0:T(8,128)(2,1)S(1)} %copy-done.16, bf16[4,1,8,256]{3,2,1,0:T(8,128)(2,1)S(1)} %get-tuple-element.8, bf16[4,1024,8,256]{3,2,1,0:T(8,128)(2,1)} %fusion.6, bf16[4,1,8,256]{3,2,1,0:T(8,128)(2,1)S(1)} %get-tuple-element.7, ...), kind=kOutput, calls=%fused_computation.27 | convolution fusion | flops 5230657536 | bytes 21650196 | tf_op jit(solution)/shard_map/conv_general_dilated | solution.py:32
  131.7 1.9 copy-done.1
  133.6 2.5 %fusion.21 = f32[4,2,8,256]{3,2,1,0:T(8,128)} fusion(f32[4,2,69,256]{3,2,1,0:T(8,128)S(1)} %copy-done.4, bf16[2,4,256,8,69]{4,3,2,1,0:T(8,128)(2,1)S(1)} %bitcast.111, s32[4,2,256]{2,1,0:T(2,128)S(1)} %copy-done.8), kind=kOutput, calls=%fused_computation.29 | convolution fusion | flops 581582848 | bytes 2899968 | tf_op jit(solution)/shard_map/iqlmc,qiol->qicmo/dot_general | solution.py:84
  136.2 4.8 %all-to-all-start = ((f32[4,2,8,256]{3,2,1,0:T(8,128)}), f32[4,2,8,256]{3,2,1,0:T(8,128)S(1)}, u32[]{:S(2)}, u32[]{:S(2)}) async-start(f32[4,2,8,256]{3,2,1,0:T(8,128)} %fusion.21), calls=%async_computation | async-start | bytes 131072 | tf_op jit(solution)/shard_map/all_to_all | solution.py:94
  141.0 0.6 pad_clamp_fusion
  141.5 2.7 %all-to-all-done = f32[4,2,8,256]{3,2,1,0:T(8,128)S(1)} async-done(((f32[4,2,8,256]{3,2,1,0:T(8,128)}), f32[4,2,8,256]{3,2,1,0:T(8,128)S(1)}, u32[]{:S(2)}, u32[]{:S(2)}) %all-to-all-start) | async-done | bytes 65568 | tf_op jit(solution)/shard_map/all_to_all | solution.py:94
  144.4 0.3 copy.105
  144.7 1.6 gather_fusion
  146.7 1.0 broadcast_in_dim.103
  147.7 11.9 %all-to-all-start.1 = ((f32[128,2,560]{2,1,0:T(2,128)}), f32[128,2,560]{2,1,0:T(2,128)}, u32[]{:S(2)}, u32[]{:S(2)}) async-start(f32[128,2,560]{2,1,0:T(2,128)} %broadcast_in_dim.103), calls=%async_computation.1 | async-start | bytes 1310720 | tf_op jit(solution)/shard_map/all_to_all | solution.py:128
  159.6 0.6 iota_compare_fusion.4
  160.3 3.5 %constant_dynamic-slice_fusion.3 = (bf16[2,1,256,8,69]{4,3,2,1,0:T(8,128)(2,1)S(1)}, bf16[2,1,256,8,69]{4,3,2,1,0:T(8,128)(2,1)S(1)}, bf16[2,1,256,8,69]{4,3,2,1,0:T(8,128)(2,1)S(1)}, bf16[2,1,256,8,69]{4,3,2,1,0:T(8,128)(2,1)}) fusion(bf16[2,4,256,8,69]{4,3,2,1,0:T(8,128)(2,1)} %bitcast.112, s32[]{:T(128)S(6)} %select_n.86, s32[]{:T(128)S(6)} %select_n.90, ...), kind=kLoop, calls=%fused_computation.113 | loop fusion | bytes 4522000 | tf_op jit(solution)/shard_map/jit(dynamic_index_in_dim)/dynamic_slice | solution.py:96
  163.8 2.7 %copy.110 = bf16[2,1,256,8,69]{2,3,4,1,0:T(8,128)(2,1)} copy(bf16[2,1,256,8,69]{4,3,2,1,0:T(8,128)(2,1)} %get-tuple-element.12) | data formatting | bytes 1130496
  166.5 1.1 collective-permute-start.4
  167.6 1.6 copy.108
  169.3 0.6 collective-permute-start.2
  169.9 0.9 copy.109
  170.8 1.5 collective-permute-start.3
  172.3 0.9 copy.107
  173.3 0.5 all-to-all-done.1
  173.7 1.5 reshape.166
  175.3 0.3 fusion.75
  175.8 2.8 %gather_fusion.1 = f32[1024,2]{1,0:T(8,128)S(1)} fusion(f32[2,560]{0,1:T(8,128)S(1)} %copy.89, s32[1024]{0:T(1024)S(1)} %broadcast_clamp_fusion), kind=kCustom, calls=%fused_computation.1 | custom fusion | bytes 20480 | tf_op jit(solution)/shard_map/gather | solution.py:138
  178.6 0.3 copy.106
  178.9 0.8 multiply_reduce_fusion
  179.7 0.2 fusion.43
  182.9 0.7 gather_fusion.2
  183.6 10.6 %collective-permute-done.3 = bf16[2,256,8,69]{1,2,3,0:T(8,128)(2,1)} collective-permute-done((bf16[2,256,8,69]{1,2,3,0:T(8,128)(2,1)S(1)}, bf16[2,256,8,69]{1,2,3,0:T(8,128)(2,1)}, u32[]{:S(2)}, u32[]{:S(2)}) %collective-permute-start.3) | collective-permute-done | bytes 565280 | tf_op jit(solution)/shard_map/ppermute | solution.py:100
  194.2 3.9 %fusion.29 = f32[32,69,2,256]{3,0,1,2:T(8,128)S(1)} fusion(pred[2,2]{0,1:T(4,128)(4,1)} %iota_compare_fusion.4, f32[2,4,8,32]{3,0,2,1:T(2,128)S(1)} %bitcast.123, pred[4,8]{1,0:T(4,128)(4,1)} %compare_and_fusion, bf16[1,2,256,8,69]{2,3,4,1,0:T(8,128)(2,1)} %bitcast.10, bf16[1,2,256,8,69]{2,3,4,1,0:T(8,128)(2,1)} %bitcast.8, ...), kind=kOutput, calls=%fused_computation.37 | convolution fusion | flops 440895488 | bytes 6791204 | tf_op jit(solution)/shard_map/ajnm,jailnc->mcil/dot_general | solution.py:172
  198.2 5.6 %copy.93 = f32[32,69,2,256]{3,2,1,0:T(2,128)} copy(f32[32,69,2,256]{3,0,1,2:T(8,128)S(1)} %fusion.29) | data formatting | bytes 9043968 | tf_op jit(solution)/shard_map/ajnm,jailnc->mcil/transpose | solution.py:172
  (78 shorter events, 4.0 us)
Async XLA Ops:
  0.0 68.0 %copy-start = (bf16[3,3,256,69]{2,3,1,0:T(8,128)(2,1)S(1)}, bf16[3,3,256,69]{2,3,1,0:T(8,128)(2,1)}, u32[]{:S(2)}) copy-start(bf16[3,3,256,69]{2,3,1,0:T(8,128)(2,1)} %param.15) | copy-start | bytes 953860
  0.0 22.6 %copy-start.10 = (s32[528]{0:T(1024)S(1)}, s32[528]{0:T(1024)}, u32[]{:S(2)}) copy-start(s32[528]{0:T(1024)} %constant.160) | copy-start | bytes 6340
  0.0 16.7 %copy-start.11 = (s32[2,256]{1,0:T(2,128)S(1)}, s32[2,256]{1,0:T(2,128)}, u32[]{:S(2)}) copy-start(s32[2,256]{1,0:T(2,128)} %param.19) | copy-start | bytes 6148
  2.4 52.2 %collective-permute-start = (bf16[2,1024,8,69]{1,2,3,0:T(8,128)(2,1)S(1)}, bf16[2,1024,8,69]{1,2,3,0:T(8,128)(2,1)}, u32[]{:S(2)}, u32[]{:S(2)}) collective-permute-start(bf16[2,1024,8,69]{1,2,3,0:T(8,128)(2,1)S(1)} %bitcast.114), channel_id=1, source_target_pairs={{0,1},{1,2},{2,3},{3,4},{4,5},{5,6},{6,7},{7,8},{8,9},{9,10},{10,1... | collective-permute-start | bytes 6782984 | tf_op jit(solution)/shard_map/ppermute | solution.py:22
  8.2 53.2 %collective-permute-start.1 = (bf16[2,1024,8,69]{1,2,3,0:T(8,128)(2,1)S(1)}, bf16[2,1024,8,69]{1,2,3,0:T(8,128)(2,1)}, u32[]{:S(2)}, u32[]{:S(2)}) collective-permute-start(bf16[2,1024,8,69]{1,2,3,0:T(8,128)(2,1)S(1)} %bitcast.115), channel_id=1, source_target_pairs={{1,0},{2,1},{3,2},{4,3},{5,4},{6,5},{7,6},{8,7},{9,8},{10,9},{11,1... | collective-permute-start | bytes 6782984 | tf_op jit(solution)/shard_map/ppermute | solution.py:24
  16.5 51.5 %copy-start.17 = (f32[256]{0:T(256)S(1)}, f32[256]{0:T(256)}, u32[]{:S(2)}) copy-start(f32[256]{0:T(256)} %param.16) | copy-start | bytes 3076
  68.0 40.6 %copy-start.2 = (bf16[8,69,2,1024]{1,0,3,2:T(8,128)(2,1)S(1)}, bf16[8,69,2,1024]{1,0,3,2:T(8,128)(2,1)}, u32[]{:S(2)}) copy-start(bf16[8,69,2,1024]{1,0,3,2:T(8,128)(2,1)} %copy.75) | copy-start | bytes 6782980
  68.0 40.6 %copy-start.16 = (bf16[3,3,69,256]{3,2,1,0:T(8,128)(2,1)S(1)}, bf16[3,3,69,256]{3,2,1,0:T(8,128)(2,1)}, u32[]{:S(2)}) copy-start(bf16[3,3,69,256]{3,2,1,0:T(8,128)(2,1)} %param.17) | copy-start | bytes 953860
  68.1 40.6 %copy-start.18 = (f32[69]{0:T(128)S(1)}, f32[69]{0:T(128)}, u32[]{:S(2)}) copy-start(f32[69]{0:T(128)} %param.18) | copy-start | bytes 832
  108.6 25.0 %copy-start.4 = (f32[4,2,69,256]{3,2,1,0:T(8,128)S(1)}, f32[4,2,69,256]{3,2,1,0:T(8,128)}, u32[]{:S(2)}) copy-start(f32[4,2,69,256]{3,2,1,0:T(8,128)} %fusion.45) | copy-start | bytes 1695748
  108.6 25.0 %copy-start.8 = (s32[4,2,256]{2,1,0:T(2,128)S(1)}, s32[4,2,256]{2,1,0:T(2,128)}, u32[]{:S(2)}) copy-start(s32[4,2,256]{2,1,0:T(2,128)} %get-tuple-element.13) | copy-start | bytes 24580
  131.6 2.0 copy-start.1
  131.6 9.4 %copy-start.15 = (s32[32]{0:T(128)S(1)}, s32[32]{0:T(128)}, u32[]{:S(2)}) copy-start(s32[32]{0:T(128)} %fusion.69) | copy-start | bytes 388
  131.6 12.6 %copy-start.7 = (f32[2,256]{1,0:T(2,128)S(1)}, f32[2,256]{1,0:T(2,128)}, u32[]{:S(2)}) copy-start(f32[2,256]{1,0:T(2,128)} %param.21) | copy-start | bytes 6148
  131.6 12.6 %copy-start.12 = (f32[2,256]{1,0:T(2,128)S(1)}, f32[2,256]{1,0:T(2,128)}, u32[]{:S(2)}) copy-start(f32[2,256]{1,0:T(2,128)} %param.20) | copy-start | bytes 6148
  131.6 13.1 %copy-start.6 = (s32[1024]{0:T(1024)S(1)}, s32[1024]{0:T(1024)}, u32[]{:S(2)}) copy-start(s32[1024]{0:T(1024)} %pad_clamp_fusion.1) | copy-start | bytes 12292
  131.6 28.6 %copy-start.13 = (f32[2,8]{1,0:T(2,128)S(1)}, f32[2,8]{1,0:T(2,128)}, u32[]{:S(2)}) copy-start(f32[2,8]{1,0:T(2,128)} %param.23) | copy-start | bytes 196
  131.7 28.6 %copy-start.14 = (s32[2,8]{1,0:T(2,128)S(1)}, s32[2,8]{1,0:T(2,128)}, u32[]{:S(2)}) copy-start(s32[2,8]{1,0:T(2,128)} %param.22) | copy-start | bytes 196
  131.7 28.6 %copy-start.9 = (s32[1024]{0:T(1024)S(1)}, s32[1024]{0:T(1024)}, u32[]{:S(2)}) copy-start(s32[1024]{0:T(1024)} %constant.161) | copy-start | bytes 12292
  136.2 8.1 %all-to-all-start = ((f32[4,2,8,256]{3,2,1,0:T(8,128)}), f32[4,2,8,256]{3,2,1,0:T(8,128)S(1)}, u32[]{:S(2)}, u32[]{:S(2)}) async-start(f32[4,2,8,256]{3,2,1,0:T(8,128)} %fusion.21), calls=%async_computation | async-start | bytes 131072 | tf_op jit(solution)/shard_map/all_to_all | solution.py:94
  147.7 26.0 %all-to-all-start.1 = ((f32[128,2,560]{2,1,0:T(2,128)}), f32[128,2,560]{2,1,0:T(2,128)}, u32[]{:S(2)}, u32[]{:S(2)}) async-start(f32[128,2,560]{2,1,0:T(2,128)} %broadcast_in_dim.103), calls=%async_computation.1 | async-start | bytes 1310720 | tf_op jit(solution)/shard_map/all_to_all | solution.py:128
  160.3 19.4 %copy-start.3 = (f32[32,32]{1,0:T(8,128)S(1)}, f32[32,32]{1,0:T(8,128)}, u32[]{:S(2)}) copy-start(f32[32,32]{1,0:T(8,128)} %fusion.62) | copy-start | bytes 12292
  160.3 19.4 %copy-start.5 = (f32[32,32]{1,0:T(8,128)S(1)}, f32[32,32]{1,0:T(8,128)}, u32[]{:S(2)}) copy-start(f32[32,32]{1,0:T(8,128)} %fusion.61) | copy-start | bytes 12292
  166.5 17.1 %collective-permute-start.4 = (bf16[2,256,8,69]{1,2,3,0:T(8,128)(2,1)}, bf16[2,256,8,69]{1,2,3,0:T(8,128)(2,1)}, u32[]{:S(2)}, u32[]{:S(2)}) collective-permute-start(bf16[2,256,8,69]{1,2,3,0:T(8,128)(2,1)} %bitcast.117), channel_id=1, source_target_pairs={{0,96},{32,0},{64,32},{96,64},{1,97},{33,1},{65,33},{97,65},{2,98}... | collective-permute-start | bytes 1695752 | tf_op jit(solution)/shard_map/ppermute | solution.py:100
  169.3 14.4 %collective-permute-start.2 = (bf16[2,256,8,69]{1,2,3,0:T(8,128)(2,1)}, bf16[2,256,8,69]{1,2,3,0:T(8,128)(2,1)}, u32[]{:S(2)}, u32[]{:S(2)}) collective-permute-start(bf16[2,256,8,69]{1,2,3,0:T(8,128)(2,1)} %bitcast.119), channel_id=1, source_target_pairs={{0,32},{32,64},{64,96},{96,0},{1,33},{33,65},{65,97},{97,1},{2,34}... | collective-permute-start | bytes 1695752 | tf_op jit(solution)/shard_map/ppermute | solution.py:100
  170.8 23.4 %collective-permute-start.3 = (bf16[2,256,8,69]{1,2,3,0:T(8,128)(2,1)S(1)}, bf16[2,256,8,69]{1,2,3,0:T(8,128)(2,1)}, u32[]{:S(2)}, u32[]{:S(2)}) collective-permute-start(bf16[2,256,8,69]{1,2,3,0:T(8,128)(2,1)S(1)} %bitcast.120), channel_id=1, source_target_pairs={{0,64},{32,96},{64,0},{96,32},{1,65},{33,97},{65,1},{97,33},{2,66}... | collective-permute-start | bytes 1695752 | tf_op jit(solution)/shard_map/ppermute | solution.py:100
